TPU v7x, 32 devices: a whole 2x2x4 slice. The times are simulated.
32 devices in a mesh: users: 16 (over z, y, core), items: 2 (over x).
Axes of the slice: x: 2, y: 2, z: 4, core: 2. Of those that a mesh axis runs over, the one named last changes fastest.
Arguments:
- ratings: bfloat16 [64, 6, 128, 128], P('users', 'items')
- residual: bfloat16 [64, 6, 128, 128], P('users', 'items')
- tile_columns: int32 [64, 6], P('users', 'items'), may hold values from 0 to 2, as said below
- occupied: int32 [64, 6], P('users', 'items'), may hold values from 0 to 1, as said below
- chosen: int32 [64], P('users'), may hold values from 0 to 1, as said below
- user_factors: bfloat16 [64, 8192], P(None, 'users'), may hold values from -5 to 5
- item_factors: bfloat16 [2, 64, 384], P('items'), may hold values from -5 to 5
- start_block: bfloat16 [2, 32, 384], P('items'), may hold values from -0.5 to 0.5
Outputs:
- updated: bfloat16 [64, 6, 128, 128], P('users', 'items')
- left_block: float32 [32, 8192], P(None, 'users')
- right_block: float32 [2, 32, 384], P('items')
Inputs may be any that keep to these rules, and one draw needn't show every extreme that they name: `tile_columns`: within one tile row and one item block the 3 slots name different tile columns. Within one tile row and one item block the occupied slots come first, at least one is occupied, and some tile rows have all 3 occupied. Exactly 16 tile rows are chosen.
All inputs are finite; a program needn't handle non-finite values.
Results may differ from a plain program's by a relative error of at most 0.0033.
Values sent between devices are 32-bit elements; how exact they have to be, the bound alone decides.
No kernel may reach another device: no remote copies, remote signals or barrier semaphores. Data moves between devices by JAX's collectives and lax.ppermute only.
A program may use at most 64 MiB of HBM per device.

v0:
```python
import jax
import jax.numpy as jnp
from jax import lax
from jax.sharding import PartitionSpec as P


def local(
    ratings, residual, tile_columns, occupied, chosen, user_factors, item_factors, start_block
):
    rows_dev = ratings.shape[0]
    width = ratings.shape[2]
    rank_size = user_factors.shape[0]
    block_size = start_block.shape[1]
    item_count = item_factors.shape[2] // width
    user_total = user_factors.shape[1] * lax.axis_size("users")
    root = float(user_total) ** 0.5
    item_tiles = item_factors[0].reshape(rank_size, item_count, width)
    factors = jnp.take(item_tiles, tile_columns, axis=1)
    user_tiles = user_factors.reshape(rank_size, rows_dev, width)
    estimate = jnp.einsum("rta,rtkb->tkab", user_tiles, factors, preferred_element_type=jnp.float32)
    live_slot = (occupied > 0)[:, :, None, None]
    selected = live_slot & (chosen > 0)[:, None, None, None]
    updated = jnp.where(
        selected, ratings.astype(jnp.float32) - estimate, residual.astype(jnp.float32)
    )
    updated = jnp.where(live_slot, updated, jnp.float32(0.0)).astype(jnp.bfloat16)
    start_tiles = jnp.take(
        start_block[0].reshape(block_size, item_count, width), tile_columns, axis=1
    )
    partial_products = jnp.einsum(
        "tkab,jtkb->jta", updated, start_tiles, preferred_element_type=jnp.float32
    )
    partial_products = partial_products.reshape(block_size, rows_dev * width)
    share = lax.psum_scatter(partial_products, "items", scatter_dimension=1, tiled=True)
    gram_part = jnp.dot(share, share.T, precision=lax.Precision.HIGHEST)
    gram = lax.psum(gram_part, ("users", "items")) / user_total
    lower = jnp.linalg.cholesky(gram)
    left_share = jax.scipy.linalg.solve_triangular(lower, share, lower=True)
    left_block = lax.all_gather(left_share, "items", axis=1, tiled=True)
    left_rounded = left_block.astype(jnp.bfloat16).reshape(block_size, rows_dev, width)
    slot_terms = jnp.einsum(
        "tkab,jta->jtkb", updated, left_rounded, preferred_element_type=jnp.float32
    )
    one_hot = (
        tile_columns[:, :, None] == jnp.arange(item_count, dtype=jnp.int32)[None, None, :]
    ).astype(jnp.float32)
    item_terms = jnp.einsum("jtkb,tkc->jcb", slot_terms, one_hot, precision=lax.Precision.HIGHEST)
    item_terms = item_terms.reshape(1, block_size, item_count * width)
    summed = lax.psum(item_terms, "users")
    start_term = jnp.einsum(
        "ji,bjn->bin", lower, start_block.astype(jnp.float32), precision=lax.Precision.HIGHEST
    )
    right_block = summed / root - root * start_term
    return (updated, left_block, right_block)


def solution(mesh):
    placed = (
        P("users", "items", None, None),
        P("users", "items", None, None),
        P("users", "items"),
        P("users", "items"),
        P("users"),
        P(None, "users"),
        P("items", None, None),
        P("items", None, None),
    )
    return jax.shard_map(
        local,
        mesh=mesh,
        in_specs=placed,
        out_specs=(P("users", "items", None, None), P(None, "users"), P("items", None, None)),
        check_vma=False,
    )
```

profile of v0, /device:TPU:0, one launch (start us, length us, event | category | flops | bytes accessed | tf_op | source)
XLA Modules:
  0.0 148.7 jit_solution(266476572557245708)
XLA Ops:
  7.2 0.0 reduce-scatter.2.cloned.1.call-start
  7.2 0.7 broadcast_compare_fusion.1
  7.9 0.7 compare_select_fusion
  8.6 0.1 reshape.53
  8.6 0.8 reshape_squeeze.6
  9.5 0.0 copy-start
  9.5 1.3 copy.21
  10.8 0.0 copy-done
  10.8 0.0 copy-start.3
  10.8 0.2 copy.24
  11.0 0.6 copy-done.3
  11.6 0.0 copy-start.2
  11.6 0.7 copy-done.2
  12.4 0.6 gather_fusion
  13.0 0.0 copy-start.4
  13.0 0.0 copy-start.5
  13.0 0.6 gather_fusion.1
  13.6 0.1 copy-done.4
  13.7 0.0 copy-done.5
  13.7 0.1 broadcast_and_fusion
  13.8 0.5 fusion.3
  14.2 0.2 convolution_bitcast_fusion.2
  14.5 0.6 copy.51
  15.1 0.0 reduce-scatter.2.cloned.1.call-update
  15.1 0.1 copy.30
  15.2 0.9 copy.31
  16.1 11.7 %reduce-scatter.2.cloned.1.call-done = f32[32,256]{1,0:T(8,128)} async-done(((f32[32,512]{1,0:T(8,128)}), f32[32,256]{1,0:T(8,128)}) %reduce-scatter.2.cloned.1.call-update) | async-done | bytes 32784 | tf_op jit(solution)/shard_map/reduce_scatter | solution.py:34
  27.9 1.0 fusion.33
  28.9 39.5 %psum.14 = f32[32,32]{0,1:T(8,128)S(1)} all-reduce(f32[32,32]{0,1:T(8,128)S(1)} %fusion.33), channel_id=1, replica_groups=mesh['users'=16,'items'=2] {'users','items'}, use_global_device_ids=true, to_apply=%region_1.2 | all-reduce | flops 1024 | bytes 8192 | tf_op jit(solution)/shard_map/psum | solution.py:36
  68.3 0.1 copy.29
  68.4 0.0 copy-start.1
  68.4 2.9 %cholesky.16 = f32[32,32]{1,0:T(8,128)S(1)} custom-call(f32[32,32]{1,0:T(8,128)S(1)} %fusion.22), custom_call_target="Cholesky" | custom-call | tf_op jit(solution)/shard_map/jit(cholesky)/cholesky | solution.py:37
  71.3 0.6 compare_reduce_fusion
  72.0 0.7 select_bitcast_fusion
  72.7 2.4 %custom-call.7 = f32[1,32,32]{1,2,0:T(8,128)S(1)} custom-call(f32[1,32,32]{2,1,0:T(8,128)S(1)} %select_bitcast_fusion), custom_call_target="InvertDiagBlocksLowerTriangular" | custom-call | tf_op jit(solution)/shard_map/jit(_solve_triangular)/triangular_solve | solution.py:38
  75.1 0.0 copy-done.1
  75.1 0.2 fusion.20
  75.3 4.8 %all_gather.3 = f32[32,512]{1,0:T(8,128)S(1)} all-gather(f32[32,256]{1,0:T(8,128)S(1)} %fusion.20), channel_id=1, replica_groups=mesh['users'=16,'items'=2] {'items'}, dimensions={1}, use_global_device_ids=true | all-gather | bytes 98304 | tf_op jit(solution)/shard_map/all_gather | solution.py:39
  80.2 0.2 fusion.17
  80.4 0.4 convolution_bitcast_fusion.1
  80.9 58.8 %psum.15 = f32[1,32,384]{2,1,0:T(8,128)S(1)} all-reduce(f32[1,32,384]{2,1,0:T(8,128)S(1)} %reshape.49), channel_id=1, replica_groups=mesh['users'=16,'items'=2] {'users'}, use_global_device_ids=true, to_apply=%region_4.5 | all-reduce | flops 12288 | bytes 98304 | tf_op jit(solution)/shard_map/psum | solution.py:49
  139.7 1.5 %fusion.5 = f32[1,32,384]{2,1,0:T(8,128)} fusion(f32[1,32,384]{2,1,0:T(8,128)S(1)} %psum.15, bf16[1,32,384]{2,1,0:T(8,128)(2,1)S(1)} %copy-done.2, f32[32,32]{1,0:T(8,128)S(1)} %cholesky.16, pred[]{:T(512)} %compare_reduce_fusion), kind=kOutput, calls=%fused_computation.11 | convolution fusion | flops 4758528 | bytes 126977 | tf_op jit(solution)/shard_map/ji,bjn->bin/dot_general | solution.py:50
  141.2 0.6 copy.53
  (11 shorter events, 0.2 us)
Async XLA Ops:
  7.2 20.7 %reduce-scatter.2.cloned.1.call-start = ((), (), s32[]{:S(2)}) async-start(), calls=%async_computation.1 | async-start | bytes 98304 | tf_op jit(solution)/shard_map/reduce_scatter | solution.py:34
  9.5 1.3 copy-start
  10.8 0.8 copy-start.3
  11.6 0.7 copy-start.2
  13.0 0.7 copy-start.4
  13.0 0.7 copy-start.5
  68.4 6.7 %copy-start.1 = (f32[32,256]{1,0:T(8,128)S(1)}, f32[32,256]{1,0:T(8,128)}, u32[]{:S(2)}) copy-start(f32[32,256]{1,0:T(8,128)} %reduce-scatter.2.cloned.1.call-done) | copy-start | bytes 98308
Sparse Core Ops, SparseCore 0:
  15.2 12.5 reduce-scatter.1
where the time goes:
time: 149 us
  blocking collectives  103 us (69%)
  between operations  14.2 us (10%)
  waiting for transfers between devices  11.7 us (8%)
  other arithmetic  8.12 us (5%)
  local copies, waits for them, and re-layouts  7.45 us (5%)
  matrix products  4.09 us (3%)
    psum x1, blocking collectives, local(): summed = lax.psum(item_terms, 'users')  58.8 us
    psum x1, blocking collectives, local(): gram = lax.psum(gram_part, ('users', 'items')) / user_total  39.5 us
    reduce_scatter x1, waiting for transfers between devices, local(): lax.psum_scatter(partial_products, 'items', scatter_dimension=1, tiled=True)  11.7 us
    all_gather x1, blocking collectives, local(): left_block = lax.all_gather(left_share, 'items', axis=1, tiled=True)  4.82 us
    unnamed x17, local copies, waits for them, and re-layouts  4.58 us
    another operation x3, other arithmetic, local(): lower = jnp.linalg.cholesky(gram)  3.59 us
    another operation x2, other arithmetic, local(): left_share = jax.scipy.linalg.solve_triangular(lower, share, lower=True)  3.09 us
  transfers between devices with their start and end apart: 1, of which 1 were waited for; matrix products, arithmetic and copies ran while one was open for 1% of the time, Pallas kernels for 0%

commit v1 on v0

--- a/solution.py
+++ b/solution.py
@@ -2,6 +2,17 @@
 import jax.numpy as jnp
 from jax import lax
 from jax.sharding import PartitionSpec as P
+
+
+def all_sum(x, axis):
+    n = lax.axis_size(axis)
+    if n & (n - 1):
+        return lax.psum(x, axis)
+    step = 1
+    while step < n:
+        x = x + lax.ppermute(x, axis, [(i, i ^ step) for i in range(n)])
+        step *= 2
+    return x
 
 
 def local(
@@ -30,23 +41,27 @@
     partial_products = jnp.einsum(
         "tkab,jtkb->jta", updated, start_tiles, preferred_element_type=jnp.float32
     )
-    partial_products = partial_products.reshape(block_size, rows_dev * width)
-    share = lax.psum_scatter(partial_products, "items", scatter_dimension=1, tiled=True)
-    gram_part = jnp.dot(share, share.T, precision=lax.Precision.HIGHEST)
-    gram = lax.psum(gram_part, ("users", "items")) / user_total
-    lower = jnp.linalg.cholesky(gram)
-    left_share = jax.scipy.linalg.solve_triangular(lower, share, lower=True)
-    left_block = lax.all_gather(left_share, "items", axis=1, tiled=True)
-    left_rounded = left_block.astype(jnp.bfloat16).reshape(block_size, rows_dev, width)
+    projected = all_sum(partial_products.reshape(block_size, rows_dev * width), "items")
+    gram_part = jnp.dot(projected, projected.T, precision=lax.Precision.HIGHEST)
     slot_terms = jnp.einsum(
-        "tkab,jta->jtkb", updated, left_rounded, preferred_element_type=jnp.float32
+        "jta,tkab->jtkb",
+        projected.reshape(block_size, rows_dev, width),
+        updated.astype(jnp.float32),
+        precision=lax.Precision.HIGHEST,
     )
     one_hot = (
         tile_columns[:, :, None] == jnp.arange(item_count, dtype=jnp.int32)[None, None, :]
     ).astype(jnp.float32)
     item_terms = jnp.einsum("jtkb,tkc->jcb", slot_terms, one_hot, precision=lax.Precision.HIGHEST)
-    item_terms = item_terms.reshape(1, block_size, item_count * width)
-    summed = lax.psum(item_terms, "users")
+    item_terms = item_terms.reshape(block_size, item_count * width)
+    reduced = all_sum(jnp.concatenate([gram_part, item_terms], axis=1), "users")
+    gram = reduced[:, :block_size] / user_total
+    lower = jnp.linalg.cholesky(gram)
+    solved = jax.scipy.linalg.solve_triangular(
+        lower, jnp.concatenate([projected, reduced[:, block_size:]], axis=1), lower=True
+    )
+    left_block = solved[:, : rows_dev * width]
+    summed = solved[:, rows_dev * width :].reshape(1, block_size, item_count * width)
     start_term = jnp.einsum(
         "ji,bjn->bin", lower, start_block.astype(jnp.float32), precision=lax.Precision.HIGHEST
     )

time: 149 us -> 51.9 us (0.35)
  blocking collectives: 103 us -> 0 us
  between operations: 14.2 us -> 0.85 us
  waiting for transfers between devices: 11.7 us -> 22.1 us
  starting transfers between devices: 0.04 us -> 9.61 us
    psum x2 -> x0, blocking collectives: 98.2 us -> none  [the longest x1 58.8 us: local(): summed = lax.psum(item_terms, 'users')]
    ppermute x0 -> x5, waiting for transfers between devices: none -> 22.1 us  [all_sum(): x = x + lax.ppermute(x, axis, [(i, i ^ step) for i in range(n)])]
    reduce_scatter x1 -> x0, waiting for transfers between devices: 11.7 us -> none  [local(): lax.psum_scatter(partial_products, 'items', scatter_dimension=1, tiled=True)]
    ppermute x0 -> x5, starting transfers between devices: none -> 9.61 us  [all_sum(): x = x + lax.ppermute(x, axis, [(i, i ^ step) for i in range(n)])]
    all_gather x1 -> x0, blocking collectives: 4.82 us -> none  [local(): left_block = lax.all_gather(left_share, 'items', axis=1, tiled=True)]
    unnamed x17 -> x15, local copies, waits for them, and re-layouts: 4.58 us -> 3.95 us
  transfers between devices with their start and end apart: 1 -> 5, of which waited for: 1 -> 5; matrix products, arithmetic and copies ran while one was open for 1% -> 2% of each run, Pallas kernels for 0% -> 0%
where the time goes in v1:
time: 51.9 us; the launch traced here: 51.5 us
  waiting for transfers between devices  22.1 us (43%)
  starting transfers between devices  9.61 us (19%)
  other arithmetic  8.31 us (16%)
  local copies, waits for them, and re-layouts  7.06 us (14%)
  matrix products  3.63 us (7%)
  between operations  0.85 us (2%)
    ppermute x5, waiting for transfers between devices, all_sum(): x = x + lax.ppermute(x, axis, [(i, i ^ step) for i in range(n)])  22.1 us
    ppermute x5, starting transfers between devices, all_sum(): x = x + lax.ppermute(x, axis, [(i, i ^ step) for i in range(n)])  9.61 us
    unnamed x15, local copies, waits for them, and re-layouts  3.95 us
    another operation x3, other arithmetic, local(): lower = jnp.linalg.cholesky(gram)  3.6 us
    another operation x2, other arithmetic, local(): jax.scipy.linalg.solve_triangular(lower, jnp.concatenate([projected, redu...  3.09 us
    dot_general x1, matrix products, local(): jnp.einsum('ji,bjn->bin', lower, start_block.astype(jnp.float32), precisi...  1.49 us
  transfers between devices with their start and end apart: 5, of which 5 were waited for; matrix products, arithmetic and copies ran while one was open for 2% of the time, Pallas kernels for 0%

profile of v1, /device:TPU:0, one launch (start us, length us, event | category | flops | bytes accessed | tf_op | source)
XLA Modules:
  0.0 51.5 jit_solution(9520328725908842933)
XLA Ops:
  0.6 0.7 %broadcast_compare_fusion.1 = pred[4]{0:T(512)(128)(4,1)S(1)} fusion(s32[4]{0:T(128)} %param.12), kind=kLoop, calls=%fused_computation.55 | loop fusion | flops 4 | bytes 20 | tf_op jit(solution)/shard_map/gt | solution.py:33
  1.3 0.7 %compare_select_fusion = s32[4,3]{1,0:T(4,128)S(1)} fusion(s32[4,3]{1,0:T(4,128)} %param.10), kind=kLoop, calls=%fused_computation.48 | loop fusion | flops 36 | bytes 96 | tf_op jit(solution)/shard_map/jit(_take)/jit(_where)/select_n | solution.py:29
  2.0 0.1 reshape.55
  2.1 0.8 %reshape_squeeze.6 = bf16[64,3,128]{2,1,0:T(4,128)(2,1)S(1)} reshape(bf16[1,64,384]{2,1,0:T(8,128)(2,1)} %param.14) | data formatting | bytes 98304 | tf_op jit(solution)/shard_map/reshape;squeeze | solution.py:28
  2.9 0.0 copy-start
  2.9 1.3 %copy.52 = bf16[4,3,128,128]{2,3,1,0:T(8,128)(2,1)S(1)} copy(bf16[4,3,128,128]{3,2,1,0:T(8,128)(2,1)} %param.8) | data formatting | bytes 786432 | tf_op args[0]
  4.2 0.0 copy-done
  4.2 0.0 copy-start.2
  4.2 0.2 copy.55
  4.4 0.6 %copy-done.2 = bf16[64,512]{1,0:T(8,128)(2,1)S(1)} copy-done((bf16[64,512]{1,0:T(8,128)(2,1)S(1)}, bf16[64,512]{1,0:T(8,128)(2,1)}, u32[]{:S(2)}) %copy-start.2) | copy-done | bytes 65560
  5.0 0.0 copy-start.1
  5.1 0.7 %copy-done.1 = bf16[1,32,384]{2,1,0:T(8,128)(2,1)S(1)} copy-done((bf16[1,32,384]{2,1,0:T(8,128)(2,1)S(1)}, bf16[1,32,384]{2,1,0:T(8,128)(2,1)}, u32[]{:S(2)}) %copy-start.1) | copy-done | bytes 24600
  5.8 0.6 %gather_fusion = bf16[12,64,128]{2,1,0:T(8,128)(2,1)S(1)} fusion(bf16[64,3,128]{2,0,1:T(8,128)(2,1)S(1)} %copy.53, s32[1024]{0:T(1024)S(1)} %pad_clamp_fusion), kind=kCustom, calls=%fused_computation | custom fusion | bytes 393264 | tf_op jit(solution)/shard_map/jit(_take)/gather | solution.py:29
  6.4 0.0 copy-start.3
  6.4 0.0 copy-start.4
  6.4 0.6 %gather_fusion.1 = bf16[12,32,128]{2,1,0:T(8,128)(2,1)S(1)} fusion(bf16[32,3,128]{2,0,1:T(8,128)(2,1)S(1)} %copy.56, s32[1024]{0:T(1024)S(1)} %pad_clamp_fusion), kind=kCustom, calls=%fused_computation.1 | custom fusion | bytes 196656 | tf_op jit(solution)/shard_map/jit(_take)/gather | solution.py:38
  7.0 0.1 copy-done.3
  7.1 0.0 copy-done.4
  7.1 0.1 broadcast_and_fusion
  7.2 0.5 fusion.3
  7.6 0.2 convolution_bitcast_fusion.2
  7.9 3.0 %collective-permute-start = (f32[32,512]{1,0:T(8,128)S(1)}, f32[32,512]{1,0:T(8,128)S(1)}, u32[]{:S(2)}, u32[]{:S(2)}) collective-permute-start(f32[32,512]{1,0:T(8,128)S(1)} %bitcast.78), channel_id=1, source_target_pairs={{0,1},{1,0},{2,3},{3,2},{4,5},{5,4},{6,7},{7,6},{8,9},{9,8},{10,11... | collective-permute-start | bytes 196616 | tf_op jit(solution)/shard_map/ppermute | solution.py:13
  10.9 0.1 copy.59
  11.0 2.2 %collective-permute-done = f32[32,512]{1,0:T(8,128)S(1)} collective-permute-done((f32[32,512]{1,0:T(8,128)S(1)}, f32[32,512]{1,0:T(8,128)S(1)}, u32[]{:S(2)}, u32[]{:S(2)}) %collective-permute-start) | collective-permute-done | bytes 65568 | tf_op jit(solution)/shard_map/ppermute | solution.py:13
  13.2 0.2 fusion.38
  13.4 0.5 %convolution_bitcast_fusion.1 = f32[32,4,3,128]{3,0,2,1:T(8,128)S(1)} fusion(bf16[4,3,128,128]{2,3,1,0:T(8,128)(2,1)S(1)} %fusion.3, f32[32,4,128,1]{2,1,0,3:T(4,128)S(1)} %bitcast.74), kind=kOutput, calls=%fused_computation.7 | convolution fusion | flops 75497472 | bytes 655360 | tf_op jit(solution)/shard_map/jta,tkab->jtkb/dot_general | solution.py:46
  13.9 0.4 fusion.7
  14.4 0.1 pad_maximum_fusion
  14.4 0.1 copy.64
  14.6 0.1 collective-permute-start.1
  14.7 1.5 %collective-permute-done.1 = f32[32,416]{0,1:T(8,128)S(1)} collective-permute-done((f32[32,416]{0,1:T(8,128)S(1)}, f32[32,416]{0,1:T(8,128)S(1)}, u32[]{:S(2)}, u32[]{:S(2)}) %collective-permute-start.1) | collective-permute-done | bytes 53280 | tf_op jit(solution)/shard_map/ppermute | solution.py:13
  16.1 2.1 %collective-permute-start.2 = (f32[32,416]{0,1:T(8,128)S(1)}, f32[32,416]{0,1:T(8,128)S(1)}, u32[]{:S(2)}, u32[]{:S(2)}) collective-permute-start(f32[32,416]{0,1:T(8,128)S(1)} %add.35), channel_id=1, source_target_pairs={{0,4},{2,6},{4,0},{6,2},{8,12},{10,14},{12,8},{14,10},{16,20},{18,... | collective-permute-start | bytes 159752 | tf_op jit(solution)/shard_map/ppermute | solution.py:13
  18.3 5.6 %collective-permute-done.2 = f32[32,416]{0,1:T(8,128)S(1)} collective-permute-done((f32[32,416]{0,1:T(8,128)S(1)}, f32[32,416]{0,1:T(8,128)S(1)}, u32[]{:S(2)}, u32[]{:S(2)}) %collective-permute-start.2) | collective-permute-done | bytes 53280 | tf_op jit(solution)/shard_map/ppermute | solution.py:13
  23.8 1.9 %collective-permute-start.3 = (f32[32,416]{0,1:T(8,128)S(1)}, f32[32,416]{0,1:T(8,128)S(1)}, u32[]{:S(2)}, u32[]{:S(2)}) collective-permute-start(f32[32,416]{0,1:T(8,128)S(1)} %add.36), channel_id=1, source_target_pairs={{0,8},{2,10},{4,12},{6,14},{8,0},{10,2},{12,4},{14,6},{16,24},{18,... | collective-permute-start | bytes 159752 | tf_op jit(solution)/shard_map/ppermute | solution.py:13
  25.7 5.0 %collective-permute-done.3 = f32[32,416]{0,1:T(8,128)S(1)} collective-permute-done((f32[32,416]{0,1:T(8,128)S(1)}, f32[32,416]{0,1:T(8,128)S(1)}, u32[]{:S(2)}, u32[]{:S(2)}) %collective-permute-start.3) | collective-permute-done | bytes 53280 | tf_op jit(solution)/shard_map/ppermute | solution.py:13
  30.7 2.6 %collective-permute-start.4 = (f32[32,416]{0,1:T(8,128)S(1)}, f32[32,416]{0,1:T(8,128)S(1)}, u32[]{:S(2)}, u32[]{:S(2)}) collective-permute-start(f32[32,416]{0,1:T(8,128)S(1)} %add.37), channel_id=1, source_target_pairs={{0,16},{2,18},{4,20},{6,22},{8,24},{10,26},{12,28},{14,30},{16,0},... | collective-permute-start | bytes 159752 | tf_op jit(solution)/shard_map/ppermute | solution.py:13
  33.3 0.9 %copy.67 = bf16[4,3,128,128]{3,2,1,0:T(8,128)(2,1)} copy(bf16[4,3,128,128]{2,3,1,0:T(8,128)(2,1)S(1)} %fusion.3) | data formatting | bytes 786432
  34.2 7.9 %collective-permute-done.4 = f32[32,416]{0,1:T(8,128)S(1)} collective-permute-done((f32[32,416]{0,1:T(8,128)S(1)}, f32[32,416]{0,1:T(8,128)S(1)}, u32[]{:S(2)}, u32[]{:S(2)}) %collective-permute-start.4) | collective-permute-done | bytes 53280 | tf_op jit(solution)/shard_map/ppermute | solution.py:13
  42.2 0.1 copy.65
  42.3 2.9 %cholesky.16 = f32[32,32]{1,0:T(8,128)S(1)} custom-call(f32[32,32]{1,0:T(8,128)S(1)} %fusion.25), custom_call_target="Cholesky" | custom-call | tf_op jit(solution)/shard_map/jit(cholesky)/cholesky | solution.py:59
  45.2 0.6 %compare_reduce_fusion = pred[]{:T(512)} fusion(f32[32]{0:T(128)S(1)} %select_reduce_fusion), kind=kLoop, calls=%fused_computation.51 | loop fusion | flops 63 | bytes 129 | tf_op jit(solution)/shard_map/jit(cholesky)/cholesky | solution.py:59
  45.9 0.7 %select_bitcast_fusion = f32[1,32,32]{2,1,0:T(8,128)S(1)} fusion(f32[32,32]{1,0:T(8,128)S(1)} %cholesky.16, pred[]{:T(512)} %compare_reduce_fusion), kind=kLoop, calls=%fused_computation.38 | loop fusion | flops 4096 | bytes 8193 | tf_op jit(solution)/shard_map/jit(_solve_triangular)/triangular_solve | solution.py:60
  46.5 2.4 %custom-call.7 = f32[1,32,32]{1,2,0:T(8,128)S(1)} custom-call(f32[1,32,32]{2,1,0:T(8,128)S(1)} %select_bitcast_fusion), custom_call_target="InvertDiagBlocksLowerTriangular" | custom-call | tf_op jit(solution)/shard_map/jit(_solve_triangular)/triangular_solve | solution.py:60
  49.0 0.1 copy.66
  49.1 0.3 fusion.11
  49.4 1.5 %fusion.5 = f32[1,32,384]{2,1,0:T(8,128)} fusion(f32[32,896]{1,0:T(8,128)S(1)} %fusion.11, bf16[1,32,384]{2,1,0:T(8,128)(2,1)S(1)} %copy-done.1, f32[32,32]{1,0:T(8,128)S(1)} %cholesky.16, pred[]{:T(512)} %compare_reduce_fusion), kind=kOutput, calls=%fused_computation.11 | convolution fusion | flops 4758528 | bytes 126977 | tf_op jit(solution)/shard_map/ji,bjn->bin/dot_general | solution.py:65
  50.9 0.6 %slice.34 = f32[32,512]{1,0:T(8,128)} slice(f32[32,896]{1,0:T(8,128)S(1)} %fusion.11), slice={[0:32], [0:512]} | slice | bytes 131072 | tf_op jit(solution)/shard_map/slice | solution.py:63
  (17 shorter events, 0.3 us)
Async XLA Ops:
  2.9 1.3 %copy-start = (bf16[4,3,128,128]{3,2,1,0:T(8,128)(2,1)S(1)}, bf16[4,3,128,128]{3,2,1,0:T(8,128)(2,1)}, u32[]{:S(2)}) copy-start(bf16[4,3,128,128]{3,2,1,0:T(8,128)(2,1)} %param.9) | copy-start | bytes 1179652
  4.2 0.8 %copy-start.2 = (bf16[64,512]{1,0:T(8,128)(2,1)S(1)}, bf16[64,512]{1,0:T(8,128)(2,1)}, u32[]{:S(2)}) copy-start(bf16[64,512]{1,0:T(8,128)(2,1)} %param.13) | copy-start | bytes 196612
  5.0 0.7 %copy-start.1 = (bf16[1,32,384]{2,1,0:T(8,128)(2,1)S(1)}, bf16[1,32,384]{2,1,0:T(8,128)(2,1)}, u32[]{:S(2)}) copy-start(bf16[1,32,384]{2,1,0:T(8,128)(2,1)} %param.15) | copy-start | bytes 73732
  6.4 0.7 %copy-start.3 = (s32[4,3]{1,0:T(4,128)S(1)}, s32[4,3]{1,0:T(4,128)}, u32[]{:S(2)}) copy-start(s32[4,3]{1,0:T(4,128)} %param.10) | copy-start | bytes 148
  6.4 0.7 %copy-start.4 = (s32[4,3]{1,0:T(4,128)S(1)}, s32[4,3]{1,0:T(4,128)}, u32[]{:S(2)}) copy-start(s32[4,3]{1,0:T(4,128)} %param.11) | copy-start | bytes 148
  7.9 5.2 %collective-permute-start = (f32[32,512]{1,0:T(8,128)S(1)}, f32[32,512]{1,0:T(8,128)S(1)}, u32[]{:S(2)}, u32[]{:S(2)}) collective-permute-start(f32[32,512]{1,0:T(8,128)S(1)} %bitcast.78), channel_id=1, source_target_pairs={{0,1},{1,0},{2,3},{3,2},{4,5},{5,4},{6,7},{7,6},{8,9},{9,8},{10,11... | collective-permute-start | bytes 196616 | tf_op jit(solution)/shard_map/ppermute | solution.py:13
  14.6 1.5 %collective-permute-start.1 = (f32[32,416]{0,1:T(8,128)S(1)}, f32[32,416]{0,1:T(8,128)S(1)}, u32[]{:S(2)}, u32[]{:S(2)}) collective-permute-start(f32[32,416]{0,1:T(8,128)S(1)} %copy.64), channel_id=1, source_target_pairs={{0,2},{2,0},{4,6},{6,4},{8,10},{10,8},{12,14},{14,12},{16,18},{18,... | collective-permute-start | bytes 159752 | tf_op jit(solution)/shard_map/ppermute | solution.py:13
  16.1 7.7 %collective-permute-start.2 = (f32[32,416]{0,1:T(8,128)S(1)}, f32[32,416]{0,1:T(8,128)S(1)}, u32[]{:S(2)}, u32[]{:S(2)}) collective-permute-start(f32[32,416]{0,1:T(8,128)S(1)} %add.35), channel_id=1, source_target_pairs={{0,4},{2,6},{4,0},{6,2},{8,12},{10,14},{12,8},{14,10},{16,20},{18,... | collective-permute-start | bytes 159752 | tf_op jit(solution)/shard_map/ppermute | solution.py:13
  23.8 6.8 %collective-permute-start.3 = (f32[32,416]{0,1:T(8,128)S(1)}, f32[32,416]{0,1:T(8,128)S(1)}, u32[]{:S(2)}, u32[]{:S(2)}) collective-permute-start(f32[32,416]{0,1:T(8,128)S(1)} %add.36), channel_id=1, source_target_pairs={{0,8},{2,10},{4,12},{6,14},{8,0},{10,2},{12,4},{14,6},{16,24},{18,... | collective-permute-start | bytes 159752 | tf_op jit(solution)/shard_map/ppermute | solution.py:13
  30.7 11.4 %collective-permute-start.4 = (f32[32,416]{0,1:T(8,128)S(1)}, f32[32,416]{0,1:T(8,128)S(1)}, u32[]{:S(2)}, u32[]{:S(2)}) collective-permute-start(f32[32,416]{0,1:T(8,128)S(1)} %add.37), channel_id=1, source_target_pairs={{0,16},{2,18},{4,20},{6,22},{8,24},{10,26},{12,28},{14,30},{16,0},... | collective-permute-start | bytes 159752 | tf_op jit(solution)/shard_map/ppermute | solution.py:13

commit v2 on v1

--- a/solution.py
+++ b/solution.py
@@ -54,11 +54,13 @@
     ).astype(jnp.float32)
     item_terms = jnp.einsum("jtkb,tkc->jcb", slot_terms, one_hot, precision=lax.Precision.HIGHEST)
     item_terms = item_terms.reshape(block_size, item_count * width)
-    reduced = all_sum(jnp.concatenate([gram_part, item_terms], axis=1), "users")
-    gram = reduced[:, :block_size] / user_total
+    payload = jnp.concatenate([gram_part.reshape(-1), item_terms.reshape(-1)])
+    reduced = all_sum(payload.reshape(-1, width), "users").reshape(-1)
+    gram = reduced[: block_size * block_size].reshape(block_size, block_size) / user_total
+    item_sums = reduced[block_size * block_size :].reshape(block_size, item_count * width)
     lower = jnp.linalg.cholesky(gram)
     solved = jax.scipy.linalg.solve_triangular(
-        lower, jnp.concatenate([projected, reduced[:, block_size:]], axis=1), lower=True
+        lower, jnp.concatenate([projected, item_sums], axis=1), lower=True
     )
     left_block = solved[:, : rows_dev * width]
     summed = solved[:, rows_dev * width :].reshape(1, block_size, item_count * width)

time: 51.9 us -> 39.9 us (0.77)
  waiting for transfers between devices: 22.1 us -> 8.79 us
  starting transfers between devices: 9.61 us -> 10.4 us
  local copies, waits for them, and re-layouts: 7.06 us -> 7.6 us
    ppermute x5, waiting for transfers between devices: 22.1 us -> 8.79 us  [all_sum(): x = x + lax.ppermute(x, axis, [(i, i ^ step) for i in range(n)])]
    ppermute x5, starting transfers between devices: 9.61 us -> 10.4 us  [all_sum(): x = x + lax.ppermute(x, axis, [(i, i ^ step) for i in range(n)])]
    unnamed x15 -> x16, local copies, waits for them, and re-layouts: 3.95 us -> 4.55 us
  transfers between devices with their start and end apart: 5 -> 5, of which waited for: 5 -> 5; matrix products, arithmetic and copies ran while one was open for 2% -> 3% of each run, Pallas kernels for 0% -> 0%
where the time goes in v2:
time: 39.9 us; the launch traced here: 39.5 us
  starting transfers between devices  10.4 us (26%)
  waiting for transfers between devices  8.79 us (22%)
  other arithmetic  8.27 us (21%)
  local copies, waits for them, and re-layouts  7.6 us (19%)
  matrix products  3.64 us (9%)
  between operations  0.85 us (2%)
    ppermute x5, starting transfers between devices, all_sum(): x = x + lax.ppermute(x, axis, [(i, i ^ step) for i in range(n)])  10.4 us
    ppermute x5, waiting for transfers between devices, all_sum(): x = x + lax.ppermute(x, axis, [(i, i ^ step) for i in range(n)])  8.79 us
    unnamed x16, local copies, waits for them, and re-layouts  4.55 us
    another operation x3, other arithmetic, local(): lower = jnp.linalg.cholesky(gram)  3.66 us
    another operation x2, other arithmetic, local(): jax.scipy.linalg.solve_triangular(lower, jnp.concatenate([projected, item...  3.12 us
    dot_general x1, matrix products, local(): jnp.einsum('ji,bjn->bin', lower, start_block.astype(jnp.float32), precisi...  1.53 us
    another operation x2, local copies, waits for them, and re-layouts, local(): item_tiles = item_factors[0].reshape(rank_size, item_count, width)  0.83 us
  transfers between devices with their start and end apart: 5, of which 5 were waited for; matrix products, arithmetic and copies ran while one was open for 3% of the time, Pallas kernels for 0%

profile of v2, /device:TPU:0, one launch (start us, length us, event | category | flops | bytes accessed | tf_op | source)
XLA Modules:
  0.0 39.5 jit_solution(3218945565904286477)
XLA Ops:
  0.6 0.7 %broadcast_compare_fusion.1 = pred[4]{0:T(512)(128)(4,1)S(1)} fusion(s32[4]{0:T(128)} %param.12), kind=kLoop, calls=%fused_computation.55 | loop fusion | flops 4 | bytes 20 | tf_op jit(solution)/shard_map/gt | solution.py:33
  1.3 0.7 %compare_select_fusion = s32[4,3]{1,0:T(4,128)S(1)} fusion(s32[4,3]{1,0:T(4,128)} %param.10), kind=kLoop, calls=%fused_computation.47 | loop fusion | flops 36 | bytes 96 | tf_op jit(solution)/shard_map/jit(_take)/jit(_where)/select_n | solution.py:29
  2.0 0.1 reshape.71
  2.1 0.8 %reshape_squeeze.6 = bf16[64,3,128]{2,1,0:T(4,128)(2,1)S(1)} reshape(bf16[1,64,384]{2,1,0:T(8,128)(2,1)} %param.14) | data formatting | bytes 98304 | tf_op jit(solution)/shard_map/reshape;squeeze | solution.py:28
  2.9 0.0 copy-start
  2.9 1.3 %copy.20 = bf16[4,3,128,128]{2,3,1,0:T(8,128)(2,1)S(1)} copy(bf16[4,3,128,128]{3,2,1,0:T(8,128)(2,1)} %param.8) | data formatting | bytes 786432 | tf_op args[0]
  4.2 0.0 copy-done
  4.2 0.0 copy-start.3
  4.2 0.2 copy.23
  4.4 0.6 %copy-done.3 = bf16[64,512]{1,0:T(8,128)(2,1)S(1)} copy-done((bf16[64,512]{1,0:T(8,128)(2,1)S(1)}, bf16[64,512]{1,0:T(8,128)(2,1)}, u32[]{:S(2)}) %copy-start.3) | copy-done | bytes 65560
  5.1 0.7 %copy-done.2 = bf16[1,32,384]{2,1,0:T(8,128)(2,1)S(1)} copy-done((bf16[1,32,384]{2,1,0:T(8,128)(2,1)S(1)}, bf16[1,32,384]{2,1,0:T(8,128)(2,1)}, u32[]{:S(2)}) %copy-start.2) | copy-done | bytes 24600
  5.8 0.6 %gather_fusion = bf16[12,64,128]{2,1,0:T(8,128)(2,1)S(1)} fusion(bf16[64,3,128]{2,0,1:T(8,128)(2,1)S(1)} %copy.21, s32[1024]{0:T(1024)S(1)} %pad_clamp_fusion), kind=kCustom, calls=%fused_computation | custom fusion | bytes 393264 | tf_op jit(solution)/shard_map/jit(_take)/gather | solution.py:29
  6.4 0.0 copy-start.4
  6.4 0.0 copy-start.5
  6.4 0.6 %gather_fusion.1 = bf16[12,32,128]{2,1,0:T(8,128)(2,1)S(1)} fusion(bf16[32,3,128]{2,0,1:T(8,128)(2,1)S(1)} %copy.24, s32[1024]{0:T(1024)S(1)} %pad_clamp_fusion), kind=kCustom, calls=%fused_computation.1 | custom fusion | bytes 196656 | tf_op jit(solution)/shard_map/jit(_take)/gather | solution.py:38
  7.0 0.1 copy-done.4
  7.1 0.0 copy-done.5
  7.1 0.1 broadcast_and_fusion
  7.2 0.5 %fusion.3 = bf16[4,3,128,128]{2,3,1,0:T(8,128)(2,1)S(1)} fusion(bf16[4,3,128,128]{2,3,1,0:T(8,128)(2,1)S(1)} %copy.23, bf16[4,3,128,128]{2,3,1,0:T(8,128)(2,1)S(1)} %copy.20, pred[4,3]{1,0:T(4,128)(4,1)S(1)} %get-tuple-element.9, pred[4,3]{1,0:T(4,128)(4,1)S(1)} %get-tuple-element.10, bf16[4,3,64,128]{3,2,1,0:T(8,128)(2,1)S(1)} %bitcast.76, ...), kind=kOutput, calls=%fused_computation.6 | convolution fusion | flops 26443776 | bytes 1441828 | tf_op jit(solution)/shard_map/rta,rtkb->tkab/dot_general | solution.py:31
  7.6 0.2 convolution_bitcast_fusion.2
  7.9 3.0 %collective-permute-start = (f32[32,512]{1,0:T(8,128)S(1)}, f32[32,512]{1,0:T(8,128)S(1)}, u32[]{:S(2)}, u32[]{:S(2)}) collective-permute-start(f32[32,512]{1,0:T(8,128)S(1)} %bitcast.78), channel_id=1, source_target_pairs={{0,1},{1,0},{2,3},{3,2},{4,5},{5,4},{6,7},{7,6},{8,9},{9,8},{10,11... | collective-permute-start | bytes 196616 | tf_op jit(solution)/shard_map/ppermute | solution.py:13
  10.9 0.1 copy.27
  11.0 2.2 %collective-permute-done = f32[32,512]{1,0:T(8,128)S(1)} collective-permute-done((f32[32,512]{1,0:T(8,128)S(1)}, f32[32,512]{1,0:T(8,128)S(1)}, u32[]{:S(2)}, u32[]{:S(2)}) %collective-permute-start) | collective-permute-done | bytes 65568 | tf_op jit(solution)/shard_map/ppermute | solution.py:13
  13.2 0.2 fusion.40
  13.4 0.5 %fusion.20 = f32[4,3,128,32]{2,3,1,0:T(8,128)S(1)} fusion(bf16[4,3,128,128]{2,3,1,0:T(8,128)(2,1)S(1)} %fusion.3, f32[32,4,128,1]{2,1,0,3:T(4,128)S(1)} %reshape.91), kind=kOutput, calls=%fused_computation.27 | convolution fusion | flops 75497472 | bytes 655360 | tf_op jit(solution)/shard_map/jta,tkab->jtkb/dot_general | solution.py:46
  13.9 0.4 %convolution_bitcast_fusion.1 = f32[32,3,128]{2,1,0:T(4,128)S(1)} fusion(f32[4,3,128,32]{2,3,1,0:T(8,128)S(1)} %fusion.20, s32[4,3]{0,1:T(4,128)S(1)} %copy.27), kind=kOutput, calls=%fused_computation.7 | convolution fusion | flops 1769508 | bytes 245808 | tf_op jit(solution)/shard_map/jtkb,tkc->jcb/dot_general | solution.py:55
  14.4 0.1 reshape.64
  14.5 0.0 collective-permute-start.1
  14.5 1.2 %collective-permute-done.1 = f32[104,128]{1,0:T(8,128)S(1)} collective-permute-done((f32[104,128]{1,0:T(8,128)S(1)}, f32[104,128]{1,0:T(8,128)S(1)}, u32[]{:S(2)}, u32[]{:S(2)}) %collective-permute-start.1) | collective-permute-done | bytes 53280 | tf_op jit(solution)/shard_map/ppermute | solution.py:13
  15.7 2.1 %collective-permute-start.2 = (f32[104,128]{1,0:T(8,128)S(1)}, f32[104,128]{1,0:T(8,128)S(1)}, u32[]{:S(2)}, u32[]{:S(2)}) collective-permute-start(f32[104,128]{1,0:T(8,128)S(1)} %fusion.39), channel_id=1, source_target_pairs={{0,4},{2,6},{4,0},{6,2},{8,12},{10,14},{12,8},{14,10},{16,20},{18,... | collective-permute-start | bytes 159752 | tf_op jit(solution)/shard_map/ppermute | solution.py:13
  17.8 2.1 %collective-permute-done.2 = f32[104,128]{1,0:T(8,128)S(1)} collective-permute-done((f32[104,128]{1,0:T(8,128)S(1)}, f32[104,128]{1,0:T(8,128)S(1)}, u32[]{:S(2)}, u32[]{:S(2)}) %collective-permute-start.2) | collective-permute-done | bytes 53280 | tf_op jit(solution)/shard_map/ppermute | solution.py:13
  20.0 2.1 %collective-permute-start.3 = (f32[104,128]{1,0:T(8,128)S(1)}, f32[104,128]{1,0:T(8,128)S(1)}, u32[]{:S(2)}, u32[]{:S(2)}) collective-permute-start(f32[104,128]{1,0:T(8,128)S(1)} %fusion.45), channel_id=1, source_target_pairs={{0,8},{2,10},{4,12},{6,14},{8,0},{10,2},{12,4},{14,6},{16,24},{18,... | collective-permute-start | bytes 159752 | tf_op jit(solution)/shard_map/ppermute | solution.py:13
  22.1 2.1 %collective-permute-done.3 = f32[104,128]{1,0:T(8,128)S(1)} collective-permute-done((f32[104,128]{1,0:T(8,128)S(1)}, f32[104,128]{1,0:T(8,128)S(1)}, u32[]{:S(2)}, u32[]{:S(2)}) %collective-permute-start.3) | collective-permute-done | bytes 53280 | tf_op jit(solution)/shard_map/ppermute | solution.py:13
  24.2 3.1 %collective-permute-start.4 = (f32[104,128]{1,0:T(8,128)S(1)}, f32[104,128]{1,0:T(8,128)S(1)}, u32[]{:S(2)}, u32[]{:S(2)}) collective-permute-start(f32[104,128]{1,0:T(8,128)S(1)} %add.37), channel_id=1, source_target_pairs={{0,16},{2,18},{4,20},{6,22},{8,24},{10,26},{12,28},{14,30},{16,0},... | collective-permute-start | bytes 159752 | tf_op jit(solution)/shard_map/ppermute | solution.py:13
  27.3 0.9 %copy.29 = bf16[4,3,128,128]{3,2,1,0:T(8,128)(2,1)} copy(bf16[4,3,128,128]{2,3,1,0:T(8,128)(2,1)S(1)} %fusion.3) | data formatting | bytes 786432
  28.3 1.2 %collective-permute-done.4 = f32[104,128]{1,0:T(8,128)S(1)} collective-permute-done((f32[104,128]{1,0:T(8,128)S(1)}, f32[104,128]{1,0:T(8,128)S(1)}, u32[]{:S(2)}, u32[]{:S(2)}) %collective-permute-start.4) | collective-permute-done | bytes 53280 | tf_op jit(solution)/shard_map/ppermute | solution.py:13
  29.5 0.0 copy-start.1
  29.5 0.6 %copy-done.1 = f32[104,128]{1,0:T(8,128)} copy-done((f32[104,128]{1,0:T(8,128)}, f32[104,128]{1,0:T(8,128)S(1)}, u32[]{:S(2)}) %copy-start.1) | copy-done | bytes 53272
  30.1 0.1 div.23
  30.2 0.1 copy.28
  30.2 2.9 %cholesky.16 = f32[32,32]{1,0:T(8,128)S(1)} custom-call(f32[32,32]{1,0:T(8,128)S(1)} %fusion.26), custom_call_target="Cholesky" | custom-call | tf_op jit(solution)/shard_map/jit(cholesky)/cholesky | solution.py:61
  33.2 0.7 %compare_reduce_fusion = pred[]{:T(512)} fusion(f32[32]{0:T(128)S(1)} %select_reduce_fusion), kind=kLoop, calls=%fused_computation.51 | loop fusion | flops 63 | bytes 129 | tf_op jit(solution)/shard_map/jit(cholesky)/cholesky | solution.py:61
  33.9 0.7 %select_bitcast_fusion = f32[1,32,32]{2,1,0:T(8,128)S(1)} fusion(f32[32,32]{1,0:T(8,128)S(1)} %cholesky.16, pred[]{:T(512)} %compare_reduce_fusion), kind=kLoop, calls=%fused_computation.37 | loop fusion | flops 4096 | bytes 8193 | tf_op jit(solution)/shard_map/jit(_solve_triangular)/triangular_solve | solution.py:62
  34.6 2.4 %custom-call.7 = f32[1,32,32]{1,2,0:T(8,128)S(1)} custom-call(f32[1,32,32]{2,1,0:T(8,128)S(1)} %select_bitcast_fusion), custom_call_target="InvertDiagBlocksLowerTriangular" | custom-call | tf_op jit(solution)/shard_map/jit(_solve_triangular)/triangular_solve | solution.py:62
  37.0 0.0 slice-done
  37.1 0.3 fusion.11
  37.4 1.5 %fusion.5 = f32[1,32,384]{2,1,0:T(8,128)} fusion(f32[32,896]{1,0:T(8,128)S(1)} %fusion.11, bf16[1,32,384]{2,1,0:T(8,128)(2,1)S(1)} %copy-done.2, f32[32,32]{1,0:T(8,128)S(1)} %cholesky.16, pred[]{:T(512)} %compare_reduce_fusion), kind=kOutput, calls=%fused_computation.11 | convolution fusion | flops 4758528 | bytes 126977 | tf_op jit(solution)/shard_map/ji,bjn->bin/dot_general | solution.py:67
  38.9 0.6 %slice.36 = f32[32,512]{1,0:T(8,128)} slice(f32[32,896]{1,0:T(8,128)S(1)} %fusion.11), slice={[0:32], [0:512]} | slice | bytes 131072 | tf_op jit(solution)/shard_map/slice | solution.py:65
  (20 shorter events, 0.3 us)
Async XLA Ops:
  2.9 1.3 %copy-start = (bf16[4,3,128,128]{3,2,1,0:T(8,128)(2,1)S(1)}, bf16[4,3,128,128]{3,2,1,0:T(8,128)(2,1)}, u32[]{:S(2)}) copy-start(bf16[4,3,128,128]{3,2,1,0:T(8,128)(2,1)} %param.9) | copy-start | bytes 1179652
  4.2 0.8 %copy-start.3 = (bf16[64,512]{1,0:T(8,128)(2,1)S(1)}, bf16[64,512]{1,0:T(8,128)(2,1)}, u32[]{:S(2)}) copy-start(bf16[64,512]{1,0:T(8,128)(2,1)} %param.13) | copy-start | bytes 196612
  5.0 0.7 %copy-start.2 = (bf16[1,32,384]{2,1,0:T(8,128)(2,1)S(1)}, bf16[1,32,384]{2,1,0:T(8,128)(2,1)}, u32[]{:S(2)}) copy-start(bf16[1,32,384]{2,1,0:T(8,128)(2,1)} %param.15) | copy-start | bytes 73732
  6.4 0.7 %copy-start.4 = (s32[4,3]{1,0:T(4,128)S(1)}, s32[4,3]{1,0:T(4,128)}, u32[]{:S(2)}) copy-start(s32[4,3]{1,0:T(4,128)} %param.10) | copy-start | bytes 148
  6.4 0.7 %copy-start.5 = (s32[4,3]{1,0:T(4,128)S(1)}, s32[4,3]{1,0:T(4,128)}, u32[]{:S(2)}) copy-start(s32[4,3]{1,0:T(4,128)} %param.11) | copy-start | bytes 148
  7.9 5.2 %collective-permute-start = (f32[32,512]{1,0:T(8,128)S(1)}, f32[32,512]{1,0:T(8,128)S(1)}, u32[]{:S(2)}, u32[]{:S(2)}) collective-permute-start(f32[32,512]{1,0:T(8,128)S(1)} %bitcast.78), channel_id=1, source_target_pairs={{0,1},{1,0},{2,3},{3,2},{4,5},{5,4},{6,7},{7,6},{8,9},{9,8},{10,11... | collective-permute-start | bytes 196616 | tf_op jit(solution)/shard_map/ppermute | solution.py:13
  14.5 1.3 %collective-permute-start.1 = (f32[104,128]{1,0:T(8,128)S(1)}, f32[104,128]{1,0:T(8,128)S(1)}, u32[]{:S(2)}, u32[]{:S(2)}) collective-permute-start(f32[104,128]{1,0:T(8,128)S(1)} %maximum_bitcast_fusion), channel_id=1, source_target_pairs={{0,2},{2,0},{4,6},{6,4},{8,10},{10,8},{12,14},{14,12},{16,18},{18,... | collective-permute-start | bytes 159752 | tf_op jit(solution)/shard_map/ppermute | solution.py:13
  15.7 4.2 %collective-permute-start.2 = (f32[104,128]{1,0:T(8,128)S(1)}, f32[104,128]{1,0:T(8,128)S(1)}, u32[]{:S(2)}, u32[]{:S(2)}) collective-permute-start(f32[104,128]{1,0:T(8,128)S(1)} %fusion.39), channel_id=1, source_target_pairs={{0,4},{2,6},{4,0},{6,2},{8,12},{10,14},{12,8},{14,10},{16,20},{18,... | collective-permute-start | bytes 159752 | tf_op jit(solution)/shard_map/ppermute | solution.py:13
  20.0 4.3 %collective-permute-start.3 = (f32[104,128]{1,0:T(8,128)S(1)}, f32[104,128]{1,0:T(8,128)S(1)}, u32[]{:S(2)}, u32[]{:S(2)}) collective-permute-start(f32[104,128]{1,0:T(8,128)S(1)} %fusion.45), channel_id=1, source_target_pairs={{0,8},{2,10},{4,12},{6,14},{8,0},{10,2},{12,4},{14,6},{16,24},{18,... | collective-permute-start | bytes 159752 | tf_op jit(solution)/shard_map/ppermute | solution.py:13
  24.2 5.2 %collective-permute-start.4 = (f32[104,128]{1,0:T(8,128)S(1)}, f32[104,128]{1,0:T(8,128)S(1)}, u32[]{:S(2)}, u32[]{:S(2)}) collective-permute-start(f32[104,128]{1,0:T(8,128)S(1)} %add.37), channel_id=1, source_target_pairs={{0,16},{2,18},{4,20},{6,22},{8,24},{10,26},{12,28},{14,30},{16,0},... | collective-permute-start | bytes 159752 | tf_op jit(solution)/shard_map/ppermute | solution.py:13
  29.5 0.6 %copy-start.1 = (f32[104,128]{1,0:T(8,128)}, f32[104,128]{1,0:T(8,128)S(1)}, u32[]{:S(2)}) copy-start(f32[104,128]{1,0:T(8,128)S(1)} %add.38) | copy-start | bytes 159748
  30.2 6.8 %slice-start = ((f32[104,128]{1,0:T(8,128)}), f32[96,128]{1,0:T(8,128)S(1)}, s32[]{:S(2)}) async-start(f32[104,128]{1,0:T(8,128)} %copy-done.1), calls=%async_computation | async-start | bytes 98304 | tf_op jit(solution)/shard_map/slice | solution.py:60

commit v3 on v2

--- a/solution.py
+++ b/solution.py
@@ -1,6 +1,10 @@
+import functools
+
 import jax
 import jax.numpy as jnp
 from jax import lax
+from jax.experimental import pallas as pl
+from jax.experimental.pallas import tpu as pltpu
 from jax.sharding import PartitionSpec as P
 
 
@@ -13,6 +17,53 @@
         x = x + lax.ppermute(x, axis, [(i, i ^ step) for i in range(n)])
         step *= 2
     return x
+
+
+def tail_kernel(gram_ref, proj_ref, sums_ref, start_ref, left_ref, right_ref, *, scale, root):
+    n = gram_ref.shape[0]
+    a = gram_ref[...] * scale
+    a = 0.5 * (a + a.T)
+    rows = lax.broadcasted_iota(jnp.int32, (n, n), 0)
+    cols = lax.broadcasted_iota(jnp.int32, (n, n), 1)
+    lower = jnp.zeros((n, n), jnp.float32)
+    upper = jnp.zeros((n, n), jnp.float32)
+    for k in range(n):
+        pivot = jnp.sqrt(a[k : k + 1, k : k + 1])
+        col = jnp.where(rows[:, k : k + 1] >= k, a[:, k : k + 1] / pivot, 0.0)
+        row = jnp.where(cols[k : k + 1, :] >= k, a[k : k + 1, :] / pivot, 0.0)
+        a = a - col * row
+        lower = jnp.where(cols == k, col, lower)
+        upper = jnp.where(rows == k, row, upper)
+    inverse = (rows == cols).astype(jnp.float32)
+    for k in range(n):
+        head = inverse[k : k + 1, :] / lower[k : k + 1, k : k + 1]
+        below = jnp.where(rows[:, k : k + 1] > k, lower[:, k : k + 1], 0.0)
+        inverse = jnp.where(rows == k, head, inverse - below * head)
+    hi = lax.Precision.HIGHEST
+    left_ref[...] = jnp.dot(inverse, proj_ref[...], precision=hi, preferred_element_type=jnp.float32)
+    summed = jnp.dot(inverse, sums_ref[...], precision=hi, preferred_element_type=jnp.float32)
+    start_term = jnp.dot(
+        upper, start_ref[...].astype(jnp.float32), precision=hi, preferred_element_type=jnp.float32
+    )
+    right_ref[...] = summed / root - root * start_term
+
+
+def tail(gram, projected, item_sums, start, user_total):
+    n, users = projected.shape
+    items = item_sums.shape[1]
+    vmem = pl.BlockSpec(memory_space=pltpu.VMEM)
+    return pl.pallas_call(
+        functools.partial(tail_kernel, scale=1.0 / user_total, root=float(user_total) ** 0.5),
+        out_shape=(
+            jax.ShapeDtypeStruct((n, users), jnp.float32),
+            jax.ShapeDtypeStruct((n, items), jnp.float32),
+        ),
+        in_specs=[vmem] * 4,
+        out_specs=(vmem, vmem),
+        cost_estimate=pl.CostEstimate(
+            flops=2 * n * n * (users + 2 * items) * 6, transcendentals=n, bytes_accessed=4 * n * (n + 2 * users + 3 * items)
+        ),
+    )(gram, projected, item_sums, start)
 
 
 def local(
@@ -56,18 +107,10 @@
     item_terms = item_terms.reshape(block_size, item_count * width)
     payload = jnp.concatenate([gram_part.reshape(-1), item_terms.reshape(-1)])
     reduced = all_sum(payload.reshape(-1, width), "users").reshape(-1)
-    gram = reduced[: block_size * block_size].reshape(block_size, block_size) / user_total
+    gram = reduced[: block_size * block_size].reshape(block_size, block_size)
     item_sums = reduced[block_size * block_size :].reshape(block_size, item_count * width)
-    lower = jnp.linalg.cholesky(gram)
-    solved = jax.scipy.linalg.solve_triangular(
-        lower, jnp.concatenate([projected, item_sums], axis=1), lower=True
-    )
-    left_block = solved[:, : rows_dev * width]
-    summed = solved[:, rows_dev * width :].reshape(1, block_size, item_count * width)
-    start_term = jnp.einsum(
-        "ji,bjn->bin", lower, start_block.astype(jnp.float32), precision=lax.Precision.HIGHEST
-    )
-    right_block = summed / root - root * start_term
+    left_block, right_block = tail(gram, projected, item_sums, start_block[0], user_total)
+    right_block = right_block.reshape(1, block_size, item_count * width)
     return (updated, left_block, right_block)
 
 

time: 39.9 us -> 37.5 us (0.940)
  other arithmetic: 8.27 us -> 1.49 us
  Pallas kernels: 0 us -> 5.04 us
  matrix products: 3.64 us -> 1.82 us
  local copies, waits for them, and re-layouts: 7.6 us -> 8.71 us
    another operation x5 -> x0, other arithmetic: 6.78 us -> none  [the longest x3 3.66 us: local(): lower = jnp.linalg.cholesky(gram)]
    pallas_call x0 -> x1, Pallas kernels: none -> 5.04 us  [tail(): pl.pallas_call(functools.partial(tail_kernel, scale=1.0 / user_total, roo...]
    dot_general x1 -> x0, matrix products: 1.53 us -> none  [local(): jnp.einsum('ji,bjn->bin', lower, start_block.astype(jnp.float32), precisi...]
    reshape x0 -> x1, local copies, waits for them, and re-layouts: none -> 0.67 us  [local(): gram = reduced[:block_size * block_size].reshape(block_size, block_size)]
    reshape x1, local copies, waits for them, and re-layouts: 0.04 us -> 0.63 us  [local(): reduced[block_size * block_size:].reshape(block_size, item_count * width)]
    slice x1 -> x2, local copies, waits for them, and re-layouts: 0.63 us -> 0.06 us  [local(): gram = reduced[:block_size * block_size].reshape(block_size, block_size)]
    unnamed x16 -> x18, local copies, waits for them, and re-layouts: 4.55 us -> 5.13 us
where the time goes in v3:
time: 37.5 us; the launch traced here: 37.1 us
  starting transfers between devices  10.4 us (28%)
  waiting for transfers between devices  8.79 us (23%)
  local copies, waits for them, and re-layouts  8.71 us (23%)
  Pallas kernels  5.04 us (13%)
  matrix products  1.82 us (5%)
  other arithmetic  1.49 us (4%)
  between operations  0.83 us (2%)
    ppermute x5, starting transfers between devices, all_sum(): x = x + lax.ppermute(x, axis, [(i, i ^ step) for i in range(n)])  10.4 us
    ppermute x5, waiting for transfers between devices, all_sum(): x = x + lax.ppermute(x, axis, [(i, i ^ step) for i in range(n)])  8.79 us
    unnamed x18, local copies, waits for them, and re-layouts  5.13 us
    pallas_call x1, Pallas kernels, tail(): pl.pallas_call(functools.partial(tail_kernel, scale=1.0 / user_total, roo...  5.04 us
    another operation x2, local copies, waits for them, and re-layouts, local(): item_tiles = item_factors[0].reshape(rank_size, item_count, width)  0.83 us
  transfers between devices with their start and end apart: 5, of which 5 were waited for; matrix products, arithmetic and copies ran while one was open for 3% of the time, Pallas kernels for 0%

profile of v3, /device:TPU:0, one launch (start us, length us, event | category | flops | bytes accessed | tf_op | source)
XLA Modules:
  0.0 37.1 jit_solution(6577604662897641828)
XLA Ops:
  0.6 0.7 %broadcast_compare_fusion.1 = pred[4]{0:T(512)(128)(4,1)S(1)} fusion(s32[4]{0:T(128)} %param.12), kind=kLoop, calls=%fused_computation.32 | loop fusion | flops 4 | bytes 20 | tf_op jit(solution)/shard_map/gt | solution.py:84
  1.3 0.7 %compare_select_fusion = s32[4,3]{1,0:T(4,128)S(1)} fusion(s32[4,3]{1,0:T(4,128)} %param.10), kind=kLoop, calls=%fused_computation.26 | loop fusion | flops 36 | bytes 96 | tf_op jit(solution)/shard_map/jit(_take)/jit(_where)/select_n | solution.py:80
  2.0 0.1 reshape.57
  2.1 0.8 %reshape_squeeze.6 = bf16[64,3,128]{2,1,0:T(4,128)(2,1)S(1)} reshape(bf16[1,64,384]{2,1,0:T(8,128)(2,1)} %param.14) | data formatting | bytes 98304 | tf_op jit(solution)/shard_map/reshape;squeeze | solution.py:79
  2.9 0.0 copy-start.1
  2.9 1.3 %copy.20 = bf16[4,3,128,128]{2,3,1,0:T(8,128)(2,1)S(1)} copy(bf16[4,3,128,128]{3,2,1,0:T(8,128)(2,1)} %param.8) | data formatting | bytes 786432 | tf_op args[0]
  4.2 0.0 copy-done.1
  4.2 0.0 copy-start.4
  4.2 0.2 copy.23
  4.4 0.6 %copy-done.4 = bf16[64,512]{1,0:T(8,128)(2,1)S(1)} copy-done((bf16[64,512]{1,0:T(8,128)(2,1)S(1)}, bf16[64,512]{1,0:T(8,128)(2,1)}, u32[]{:S(2)}) %copy-start.4) | copy-done | bytes 65560
  5.0 0.0 copy-start.3
  5.1 0.7 %copy-done.3 = bf16[1,32,384]{2,1,0:T(8,128)(2,1)S(1)} copy-done((bf16[1,32,384]{2,1,0:T(8,128)(2,1)S(1)}, bf16[1,32,384]{2,1,0:T(8,128)(2,1)}, u32[]{:S(2)}) %copy-start.3) | copy-done | bytes 24600
  5.8 0.6 %gather_fusion = bf16[12,64,128]{2,1,0:T(8,128)(2,1)S(1)} fusion(bf16[64,3,128]{2,0,1:T(8,128)(2,1)S(1)} %copy.21, s32[1024]{0:T(1024)S(1)} %pad_clamp_fusion), kind=kCustom, calls=%fused_computation | custom fusion | bytes 393264 | tf_op jit(solution)/shard_map/jit(_take)/gather | solution.py:80
  6.4 0.0 copy-start.5
  6.4 0.0 copy-start.6
  6.4 0.6 %gather_fusion.1 = bf16[12,32,128]{2,1,0:T(8,128)(2,1)S(1)} fusion(bf16[32,3,128]{2,0,1:T(8,128)(2,1)S(1)} %copy.24, s32[1024]{0:T(1024)S(1)} %pad_clamp_fusion), kind=kCustom, calls=%fused_computation.1 | custom fusion | bytes 196656 | tf_op jit(solution)/shard_map/jit(_take)/gather | solution.py:89
  7.0 0.1 copy-done.5
  7.1 0.0 copy-done.6
  7.1 0.1 broadcast_and_fusion
  7.2 0.5 %fusion.3 = bf16[4,3,128,128]{2,3,1,0:T(8,128)(2,1)S(1)} fusion(bf16[4,3,128,128]{2,3,1,0:T(8,128)(2,1)S(1)} %copy.23, bf16[4,3,128,128]{2,3,1,0:T(8,128)(2,1)S(1)} %copy.20, pred[4,3]{1,0:T(4,128)(4,1)S(1)} %get-tuple-element.13, pred[4,3]{1,0:T(4,128)(4,1)S(1)} %get-tuple-element.14, bf16[4,3,64,128]{3,2,1,0:T(8,128)(2,1)S(1)} %bitcast.54, ...), kind=kOutput, calls=%fused_computation.6 | convolution fusion | flops 26443776 | bytes 1441828 | tf_op jit(solution)/shard_map/rta,rtkb->tkab/dot_general | solution.py:82
  7.6 0.2 convolution_bitcast_fusion.2
  7.9 3.0 %collective-permute-start = (f32[32,512]{1,0:T(8,128)S(1)}, f32[32,512]{1,0:T(8,128)S(1)}, u32[]{:S(2)}, u32[]{:S(2)}) collective-permute-start(f32[32,512]{1,0:T(8,128)S(1)} %bitcast.57), channel_id=1, source_target_pairs={{0,1},{1,0},{2,3},{3,2},{4,5},{5,4},{6,7},{7,6},{8,9},{9,8},{10,11... | collective-permute-start | bytes 196616 | tf_op jit(solution)/shard_map/ppermute | solution.py:17
  10.9 0.1 copy.27
  11.0 2.2 %collective-permute-done = f32[32,512]{1,0:T(8,128)S(1)} collective-permute-done((f32[32,512]{1,0:T(8,128)S(1)}, f32[32,512]{1,0:T(8,128)S(1)}, u32[]{:S(2)}, u32[]{:S(2)}) %collective-permute-start) | collective-permute-done | bytes 65568 | tf_op jit(solution)/shard_map/ppermute | solution.py:17
  13.2 0.0 copy-start
  13.2 0.6 %copy-done = f32[32,512]{1,0:T(8,128)} copy-done((f32[32,512]{1,0:T(8,128)}, f32[32,512]{1,0:T(8,128)S(1)}, u32[]{:S(2)}) %copy-start) | copy-done | bytes 65560
  13.8 0.2 fusion.24
  14.0 0.5 %fusion.14 = f32[4,3,128,32]{2,3,1,0:T(8,128)S(1)} fusion(bf16[4,3,128,128]{2,3,1,0:T(8,128)(2,1)S(1)} %fusion.3, f32[32,4,128,1]{2,1,0,3:T(4,128)S(1)} %reshape.77), kind=kOutput, calls=%fused_computation.20 | convolution fusion | flops 75497472 | bytes 655360 | tf_op jit(solution)/shard_map/jta,tkab->jtkb/dot_general | solution.py:97
  14.5 0.4 %convolution_bitcast_fusion.1 = f32[32,3,128]{2,1,0:T(4,128)S(1)} fusion(f32[4,3,128,32]{2,3,1,0:T(8,128)S(1)} %fusion.14, s32[4,3]{0,1:T(4,128)S(1)} %copy.27), kind=kOutput, calls=%fused_computation.7 | convolution fusion | flops 1769508 | bytes 245808 | tf_op jit(solution)/shard_map/jtkb,tkc->jcb/dot_general | solution.py:106
  15.0 0.1 reshape.49
  15.0 0.0 collective-permute-start.1
  15.1 1.2 %collective-permute-done.1 = f32[104,128]{1,0:T(8,128)S(1)} collective-permute-done((f32[104,128]{1,0:T(8,128)S(1)}, f32[104,128]{1,0:T(8,128)S(1)}, u32[]{:S(2)}, u32[]{:S(2)}) %collective-permute-start.1) | collective-permute-done | bytes 53280 | tf_op jit(solution)/shard_map/ppermute | solution.py:17
  16.3 2.1 %collective-permute-start.2 = (f32[104,128]{1,0:T(8,128)S(1)}, f32[104,128]{1,0:T(8,128)S(1)}, u32[]{:S(2)}, u32[]{:S(2)}) collective-permute-start(f32[104,128]{1,0:T(8,128)S(1)} %fusion.23), channel_id=1, source_target_pairs={{0,4},{2,6},{4,0},{6,2},{8,12},{10,14},{12,8},{14,10},{16,20},{18,... | collective-permute-start | bytes 159752 | tf_op jit(solution)/shard_map/ppermute | solution.py:17
  18.4 2.1 %collective-permute-done.2 = f32[104,128]{1,0:T(8,128)S(1)} collective-permute-done((f32[104,128]{1,0:T(8,128)S(1)}, f32[104,128]{1,0:T(8,128)S(1)}, u32[]{:S(2)}, u32[]{:S(2)}) %collective-permute-start.2) | collective-permute-done | bytes 53280 | tf_op jit(solution)/shard_map/ppermute | solution.py:17
  20.6 2.1 %collective-permute-start.3 = (f32[104,128]{1,0:T(8,128)S(1)}, f32[104,128]{1,0:T(8,128)S(1)}, u32[]{:S(2)}, u32[]{:S(2)}) collective-permute-start(f32[104,128]{1,0:T(8,128)S(1)} %fusion.29), channel_id=1, source_target_pairs={{0,8},{2,10},{4,12},{6,14},{8,0},{10,2},{12,4},{14,6},{16,24},{18,... | collective-permute-start | bytes 159752 | tf_op jit(solution)/shard_map/ppermute | solution.py:17
  22.7 2.1 %collective-permute-done.3 = f32[104,128]{1,0:T(8,128)S(1)} collective-permute-done((f32[104,128]{1,0:T(8,128)S(1)}, f32[104,128]{1,0:T(8,128)S(1)}, u32[]{:S(2)}, u32[]{:S(2)}) %collective-permute-start.3) | collective-permute-done | bytes 53280 | tf_op jit(solution)/shard_map/ppermute | solution.py:17
  24.8 3.1 %collective-permute-start.4 = (f32[104,128]{1,0:T(8,128)S(1)}, f32[104,128]{1,0:T(8,128)S(1)}, u32[]{:S(2)}, u32[]{:S(2)}) collective-permute-start(f32[104,128]{1,0:T(8,128)S(1)} %add.25), channel_id=1, source_target_pairs={{0,16},{2,18},{4,20},{6,22},{8,24},{10,26},{12,28},{14,30},{16,0},... | collective-permute-start | bytes 159752 | tf_op jit(solution)/shard_map/ppermute | solution.py:17
  27.9 0.9 %copy.28 = bf16[4,3,128,128]{3,2,1,0:T(8,128)(2,1)} copy(bf16[4,3,128,128]{2,3,1,0:T(8,128)(2,1)S(1)} %fusion.3) | data formatting | bytes 786432
  28.8 1.2 %collective-permute-done.4 = f32[104,128]{1,0:T(8,128)S(1)} collective-permute-done((f32[104,128]{1,0:T(8,128)S(1)}, f32[104,128]{1,0:T(8,128)S(1)}, u32[]{:S(2)}, u32[]{:S(2)}) %collective-permute-start.4) | collective-permute-done | bytes 53280 | tf_op jit(solution)/shard_map/ppermute | solution.py:17
  30.0 0.0 copy-start.2
  30.1 0.6 %copy-done.2 = f32[104,128]{1,0:T(8,128)} copy-done((f32[104,128]{1,0:T(8,128)}, f32[104,128]{1,0:T(8,128)S(1)}, u32[]{:S(2)}) %copy-start.2) | copy-done | bytes 53272
  30.7 0.0 slice-start
  30.7 0.6 %reshape.53.sums_ref = f32[32,384]{1,0:T(8,128)} reshape(f32[96,128]{1,0:T(8,128)S(1)} %slice.15) | data formatting | bytes 98304 | tf_op jit(solution)/shard_map/reshape | solution.py:111
  31.3 0.1 slice-done
  31.4 0.7 %reshape.52.gram_ref = f32[32,32]{1,0:T(8,128)} reshape(f32[8,128]{1,0:T(8,128)S(1)} %slice-done) | data formatting | bytes 8192 | tf_op jit(solution)/shard_map/reshape | solution.py:110
  32.0 5.0 %shard_map.103 = (f32[32,512]{1,0:T(8,128)}, f32[32,384]{1,0:T(8,128)}) custom-call(f32[32,32]{1,0:T(8,128)} %reshape.52.gram_ref, f32[32,512]{1,0:T(8,128)} %copy-done, f32[32,384]{1,0:T(8,128)} %reshape.53.sums_ref, bf16[32,384]{1,0:T(8,128)(2,1)} %bitcast.55), custom_call_target="tpu_custom_call" | custom-call | flops 15728640 | bytes 282624 | tf_op jit(solution)/shard_map/pallas_call | solution.py:55
  (15 shorter events, 0.2 us)
Async XLA Ops:
  2.9 1.3 %copy-start.1 = (bf16[4,3,128,128]{3,2,1,0:T(8,128)(2,1)S(1)}, bf16[4,3,128,128]{3,2,1,0:T(8,128)(2,1)}, u32[]{:S(2)}) copy-start(bf16[4,3,128,128]{3,2,1,0:T(8,128)(2,1)} %param.9) | copy-start | bytes 1179652
  4.2 0.8 %copy-start.4 = (bf16[64,512]{1,0:T(8,128)(2,1)S(1)}, bf16[64,512]{1,0:T(8,128)(2,1)}, u32[]{:S(2)}) copy-start(bf16[64,512]{1,0:T(8,128)(2,1)} %param.13) | copy-start | bytes 196612
  5.0 0.7 %copy-start.3 = (bf16[1,32,384]{2,1,0:T(8,128)(2,1)S(1)}, bf16[1,32,384]{2,1,0:T(8,128)(2,1)}, u32[]{:S(2)}) copy-start(bf16[1,32,384]{2,1,0:T(8,128)(2,1)} %param.15) | copy-start | bytes 73732
  6.4 0.7 %copy-start.5 = (s32[4,3]{1,0:T(4,128)S(1)}, s32[4,3]{1,0:T(4,128)}, u32[]{:S(2)}) copy-start(s32[4,3]{1,0:T(4,128)} %param.10) | copy-start | bytes 148
  6.4 0.7 %copy-start.6 = (s32[4,3]{1,0:T(4,128)S(1)}, s32[4,3]{1,0:T(4,128)}, u32[]{:S(2)}) copy-start(s32[4,3]{1,0:T(4,128)} %param.11) | copy-start | bytes 148
  7.9 5.2 %collective-permute-start = (f32[32,512]{1,0:T(8,128)S(1)}, f32[32,512]{1,0:T(8,128)S(1)}, u32[]{:S(2)}, u32[]{:S(2)}) collective-permute-start(f32[32,512]{1,0:T(8,128)S(1)} %bitcast.57), channel_id=1, source_target_pairs={{0,1},{1,0},{2,3},{3,2},{4,5},{5,4},{6,7},{7,6},{8,9},{9,8},{10,11... | collective-permute-start | bytes 196616 | tf_op jit(solution)/shard_map/ppermute | solution.py:17
  13.2 0.6 %copy-start = (f32[32,512]{1,0:T(8,128)}, f32[32,512]{1,0:T(8,128)S(1)}, u32[]{:S(2)}) copy-start(f32[32,512]{1,0:T(8,128)S(1)} %fusion.22.proj_ref) | copy-start | bytes 196612
  15.0 1.3 %collective-permute-start.1 = (f32[104,128]{1,0:T(8,128)S(1)}, f32[104,128]{1,0:T(8,128)S(1)}, u32[]{:S(2)}, u32[]{:S(2)}) collective-permute-start(f32[104,128]{1,0:T(8,128)S(1)} %maximum_bitcast_fusion), channel_id=1, source_target_pairs={{0,2},{2,0},{4,6},{6,4},{8,10},{10,8},{12,14},{14,12},{16,18},{18,... | collective-permute-start | bytes 159752 | tf_op jit(solution)/shard_map/ppermute | solution.py:17
  16.3 4.2 %collective-permute-start.2 = (f32[104,128]{1,0:T(8,128)S(1)}, f32[104,128]{1,0:T(8,128)S(1)}, u32[]{:S(2)}, u32[]{:S(2)}) collective-permute-start(f32[104,128]{1,0:T(8,128)S(1)} %fusion.23), channel_id=1, source_target_pairs={{0,4},{2,6},{4,0},{6,2},{8,12},{10,14},{12,8},{14,10},{16,20},{18,... | collective-permute-start | bytes 159752 | tf_op jit(solution)/shard_map/ppermute | solution.py:17
  20.6 4.3 %collective-permute-start.3 = (f32[104,128]{1,0:T(8,128)S(1)}, f32[104,128]{1,0:T(8,128)S(1)}, u32[]{:S(2)}, u32[]{:S(2)}) collective-permute-start(f32[104,128]{1,0:T(8,128)S(1)} %fusion.29), channel_id=1, source_target_pairs={{0,8},{2,10},{4,12},{6,14},{8,0},{10,2},{12,4},{14,6},{16,24},{18,... | collective-permute-start | bytes 159752 | tf_op jit(solution)/shard_map/ppermute | solution.py:17
  24.8 5.2 %collective-permute-start.4 = (f32[104,128]{1,0:T(8,128)S(1)}, f32[104,128]{1,0:T(8,128)S(1)}, u32[]{:S(2)}, u32[]{:S(2)}) collective-permute-start(f32[104,128]{1,0:T(8,128)S(1)} %add.25), channel_id=1, source_target_pairs={{0,16},{2,18},{4,20},{6,22},{8,24},{10,26},{12,28},{14,30},{16,0},... | collective-permute-start | bytes 159752 | tf_op jit(solution)/shard_map/ppermute | solution.py:17
  30.0 0.6 %copy-start.2 = (f32[104,128]{1,0:T(8,128)}, f32[104,128]{1,0:T(8,128)S(1)}, u32[]{:S(2)}) copy-start(f32[104,128]{1,0:T(8,128)S(1)} %add.26) | copy-start | bytes 159748
  30.7 0.7 %slice-start = ((f32[104,128]{1,0:T(8,128)}), f32[8,128]{1,0:T(8,128)S(1)}, s32[]{:S(2)}) async-start(f32[104,128]{1,0:T(8,128)} %copy-done.2), calls=%async_computation | async-start | bytes 8192 | tf_op jit(solution)/shard_map/slice | solution.py:110

commit v4 on v3

--- a/solution.py
+++ b/solution.py
@@ -19,38 +19,33 @@
     return x
 
 
-def tail_kernel(gram_ref, proj_ref, sums_ref, start_ref, left_ref, right_ref, *, scale, root):
-    n = gram_ref.shape[0]
-    a = gram_ref[...] * scale
-    a = 0.5 * (a + a.T)
-    rows = lax.broadcasted_iota(jnp.int32, (n, n), 0)
-    cols = lax.broadcasted_iota(jnp.int32, (n, n), 1)
-    lower = jnp.zeros((n, n), jnp.float32)
-    upper = jnp.zeros((n, n), jnp.float32)
+def tail_kernel(reduced_ref, proj_ref, start_ref, left_ref, right_ref, *, scale, root):
+    n = start_ref.shape[0]
+    lanes = reduced_ref.shape[1] - start_ref.shape[1]
+    g = reduced_ref[:, :n] * scale
+    g = 0.5 * (g + g.T)
+    rows = lax.broadcasted_iota(jnp.int32, (n, 2 * n), 0)
+    cols = lax.broadcasted_iota(jnp.int32, (n, 2 * n), 1)
+    aug = jnp.concatenate([g, (rows[:, :n] == cols[:, :n]).astype(jnp.float32)], axis=1)
     for k in range(n):
-        pivot = jnp.sqrt(a[k : k + 1, k : k + 1])
-        col = jnp.where(rows[:, k : k + 1] >= k, a[:, k : k + 1] / pivot, 0.0)
-        row = jnp.where(cols[k : k + 1, :] >= k, a[k : k + 1, :] / pivot, 0.0)
-        a = a - col * row
-        lower = jnp.where(cols == k, col, lower)
-        upper = jnp.where(rows == k, row, upper)
-    inverse = (rows == cols).astype(jnp.float32)
-    for k in range(n):
-        head = inverse[k : k + 1, :] / lower[k : k + 1, k : k + 1]
-        below = jnp.where(rows[:, k : k + 1] > k, lower[:, k : k + 1], 0.0)
-        inverse = jnp.where(rows == k, head, inverse - below * head)
+        inv_pivot = lax.rsqrt(aug[k : k + 1, k : k + 1])
+        head = aug[k : k + 1, :] * inv_pivot
+        factor = jnp.where(rows[:, :1] > k, aug[:, k : k + 1] * inv_pivot, 0.0)
+        aug = jnp.where(rows == k, head, aug - factor * head)
+    upper = aug[:, :n]
+    inverse = aug[:, n:]
     hi = lax.Precision.HIGHEST
     left_ref[...] = jnp.dot(inverse, proj_ref[...], precision=hi, preferred_element_type=jnp.float32)
-    summed = jnp.dot(inverse, sums_ref[...], precision=hi, preferred_element_type=jnp.float32)
+    summed = jnp.dot(inverse, reduced_ref[:, lanes:], precision=hi, preferred_element_type=jnp.float32)
     start_term = jnp.dot(
         upper, start_ref[...].astype(jnp.float32), precision=hi, preferred_element_type=jnp.float32
     )
     right_ref[...] = summed / root - root * start_term
 
 
-def tail(gram, projected, item_sums, start, user_total):
+def tail(reduced, projected, start, user_total):
     n, users = projected.shape
-    items = item_sums.shape[1]
+    items = start.shape[1]
     vmem = pl.BlockSpec(memory_space=pltpu.VMEM)
     return pl.pallas_call(
         functools.partial(tail_kernel, scale=1.0 / user_total, root=float(user_total) ** 0.5),
@@ -58,12 +53,12 @@
             jax.ShapeDtypeStruct((n, users), jnp.float32),
             jax.ShapeDtypeStruct((n, items), jnp.float32),
         ),
-        in_specs=[vmem] * 4,
+        in_specs=[vmem] * 3,
         out_specs=(vmem, vmem),
         cost_estimate=pl.CostEstimate(
-            flops=2 * n * n * (users + 2 * items) * 6, transcendentals=n, bytes_accessed=4 * n * (n + 2 * users + 3 * items)
+            flops=2 * n * n * (users + 2 * items) * 6, transcendentals=n, bytes_accessed=4 * n * (2 * users + 3 * items)
         ),
-    )(gram, projected, item_sums, start)
+    )(reduced, projected, start)
 
 
 def local(
@@ -105,11 +100,10 @@
     ).astype(jnp.float32)
     item_terms = jnp.einsum("jtkb,tkc->jcb", slot_terms, one_hot, precision=lax.Precision.HIGHEST)
     item_terms = item_terms.reshape(block_size, item_count * width)
-    payload = jnp.concatenate([gram_part.reshape(-1), item_terms.reshape(-1)])
-    reduced = all_sum(payload.reshape(-1, width), "users").reshape(-1)
-    gram = reduced[: block_size * block_size].reshape(block_size, block_size)
-    item_sums = reduced[block_size * block_size :].reshape(block_size, item_count * width)
-    left_block, right_block = tail(gram, projected, item_sums, start_block[0], user_total)
+    lanes = -(-block_size // width) * width
+    gram_lanes = jnp.pad(gram_part, ((0, 0), (0, lanes - block_size)))
+    reduced = all_sum(jnp.concatenate([gram_lanes, item_terms], axis=1), "users")
+    left_block, right_block = tail(reduced, projected, start_block[0], user_total)
     right_block = right_block.reshape(1, block_size, item_count * width)
     return (updated, left_block, right_block)
 

time: 37.5 us -> 36 us (0.960)
  local copies, waits for them, and re-layouts: 8.71 us -> 6.67 us
  waiting for transfers between devices: 8.79 us -> 9.49 us
  other arithmetic: 1.49 us -> 2.12 us
  Pallas kernels: 5.04 us -> 4.57 us
    reshape x3 -> x0, local copies, waits for them, and re-layouts: 1.37 us -> none  [the longest x1 0.67 us: local(): gram = reduced[:block_size * block_size].reshape(block_size, block_size)]
    ppermute x5, waiting for transfers between devices: 8.79 us -> 9.49 us  [all_sum(): x = x + lax.ppermute(x, axis, [(i, i ^ step) for i in range(n)])]
    add x5, other arithmetic: 0.05 us -> 0.68 us  [all_sum(): x = x + lax.ppermute(x, axis, [(i, i ^ step) for i in range(n)])]
    unnamed x18 -> x17, local copies, waits for them, and re-layouts: 5.13 us -> 4.53 us
    pallas_call x1, Pallas kernels: 5.04 us -> 4.57 us  [tail(): pl.pallas_call(functools.partial(tail_kernel, scale=1.0 / user_total, roo...]
where the time goes in v4:
time: 36 us; the launch traced here: 35.6 us
  starting transfers between devices  10.1 us (28%)
  waiting for transfers between devices  9.49 us (26%)
  local copies, waits for them, and re-layouts  6.67 us (19%)
  Pallas kernels  4.57 us (13%)
  other arithmetic  2.12 us (6%)
  matrix products  1.82 us (5%)
  between operations  0.82 us (2%)
    ppermute x5, starting transfers between devices, all_sum(): x = x + lax.ppermute(x, axis, [(i, i ^ step) for i in range(n)])  10.1 us
    ppermute x5, waiting for transfers between devices, all_sum(): x = x + lax.ppermute(x, axis, [(i, i ^ step) for i in range(n)])  9.49 us
    pallas_call x1, Pallas kernels, tail(): pl.pallas_call(functools.partial(tail_kernel, scale=1.0 / user_total, roo...  4.57 us
    unnamed x17, local copies, waits for them, and re-layouts  4.53 us
    another operation x2, local copies, waits for them, and re-layouts, local(): item_tiles = item_factors[0].reshape(rank_size, item_count, width)  0.83 us
  transfers between devices with their start and end apart: 5, of which 5 were waited for; matrix products, arithmetic and copies ran while one was open for 3% of the time, Pallas kernels for 0%

profile of v4, /device:TPU:0, one launch (start us, length us, event | category | flops | bytes accessed | tf_op | source)
XLA Modules:
  0.0 35.6 jit_solution(13149899871375135654)
XLA Ops:
  0.6 0.7 %broadcast_compare_fusion.1 = pred[4]{0:T(512)(128)(4,1)S(1)} fusion(s32[4]{0:T(128)} %param.12), kind=kLoop, calls=%fused_computation.34 | loop fusion | flops 4 | bytes 20 | tf_op jit(solution)/shard_map/gt | solution.py:79
  1.3 0.7 %compare_select_fusion = s32[4,3]{1,0:T(4,128)S(1)} fusion(s32[4,3]{1,0:T(4,128)} %param.10), kind=kLoop, calls=%fused_computation.28 | loop fusion | flops 36 | bytes 96 | tf_op jit(solution)/shard_map/jit(_take)/jit(_where)/select_n | solution.py:75
  2.0 0.1 reshape.40
  2.1 0.8 %reshape_squeeze.6 = bf16[64,3,128]{2,1,0:T(4,128)(2,1)S(1)} reshape(bf16[1,64,384]{2,1,0:T(8,128)(2,1)} %param.14) | data formatting | bytes 98304 | tf_op jit(solution)/shard_map/reshape;squeeze | solution.py:74
  2.9 0.0 copy-start.1
  2.9 1.3 %copy.20 = bf16[4,3,128,128]{2,3,1,0:T(8,128)(2,1)S(1)} copy(bf16[4,3,128,128]{3,2,1,0:T(8,128)(2,1)} %param.8) | data formatting | bytes 786432 | tf_op args[0]
  4.2 0.0 copy-done.1
  4.2 0.0 copy-start.3
  4.2 0.2 copy.23
  4.4 0.6 %copy-done.3 = bf16[64,512]{1,0:T(8,128)(2,1)S(1)} copy-done((bf16[64,512]{1,0:T(8,128)(2,1)S(1)}, bf16[64,512]{1,0:T(8,128)(2,1)}, u32[]{:S(2)}) %copy-start.3) | copy-done | bytes 65560
  5.0 0.0 copy-start.2
  5.1 0.7 %copy-done.2 = bf16[1,32,384]{2,1,0:T(8,128)(2,1)S(1)} copy-done((bf16[1,32,384]{2,1,0:T(8,128)(2,1)S(1)}, bf16[1,32,384]{2,1,0:T(8,128)(2,1)}, u32[]{:S(2)}) %copy-start.2) | copy-done | bytes 24600
  5.8 0.6 %gather_fusion = bf16[12,64,128]{2,1,0:T(8,128)(2,1)S(1)} fusion(bf16[64,3,128]{2,0,1:T(8,128)(2,1)S(1)} %copy.21, s32[1024]{0:T(1024)S(1)} %pad_clamp_fusion), kind=kCustom, calls=%fused_computation | custom fusion | bytes 393264 | tf_op jit(solution)/shard_map/jit(_take)/gather | solution.py:75
  6.4 0.0 copy-start.4
  6.4 0.0 copy-start.5
  6.4 0.6 %gather_fusion.1 = bf16[12,32,128]{2,1,0:T(8,128)(2,1)S(1)} fusion(bf16[32,3,128]{2,0,1:T(8,128)(2,1)S(1)} %copy.24, s32[1024]{0:T(1024)S(1)} %pad_clamp_fusion), kind=kCustom, calls=%fused_computation.1 | custom fusion | bytes 196656 | tf_op jit(solution)/shard_map/jit(_take)/gather | solution.py:84
  7.0 0.1 copy-done.4
  7.1 0.0 copy-done.5
  7.1 0.1 broadcast_and_fusion
  7.2 0.5 %fusion.3 = bf16[4,3,128,128]{2,3,1,0:T(8,128)(2,1)S(1)} fusion(bf16[4,3,128,128]{2,3,1,0:T(8,128)(2,1)S(1)} %copy.23, bf16[4,3,128,128]{2,3,1,0:T(8,128)(2,1)S(1)} %copy.20, pred[4,3]{1,0:T(4,128)(4,1)S(1)} %get-tuple-element.13, pred[4,3]{1,0:T(4,128)(4,1)S(1)} %get-tuple-element.14, bf16[4,3,64,128]{3,2,1,0:T(8,128)(2,1)S(1)} %bitcast.53, ...), kind=kOutput, calls=%fused_computation.6 | convolution fusion | flops 26443776 | bytes 1441828 | tf_op jit(solution)/shard_map/rta,rtkb->tkab/dot_general | solution.py:77
  7.6 0.2 convolution_bitcast_fusion.1
  7.9 3.0 %collective-permute-start = (f32[32,512]{1,0:T(8,128)S(1)}, f32[32,512]{1,0:T(8,128)S(1)}, u32[]{:S(2)}, u32[]{:S(2)}) collective-permute-start(f32[32,512]{1,0:T(8,128)S(1)} %bitcast.57), channel_id=1, source_target_pairs={{0,1},{1,0},{2,3},{3,2},{4,5},{5,4},{6,7},{7,6},{8,9},{9,8},{10,11... | collective-permute-start | bytes 196616 | tf_op jit(solution)/shard_map/ppermute | solution.py:17
  10.9 0.1 copy.27
  11.0 2.2 %collective-permute-done = f32[32,512]{1,0:T(8,128)S(1)} collective-permute-done((f32[32,512]{1,0:T(8,128)S(1)}, f32[32,512]{1,0:T(8,128)S(1)}, u32[]{:S(2)}, u32[]{:S(2)}) %collective-permute-start) | collective-permute-done | bytes 65568 | tf_op jit(solution)/shard_map/ppermute | solution.py:17
  13.2 0.0 copy-start
  13.2 0.6 %copy-done = f32[32,512]{1,0:T(8,128)} copy-done((f32[32,512]{1,0:T(8,128)}, f32[32,512]{1,0:T(8,128)S(1)}, u32[]{:S(2)}) %copy-start) | copy-done | bytes 65560
  13.8 0.2 fusion.25
  14.0 0.5 %fusion.15 = f32[4,3,128,32]{2,3,1,0:T(8,128)S(1)} fusion(bf16[4,3,128,128]{2,3,1,0:T(8,128)(2,1)S(1)} %fusion.3, f32[32,4,128,1]{2,1,0,3:T(4,128)S(1)} %reshape.60), kind=kOutput, calls=%fused_computation.22 | convolution fusion | flops 75497472 | bytes 655360 | tf_op jit(solution)/shard_map/jta,tkab->jtkb/dot_general | solution.py:92
  14.5 0.4 %fusion.4 = f32[3,32,128,1]{2,0,3,1:T(4,128)S(1)} fusion(f32[4,3,128,32]{2,3,1,0:T(8,128)S(1)} %fusion.15, s32[4,3]{0,1:T(4,128)S(1)} %copy.27), kind=kOutput, calls=%fused_computation.8 | convolution fusion | flops 1769508 | bytes 245808 | tf_op jit(solution)/shard_map/jtkb,tkc->jcb/dot_general | solution.py:101
  15.0 0.1 collective-permute-start.1
  15.0 1.2 %collective-permute-done.1 = f32[32,512]{1,0:T(8,128)S(1)} collective-permute-done((f32[32,512]{1,0:T(8,128)S(1)}, f32[32,512]{1,0:T(8,128)S(1)}, u32[]{:S(2)}, u32[]{:S(2)}) %collective-permute-start.1) | collective-permute-done | bytes 65568 | tf_op jit(solution)/shard_map/ppermute | solution.py:17
  16.3 2.1 %collective-permute-start.2 = (f32[32,512]{1,0:T(8,128)S(1)}, f32[32,512]{1,0:T(8,128)S(1)}, u32[]{:S(2)}, u32[]{:S(2)}) collective-permute-start(f32[32,512]{1,0:T(8,128)S(1)} %fusion.24), channel_id=1, source_target_pairs={{0,4},{2,6},{4,0},{6,2},{8,12},{10,14},{12,8},{14,10},{16,20},{18,... | collective-permute-start | bytes 196616 | tf_op jit(solution)/shard_map/ppermute | solution.py:17
  18.4 2.4 %collective-permute-done.2 = f32[32,512]{1,0:T(8,128)S(1)} collective-permute-done((f32[32,512]{1,0:T(8,128)S(1)}, f32[32,512]{1,0:T(8,128)S(1)}, u32[]{:S(2)}, u32[]{:S(2)}) %collective-permute-start.2) | collective-permute-done | bytes 65568 | tf_op jit(solution)/shard_map/ppermute | solution.py:17
  20.8 2.0 %collective-permute-start.3 = (f32[32,512]{1,0:T(8,128)S(1)}, f32[32,512]{1,0:T(8,128)S(1)}, u32[]{:S(2)}, u32[]{:S(2)}) collective-permute-start(f32[32,512]{1,0:T(8,128)S(1)} %add.26), channel_id=1, source_target_pairs={{0,8},{2,10},{4,12},{6,14},{8,0},{10,2},{12,4},{14,6},{16,24},{18,... | collective-permute-start | bytes 196616 | tf_op jit(solution)/shard_map/ppermute | solution.py:17
  22.8 2.4 %collective-permute-done.3 = f32[32,512]{1,0:T(8,128)S(1)} collective-permute-done((f32[32,512]{1,0:T(8,128)S(1)}, f32[32,512]{1,0:T(8,128)S(1)}, u32[]{:S(2)}, u32[]{:S(2)}) %collective-permute-start.3) | collective-permute-done | bytes 65568 | tf_op jit(solution)/shard_map/ppermute | solution.py:17
  25.2 3.0 %collective-permute-start.4 = (f32[32,512]{1,0:T(8,128)S(1)}, f32[32,512]{1,0:T(8,128)S(1)}, u32[]{:S(2)}, u32[]{:S(2)}) collective-permute-start(f32[32,512]{1,0:T(8,128)S(1)} %add.27), channel_id=1, source_target_pairs={{0,16},{2,18},{4,20},{6,22},{8,24},{10,26},{12,28},{14,30},{16,0},... | collective-permute-start | bytes 196616 | tf_op jit(solution)/shard_map/ppermute | solution.py:17
  28.2 0.9 %copy.28 = bf16[4,3,128,128]{3,2,1,0:T(8,128)(2,1)} copy(bf16[4,3,128,128]{2,3,1,0:T(8,128)(2,1)S(1)} %fusion.3) | data formatting | bytes 786432
  29.1 1.3 %collective-permute-done.4 = f32[32,512]{1,0:T(8,128)S(1)} collective-permute-done((f32[32,512]{1,0:T(8,128)S(1)}, f32[32,512]{1,0:T(8,128)S(1)}, u32[]{:S(2)}, u32[]{:S(2)}) %collective-permute-start.4) | collective-permute-done | bytes 65568 | tf_op jit(solution)/shard_map/ppermute | solution.py:17
  30.4 0.6 %add.28.reduced_ref = f32[32,512]{1,0:T(8,128)} add(f32[32,512]{1,0:T(8,128)S(1)} %add.27, f32[32,512]{1,0:T(8,128)S(1)} %collective-permute-done.4) | non-fusion elementwise | flops 16384 | bytes 196608 | tf_op jit(solution)/shard_map/add | solution.py:17
  31.1 4.6 %shard_map.103 = (f32[32,512]{1,0:T(8,128)}, f32[32,384]{1,0:T(8,128)}) custom-call(f32[32,512]{1,0:T(8,128)} %add.28.reduced_ref, f32[32,512]{1,0:T(8,128)} %copy-done, bf16[32,384]{1,0:T(8,128)(2,1)} %bitcast.55), custom_call_target="tpu_custom_call" | custom-call | flops 15728640 | bytes 278528 | tf_op jit(solution)/shard_map/pallas_call | solution.py:50
  (13 shorter events, 0.1 us)
Async XLA Ops:
  2.9 1.3 %copy-start.1 = (bf16[4,3,128,128]{3,2,1,0:T(8,128)(2,1)S(1)}, bf16[4,3,128,128]{3,2,1,0:T(8,128)(2,1)}, u32[]{:S(2)}) copy-start(bf16[4,3,128,128]{3,2,1,0:T(8,128)(2,1)} %param.9) | copy-start | bytes 1179652
  4.2 0.8 %copy-start.3 = (bf16[64,512]{1,0:T(8,128)(2,1)S(1)}, bf16[64,512]{1,0:T(8,128)(2,1)}, u32[]{:S(2)}) copy-start(bf16[64,512]{1,0:T(8,128)(2,1)} %param.13) | copy-start | bytes 196612
  5.0 0.7 %copy-start.2 = (bf16[1,32,384]{2,1,0:T(8,128)(2,1)S(1)}, bf16[1,32,384]{2,1,0:T(8,128)(2,1)}, u32[]{:S(2)}) copy-start(bf16[1,32,384]{2,1,0:T(8,128)(2,1)} %param.15) | copy-start | bytes 73732
  6.4 0.7 %copy-start.4 = (s32[4,3]{1,0:T(4,128)S(1)}, s32[4,3]{1,0:T(4,128)}, u32[]{:S(2)}) copy-start(s32[4,3]{1,0:T(4,128)} %param.10) | copy-start | bytes 148
  6.4 0.7 %copy-start.5 = (s32[4,3]{1,0:T(4,128)S(1)}, s32[4,3]{1,0:T(4,128)}, u32[]{:S(2)}) copy-start(s32[4,3]{1,0:T(4,128)} %param.11) | copy-start | bytes 148
  7.9 5.2 %collective-permute-start = (f32[32,512]{1,0:T(8,128)S(1)}, f32[32,512]{1,0:T(8,128)S(1)}, u32[]{:S(2)}, u32[]{:S(2)}) collective-permute-start(f32[32,512]{1,0:T(8,128)S(1)} %bitcast.57), channel_id=1, source_target_pairs={{0,1},{1,0},{2,3},{3,2},{4,5},{5,4},{6,7},{7,6},{8,9},{9,8},{10,11... | collective-permute-start | bytes 196616 | tf_op jit(solution)/shard_map/ppermute | solution.py:17
  13.2 0.6 %copy-start = (f32[32,512]{1,0:T(8,128)}, f32[32,512]{1,0:T(8,128)S(1)}, u32[]{:S(2)}) copy-start(f32[32,512]{1,0:T(8,128)S(1)} %fusion.23.proj_ref) | copy-start | bytes 196612
  15.0 1.3 %collective-permute-start.1 = (f32[32,512]{1,0:T(8,128)S(1)}, f32[32,512]{1,0:T(8,128)S(1)}, u32[]{:S(2)}, u32[]{:S(2)}) collective-permute-start(f32[32,512]{1,0:T(8,128)S(1)} %select_maximum_fusion), channel_id=1, source_target_pairs={{0,2},{2,0},{4,6},{6,4},{8,10},{10,8},{12,14},{14,12},{16,18},{18,... | collective-permute-start | bytes 196616 | tf_op jit(solution)/shard_map/ppermute | solution.py:17
  16.3 4.5 %collective-permute-start.2 = (f32[32,512]{1,0:T(8,128)S(1)}, f32[32,512]{1,0:T(8,128)S(1)}, u32[]{:S(2)}, u32[]{:S(2)}) collective-permute-start(f32[32,512]{1,0:T(8,128)S(1)} %fusion.24), channel_id=1, source_target_pairs={{0,4},{2,6},{4,0},{6,2},{8,12},{10,14},{12,8},{14,10},{16,20},{18,... | collective-permute-start | bytes 196616 | tf_op jit(solution)/shard_map/ppermute | solution.py:17
  20.8 4.3 %collective-permute-start.3 = (f32[32,512]{1,0:T(8,128)S(1)}, f32[32,512]{1,0:T(8,128)S(1)}, u32[]{:S(2)}, u32[]{:S(2)}) collective-permute-start(f32[32,512]{1,0:T(8,128)S(1)} %add.26), channel_id=1, source_target_pairs={{0,8},{2,10},{4,12},{6,14},{8,0},{10,2},{12,4},{14,6},{16,24},{18,... | collective-permute-start | bytes 196616 | tf_op jit(solution)/shard_map/ppermute | solution.py:17
  25.2 5.2 %collective-permute-start.4 = (f32[32,512]{1,0:T(8,128)S(1)}, f32[32,512]{1,0:T(8,128)S(1)}, u32[]{:S(2)}, u32[]{:S(2)}) collective-permute-start(f32[32,512]{1,0:T(8,128)S(1)} %add.27), channel_id=1, source_target_pairs={{0,16},{2,18},{4,20},{6,22},{8,24},{10,26},{12,28},{14,30},{16,0},... | collective-permute-start | bytes 196616 | tf_op jit(solution)/shard_map/ppermute | solution.py:17

commit v5 on v4

--- a/solution.py
+++ b/solution.py
@@ -61,33 +61,80 @@
     )(reduced, projected, start)
 
 
+def update_kernel(cols_ref, live_ref, chosen_ref, rat_ref, res_ref, user_ref, item_ref, start_ref, upd_ref, part_ref):
+    t = pl.program_id(0)
+    width = rat_ref.shape[2]
+    slots = rat_ref.shape[1]
+    tiles = item_ref.shape[1] // width
+    user = user_ref[...]
+    pick = chosen_ref[t] > 0
+    acc = jnp.zeros(part_ref.shape, jnp.float32)
+    for k in range(slots):
+        c = cols_ref[t, k]
+        live = live_ref[t, k] > 0
+        factor = item_ref[:, 0:width]
+        start = start_ref[:, 0:width]
+        for j in range(1, tiles):
+            factor = jnp.where(c == j, item_ref[:, j * width : (j + 1) * width], factor)
+            start = jnp.where(c == j, start_ref[:, j * width : (j + 1) * width], start)
+        estimate = lax.dot_general(
+            user, factor, (((0,), (0,)), ((), ())), preferred_element_type=jnp.float32
+        )
+        fresh = jnp.where(
+            live & pick, rat_ref[0, k].astype(jnp.float32) - estimate, res_ref[0, k].astype(jnp.float32)
+        )
+        fresh = jnp.where(live, fresh, 0.0).astype(jnp.bfloat16)
+        upd_ref[0, k] = fresh
+        acc = acc + lax.dot_general(
+            start, fresh, (((1,), (1,)), ((), ())), preferred_element_type=jnp.float32
+        )
+    part_ref[...] = acc
+
+
+def update(ratings, residual, tile_columns, occupied, chosen, user_factors, items, start):
+    rows, slots, width, _ = ratings.shape
+    rank = user_factors.shape[0]
+    block = start.shape[0]
+    smem = pl.BlockSpec(memory_space=pltpu.SMEM)
+    tile = pl.BlockSpec((1, slots, width, width), lambda t: (t, 0, 0, 0))
+    return pl.pallas_call(
+        update_kernel,
+        grid=(rows,),
+        out_shape=(
+            jax.ShapeDtypeStruct(ratings.shape, jnp.bfloat16),
+            jax.ShapeDtypeStruct((block, rows * width), jnp.float32),
+        ),
+        in_specs=[
+            smem,
+            smem,
+            smem,
+            tile,
+            tile,
+            pl.BlockSpec((rank, width), lambda t: (0, t)),
+            pl.BlockSpec(items.shape, lambda t: (0, 0)),
+            pl.BlockSpec(start.shape, lambda t: (0, 0)),
+        ],
+        out_specs=(tile, pl.BlockSpec((block, width), lambda t: (0, t))),
+        cost_estimate=pl.CostEstimate(
+            flops=2 * rows * slots * width * width * (rank + block),
+            transcendentals=0,
+            bytes_accessed=6 * ratings.size + 4 * block * rows * width,
+        ),
+    )(tile_columns, occupied, chosen, ratings, residual, user_factors, items, start)
+
+
 def local(
     ratings, residual, tile_columns, occupied, chosen, user_factors, item_factors, start_block
 ):
     rows_dev = ratings.shape[0]
     width = ratings.shape[2]
-    rank_size = user_factors.shape[0]
     block_size = start_block.shape[1]
     item_count = item_factors.shape[2] // width
     user_total = user_factors.shape[1] * lax.axis_size("users")
-    root = float(user_total) ** 0.5
-    item_tiles = item_factors[0].reshape(rank_size, item_count, width)
-    factors = jnp.take(item_tiles, tile_columns, axis=1)
-    user_tiles = user_factors.reshape(rank_size, rows_dev, width)
-    estimate = jnp.einsum("rta,rtkb->tkab", user_tiles, factors, preferred_element_type=jnp.float32)
-    live_slot = (occupied > 0)[:, :, None, None]
-    selected = live_slot & (chosen > 0)[:, None, None, None]
-    updated = jnp.where(
-        selected, ratings.astype(jnp.float32) - estimate, residual.astype(jnp.float32)
+    updated, partial_products = update(
+        ratings, residual, tile_columns, occupied, chosen, user_factors, item_factors[0], start_block[0]
     )
-    updated = jnp.where(live_slot, updated, jnp.float32(0.0)).astype(jnp.bfloat16)
-    start_tiles = jnp.take(
-        start_block[0].reshape(block_size, item_count, width), tile_columns, axis=1
-    )
-    partial_products = jnp.einsum(
-        "tkab,jtkb->jta", updated, start_tiles, preferred_element_type=jnp.float32
-    )
-    projected = all_sum(partial_products.reshape(block_size, rows_dev * width), "items")
+    projected = all_sum(partial_products, "items")
     gram_part = jnp.dot(projected, projected.T, precision=lax.Precision.HIGHEST)
     slot_terms = jnp.einsum(
         "jta,tkab->jtkb",

time: 36 us -> 33.7 us (0.936)
  local copies, waits for them, and re-layouts: 6.67 us -> 0.71 us
  Pallas kernels: 4.57 us -> 8.74 us
  waiting for transfers between devices: 9.49 us -> 10.6 us
  matrix products: 1.82 us -> 0.93 us
  other arithmetic: 2.12 us -> 1.52 us
    pallas_call x0 -> x1, Pallas kernels: none -> 4.16 us  [update(): pl.pallas_call(update_kernel, grid=(rows,), out_shape=(jax.ShapeDtypeStru...]
    unnamed x17 -> x8, local copies, waits for them, and re-layouts: 4.53 us -> 0.69 us
    gather x2 -> x0, local copies, waits for them, and re-layouts: 1.15 us -> none  [the longest x1 0.58 us: local(): factors = jnp.take(item_tiles, tile_columns, axis=1)]
    ppermute x5, waiting for transfers between devices: 9.49 us -> 10.6 us  [all_sum(): x = x + lax.ppermute(x, axis, [(i, i ^ step) for i in range(n)])]
    another operation x4 -> x0, local copies, waits for them, and re-layouts: 0.85 us -> none  [the longest x2 0.83 us: local(): item_tiles = item_factors[0].reshape(rank_size, item_count, width)]
    add x5, other arithmetic: 0.68 us -> 1.51 us  [all_sum(): x = x + lax.ppermute(x, axis, [(i, i ^ step) for i in range(n)])]
    dot_general x2 -> x0, matrix products: 0.69 us -> none  [the longest x1 0.45 us: local(): jnp.einsum('rta,rtkb->tkab', user_tiles, factors, preferred_element_type=...]
    select_n x1 -> x0, other arithmetic: 0.68 us -> none  [local(): factors = jnp.take(item_tiles, tile_columns, axis=1)]
  transfers between devices with their start and end apart: 5 -> 5, of which waited for: 5 -> 5; matrix products, arithmetic and copies ran while one was open for 3% -> 0% of each run, Pallas kernels for 0% -> 0%
where the time goes in v5:
time: 33.7 us; the launch traced here: 33.4 us
  waiting for transfers between devices  10.6 us (31%)
  starting transfers between devices  10.1 us (30%)
  Pallas kernels  8.74 us (26%)
  other arithmetic  1.52 us (5%)
  matrix products  0.93 us (3%)
  between operations  0.73 us (2%)
  local copies, waits for them, and re-layouts  0.71 us (2%)
    ppermute x5, waiting for transfers between devices, all_sum(): x = x + lax.ppermute(x, axis, [(i, i ^ step) for i in range(n)])  10.6 us
    ppermute x5, starting transfers between devices, all_sum(): x = x + lax.ppermute(x, axis, [(i, i ^ step) for i in range(n)])  10.1 us
    pallas_call x1, Pallas kernels, tail(): pl.pallas_call(functools.partial(tail_kernel, scale=1.0 / user_total, roo...  4.57 us
    pallas_call x1, Pallas kernels, update(): pl.pallas_call(update_kernel, grid=(rows,), out_shape=(jax.ShapeDtypeStru...  4.16 us
    add x5, other arithmetic, all_sum(): x = x + lax.ppermute(x, axis, [(i, i ^ step) for i in range(n)])  1.51 us
    unnamed x8, local copies, waits for them, and re-layouts  0.69 us
  transfers between devices with their start and end apart: 5, of which 5 were waited for; matrix products, arithmetic and copies ran while one was open for 0% of the time, Pallas kernels for 0%

profile of v5, /device:TPU:0, one launch (start us, length us, event | category | flops | bytes accessed | tf_op | source)
XLA Modules:
  0.0 33.4 jit_solution(10693008960917925531)
XLA Ops:
  0.6 0.0 copy-start.2
  0.6 4.2 %shard_map.103 = (bf16[4,3,128,128]{3,2,1,0:T(8,128)(2,1)}, f32[32,512]{1,0:T(8,128)}) custom-call(s32[4,3]{1,0:T(4,128)} %cols_ref.1, s32[4,3]{1,0:T(4,128)} %live_ref.1, s32[4]{0:T(128)} %chosen_ref.1, bf16[4,3,128,128]{3,2,1,0:T(8,128)(2,1)} %rat_ref.1, bf16[4,3,128,128]{3,2,1,0:T(8,128)(2,1)} %res_ref.1, bf16[64,512]{1,0:T(8,128)(2,1)} %user_ref.1, ...), custom_call_target="tpu_custom_call" | custom-call | flops 37748736 | bytes 1245184 | tf_op jit(solution)/shard_map/pallas_call | solution.py:100
  4.8 0.0 copy-start.1
  4.8 3.0 %collective-permute-start = (f32[32,512]{1,0:T(8,128)}, f32[32,512]{1,0:T(8,128)S(1)}, u32[]{:S(2)}, u32[]{:S(2)}) collective-permute-start(f32[32,512]{1,0:T(8,128)} %get-tuple-element.8), channel_id=1, source_target_pairs={{0,1},{1,0},{2,3},{3,2},{4,5},{5,4},{6,7},{7,6},{8,9},{9,8},{10,11... | collective-permute-start | bytes 196616 | tf_op jit(solution)/shard_map/ppermute | solution.py:17
  7.8 0.0 copy-done.2
  7.8 0.1 copy.12
  7.9 2.4 %collective-permute-done = f32[32,512]{1,0:T(8,128)S(1)} collective-permute-done((f32[32,512]{1,0:T(8,128)}, f32[32,512]{1,0:T(8,128)S(1)}, u32[]{:S(2)}, u32[]{:S(2)}) %collective-permute-start) | collective-permute-done | bytes 65568 | tf_op jit(solution)/shard_map/ppermute | solution.py:17
  10.3 0.8 %add.17.proj_ref = f32[32,512]{1,0:T(8,128)S(1)} add(f32[32,512]{1,0:T(8,128)} %get-tuple-element.8, f32[32,512]{1,0:T(8,128)S(1)} %collective-permute-done) | non-fusion elementwise | flops 16384 | bytes 196608 | tf_op jit(solution)/shard_map/add | solution.py:17
  11.1 0.0 copy-start
  11.2 0.6 %copy-done = f32[32,512]{1,0:T(8,128)} copy-done((f32[32,512]{1,0:T(8,128)}, f32[32,512]{1,0:T(8,128)S(1)}, u32[]{:S(2)}) %copy-start) | copy-done | bytes 65560
  11.7 0.2 fusion.9
  11.9 0.0 copy-done.1
  11.9 0.3 fusion.3
  12.3 0.4 %fusion = f32[3,32,128,1]{2,0,3,1:T(4,128)S(1)} fusion(f32[4,3,128,32]{2,3,1,0:T(8,128)S(1)} %fusion.3, s32[4,3]{0,1:T(4,128)S(1)} %copy.12), kind=kOutput, calls=%fused_computation | convolution fusion | flops 1769508 | bytes 245808 | tf_op jit(solution)/shard_map/jtkb,tkc->jcb/dot_general | solution.py:148
  12.7 0.1 collective-permute-start.1
  12.8 1.2 %collective-permute-done.1 = f32[32,512]{1,0:T(8,128)S(1)} collective-permute-done((f32[32,512]{1,0:T(8,128)S(1)}, f32[32,512]{1,0:T(8,128)S(1)}, u32[]{:S(2)}, u32[]{:S(2)}) %collective-permute-start.1) | collective-permute-done | bytes 65568 | tf_op jit(solution)/shard_map/ppermute | solution.py:17
  14.1 2.1 %collective-permute-start.2 = (f32[32,512]{1,0:T(8,128)S(1)}, f32[32,512]{1,0:T(8,128)S(1)}, u32[]{:S(2)}, u32[]{:S(2)}) collective-permute-start(f32[32,512]{1,0:T(8,128)S(1)} %fusion.8), channel_id=1, source_target_pairs={{0,4},{2,6},{4,0},{6,2},{8,12},{10,14},{12,8},{14,10},{16,20},{18,... | collective-permute-start | bytes 196616 | tf_op jit(solution)/shard_map/ppermute | solution.py:17
  16.2 2.4 %collective-permute-done.2 = f32[32,512]{1,0:T(8,128)S(1)} collective-permute-done((f32[32,512]{1,0:T(8,128)S(1)}, f32[32,512]{1,0:T(8,128)S(1)}, u32[]{:S(2)}, u32[]{:S(2)}) %collective-permute-start.2) | collective-permute-done | bytes 65568 | tf_op jit(solution)/shard_map/ppermute | solution.py:17
  18.6 2.0 %collective-permute-start.3 = (f32[32,512]{1,0:T(8,128)S(1)}, f32[32,512]{1,0:T(8,128)S(1)}, u32[]{:S(2)}, u32[]{:S(2)}) collective-permute-start(f32[32,512]{1,0:T(8,128)S(1)} %add.19), channel_id=1, source_target_pairs={{0,8},{2,10},{4,12},{6,14},{8,0},{10,2},{12,4},{14,6},{16,24},{18,... | collective-permute-start | bytes 196616 | tf_op jit(solution)/shard_map/ppermute | solution.py:17
  20.6 2.4 %collective-permute-done.3 = f32[32,512]{1,0:T(8,128)S(1)} collective-permute-done((f32[32,512]{1,0:T(8,128)S(1)}, f32[32,512]{1,0:T(8,128)S(1)}, u32[]{:S(2)}, u32[]{:S(2)}) %collective-permute-start.3) | collective-permute-done | bytes 65568 | tf_op jit(solution)/shard_map/ppermute | solution.py:17
  23.0 3.0 %collective-permute-start.4 = (f32[32,512]{1,0:T(8,128)S(1)}, f32[32,512]{1,0:T(8,128)S(1)}, u32[]{:S(2)}, u32[]{:S(2)}) collective-permute-start(f32[32,512]{1,0:T(8,128)S(1)} %add.20), channel_id=1, source_target_pairs={{0,16},{2,18},{4,20},{6,22},{8,24},{10,26},{12,28},{14,30},{16,0},... | collective-permute-start | bytes 196616 | tf_op jit(solution)/shard_map/ppermute | solution.py:17
  25.9 2.2 %collective-permute-done.4 = f32[32,512]{1,0:T(8,128)S(1)} collective-permute-done((f32[32,512]{1,0:T(8,128)S(1)}, f32[32,512]{1,0:T(8,128)S(1)}, u32[]{:S(2)}, u32[]{:S(2)}) %collective-permute-start.4) | collective-permute-done | bytes 65568 | tf_op jit(solution)/shard_map/ppermute | solution.py:17
  28.2 0.6 %add.21.reduced_ref = f32[32,512]{1,0:T(8,128)} add(f32[32,512]{1,0:T(8,128)S(1)} %add.20, f32[32,512]{1,0:T(8,128)S(1)} %collective-permute-done.4) | non-fusion elementwise | flops 16384 | bytes 196608 | tf_op jit(solution)/shard_map/add | solution.py:17
  28.8 4.6 %shard_map.104 = (f32[32,512]{1,0:T(8,128)}, f32[32,384]{1,0:T(8,128)}) custom-call(f32[32,512]{1,0:T(8,128)} %add.21.reduced_ref, f32[32,512]{1,0:T(8,128)} %copy-done, bf16[32,384]{1,0:T(8,128)(2,1)} %bitcast.24), custom_call_target="tpu_custom_call" | custom-call | flops 15728640 | bytes 278528 | tf_op jit(solution)/shard_map/pallas_call | solution.py:50
  (6 shorter events, 0.1 us)
Async XLA Ops:
  0.6 7.2 %copy-start.2 = (s32[4,3]{1,0:T(4,128)S(1)}, s32[4,3]{1,0:T(4,128)}, u32[]{:S(2)}) copy-start(s32[4,3]{1,0:T(4,128)} %cols_ref.1) | copy-start | bytes 148
  4.8 7.1 %copy-start.1 = (bf16[4,3,128,128]{3,2,1,0:T(8,128)(2,1)S(1)}, bf16[4,3,128,128]{3,2,1,0:T(8,128)(2,1)}, u32[]{:S(2)}) copy-start(bf16[4,3,128,128]{3,2,1,0:T(8,128)(2,1)} %get-tuple-element.4) | copy-start | bytes 1179652
  4.8 5.5 %collective-permute-start = (f32[32,512]{1,0:T(8,128)}, f32[32,512]{1,0:T(8,128)S(1)}, u32[]{:S(2)}, u32[]{:S(2)}) collective-permute-start(f32[32,512]{1,0:T(8,128)} %get-tuple-element.8), channel_id=1, source_target_pairs={{0,1},{1,0},{2,3},{3,2},{4,5},{5,4},{6,7},{7,6},{8,9},{9,8},{10,11... | collective-permute-start | bytes 196616 | tf_op jit(solution)/shard_map/ppermute | solution.py:17
  11.1 0.6 %copy-start = (f32[32,512]{1,0:T(8,128)}, f32[32,512]{1,0:T(8,128)S(1)}, u32[]{:S(2)}) copy-start(f32[32,512]{1,0:T(8,128)S(1)} %add.17.proj_ref) | copy-start | bytes 196612
  12.7 1.3 %collective-permute-start.1 = (f32[32,512]{1,0:T(8,128)S(1)}, f32[32,512]{1,0:T(8,128)S(1)}, u32[]{:S(2)}, u32[]{:S(2)}) collective-permute-start(f32[32,512]{1,0:T(8,128)S(1)} %select_maximum_fusion), channel_id=1, source_target_pairs={{0,2},{2,0},{4,6},{6,4},{8,10},{10,8},{12,14},{14,12},{16,18},{18,... | collective-permute-start | bytes 196616 | tf_op jit(solution)/shard_map/ppermute | solution.py:17
  14.1 4.5 %collective-permute-start.2 = (f32[32,512]{1,0:T(8,128)S(1)}, f32[32,512]{1,0:T(8,128)S(1)}, u32[]{:S(2)}, u32[]{:S(2)}) collective-permute-start(f32[32,512]{1,0:T(8,128)S(1)} %fusion.8), channel_id=1, source_target_pairs={{0,4},{2,6},{4,0},{6,2},{8,12},{10,14},{12,8},{14,10},{16,20},{18,... | collective-permute-start | bytes 196616 | tf_op jit(solution)/shard_map/ppermute | solution.py:17
  18.6 4.3 %collective-permute-start.3 = (f32[32,512]{1,0:T(8,128)S(1)}, f32[32,512]{1,0:T(8,128)S(1)}, u32[]{:S(2)}, u32[]{:S(2)}) collective-permute-start(f32[32,512]{1,0:T(8,128)S(1)} %add.19), channel_id=1, source_target_pairs={{0,8},{2,10},{4,12},{6,14},{8,0},{10,2},{12,4},{14,6},{16,24},{18,... | collective-permute-start | bytes 196616 | tf_op jit(solution)/shard_map/ppermute | solution.py:17
  23.0 5.2 %collective-permute-start.4 = (f32[32,512]{1,0:T(8,128)S(1)}, f32[32,512]{1,0:T(8,128)S(1)}, u32[]{:S(2)}, u32[]{:S(2)}) collective-permute-start(f32[32,512]{1,0:T(8,128)S(1)} %add.20), channel_id=1, source_target_pairs={{0,16},{2,18},{4,20},{6,22},{8,24},{10,26},{12,28},{14,30},{16,0},... | collective-permute-start | bytes 196616 | tf_op jit(solution)/shard_map/ppermute | solution.py:17

commit v6 on v5

--- a/solution.py
+++ b/solution.py
@@ -8,21 +8,25 @@
 from jax.sharding import PartitionSpec as P
 
 
-def all_sum(x, axis):
+def all_sum_parts(x, axis):
     n = lax.axis_size(axis)
     if n & (n - 1):
-        return lax.psum(x, axis)
+        return lax.psum(x, axis), jnp.zeros_like(x)
     step = 1
+    other = jnp.zeros_like(x)
     while step < n:
-        x = x + lax.ppermute(x, axis, [(i, i ^ step) for i in range(n)])
+        if step > 1:
+            x = x + other
+        other = lax.ppermute(x, axis, [(i, i ^ step) for i in range(n)])
         step *= 2
-    return x
-
-
-def tail_kernel(reduced_ref, proj_ref, start_ref, left_ref, right_ref, *, scale, root):
+    return x, other
+
+
+def tail_kernel(mine_ref, other_ref, proj_ref, start_ref, left_ref, right_ref, *, scale, root):
     n = start_ref.shape[0]
-    lanes = reduced_ref.shape[1] - start_ref.shape[1]
-    g = reduced_ref[:, :n] * scale
+    lanes = mine_ref.shape[1] - start_ref.shape[1]
+    reduced = mine_ref[...] + other_ref[...]
+    g = reduced[:, :n] * scale
     g = 0.5 * (g + g.T)
     rows = lax.broadcasted_iota(jnp.int32, (n, 2 * n), 0)
     cols = lax.broadcasted_iota(jnp.int32, (n, 2 * n), 1)
@@ -36,14 +40,14 @@
     inverse = aug[:, n:]
     hi = lax.Precision.HIGHEST
     left_ref[...] = jnp.dot(inverse, proj_ref[...], precision=hi, preferred_element_type=jnp.float32)
-    summed = jnp.dot(inverse, reduced_ref[:, lanes:], precision=hi, preferred_element_type=jnp.float32)
+    summed = jnp.dot(inverse, reduced[:, lanes:], precision=hi, preferred_element_type=jnp.float32)
     start_term = jnp.dot(
         upper, start_ref[...].astype(jnp.float32), precision=hi, preferred_element_type=jnp.float32
     )
     right_ref[...] = summed / root - root * start_term
 
 
-def tail(reduced, projected, start, user_total):
+def tail(mine, other, projected, start, user_total):
     n, users = projected.shape
     items = start.shape[1]
     vmem = pl.BlockSpec(memory_space=pltpu.VMEM)
@@ -53,12 +57,56 @@
             jax.ShapeDtypeStruct((n, users), jnp.float32),
             jax.ShapeDtypeStruct((n, items), jnp.float32),
         ),
-        in_specs=[vmem] * 3,
+        in_specs=[vmem] * 4,
         out_specs=(vmem, vmem),
         cost_estimate=pl.CostEstimate(
             flops=2 * n * n * (users + 2 * items) * 6, transcendentals=n, bytes_accessed=4 * n * (2 * users + 3 * items)
         ),
-    )(reduced, projected, start)
+    )(mine, other, projected, start)
+
+
+def mid_kernel(cols_ref, mine_ref, other_ref, upd_ref, proj_ref, pay_ref):
+    rows, slots, width, _ = upd_ref.shape
+    n = proj_ref.shape[0]
+    hi = lax.Precision.HIGHEST
+    proj = mine_ref[...] + other_ref[...]
+    proj_ref[...] = proj
+    gram = lax.dot_general(proj, proj, (((1,), (1,)), ((), ())), precision=hi, preferred_element_type=jnp.float32)
+    lanes = pay_ref.shape[1] - tiles_of(pay_ref.shape[1], n, width) * width
+    pay_ref[:, 0:lanes] = jnp.pad(gram, ((0, 0), (0, lanes - n)))
+    count = tiles_of(pay_ref.shape[1], n, width)
+    sums = [jnp.zeros((n, width), jnp.float32) for _ in range(count)]
+    for t in range(rows):
+        block = proj[:, t * width : (t + 1) * width]
+        for k in range(slots):
+            c = cols_ref[t, k]
+            term = jnp.dot(block, upd_ref[t, k].astype(jnp.float32), precision=hi, preferred_element_type=jnp.float32)
+            sums = [sums[j] + jnp.where(c == j, term, 0.0) for j in range(count)]
+    for j in range(count):
+        pay_ref[:, lanes + j * width : lanes + (j + 1) * width] = sums[j]
+
+
+def tiles_of(total, n, width):
+    return (total - (-(-n // width) * width)) // width
+
+
+def mid(tile_columns, mine, other, updated, tiles):
+    n, users = mine.shape
+    width = updated.shape[2]
+    lanes = -(-n // width) * width
+    vmem = pl.BlockSpec(memory_space=pltpu.VMEM)
+    return pl.pallas_call(
+        mid_kernel,
+        out_shape=(
+            jax.ShapeDtypeStruct((n, users), jnp.float32),
+            jax.ShapeDtypeStruct((n, lanes + tiles * width), jnp.float32),
+        ),
+        in_specs=[pl.BlockSpec(memory_space=pltpu.SMEM), vmem, vmem, vmem],
+        out_specs=(vmem, vmem),
+        cost_estimate=pl.CostEstimate(
+            flops=2 * n * users * (n + width) * 6, transcendentals=0, bytes_accessed=2 * updated.size + 16 * n * users
+        ),
+    )(tile_columns, mine, other, updated)
 
 
 def update_kernel(cols_ref, live_ref, chosen_ref, rat_ref, res_ref, user_ref, item_ref, start_ref, upd_ref, part_ref):
@@ -68,26 +116,37 @@
     tiles = item_ref.shape[1] // width
     user = user_ref[...]
     pick = chosen_ref[t] > 0
-    acc = jnp.zeros(part_ref.shape, jnp.float32)
+    factors, starts, lives = [], [], []
     for k in range(slots):
         c = cols_ref[t, k]
-        live = live_ref[t, k] > 0
+        lives.append(live_ref[t, k] > 0)
         factor = item_ref[:, 0:width]
         start = start_ref[:, 0:width]
         for j in range(1, tiles):
             factor = jnp.where(c == j, item_ref[:, j * width : (j + 1) * width], factor)
             start = jnp.where(c == j, start_ref[:, j * width : (j + 1) * width], start)
-        estimate = lax.dot_general(
-            user, factor, (((0,), (0,)), ((), ())), preferred_element_type=jnp.float32
+        factors.append(factor)
+        starts.append(start)
+    estimate = lax.dot_general(
+        user, jnp.concatenate(factors, axis=1), (((0,), (0,)), ((), ())), preferred_element_type=jnp.float32
+    )
+    fresh = []
+    for k in range(slots):
+        live = lives[k]
+        value = jnp.where(
+            live & pick,
+            rat_ref[0, k].astype(jnp.float32) - estimate[:, k * width : (k + 1) * width],
+            res_ref[0, k].astype(jnp.float32),
         )
-        fresh = jnp.where(
-            live & pick, rat_ref[0, k].astype(jnp.float32) - estimate, res_ref[0, k].astype(jnp.float32)
-        )
-        fresh = jnp.where(live, fresh, 0.0).astype(jnp.bfloat16)
-        upd_ref[0, k] = fresh
-        acc = acc + lax.dot_general(
-            start, fresh, (((1,), (1,)), ((), ())), preferred_element_type=jnp.float32
-        )
+        value = jnp.where(live, value, 0.0).astype(jnp.bfloat16)
+        upd_ref[0, k] = value
+        fresh.append(value)
+    acc = lax.dot_general(
+        jnp.concatenate(starts, axis=1),
+        jnp.concatenate(fresh, axis=1),
+        (((1,), (1,)), ((), ())),
+        preferred_element_type=jnp.float32,
+    )
     part_ref[...] = acc
 
 
@@ -134,23 +193,10 @@
     updated, partial_products = update(
         ratings, residual, tile_columns, occupied, chosen, user_factors, item_factors[0], start_block[0]
     )
-    projected = all_sum(partial_products, "items")
-    gram_part = jnp.dot(projected, projected.T, precision=lax.Precision.HIGHEST)
-    slot_terms = jnp.einsum(
-        "jta,tkab->jtkb",
-        projected.reshape(block_size, rows_dev, width),
-        updated.astype(jnp.float32),
-        precision=lax.Precision.HIGHEST,
-    )
-    one_hot = (
-        tile_columns[:, :, None] == jnp.arange(item_count, dtype=jnp.int32)[None, None, :]
-    ).astype(jnp.float32)
-    item_terms = jnp.einsum("jtkb,tkc->jcb", slot_terms, one_hot, precision=lax.Precision.HIGHEST)
-    item_terms = item_terms.reshape(block_size, item_count * width)
-    lanes = -(-block_size // width) * width
-    gram_lanes = jnp.pad(gram_part, ((0, 0), (0, lanes - block_size)))
-    reduced = all_sum(jnp.concatenate([gram_lanes, item_terms], axis=1), "users")
-    left_block, right_block = tail(reduced, projected, start_block[0], user_total)
+    mine, other = all_sum_parts(partial_products, "items")
+    projected, payload = mid(tile_columns, mine, other, updated, item_count)
+    mine, other = all_sum_parts(payload, "users")
+    left_block, right_block = tail(mine, other, projected, start_block[0], user_total)
     right_block = right_block.reshape(1, block_size, item_count * width)
     return (updated, left_block, right_block)
 

time: 33.7 us -> 35 us (1.039)
  Pallas kernels: 8.74 us -> 11 us
  matrix products: 0.93 us -> 0 us
  other arithmetic: 1.52 us -> 0.87 us
  local copies, waits for them, and re-layouts: 0.71 us -> 1.25 us
    pallas_call x0 -> x1, Pallas kernels: none -> 2.51 us  [mid(): pl.pallas_call(mid_kernel, out_shape=(jax.ShapeDtypeStruct((n, users), jn...]
    dot_general x3 -> x0, matrix products: 0.93 us -> none  [the longest x1 0.42 us: local(): jnp.einsum('jtkb,tkc->jcb', slot_terms, one_hot, precision=lax.Precision....]
    add x5 -> x3, other arithmetic: 1.51 us -> 0.87 us  [all_sum_parts(): x = x + other]
    unnamed x8 -> x6, local copies, waits for them, and re-layouts: 0.69 us -> 1.25 us
where the time goes in v6:
time: 35 us; the launch traced here: 34.7 us
  Pallas kernels  11 us (31%)
  waiting for transfers between devices  10.9 us (31%)
  starting transfers between devices  10 us (29%)
  local copies, waits for them, and re-layouts  1.25 us (4%)
  other arithmetic  0.87 us (2%)
  between operations  0.66 us (2%)
    ppermute x5, waiting for transfers between devices, all_sum_parts(): other = lax.ppermute(x, axis, [(i, i ^ step) for i in range(n)])  10.9 us
    ppermute x5, starting transfers between devices, all_sum_parts(): other = lax.ppermute(x, axis, [(i, i ^ step) for i in range(n)])  10 us
    pallas_call x1, Pallas kernels, tail(): pl.pallas_call(functools.partial(tail_kernel, scale=1.0 / user_total, roo...  4.6 us
    pallas_call x1, Pallas kernels, update(): pl.pallas_call(update_kernel, grid=(rows,), out_shape=(jax.ShapeDtypeStru...  3.86 us
    pallas_call x1, Pallas kernels, mid(): pl.pallas_call(mid_kernel, out_shape=(jax.ShapeDtypeStruct((n, users), jn...  2.51 us
    unnamed x6, local copies, waits for them, and re-layouts  1.25 us
    add x3, other arithmetic, all_sum_parts(): x = x + other  0.87 us
  transfers between devices with their start and end apart: 5, of which 5 were waited for; matrix products, arithmetic and copies ran while one was open for 0% of the time, Pallas kernels for 0%

profile of v6, /device:TPU:0, one launch (start us, length us, event | category | flops | bytes accessed | tf_op | source)
XLA Modules:
  0.0 34.7 jit_solution(1363414052150689280)
XLA Ops:
  0.6 3.9 %shard_map.103 = (bf16[4,3,128,128]{3,2,1,0:T(8,128)(2,1)}, f32[32,512]{1,0:T(8,128)}) custom-call(s32[4,3]{1,0:T(4,128)} %cols_ref.3, s32[4,3]{1,0:T(4,128)} %live_ref.1, s32[4]{0:T(128)} %chosen_ref.1, bf16[4,3,128,128]{3,2,1,0:T(8,128)(2,1)} %rat_ref.1, bf16[4,3,128,128]{3,2,1,0:T(8,128)(2,1)} %res_ref.1, bf16[64,512]{1,0:T(8,128)(2,1)} %user_ref.1, ...), custom_call_target="tpu_custom_call" | custom-call | flops 37748736 | bytes 1245184 | tf_op jit(solution)/shard_map/pallas_call | solution.py:159
  4.5 2.9 %collective-permute-start = (f32[32,512]{1,0:T(8,128)}, f32[32,512]{1,0:T(8,128)S(1)}, u32[]{:S(2)}, u32[]{:S(2)}) collective-permute-start(f32[32,512]{1,0:T(8,128)} %get-tuple-element.10.mine_ref), channel_id=1, source_target_pairs={{0,1},{1,0},{2,3},{3,2},{4,5},{5,4},{6,7},{7,6},{8,9},{9,8},{10,11... | collective-permute-start | bytes 196616 | tf_op jit(solution)/shard_map/ppermute | solution.py:20
  7.4 2.5 %collective-permute-done.other_ref = f32[32,512]{1,0:T(8,128)S(1)} collective-permute-done((f32[32,512]{1,0:T(8,128)}, f32[32,512]{1,0:T(8,128)S(1)}, u32[]{:S(2)}, u32[]{:S(2)}) %collective-permute-start) | collective-permute-done | bytes 65568 | tf_op jit(solution)/shard_map/ppermute | solution.py:20
  9.9 0.0 copy-start.2
  9.9 0.6 %copy-done.2 = f32[32,512]{1,0:T(8,128)} copy-done((f32[32,512]{1,0:T(8,128)}, f32[32,512]{1,0:T(8,128)S(1)}, u32[]{:S(2)}) %copy-start.2) | copy-done | bytes 65560
  10.5 2.5 %shard_map.104 = (f32[32,512]{1,0:T(8,128)}, f32[32,512]{1,0:T(8,128)}) custom-call(s32[4,3]{1,0:T(4,128)} %cols_ref.3, f32[32,512]{1,0:T(8,128)} %get-tuple-element.10.mine_ref, f32[32,512]{1,0:T(8,128)} %copy-done.2, bf16[4,3,128,128]{3,2,1,0:T(8,128)(2,1)} %get-tuple-element.6.upd_ref), custom_call_target="tpu_custom_call" | custom-call | flops 31457280 | bytes 655360 | tf_op jit(solution)/shard_map/pallas_call | solution.py:98
  13.0 0.0 collective-permute-start.1
  13.0 1.5 %collective-permute-done.1 = f32[32,512]{1,0:T(8,128)S(1)} collective-permute-done((f32[32,512]{1,0:T(8,128)}, f32[32,512]{1,0:T(8,128)S(1)}, u32[]{:S(2)}, u32[]{:S(2)}) %collective-permute-start.1) | collective-permute-done | bytes 65568 | tf_op jit(solution)/shard_map/ppermute | solution.py:20
  14.5 0.9 %add.9 = f32[32,512]{1,0:T(8,128)S(1)} add(f32[32,512]{1,0:T(8,128)} %get-tuple-element.11, f32[32,512]{1,0:T(8,128)S(1)} %collective-permute-done.1) | non-fusion elementwise | flops 16384 | bytes 196608 | tf_op jit(solution)/shard_map/add | solution.py:19
  15.3 2.1 %collective-permute-start.2 = (f32[32,512]{1,0:T(8,128)S(1)}, f32[32,512]{1,0:T(8,128)S(1)}, u32[]{:S(2)}, u32[]{:S(2)}) collective-permute-start(f32[32,512]{1,0:T(8,128)S(1)} %add.9), channel_id=1, source_target_pairs={{0,4},{2,6},{4,0},{6,2},{8,12},{10,14},{12,8},{14,10},{16,20},{18,... | collective-permute-start | bytes 196616 | tf_op jit(solution)/shard_map/ppermute | solution.py:20
  17.4 2.4 %collective-permute-done.2 = f32[32,512]{1,0:T(8,128)S(1)} collective-permute-done((f32[32,512]{1,0:T(8,128)S(1)}, f32[32,512]{1,0:T(8,128)S(1)}, u32[]{:S(2)}, u32[]{:S(2)}) %collective-permute-start.2) | collective-permute-done | bytes 65568 | tf_op jit(solution)/shard_map/ppermute | solution.py:20
  19.9 2.0 %collective-permute-start.3 = (f32[32,512]{1,0:T(8,128)S(1)}, f32[32,512]{1,0:T(8,128)S(1)}, u32[]{:S(2)}, u32[]{:S(2)}) collective-permute-start(f32[32,512]{1,0:T(8,128)S(1)} %add.10), channel_id=1, source_target_pairs={{0,8},{2,10},{4,12},{6,14},{8,0},{10,2},{12,4},{14,6},{16,24},{18,... | collective-permute-start | bytes 196616 | tf_op jit(solution)/shard_map/ppermute | solution.py:20
  21.8 2.4 %collective-permute-done.3 = f32[32,512]{1,0:T(8,128)S(1)} collective-permute-done((f32[32,512]{1,0:T(8,128)S(1)}, f32[32,512]{1,0:T(8,128)S(1)}, u32[]{:S(2)}, u32[]{:S(2)}) %collective-permute-start.3) | collective-permute-done | bytes 65568 | tf_op jit(solution)/shard_map/ppermute | solution.py:20
  24.2 0.0 copy-start
  24.2 3.0 %collective-permute-start.4 = (f32[32,512]{1,0:T(8,128)S(1)}, f32[32,512]{1,0:T(8,128)S(1)}, u32[]{:S(2)}, u32[]{:S(2)}) collective-permute-start(f32[32,512]{1,0:T(8,128)S(1)} %add.11.mine_ref), channel_id=1, source_target_pairs={{0,16},{2,18},{4,20},{6,22},{8,24},{10,26},{12,28},{14,30},{16,0},... | collective-permute-start | bytes 196616 | tf_op jit(solution)/shard_map/ppermute | solution.py:20
  27.2 2.2 %collective-permute-done.4.other_ref = f32[32,512]{1,0:T(8,128)S(1)} collective-permute-done((f32[32,512]{1,0:T(8,128)S(1)}, f32[32,512]{1,0:T(8,128)S(1)}, u32[]{:S(2)}, u32[]{:S(2)}) %collective-permute-start.4) | collective-permute-done | bytes 65568 | tf_op jit(solution)/shard_map/ppermute | solution.py:20
  29.5 0.0 copy-start.1
  29.5 0.0 copy-done
  29.5 0.6 %copy-done.1 = f32[32,512]{1,0:T(8,128)} copy-done((f32[32,512]{1,0:T(8,128)}, f32[32,512]{1,0:T(8,128)S(1)}, u32[]{:S(2)}) %copy-start.1) | copy-done | bytes 65560
  30.1 4.6 %shard_map.105 = (f32[32,512]{1,0:T(8,128)}, f32[32,384]{1,0:T(8,128)}) custom-call(f32[32,512]{1,0:T(8,128)} %copy-done, f32[32,512]{1,0:T(8,128)} %copy-done.1, f32[32,512]{1,0:T(8,128)} %get-tuple-element.12.proj_ref, bf16[32,384]{1,0:T(8,128)(2,1)} %bitcast.4), custom_call_target="tpu_custom_call" | custom-call | flops 15728640 | bytes 278528 | tf_op jit(solution)/shard_map/pallas_call | solution.py:54
  (2 shorter events, 0.0 us)
Async XLA Ops:
  4.5 5.4 %collective-permute-start = (f32[32,512]{1,0:T(8,128)}, f32[32,512]{1,0:T(8,128)S(1)}, u32[]{:S(2)}, u32[]{:S(2)}) collective-permute-start(f32[32,512]{1,0:T(8,128)} %get-tuple-element.10.mine_ref), channel_id=1, source_target_pairs={{0,1},{1,0},{2,3},{3,2},{4,5},{5,4},{6,7},{7,6},{8,9},{9,8},{10,11... | collective-permute-start | bytes 196616 | tf_op jit(solution)/shard_map/ppermute | solution.py:20
  9.9 0.6 %copy-start.2 = (f32[32,512]{1,0:T(8,128)}, f32[32,512]{1,0:T(8,128)S(1)}, u32[]{:S(2)}) copy-start(f32[32,512]{1,0:T(8,128)S(1)} %collective-permute-done.other_ref) | copy-start | bytes 196612
  13.0 1.5 %collective-permute-start.1 = (f32[32,512]{1,0:T(8,128)}, f32[32,512]{1,0:T(8,128)S(1)}, u32[]{:S(2)}, u32[]{:S(2)}) collective-permute-start(f32[32,512]{1,0:T(8,128)} %get-tuple-element.11), channel_id=1, source_target_pairs={{0,2},{2,0},{4,6},{6,4},{8,10},{10,8},{12,14},{14,12},{16,18},{18,... | collective-permute-start | bytes 196616 | tf_op jit(solution)/shard_map/ppermute | solution.py:20
  15.3 4.5 %collective-permute-start.2 = (f32[32,512]{1,0:T(8,128)S(1)}, f32[32,512]{1,0:T(8,128)S(1)}, u32[]{:S(2)}, u32[]{:S(2)}) collective-permute-start(f32[32,512]{1,0:T(8,128)S(1)} %add.9), channel_id=1, source_target_pairs={{0,4},{2,6},{4,0},{6,2},{8,12},{10,14},{12,8},{14,10},{16,20},{18,... | collective-permute-start | bytes 196616 | tf_op jit(solution)/shard_map/ppermute | solution.py:20
  19.9 4.3 %collective-permute-start.3 = (f32[32,512]{1,0:T(8,128)S(1)}, f32[32,512]{1,0:T(8,128)S(1)}, u32[]{:S(2)}, u32[]{:S(2)}) collective-permute-start(f32[32,512]{1,0:T(8,128)S(1)} %add.10), channel_id=1, source_target_pairs={{0,8},{2,10},{4,12},{6,14},{8,0},{10,2},{12,4},{14,6},{16,24},{18,... | collective-permute-start | bytes 196616 | tf_op jit(solution)/shard_map/ppermute | solution.py:20
  24.2 5.2 %copy-start = (f32[32,512]{1,0:T(8,128)}, f32[32,512]{1,0:T(8,128)S(1)}, u32[]{:S(2)}) copy-start(f32[32,512]{1,0:T(8,128)S(1)} %add.11.mine_ref) | copy-start | bytes 196612
  24.2 5.2 %collective-permute-start.4 = (f32[32,512]{1,0:T(8,128)S(1)}, f32[32,512]{1,0:T(8,128)S(1)}, u32[]{:S(2)}, u32[]{:S(2)}) collective-permute-start(f32[32,512]{1,0:T(8,128)S(1)} %add.11.mine_ref), channel_id=1, source_target_pairs={{0,16},{2,18},{4,20},{6,22},{8,24},{10,26},{12,28},{14,30},{16,0},... | collective-permute-start | bytes 196616 | tf_op jit(solution)/shard_map/ppermute | solution.py:20
  29.5 0.6 %copy-start.1 = (f32[32,512]{1,0:T(8,128)}, f32[32,512]{1,0:T(8,128)S(1)}, u32[]{:S(2)}) copy-start(f32[32,512]{1,0:T(8,128)S(1)} %collective-permute-done.4.other_ref) | copy-start | bytes 196612

commit v7 on v6

--- a/solution.py
+++ b/solution.py
@@ -68,20 +68,30 @@
 def mid_kernel(cols_ref, mine_ref, other_ref, upd_ref, proj_ref, pay_ref):
     rows, slots, width, _ = upd_ref.shape
     n = proj_ref.shape[0]
-    hi = lax.Precision.HIGHEST
     proj = mine_ref[...] + other_ref[...]
     proj_ref[...] = proj
-    gram = lax.dot_general(proj, proj, (((1,), (1,)), ((), ())), precision=hi, preferred_element_type=jnp.float32)
-    lanes = pay_ref.shape[1] - tiles_of(pay_ref.shape[1], n, width) * width
+    head = proj.astype(jnp.bfloat16)
+    tail = (proj - head.astype(jnp.float32)).astype(jnp.bfloat16)
+    nt = (((1,), (1,)), ((), ()))
+    f32 = jnp.float32
+    gram = lax.dot_general(head, head, nt, preferred_element_type=f32) + (
+        lax.dot_general(head, tail, nt, preferred_element_type=f32)
+        + lax.dot_general(tail, head, nt, preferred_element_type=f32)
+    )
+    count = tiles_of(pay_ref.shape[1], n, width)
+    lanes = pay_ref.shape[1] - count * width
     pay_ref[:, 0:lanes] = jnp.pad(gram, ((0, 0), (0, lanes - n)))
-    count = tiles_of(pay_ref.shape[1], n, width)
-    sums = [jnp.zeros((n, width), jnp.float32) for _ in range(count)]
+    sums = [jnp.zeros((n, width), f32) for _ in range(count)]
     for t in range(rows):
-        block = proj[:, t * width : (t + 1) * width]
+        tiles = jnp.concatenate([upd_ref[t, k] for k in range(slots)], axis=1)
+        part = slice(t * width, (t + 1) * width)
+        term = jnp.dot(head[:, part], tiles, preferred_element_type=f32) + jnp.dot(
+            tail[:, part], tiles, preferred_element_type=f32
+        )
         for k in range(slots):
             c = cols_ref[t, k]
-            term = jnp.dot(block, upd_ref[t, k].astype(jnp.float32), precision=hi, preferred_element_type=jnp.float32)
-            sums = [sums[j] + jnp.where(c == j, term, 0.0) for j in range(count)]
+            piece = term[:, k * width : (k + 1) * width]
+            sums = [sums[j] + jnp.where(c == j, piece, 0.0) for j in range(count)]
     for j in range(count):
         pay_ref[:, lanes + j * width : lanes + (j + 1) * width] = sums[j]
 
@@ -104,7 +114,7 @@
         in_specs=[pl.BlockSpec(memory_space=pltpu.SMEM), vmem, vmem, vmem],
         out_specs=(vmem, vmem),
         cost_estimate=pl.CostEstimate(
-            flops=2 * n * users * (n + width) * 6, transcendentals=0, bytes_accessed=2 * updated.size + 16 * n * users
+            flops=2 * n * users * (n + width) * 3, transcendentals=0, bytes_accessed=2 * updated.size + 16 * n * users
         ),
     )(tile_columns, mine, other, updated)
 

time: 35 us -> 34.5 us (0.986)
  Pallas kernels: 11 us -> 10.5 us
    pallas_call x1, Pallas kernels: 2.51 us -> 2.02 us  [mid(): pl.pallas_call(mid_kernel, out_shape=(jax.ShapeDtypeStruct((n, users), jn...]
where the time goes in v7:
time: 34.5 us; the launch traced here: 34.2 us
  waiting for transfers between devices  10.9 us (32%)
  Pallas kernels  10.5 us (30%)
  starting transfers between devices  10 us (29%)
  local copies, waits for them, and re-layouts  1.25 us (4%)
  other arithmetic  0.87 us (3%)
  between operations  0.66 us (2%)
    ppermute x5, waiting for transfers between devices, all_sum_parts(): other = lax.ppermute(x, axis, [(i, i ^ step) for i in range(n)])  10.9 us
    ppermute x5, starting transfers between devices, all_sum_parts(): other = lax.ppermute(x, axis, [(i, i ^ step) for i in range(n)])  10 us
    pallas_call x1, Pallas kernels, tail(): pl.pallas_call(functools.partial(tail_kernel, scale=1.0 / user_total, roo...  4.6 us
    pallas_call x1, Pallas kernels, update(): pl.pallas_call(update_kernel, grid=(rows,), out_shape=(jax.ShapeDtypeStru...  3.86 us
    pallas_call x1, Pallas kernels, mid(): pl.pallas_call(mid_kernel, out_shape=(jax.ShapeDtypeStruct((n, users), jn...  2.02 us
    unnamed x6, local copies, waits for them, and re-layouts  1.25 us
    add x3, other arithmetic, all_sum_parts(): x = x + other  0.87 us
  transfers between devices with their start and end apart: 5, of which 5 were waited for; matrix products, arithmetic and copies ran while one was open for 0% of the time, Pallas kernels for 0%

profile of v7, /device:TPU:0, one launch (start us, length us, event | category | flops | bytes accessed | tf_op | source)
XLA Modules:
  0.0 34.2 jit_solution(5620816012725065957)
XLA Ops:
  0.6 3.9 %shard_map.103 = (bf16[4,3,128,128]{3,2,1,0:T(8,128)(2,1)}, f32[32,512]{1,0:T(8,128)}) custom-call(s32[4,3]{1,0:T(4,128)} %cols_ref.3, s32[4,3]{1,0:T(4,128)} %live_ref.1, s32[4]{0:T(128)} %chosen_ref.1, bf16[4,3,128,128]{3,2,1,0:T(8,128)(2,1)} %rat_ref.1, bf16[4,3,128,128]{3,2,1,0:T(8,128)(2,1)} %res_ref.1, bf16[64,512]{1,0:T(8,128)(2,1)} %user_ref.1, ...), custom_call_target="tpu_custom_call" | custom-call | flops 37748736 | bytes 1245184 | tf_op jit(solution)/shard_map/pallas_call | solution.py:169
  4.5 2.9 %collective-permute-start = (f32[32,512]{1,0:T(8,128)}, f32[32,512]{1,0:T(8,128)S(1)}, u32[]{:S(2)}, u32[]{:S(2)}) collective-permute-start(f32[32,512]{1,0:T(8,128)} %get-tuple-element.10.mine_ref), channel_id=1, source_target_pairs={{0,1},{1,0},{2,3},{3,2},{4,5},{5,4},{6,7},{7,6},{8,9},{9,8},{10,11... | collective-permute-start | bytes 196616 | tf_op jit(solution)/shard_map/ppermute | solution.py:20
  7.4 2.5 %collective-permute-done.other_ref = f32[32,512]{1,0:T(8,128)S(1)} collective-permute-done((f32[32,512]{1,0:T(8,128)}, f32[32,512]{1,0:T(8,128)S(1)}, u32[]{:S(2)}, u32[]{:S(2)}) %collective-permute-start) | collective-permute-done | bytes 65568 | tf_op jit(solution)/shard_map/ppermute | solution.py:20
  9.9 0.0 copy-start.2
  9.9 0.6 %copy-done.2 = f32[32,512]{1,0:T(8,128)} copy-done((f32[32,512]{1,0:T(8,128)}, f32[32,512]{1,0:T(8,128)S(1)}, u32[]{:S(2)}) %copy-start.2) | copy-done | bytes 65560
  10.5 2.0 %shard_map.104 = (f32[32,512]{1,0:T(8,128)}, f32[32,512]{1,0:T(8,128)}) custom-call(s32[4,3]{1,0:T(4,128)} %cols_ref.3, f32[32,512]{1,0:T(8,128)} %get-tuple-element.10.mine_ref, f32[32,512]{1,0:T(8,128)} %copy-done.2, bf16[4,3,128,128]{3,2,1,0:T(8,128)(2,1)} %get-tuple-element.6.upd_ref), custom_call_target="tpu_custom_call" | custom-call | flops 15728640 | bytes 655360 | tf_op jit(solution)/shard_map/pallas_call | solution.py:108
  12.5 0.0 collective-permute-start.1
  12.5 1.5 %collective-permute-done.1 = f32[32,512]{1,0:T(8,128)S(1)} collective-permute-done((f32[32,512]{1,0:T(8,128)}, f32[32,512]{1,0:T(8,128)S(1)}, u32[]{:S(2)}, u32[]{:S(2)}) %collective-permute-start.1) | collective-permute-done | bytes 65568 | tf_op jit(solution)/shard_map/ppermute | solution.py:20
  14.0 0.9 %add.9 = f32[32,512]{1,0:T(8,128)S(1)} add(f32[32,512]{1,0:T(8,128)} %get-tuple-element.11, f32[32,512]{1,0:T(8,128)S(1)} %collective-permute-done.1) | non-fusion elementwise | flops 16384 | bytes 196608 | tf_op jit(solution)/shard_map/add | solution.py:19
  14.8 2.1 %collective-permute-start.2 = (f32[32,512]{1,0:T(8,128)S(1)}, f32[32,512]{1,0:T(8,128)S(1)}, u32[]{:S(2)}, u32[]{:S(2)}) collective-permute-start(f32[32,512]{1,0:T(8,128)S(1)} %add.9), channel_id=1, source_target_pairs={{0,4},{2,6},{4,0},{6,2},{8,12},{10,14},{12,8},{14,10},{16,20},{18,... | collective-permute-start | bytes 196616 | tf_op jit(solution)/shard_map/ppermute | solution.py:20
  17.0 2.4 %collective-permute-done.2 = f32[32,512]{1,0:T(8,128)S(1)} collective-permute-done((f32[32,512]{1,0:T(8,128)S(1)}, f32[32,512]{1,0:T(8,128)S(1)}, u32[]{:S(2)}, u32[]{:S(2)}) %collective-permute-start.2) | collective-permute-done | bytes 65568 | tf_op jit(solution)/shard_map/ppermute | solution.py:20
  19.4 2.0 %collective-permute-start.3 = (f32[32,512]{1,0:T(8,128)S(1)}, f32[32,512]{1,0:T(8,128)S(1)}, u32[]{:S(2)}, u32[]{:S(2)}) collective-permute-start(f32[32,512]{1,0:T(8,128)S(1)} %add.10), channel_id=1, source_target_pairs={{0,8},{2,10},{4,12},{6,14},{8,0},{10,2},{12,4},{14,6},{16,24},{18,... | collective-permute-start | bytes 196616 | tf_op jit(solution)/shard_map/ppermute | solution.py:20
  21.4 2.4 %collective-permute-done.3 = f32[32,512]{1,0:T(8,128)S(1)} collective-permute-done((f32[32,512]{1,0:T(8,128)S(1)}, f32[32,512]{1,0:T(8,128)S(1)}, u32[]{:S(2)}, u32[]{:S(2)}) %collective-permute-start.3) | collective-permute-done | bytes 65568 | tf_op jit(solution)/shard_map/ppermute | solution.py:20
  23.7 0.0 copy-start
  23.7 3.0 %collective-permute-start.4 = (f32[32,512]{1,0:T(8,128)S(1)}, f32[32,512]{1,0:T(8,128)S(1)}, u32[]{:S(2)}, u32[]{:S(2)}) collective-permute-start(f32[32,512]{1,0:T(8,128)S(1)} %add.11.mine_ref), channel_id=1, source_target_pairs={{0,16},{2,18},{4,20},{6,22},{8,24},{10,26},{12,28},{14,30},{16,0},... | collective-permute-start | bytes 196616 | tf_op jit(solution)/shard_map/ppermute | solution.py:20
  26.7 2.2 %collective-permute-done.4.other_ref = f32[32,512]{1,0:T(8,128)S(1)} collective-permute-done((f32[32,512]{1,0:T(8,128)S(1)}, f32[32,512]{1,0:T(8,128)S(1)}, u32[]{:S(2)}, u32[]{:S(2)}) %collective-permute-start.4) | collective-permute-done | bytes 65568 | tf_op jit(solution)/shard_map/ppermute | solution.py:20
  29.0 0.0 copy-start.1
  29.0 0.0 copy-done
  29.0 0.6 %copy-done.1 = f32[32,512]{1,0:T(8,128)} copy-done((f32[32,512]{1,0:T(8,128)}, f32[32,512]{1,0:T(8,128)S(1)}, u32[]{:S(2)}) %copy-start.1) | copy-done | bytes 65560
  29.6 4.6 %shard_map.105 = (f32[32,512]{1,0:T(8,128)}, f32[32,384]{1,0:T(8,128)}) custom-call(f32[32,512]{1,0:T(8,128)} %copy-done, f32[32,512]{1,0:T(8,128)} %copy-done.1, f32[32,512]{1,0:T(8,128)} %get-tuple-element.12.proj_ref, bf16[32,384]{1,0:T(8,128)(2,1)} %bitcast.4), custom_call_target="tpu_custom_call" | custom-call | flops 15728640 | bytes 278528 | tf_op jit(solution)/shard_map/pallas_call | solution.py:54
  (2 shorter events, 0.0 us)
Async XLA Ops:
  4.5 5.4 %collective-permute-start = (f32[32,512]{1,0:T(8,128)}, f32[32,512]{1,0:T(8,128)S(1)}, u32[]{:S(2)}, u32[]{:S(2)}) collective-permute-start(f32[32,512]{1,0:T(8,128)} %get-tuple-element.10.mine_ref), channel_id=1, source_target_pairs={{0,1},{1,0},{2,3},{3,2},{4,5},{5,4},{6,7},{7,6},{8,9},{9,8},{10,11... | collective-permute-start | bytes 196616 | tf_op jit(solution)/shard_map/ppermute | solution.py:20
  9.9 0.6 %copy-start.2 = (f32[32,512]{1,0:T(8,128)}, f32[32,512]{1,0:T(8,128)S(1)}, u32[]{:S(2)}) copy-start(f32[32,512]{1,0:T(8,128)S(1)} %collective-permute-done.other_ref) | copy-start | bytes 196612
  12.5 1.5 %collective-permute-start.1 = (f32[32,512]{1,0:T(8,128)}, f32[32,512]{1,0:T(8,128)S(1)}, u32[]{:S(2)}, u32[]{:S(2)}) collective-permute-start(f32[32,512]{1,0:T(8,128)} %get-tuple-element.11), channel_id=1, source_target_pairs={{0,2},{2,0},{4,6},{6,4},{8,10},{10,8},{12,14},{14,12},{16,18},{18,... | collective-permute-start | bytes 196616 | tf_op jit(solution)/shard_map/ppermute | solution.py:20
  14.8 4.5 %collective-permute-start.2 = (f32[32,512]{1,0:T(8,128)S(1)}, f32[32,512]{1,0:T(8,128)S(1)}, u32[]{:S(2)}, u32[]{:S(2)}) collective-permute-start(f32[32,512]{1,0:T(8,128)S(1)} %add.9), channel_id=1, source_target_pairs={{0,4},{2,6},{4,0},{6,2},{8,12},{10,14},{12,8},{14,10},{16,20},{18,... | collective-permute-start | bytes 196616 | tf_op jit(solution)/shard_map/ppermute | solution.py:20
  19.4 4.3 %collective-permute-start.3 = (f32[32,512]{1,0:T(8,128)S(1)}, f32[32,512]{1,0:T(8,128)S(1)}, u32[]{:S(2)}, u32[]{:S(2)}) collective-permute-start(f32[32,512]{1,0:T(8,128)S(1)} %add.10), channel_id=1, source_target_pairs={{0,8},{2,10},{4,12},{6,14},{8,0},{10,2},{12,4},{14,6},{16,24},{18,... | collective-permute-start | bytes 196616 | tf_op jit(solution)/shard_map/ppermute | solution.py:20
  23.7 5.2 %copy-start = (f32[32,512]{1,0:T(8,128)}, f32[32,512]{1,0:T(8,128)S(1)}, u32[]{:S(2)}) copy-start(f32[32,512]{1,0:T(8,128)S(1)} %add.11.mine_ref) | copy-start | bytes 196612
  23.7 5.2 %collective-permute-start.4 = (f32[32,512]{1,0:T(8,128)S(1)}, f32[32,512]{1,0:T(8,128)S(1)}, u32[]{:S(2)}, u32[]{:S(2)}) collective-permute-start(f32[32,512]{1,0:T(8,128)S(1)} %add.11.mine_ref), channel_id=1, source_target_pairs={{0,16},{2,18},{4,20},{6,22},{8,24},{10,26},{12,28},{14,30},{16,0},... | collective-permute-start | bytes 196616 | tf_op jit(solution)/shard_map/ppermute | solution.py:20
  29.0 0.6 %copy-start.1 = (f32[32,512]{1,0:T(8,128)}, f32[32,512]{1,0:T(8,128)S(1)}, u32[]{:S(2)}) copy-start(f32[32,512]{1,0:T(8,128)S(1)} %collective-permute-done.4.other_ref) | copy-start | bytes 196612

commit v8 on v5

--- a/solution.py
+++ b/solution.py
@@ -68,26 +68,37 @@
     tiles = item_ref.shape[1] // width
     user = user_ref[...]
     pick = chosen_ref[t] > 0
-    acc = jnp.zeros(part_ref.shape, jnp.float32)
+    factors, starts, lives = [], [], []
     for k in range(slots):
         c = cols_ref[t, k]
-        live = live_ref[t, k] > 0
+        lives.append(live_ref[t, k] > 0)
         factor = item_ref[:, 0:width]
         start = start_ref[:, 0:width]
         for j in range(1, tiles):
             factor = jnp.where(c == j, item_ref[:, j * width : (j + 1) * width], factor)
             start = jnp.where(c == j, start_ref[:, j * width : (j + 1) * width], start)
-        estimate = lax.dot_general(
-            user, factor, (((0,), (0,)), ((), ())), preferred_element_type=jnp.float32
+        factors.append(factor)
+        starts.append(start)
+    estimate = lax.dot_general(
+        user, jnp.concatenate(factors, axis=1), (((0,), (0,)), ((), ())), preferred_element_type=jnp.float32
+    )
+    fresh = []
+    for k in range(slots):
+        live = lives[k]
+        value = jnp.where(
+            live & pick,
+            rat_ref[0, k].astype(jnp.float32) - estimate[:, k * width : (k + 1) * width],
+            res_ref[0, k].astype(jnp.float32),
         )
-        fresh = jnp.where(
-            live & pick, rat_ref[0, k].astype(jnp.float32) - estimate, res_ref[0, k].astype(jnp.float32)
-        )
-        fresh = jnp.where(live, fresh, 0.0).astype(jnp.bfloat16)
-        upd_ref[0, k] = fresh
-        acc = acc + lax.dot_general(
-            start, fresh, (((1,), (1,)), ((), ())), preferred_element_type=jnp.float32
-        )
+        value = jnp.where(live, value, 0.0).astype(jnp.bfloat16)
+        upd_ref[0, k] = value
+        fresh.append(value)
+    acc = lax.dot_general(
+        jnp.concatenate(starts, axis=1),
+        jnp.concatenate(fresh, axis=1),
+        (((1,), (1,)), ((), ())),
+        preferred_element_type=jnp.float32,
+    )
     part_ref[...] = acc
 
 

time: 33.7 us -> 33.4 us (level)
  no operation moved by 1% of the time
where the time goes in v8:
time: 33.4 us; the launch traced here: 33.1 us
  waiting for transfers between devices  10.6 us (32%)
  starting transfers between devices  10.1 us (30%)
  Pallas kernels  8.43 us (25%)
  other arithmetic  1.52 us (5%)
  matrix products  0.93 us (3%)
  between operations  0.73 us (2%)
  local copies, waits for them, and re-layouts  0.71 us (2%)
    ppermute x5, waiting for transfers between devices, all_sum(): x = x + lax.ppermute(x, axis, [(i, i ^ step) for i in range(n)])  10.6 us
    ppermute x5, starting transfers between devices, all_sum(): x = x + lax.ppermute(x, axis, [(i, i ^ step) for i in range(n)])  10.1 us
    pallas_call x1, Pallas kernels, tail(): pl.pallas_call(functools.partial(tail_kernel, scale=1.0 / user_total, roo...  4.57 us
    pallas_call x1, Pallas kernels, update(): pl.pallas_call(update_kernel, grid=(rows,), out_shape=(jax.ShapeDtypeStru...  3.85 us
    add x5, other arithmetic, all_sum(): x = x + lax.ppermute(x, axis, [(i, i ^ step) for i in range(n)])  1.51 us
    unnamed x8, local copies, waits for them, and re-layouts  0.69 us
  transfers between devices with their start and end apart: 5, of which 5 were waited for; matrix products, arithmetic and copies ran while one was open for 0% of the time, Pallas kernels for 0%

profile of v8, /device:TPU:0, one launch (start us, length us, event | category | flops | bytes accessed | tf_op | source)
XLA Modules:
  0.0 33.1 jit_solution(3166914834513980257)
XLA Ops:
  0.6 0.0 copy-start.2
  0.6 3.9 %shard_map.103 = (bf16[4,3,128,128]{3,2,1,0:T(8,128)(2,1)}, f32[32,512]{1,0:T(8,128)}) custom-call(s32[4,3]{1,0:T(4,128)} %cols_ref.1, s32[4,3]{1,0:T(4,128)} %live_ref.1, s32[4]{0:T(128)} %chosen_ref.1, bf16[4,3,128,128]{3,2,1,0:T(8,128)(2,1)} %rat_ref.1, bf16[4,3,128,128]{3,2,1,0:T(8,128)(2,1)} %res_ref.1, bf16[64,512]{1,0:T(8,128)(2,1)} %user_ref.1, ...), custom_call_target="tpu_custom_call" | custom-call | flops 37748736 | bytes 1245184 | tf_op jit(solution)/shard_map/pallas_call | solution.py:111
  4.5 0.0 copy-start.1
  4.5 3.0 %collective-permute-start = (f32[32,512]{1,0:T(8,128)}, f32[32,512]{1,0:T(8,128)S(1)}, u32[]{:S(2)}, u32[]{:S(2)}) collective-permute-start(f32[32,512]{1,0:T(8,128)} %get-tuple-element.8), channel_id=1, source_target_pairs={{0,1},{1,0},{2,3},{3,2},{4,5},{5,4},{6,7},{7,6},{8,9},{9,8},{10,11... | collective-permute-start | bytes 196616 | tf_op jit(solution)/shard_map/ppermute | solution.py:17
  7.5 0.0 copy-done.2
  7.5 0.1 copy.12
  7.6 2.4 %collective-permute-done = f32[32,512]{1,0:T(8,128)S(1)} collective-permute-done((f32[32,512]{1,0:T(8,128)}, f32[32,512]{1,0:T(8,128)S(1)}, u32[]{:S(2)}, u32[]{:S(2)}) %collective-permute-start) | collective-permute-done | bytes 65568 | tf_op jit(solution)/shard_map/ppermute | solution.py:17
  10.0 0.8 %add.17.proj_ref = f32[32,512]{1,0:T(8,128)S(1)} add(f32[32,512]{1,0:T(8,128)} %get-tuple-element.8, f32[32,512]{1,0:T(8,128)S(1)} %collective-permute-done) | non-fusion elementwise | flops 16384 | bytes 196608 | tf_op jit(solution)/shard_map/add | solution.py:17
  10.8 0.0 copy-start
  10.8 0.6 %copy-done = f32[32,512]{1,0:T(8,128)} copy-done((f32[32,512]{1,0:T(8,128)}, f32[32,512]{1,0:T(8,128)S(1)}, u32[]{:S(2)}) %copy-start) | copy-done | bytes 65560
  11.4 0.2 fusion.9
  11.6 0.0 copy-done.1
  11.6 0.3 fusion.3
  12.0 0.4 %fusion = f32[3,32,128,1]{2,0,3,1:T(4,128)S(1)} fusion(f32[4,3,128,32]{2,3,1,0:T(8,128)S(1)} %fusion.3, s32[4,3]{0,1:T(4,128)S(1)} %copy.12), kind=kOutput, calls=%fused_computation | convolution fusion | flops 1769508 | bytes 245808 | tf_op jit(solution)/shard_map/jtkb,tkc->jcb/dot_general | solution.py:159
  12.4 0.1 collective-permute-start.1
  12.5 1.2 %collective-permute-done.1 = f32[32,512]{1,0:T(8,128)S(1)} collective-permute-done((f32[32,512]{1,0:T(8,128)S(1)}, f32[32,512]{1,0:T(8,128)S(1)}, u32[]{:S(2)}, u32[]{:S(2)}) %collective-permute-start.1) | collective-permute-done | bytes 65568 | tf_op jit(solution)/shard_map/ppermute | solution.py:17
  13.8 2.1 %collective-permute-start.2 = (f32[32,512]{1,0:T(8,128)S(1)}, f32[32,512]{1,0:T(8,128)S(1)}, u32[]{:S(2)}, u32[]{:S(2)}) collective-permute-start(f32[32,512]{1,0:T(8,128)S(1)} %fusion.8), channel_id=1, source_target_pairs={{0,4},{2,6},{4,0},{6,2},{8,12},{10,14},{12,8},{14,10},{16,20},{18,... | collective-permute-start | bytes 196616 | tf_op jit(solution)/shard_map/ppermute | solution.py:17
  15.9 2.4 %collective-permute-done.2 = f32[32,512]{1,0:T(8,128)S(1)} collective-permute-done((f32[32,512]{1,0:T(8,128)S(1)}, f32[32,512]{1,0:T(8,128)S(1)}, u32[]{:S(2)}, u32[]{:S(2)}) %collective-permute-start.2) | collective-permute-done | bytes 65568 | tf_op jit(solution)/shard_map/ppermute | solution.py:17
  18.3 2.0 %collective-permute-start.3 = (f32[32,512]{1,0:T(8,128)S(1)}, f32[32,512]{1,0:T(8,128)S(1)}, u32[]{:S(2)}, u32[]{:S(2)}) collective-permute-start(f32[32,512]{1,0:T(8,128)S(1)} %add.19), channel_id=1, source_target_pairs={{0,8},{2,10},{4,12},{6,14},{8,0},{10,2},{12,4},{14,6},{16,24},{18,... | collective-permute-start | bytes 196616 | tf_op jit(solution)/shard_map/ppermute | solution.py:17
  20.3 2.4 %collective-permute-done.3 = f32[32,512]{1,0:T(8,128)S(1)} collective-permute-done((f32[32,512]{1,0:T(8,128)S(1)}, f32[32,512]{1,0:T(8,128)S(1)}, u32[]{:S(2)}, u32[]{:S(2)}) %collective-permute-start.3) | collective-permute-done | bytes 65568 | tf_op jit(solution)/shard_map/ppermute | solution.py:17
  22.6 3.0 %collective-permute-start.4 = (f32[32,512]{1,0:T(8,128)S(1)}, f32[32,512]{1,0:T(8,128)S(1)}, u32[]{:S(2)}, u32[]{:S(2)}) collective-permute-start(f32[32,512]{1,0:T(8,128)S(1)} %add.20), channel_id=1, source_target_pairs={{0,16},{2,18},{4,20},{6,22},{8,24},{10,26},{12,28},{14,30},{16,0},... | collective-permute-start | bytes 196616 | tf_op jit(solution)/shard_map/ppermute | solution.py:17
  25.6 2.2 %collective-permute-done.4 = f32[32,512]{1,0:T(8,128)S(1)} collective-permute-done((f32[32,512]{1,0:T(8,128)S(1)}, f32[32,512]{1,0:T(8,128)S(1)}, u32[]{:S(2)}, u32[]{:S(2)}) %collective-permute-start.4) | collective-permute-done | bytes 65568 | tf_op jit(solution)/shard_map/ppermute | solution.py:17
  27.9 0.6 %add.21.reduced_ref = f32[32,512]{1,0:T(8,128)} add(f32[32,512]{1,0:T(8,128)S(1)} %add.20, f32[32,512]{1,0:T(8,128)S(1)} %collective-permute-done.4) | non-fusion elementwise | flops 16384 | bytes 196608 | tf_op jit(solution)/shard_map/add | solution.py:17
  28.5 4.6 %shard_map.104 = (f32[32,512]{1,0:T(8,128)}, f32[32,384]{1,0:T(8,128)}) custom-call(f32[32,512]{1,0:T(8,128)} %add.21.reduced_ref, f32[32,512]{1,0:T(8,128)} %copy-done, bf16[32,384]{1,0:T(8,128)(2,1)} %bitcast.24), custom_call_target="tpu_custom_call" | custom-call | flops 15728640 | bytes 278528 | tf_op jit(solution)/shard_map/pallas_call | solution.py:50
  (6 shorter events, 0.1 us)
Async XLA Ops:
  0.6 6.9 %copy-start.2 = (s32[4,3]{1,0:T(4,128)S(1)}, s32[4,3]{1,0:T(4,128)}, u32[]{:S(2)}) copy-start(s32[4,3]{1,0:T(4,128)} %cols_ref.1) | copy-start | bytes 148
  4.5 7.1 %copy-start.1 = (bf16[4,3,128,128]{3,2,1,0:T(8,128)(2,1)S(1)}, bf16[4,3,128,128]{3,2,1,0:T(8,128)(2,1)}, u32[]{:S(2)}) copy-start(bf16[4,3,128,128]{3,2,1,0:T(8,128)(2,1)} %get-tuple-element.4) | copy-start | bytes 1179652
  4.5 5.5 %collective-permute-start = (f32[32,512]{1,0:T(8,128)}, f32[32,512]{1,0:T(8,128)S(1)}, u32[]{:S(2)}, u32[]{:S(2)}) collective-permute-start(f32[32,512]{1,0:T(8,128)} %get-tuple-element.8), channel_id=1, source_target_pairs={{0,1},{1,0},{2,3},{3,2},{4,5},{5,4},{6,7},{7,6},{8,9},{9,8},{10,11... | collective-permute-start | bytes 196616 | tf_op jit(solution)/shard_map/ppermute | solution.py:17
  10.8 0.6 %copy-start = (f32[32,512]{1,0:T(8,128)}, f32[32,512]{1,0:T(8,128)S(1)}, u32[]{:S(2)}) copy-start(f32[32,512]{1,0:T(8,128)S(1)} %add.17.proj_ref) | copy-start | bytes 196612
  12.4 1.3 %collective-permute-start.1 = (f32[32,512]{1,0:T(8,128)S(1)}, f32[32,512]{1,0:T(8,128)S(1)}, u32[]{:S(2)}, u32[]{:S(2)}) collective-permute-start(f32[32,512]{1,0:T(8,128)S(1)} %select_maximum_fusion), channel_id=1, source_target_pairs={{0,2},{2,0},{4,6},{6,4},{8,10},{10,8},{12,14},{14,12},{16,18},{18,... | collective-permute-start | bytes 196616 | tf_op jit(solution)/shard_map/ppermute | solution.py:17
  13.8 4.5 %collective-permute-start.2 = (f32[32,512]{1,0:T(8,128)S(1)}, f32[32,512]{1,0:T(8,128)S(1)}, u32[]{:S(2)}, u32[]{:S(2)}) collective-permute-start(f32[32,512]{1,0:T(8,128)S(1)} %fusion.8), channel_id=1, source_target_pairs={{0,4},{2,6},{4,0},{6,2},{8,12},{10,14},{12,8},{14,10},{16,20},{18,... | collective-permute-start | bytes 196616 | tf_op jit(solution)/shard_map/ppermute | solution.py:17
  18.3 4.3 %collective-permute-start.3 = (f32[32,512]{1,0:T(8,128)S(1)}, f32[32,512]{1,0:T(8,128)S(1)}, u32[]{:S(2)}, u32[]{:S(2)}) collective-permute-start(f32[32,512]{1,0:T(8,128)S(1)} %add.19), channel_id=1, source_target_pairs={{0,8},{2,10},{4,12},{6,14},{8,0},{10,2},{12,4},{14,6},{16,24},{18,... | collective-permute-start | bytes 196616 | tf_op jit(solution)/shard_map/ppermute | solution.py:17
  22.6 5.2 %collective-permute-start.4 = (f32[32,512]{1,0:T(8,128)S(1)}, f32[32,512]{1,0:T(8,128)S(1)}, u32[]{:S(2)}, u32[]{:S(2)}) collective-permute-start(f32[32,512]{1,0:T(8,128)S(1)} %add.20), channel_id=1, source_target_pairs={{0,16},{2,18},{4,20},{6,22},{8,24},{10,26},{12,28},{14,30},{16,0},... | collective-permute-start | bytes 196616 | tf_op jit(solution)/shard_map/ppermute | solution.py:17

commit v9 on v8

--- a/solution.py
+++ b/solution.py
@@ -19,9 +19,13 @@
     return x
 
 
-def tail_kernel(reduced_ref, proj_ref, start_ref, left_ref, right_ref, *, scale, root):
-    n = start_ref.shape[0]
-    lanes = reduced_ref.shape[1] - start_ref.shape[1]
+def tail_kernel(reduced_ref, proj_hbm, start_hbm, left_hbm, right_ref, proj_buf, start_buf, left_buf, sems, *, scale, root):
+    fetch_proj = pltpu.make_async_copy(proj_hbm, proj_buf, sems.at[0])
+    fetch_start = pltpu.make_async_copy(start_hbm, start_buf, sems.at[1])
+    fetch_proj.start()
+    fetch_start.start()
+    n = start_buf.shape[0]
+    lanes = reduced_ref.shape[1] - start_buf.shape[1]
     g = reduced_ref[:, :n] * scale
     g = 0.5 * (g + g.T)
     rows = lax.broadcasted_iota(jnp.int32, (n, 2 * n), 0)
@@ -35,26 +39,38 @@
     upper = aug[:, :n]
     inverse = aug[:, n:]
     hi = lax.Precision.HIGHEST
-    left_ref[...] = jnp.dot(inverse, proj_ref[...], precision=hi, preferred_element_type=jnp.float32)
+    fetch_proj.wait()
+    left_buf[...] = jnp.dot(inverse, proj_buf[...], precision=hi, preferred_element_type=jnp.float32)
+    store_left = pltpu.make_async_copy(left_buf, left_hbm, sems.at[2])
+    store_left.start()
     summed = jnp.dot(inverse, reduced_ref[:, lanes:], precision=hi, preferred_element_type=jnp.float32)
+    fetch_start.wait()
     start_term = jnp.dot(
-        upper, start_ref[...].astype(jnp.float32), precision=hi, preferred_element_type=jnp.float32
+        upper, start_buf[...].astype(jnp.float32), precision=hi, preferred_element_type=jnp.float32
     )
     right_ref[...] = summed / root - root * start_term
+    store_left.wait()
 
 
 def tail(reduced, projected, start, user_total):
     n, users = projected.shape
     items = start.shape[1]
     vmem = pl.BlockSpec(memory_space=pltpu.VMEM)
+    anywhere = pl.BlockSpec(memory_space=pl.ANY)
     return pl.pallas_call(
         functools.partial(tail_kernel, scale=1.0 / user_total, root=float(user_total) ** 0.5),
         out_shape=(
             jax.ShapeDtypeStruct((n, users), jnp.float32),
             jax.ShapeDtypeStruct((n, items), jnp.float32),
         ),
-        in_specs=[vmem] * 3,
-        out_specs=(vmem, vmem),
+        in_specs=[vmem, anywhere, anywhere],
+        out_specs=(anywhere, vmem),
+        scratch_shapes=[
+            pltpu.VMEM((n, users), jnp.float32),
+            pltpu.VMEM(start.shape, start.dtype),
+            pltpu.VMEM((n, users), jnp.float32),
+            pltpu.SemaphoreType.DMA((3,)),
+        ],
         cost_estimate=pl.CostEstimate(
             flops=2 * n * n * (users + 2 * items) * 6, transcendentals=n, bytes_accessed=4 * n * (2 * users + 3 * items)
         ),

time: 33.4 us -> 33.9 us (1.015)
  Pallas kernels: 8.43 us -> 8.95 us
    pallas_call x1, Pallas kernels: 4.57 us -> 5.09 us  [tail(): pl.pallas_call(functools.partial(tail_kernel, scale=1.0 / user_total, roo...]
where the time goes in v9:
time: 33.9 us; the launch traced here: 33.6 us
  waiting for transfers between devices  10.6 us (31%)
  starting transfers between devices  10.1 us (30%)
  Pallas kernels  8.95 us (26%)
  other arithmetic  1.52 us (4%)
  matrix products  0.93 us (3%)
  between operations  0.73 us (2%)
  local copies, waits for them, and re-layouts  0.71 us (2%)
    ppermute x5, waiting for transfers between devices, all_sum(): x = x + lax.ppermute(x, axis, [(i, i ^ step) for i in range(n)])  10.6 us
    ppermute x5, starting transfers between devices, all_sum(): x = x + lax.ppermute(x, axis, [(i, i ^ step) for i in range(n)])  10.1 us
    pallas_call x1, Pallas kernels, tail(): pl.pallas_call(functools.partial(tail_kernel, scale=1.0 / user_total, roo...  5.09 us
    pallas_call x1, Pallas kernels, update(): pl.pallas_call(update_kernel, grid=(rows,), out_shape=(jax.ShapeDtypeStru...  3.85 us
    add x5, other arithmetic, all_sum(): x = x + lax.ppermute(x, axis, [(i, i ^ step) for i in range(n)])  1.51 us
    unnamed x8, local copies, waits for them, and re-layouts  0.69 us
  transfers between devices with their start and end apart: 5, of which 5 were waited for; matrix products, arithmetic and copies ran while one was open for 0% of the time, Pallas kernels for 0%

profile of v9, /device:TPU:0, one launch (start us, length us, event | category | flops | bytes accessed | tf_op | source)
XLA Modules:
  0.0 33.6 jit_solution(15740742021759906133)
XLA Ops:
  0.6 0.0 copy-start.2
  0.6 3.9 %shard_map.103 = (bf16[4,3,128,128]{3,2,1,0:T(8,128)(2,1)}, f32[32,512]{1,0:T(8,128)}) custom-call(s32[4,3]{1,0:T(4,128)} %cols_ref.1, s32[4,3]{1,0:T(4,128)} %live_ref.1, s32[4]{0:T(128)} %chosen_ref.1, bf16[4,3,128,128]{3,2,1,0:T(8,128)(2,1)} %rat_ref.1, bf16[4,3,128,128]{3,2,1,0:T(8,128)(2,1)} %res_ref.1, bf16[64,512]{1,0:T(8,128)(2,1)} %user_ref.1, ...), custom_call_target="tpu_custom_call" | custom-call | flops 37748736 | bytes 1245184 | tf_op jit(solution)/shard_map/pallas_call | solution.py:127
  4.5 0.0 copy-start.1
  4.5 3.0 %collective-permute-start = (f32[32,512]{1,0:T(8,128)}, f32[32,512]{1,0:T(8,128)S(1)}, u32[]{:S(2)}, u32[]{:S(2)}) collective-permute-start(f32[32,512]{1,0:T(8,128)} %get-tuple-element.8), channel_id=1, source_target_pairs={{0,1},{1,0},{2,3},{3,2},{4,5},{5,4},{6,7},{7,6},{8,9},{9,8},{10,11... | collective-permute-start | bytes 196616 | tf_op jit(solution)/shard_map/ppermute | solution.py:17
  7.5 0.0 copy-done.2
  7.5 0.1 copy.12
  7.6 2.4 %collective-permute-done = f32[32,512]{1,0:T(8,128)S(1)} collective-permute-done((f32[32,512]{1,0:T(8,128)}, f32[32,512]{1,0:T(8,128)S(1)}, u32[]{:S(2)}, u32[]{:S(2)}) %collective-permute-start) | collective-permute-done | bytes 65568 | tf_op jit(solution)/shard_map/ppermute | solution.py:17
  10.0 0.8 %add.17.proj_hbm = f32[32,512]{1,0:T(8,128)S(1)} add(f32[32,512]{1,0:T(8,128)} %get-tuple-element.8, f32[32,512]{1,0:T(8,128)S(1)} %collective-permute-done) | non-fusion elementwise | flops 16384 | bytes 196608 | tf_op jit(solution)/shard_map/add | solution.py:17
  10.8 0.0 copy-start
  10.8 0.6 %copy-done = f32[32,512]{1,0:T(8,128)} copy-done((f32[32,512]{1,0:T(8,128)}, f32[32,512]{1,0:T(8,128)S(1)}, u32[]{:S(2)}) %copy-start) | copy-done | bytes 65560
  11.4 0.2 fusion.9
  11.6 0.0 copy-done.1
  11.6 0.3 fusion.3
  12.0 0.4 %fusion = f32[3,32,128,1]{2,0,3,1:T(4,128)S(1)} fusion(f32[4,3,128,32]{2,3,1,0:T(8,128)S(1)} %fusion.3, s32[4,3]{0,1:T(4,128)S(1)} %copy.12), kind=kOutput, calls=%fused_computation | convolution fusion | flops 1769508 | bytes 245808 | tf_op jit(solution)/shard_map/jtkb,tkc->jcb/dot_general | solution.py:175
  12.4 0.1 collective-permute-start.1
  12.5 1.2 %collective-permute-done.1 = f32[32,512]{1,0:T(8,128)S(1)} collective-permute-done((f32[32,512]{1,0:T(8,128)S(1)}, f32[32,512]{1,0:T(8,128)S(1)}, u32[]{:S(2)}, u32[]{:S(2)}) %collective-permute-start.1) | collective-permute-done | bytes 65568 | tf_op jit(solution)/shard_map/ppermute | solution.py:17
  13.8 2.1 %collective-permute-start.2 = (f32[32,512]{1,0:T(8,128)S(1)}, f32[32,512]{1,0:T(8,128)S(1)}, u32[]{:S(2)}, u32[]{:S(2)}) collective-permute-start(f32[32,512]{1,0:T(8,128)S(1)} %fusion.8), channel_id=1, source_target_pairs={{0,4},{2,6},{4,0},{6,2},{8,12},{10,14},{12,8},{14,10},{16,20},{18,... | collective-permute-start | bytes 196616 | tf_op jit(solution)/shard_map/ppermute | solution.py:17
  15.9 2.4 %collective-permute-done.2 = f32[32,512]{1,0:T(8,128)S(1)} collective-permute-done((f32[32,512]{1,0:T(8,128)S(1)}, f32[32,512]{1,0:T(8,128)S(1)}, u32[]{:S(2)}, u32[]{:S(2)}) %collective-permute-start.2) | collective-permute-done | bytes 65568 | tf_op jit(solution)/shard_map/ppermute | solution.py:17
  18.3 2.0 %collective-permute-start.3 = (f32[32,512]{1,0:T(8,128)S(1)}, f32[32,512]{1,0:T(8,128)S(1)}, u32[]{:S(2)}, u32[]{:S(2)}) collective-permute-start(f32[32,512]{1,0:T(8,128)S(1)} %add.19), channel_id=1, source_target_pairs={{0,8},{2,10},{4,12},{6,14},{8,0},{10,2},{12,4},{14,6},{16,24},{18,... | collective-permute-start | bytes 196616 | tf_op jit(solution)/shard_map/ppermute | solution.py:17
  20.3 2.4 %collective-permute-done.3 = f32[32,512]{1,0:T(8,128)S(1)} collective-permute-done((f32[32,512]{1,0:T(8,128)S(1)}, f32[32,512]{1,0:T(8,128)S(1)}, u32[]{:S(2)}, u32[]{:S(2)}) %collective-permute-start.3) | collective-permute-done | bytes 65568 | tf_op jit(solution)/shard_map/ppermute | solution.py:17
  22.6 3.0 %collective-permute-start.4 = (f32[32,512]{1,0:T(8,128)S(1)}, f32[32,512]{1,0:T(8,128)S(1)}, u32[]{:S(2)}, u32[]{:S(2)}) collective-permute-start(f32[32,512]{1,0:T(8,128)S(1)} %add.20), channel_id=1, source_target_pairs={{0,16},{2,18},{4,20},{6,22},{8,24},{10,26},{12,28},{14,30},{16,0},... | collective-permute-start | bytes 196616 | tf_op jit(solution)/shard_map/ppermute | solution.py:17
  25.6 2.2 %collective-permute-done.4 = f32[32,512]{1,0:T(8,128)S(1)} collective-permute-done((f32[32,512]{1,0:T(8,128)S(1)}, f32[32,512]{1,0:T(8,128)S(1)}, u32[]{:S(2)}, u32[]{:S(2)}) %collective-permute-start.4) | collective-permute-done | bytes 65568 | tf_op jit(solution)/shard_map/ppermute | solution.py:17
  27.9 0.6 %add.21.reduced_ref = f32[32,512]{1,0:T(8,128)} add(f32[32,512]{1,0:T(8,128)S(1)} %add.20, f32[32,512]{1,0:T(8,128)S(1)} %collective-permute-done.4) | non-fusion elementwise | flops 16384 | bytes 196608 | tf_op jit(solution)/shard_map/add | solution.py:17
  28.5 5.1 %shard_map.104 = (f32[32,512]{1,0:T(8,128)}, f32[32,384]{1,0:T(8,128)}) custom-call(f32[32,512]{1,0:T(8,128)} %add.21.reduced_ref, f32[32,512]{1,0:T(8,128)} %copy-done, bf16[32,384]{1,0:T(8,128)(2,1)} %bitcast.24), custom_call_target="tpu_custom_call" | custom-call | flops 15728640 | bytes 278528 | tf_op jit(solution)/shard_map/pallas_call | solution.py:60
  (6 shorter events, 0.1 us)
Async XLA Ops:
  0.6 6.9 %copy-start.2 = (s32[4,3]{1,0:T(4,128)S(1)}, s32[4,3]{1,0:T(4,128)}, u32[]{:S(2)}) copy-start(s32[4,3]{1,0:T(4,128)} %cols_ref.1) | copy-start | bytes 148
  4.5 7.1 %copy-start.1 = (bf16[4,3,128,128]{3,2,1,0:T(8,128)(2,1)S(1)}, bf16[4,3,128,128]{3,2,1,0:T(8,128)(2,1)}, u32[]{:S(2)}) copy-start(bf16[4,3,128,128]{3,2,1,0:T(8,128)(2,1)} %get-tuple-element.4) | copy-start | bytes 1179652
  4.5 5.5 %collective-permute-start = (f32[32,512]{1,0:T(8,128)}, f32[32,512]{1,0:T(8,128)S(1)}, u32[]{:S(2)}, u32[]{:S(2)}) collective-permute-start(f32[32,512]{1,0:T(8,128)} %get-tuple-element.8), channel_id=1, source_target_pairs={{0,1},{1,0},{2,3},{3,2},{4,5},{5,4},{6,7},{7,6},{8,9},{9,8},{10,11... | collective-permute-start | bytes 196616 | tf_op jit(solution)/shard_map/ppermute | solution.py:17
  10.8 0.6 %copy-start = (f32[32,512]{1,0:T(8,128)}, f32[32,512]{1,0:T(8,128)S(1)}, u32[]{:S(2)}) copy-start(f32[32,512]{1,0:T(8,128)S(1)} %add.17.proj_hbm) | copy-start | bytes 196612
  12.4 1.3 %collective-permute-start.1 = (f32[32,512]{1,0:T(8,128)S(1)}, f32[32,512]{1,0:T(8,128)S(1)}, u32[]{:S(2)}, u32[]{:S(2)}) collective-permute-start(f32[32,512]{1,0:T(8,128)S(1)} %select_maximum_fusion), channel_id=1, source_target_pairs={{0,2},{2,0},{4,6},{6,4},{8,10},{10,8},{12,14},{14,12},{16,18},{18,... | collective-permute-start | bytes 196616 | tf_op jit(solution)/shard_map/ppermute | solution.py:17
  13.8 4.5 %collective-permute-start.2 = (f32[32,512]{1,0:T(8,128)S(1)}, f32[32,512]{1,0:T(8,128)S(1)}, u32[]{:S(2)}, u32[]{:S(2)}) collective-permute-start(f32[32,512]{1,0:T(8,128)S(1)} %fusion.8), channel_id=1, source_target_pairs={{0,4},{2,6},{4,0},{6,2},{8,12},{10,14},{12,8},{14,10},{16,20},{18,... | collective-permute-start | bytes 196616 | tf_op jit(solution)/shard_map/ppermute | solution.py:17
  18.3 4.3 %collective-permute-start.3 = (f32[32,512]{1,0:T(8,128)S(1)}, f32[32,512]{1,0:T(8,128)S(1)}, u32[]{:S(2)}, u32[]{:S(2)}) collective-permute-start(f32[32,512]{1,0:T(8,128)S(1)} %add.19), channel_id=1, source_target_pairs={{0,8},{2,10},{4,12},{6,14},{8,0},{10,2},{12,4},{14,6},{16,24},{18,... | collective-permute-start | bytes 196616 | tf_op jit(solution)/shard_map/ppermute | solution.py:17
  22.6 5.2 %collective-permute-start.4 = (f32[32,512]{1,0:T(8,128)S(1)}, f32[32,512]{1,0:T(8,128)S(1)}, u32[]{:S(2)}, u32[]{:S(2)}) collective-permute-start(f32[32,512]{1,0:T(8,128)S(1)} %add.20), channel_id=1, source_target_pairs={{0,16},{2,18},{4,20},{6,22},{8,24},{10,26},{12,28},{14,30},{16,0},... | collective-permute-start | bytes 196616 | tf_op jit(solution)/shard_map/ppermute | solution.py:17

commit v10 on v8

--- a/solution.py
+++ b/solution.py
@@ -19,6 +19,11 @@
     return x
 
 
+def split(x):
+    head = x.astype(jnp.bfloat16)
+    return head, (x - head.astype(jnp.float32)).astype(jnp.bfloat16)
+
+
 def tail_kernel(reduced_ref, proj_ref, start_ref, left_ref, right_ref, *, scale, root):
     n = start_ref.shape[0]
     lanes = reduced_ref.shape[1] - start_ref.shape[1]
@@ -34,12 +39,20 @@
         aug = jnp.where(rows == k, head, aug - factor * head)
     upper = aug[:, :n]
     inverse = aug[:, n:]
-    hi = lax.Precision.HIGHEST
-    left_ref[...] = jnp.dot(inverse, proj_ref[...], precision=hi, preferred_element_type=jnp.float32)
-    summed = jnp.dot(inverse, reduced_ref[:, lanes:], precision=hi, preferred_element_type=jnp.float32)
-    start_term = jnp.dot(
-        upper, start_ref[...].astype(jnp.float32), precision=hi, preferred_element_type=jnp.float32
-    )
+    f32 = jnp.float32
+    inv_head, inv_tail = split(inverse)
+    up_head, up_tail = split(upper)
+
+    def product(x):
+        x_head, x_tail = split(x)
+        return jnp.dot(inv_head, x_head, preferred_element_type=f32) + (
+            jnp.dot(inv_head, x_tail, preferred_element_type=f32) + jnp.dot(inv_tail, x_head, preferred_element_type=f32)
+        )
+
+    left_ref[...] = product(proj_ref[...])
+    summed = product(reduced_ref[:, lanes:])
+    start = start_ref[...]
+    start_term = jnp.dot(up_head, start, preferred_element_type=f32) + jnp.dot(up_tail, start, preferred_element_type=f32)
     right_ref[...] = summed / root - root * start_term
 
 
@@ -56,7 +69,7 @@
         in_specs=[vmem] * 3,
         out_specs=(vmem, vmem),
         cost_estimate=pl.CostEstimate(
-            flops=2 * n * n * (users + 2 * items) * 6, transcendentals=n, bytes_accessed=4 * n * (2 * users + 3 * items)
+            flops=2 * n * n * (users + 2 * items) * 3, transcendentals=n, bytes_accessed=4 * n * (2 * users + 3 * items)
         ),
     )(reduced, projected, start)
 

time: 33.4 us -> 33.3 us (level)
  no operation moved by 1% of the time
where the time goes in v10:
time: 33.3 us; the launch traced here: 33 us
  waiting for transfers between devices  10.6 us (32%)
  starting transfers between devices  10.1 us (30%)
  Pallas kernels  8.33 us (25%)
  other arithmetic  1.52 us (5%)
  matrix products  0.93 us (3%)
  between operations  0.73 us (2%)
  local copies, waits for them, and re-layouts  0.71 us (2%)
    ppermute x5, waiting for transfers between devices, all_sum(): x = x + lax.ppermute(x, axis, [(i, i ^ step) for i in range(n)])  10.6 us
    ppermute x5, starting transfers between devices, all_sum(): x = x + lax.ppermute(x, axis, [(i, i ^ step) for i in range(n)])  10.1 us
    pallas_call x1, Pallas kernels, tail(): pl.pallas_call(functools.partial(tail_kernel, scale=1.0 / user_total, roo...  4.47 us
    pallas_call x1, Pallas kernels, update(): pl.pallas_call(update_kernel, grid=(rows,), out_shape=(jax.ShapeDtypeStru...  3.85 us
    add x5, other arithmetic, all_sum(): x = x + lax.ppermute(x, axis, [(i, i ^ step) for i in range(n)])  1.51 us
    unnamed x8, local copies, waits for them, and re-layouts  0.69 us
  transfers between devices with their start and end apart: 5, of which 5 were waited for; matrix products, arithmetic and copies ran while one was open for 0% of the time, Pallas kernels for 0%

profile of v10, /device:TPU:0, one launch (start us, length us, event | category | flops | bytes accessed | tf_op | source)
XLA Modules:
  0.0 33.0 jit_solution(1633846692831955437)
XLA Ops:
  0.6 0.0 copy-start.2
  0.6 3.9 %shard_map.103 = (bf16[4,3,128,128]{3,2,1,0:T(8,128)(2,1)}, f32[32,512]{1,0:T(8,128)}) custom-call(s32[4,3]{1,0:T(4,128)} %cols_ref.1, s32[4,3]{1,0:T(4,128)} %live_ref.1, s32[4]{0:T(128)} %chosen_ref.1, bf16[4,3,128,128]{3,2,1,0:T(8,128)(2,1)} %rat_ref.1, bf16[4,3,128,128]{3,2,1,0:T(8,128)(2,1)} %res_ref.1, bf16[64,512]{1,0:T(8,128)(2,1)} %user_ref.1, ...), custom_call_target="tpu_custom_call" | custom-call | flops 37748736 | bytes 1245184 | tf_op jit(solution)/shard_map/pallas_call | solution.py:124
  4.5 0.0 copy-start.1
  4.5 3.0 %collective-permute-start = (f32[32,512]{1,0:T(8,128)}, f32[32,512]{1,0:T(8,128)S(1)}, u32[]{:S(2)}, u32[]{:S(2)}) collective-permute-start(f32[32,512]{1,0:T(8,128)} %get-tuple-element.8), channel_id=1, source_target_pairs={{0,1},{1,0},{2,3},{3,2},{4,5},{5,4},{6,7},{7,6},{8,9},{9,8},{10,11... | collective-permute-start | bytes 196616 | tf_op jit(solution)/shard_map/ppermute | solution.py:17
  7.5 0.0 copy-done.2
  7.5 0.1 copy.12
  7.6 2.4 %collective-permute-done = f32[32,512]{1,0:T(8,128)S(1)} collective-permute-done((f32[32,512]{1,0:T(8,128)}, f32[32,512]{1,0:T(8,128)S(1)}, u32[]{:S(2)}, u32[]{:S(2)}) %collective-permute-start) | collective-permute-done | bytes 65568 | tf_op jit(solution)/shard_map/ppermute | solution.py:17
  10.0 0.8 %add.17.proj_ref = f32[32,512]{1,0:T(8,128)S(1)} add(f32[32,512]{1,0:T(8,128)} %get-tuple-element.8, f32[32,512]{1,0:T(8,128)S(1)} %collective-permute-done) | non-fusion elementwise | flops 16384 | bytes 196608 | tf_op jit(solution)/shard_map/add | solution.py:17
  10.8 0.0 copy-start
  10.8 0.6 %copy-done = f32[32,512]{1,0:T(8,128)} copy-done((f32[32,512]{1,0:T(8,128)}, f32[32,512]{1,0:T(8,128)S(1)}, u32[]{:S(2)}) %copy-start) | copy-done | bytes 65560
  11.4 0.2 fusion.9
  11.6 0.0 copy-done.1
  11.6 0.3 fusion.3
  12.0 0.4 %fusion = f32[3,32,128,1]{2,0,3,1:T(4,128)S(1)} fusion(f32[4,3,128,32]{2,3,1,0:T(8,128)S(1)} %fusion.3, s32[4,3]{0,1:T(4,128)S(1)} %copy.12), kind=kOutput, calls=%fused_computation | convolution fusion | flops 1769508 | bytes 245808 | tf_op jit(solution)/shard_map/jtkb,tkc->jcb/dot_general | solution.py:172
  12.4 0.1 collective-permute-start.1
  12.5 1.2 %collective-permute-done.1 = f32[32,512]{1,0:T(8,128)S(1)} collective-permute-done((f32[32,512]{1,0:T(8,128)S(1)}, f32[32,512]{1,0:T(8,128)S(1)}, u32[]{:S(2)}, u32[]{:S(2)}) %collective-permute-start.1) | collective-permute-done | bytes 65568 | tf_op jit(solution)/shard_map/ppermute | solution.py:17
  13.8 2.1 %collective-permute-start.2 = (f32[32,512]{1,0:T(8,128)S(1)}, f32[32,512]{1,0:T(8,128)S(1)}, u32[]{:S(2)}, u32[]{:S(2)}) collective-permute-start(f32[32,512]{1,0:T(8,128)S(1)} %fusion.8), channel_id=1, source_target_pairs={{0,4},{2,6},{4,0},{6,2},{8,12},{10,14},{12,8},{14,10},{16,20},{18,... | collective-permute-start | bytes 196616 | tf_op jit(solution)/shard_map/ppermute | solution.py:17
  15.9 2.4 %collective-permute-done.2 = f32[32,512]{1,0:T(8,128)S(1)} collective-permute-done((f32[32,512]{1,0:T(8,128)S(1)}, f32[32,512]{1,0:T(8,128)S(1)}, u32[]{:S(2)}, u32[]{:S(2)}) %collective-permute-start.2) | collective-permute-done | bytes 65568 | tf_op jit(solution)/shard_map/ppermute | solution.py:17
  18.3 2.0 %collective-permute-start.3 = (f32[32,512]{1,0:T(8,128)S(1)}, f32[32,512]{1,0:T(8,128)S(1)}, u32[]{:S(2)}, u32[]{:S(2)}) collective-permute-start(f32[32,512]{1,0:T(8,128)S(1)} %add.19), channel_id=1, source_target_pairs={{0,8},{2,10},{4,12},{6,14},{8,0},{10,2},{12,4},{14,6},{16,24},{18,... | collective-permute-start | bytes 196616 | tf_op jit(solution)/shard_map/ppermute | solution.py:17
  20.3 2.4 %collective-permute-done.3 = f32[32,512]{1,0:T(8,128)S(1)} collective-permute-done((f32[32,512]{1,0:T(8,128)S(1)}, f32[32,512]{1,0:T(8,128)S(1)}, u32[]{:S(2)}, u32[]{:S(2)}) %collective-permute-start.3) | collective-permute-done | bytes 65568 | tf_op jit(solution)/shard_map/ppermute | solution.py:17
  22.6 3.0 %collective-permute-start.4 = (f32[32,512]{1,0:T(8,128)S(1)}, f32[32,512]{1,0:T(8,128)S(1)}, u32[]{:S(2)}, u32[]{:S(2)}) collective-permute-start(f32[32,512]{1,0:T(8,128)S(1)} %add.20), channel_id=1, source_target_pairs={{0,16},{2,18},{4,20},{6,22},{8,24},{10,26},{12,28},{14,30},{16,0},... | collective-permute-start | bytes 196616 | tf_op jit(solution)/shard_map/ppermute | solution.py:17
  25.6 2.2 %collective-permute-done.4 = f32[32,512]{1,0:T(8,128)S(1)} collective-permute-done((f32[32,512]{1,0:T(8,128)S(1)}, f32[32,512]{1,0:T(8,128)S(1)}, u32[]{:S(2)}, u32[]{:S(2)}) %collective-permute-start.4) | collective-permute-done | bytes 65568 | tf_op jit(solution)/shard_map/ppermute | solution.py:17
  27.9 0.6 %add.21.reduced_ref = f32[32,512]{1,0:T(8,128)} add(f32[32,512]{1,0:T(8,128)S(1)} %add.20, f32[32,512]{1,0:T(8,128)S(1)} %collective-permute-done.4) | non-fusion elementwise | flops 16384 | bytes 196608 | tf_op jit(solution)/shard_map/add | solution.py:17
  28.5 4.5 %shard_map.104 = (f32[32,512]{1,0:T(8,128)}, f32[32,384]{1,0:T(8,128)}) custom-call(f32[32,512]{1,0:T(8,128)} %add.21.reduced_ref, f32[32,512]{1,0:T(8,128)} %copy-done, bf16[32,384]{1,0:T(8,128)(2,1)} %bitcast.24), custom_call_target="tpu_custom_call" | custom-call | flops 7864320 | bytes 278528 | tf_op jit(solution)/shard_map/pallas_call | solution.py:63
  (6 shorter events, 0.1 us)
Async XLA Ops:
  0.6 6.9 %copy-start.2 = (s32[4,3]{1,0:T(4,128)S(1)}, s32[4,3]{1,0:T(4,128)}, u32[]{:S(2)}) copy-start(s32[4,3]{1,0:T(4,128)} %cols_ref.1) | copy-start | bytes 148
  4.5 7.1 %copy-start.1 = (bf16[4,3,128,128]{3,2,1,0:T(8,128)(2,1)S(1)}, bf16[4,3,128,128]{3,2,1,0:T(8,128)(2,1)}, u32[]{:S(2)}) copy-start(bf16[4,3,128,128]{3,2,1,0:T(8,128)(2,1)} %get-tuple-element.4) | copy-start | bytes 1179652
  4.5 5.5 %collective-permute-start = (f32[32,512]{1,0:T(8,128)}, f32[32,512]{1,0:T(8,128)S(1)}, u32[]{:S(2)}, u32[]{:S(2)}) collective-permute-start(f32[32,512]{1,0:T(8,128)} %get-tuple-element.8), channel_id=1, source_target_pairs={{0,1},{1,0},{2,3},{3,2},{4,5},{5,4},{6,7},{7,6},{8,9},{9,8},{10,11... | collective-permute-start | bytes 196616 | tf_op jit(solution)/shard_map/ppermute | solution.py:17
  10.8 0.6 %copy-start = (f32[32,512]{1,0:T(8,128)}, f32[32,512]{1,0:T(8,128)S(1)}, u32[]{:S(2)}) copy-start(f32[32,512]{1,0:T(8,128)S(1)} %add.17.proj_ref) | copy-start | bytes 196612
  12.4 1.3 %collective-permute-start.1 = (f32[32,512]{1,0:T(8,128)S(1)}, f32[32,512]{1,0:T(8,128)S(1)}, u32[]{:S(2)}, u32[]{:S(2)}) collective-permute-start(f32[32,512]{1,0:T(8,128)S(1)} %select_maximum_fusion), channel_id=1, source_target_pairs={{0,2},{2,0},{4,6},{6,4},{8,10},{10,8},{12,14},{14,12},{16,18},{18,... | collective-permute-start | bytes 196616 | tf_op jit(solution)/shard_map/ppermute | solution.py:17
  13.8 4.5 %collective-permute-start.2 = (f32[32,512]{1,0:T(8,128)S(1)}, f32[32,512]{1,0:T(8,128)S(1)}, u32[]{:S(2)}, u32[]{:S(2)}) collective-permute-start(f32[32,512]{1,0:T(8,128)S(1)} %fusion.8), channel_id=1, source_target_pairs={{0,4},{2,6},{4,0},{6,2},{8,12},{10,14},{12,8},{14,10},{16,20},{18,... | collective-permute-start | bytes 196616 | tf_op jit(solution)/shard_map/ppermute | solution.py:17
  18.3 4.3 %collective-permute-start.3 = (f32[32,512]{1,0:T(8,128)S(1)}, f32[32,512]{1,0:T(8,128)S(1)}, u32[]{:S(2)}, u32[]{:S(2)}) collective-permute-start(f32[32,512]{1,0:T(8,128)S(1)} %add.19), channel_id=1, source_target_pairs={{0,8},{2,10},{4,12},{6,14},{8,0},{10,2},{12,4},{14,6},{16,24},{18,... | collective-permute-start | bytes 196616 | tf_op jit(solution)/shard_map/ppermute | solution.py:17
  22.6 5.2 %collective-permute-start.4 = (f32[32,512]{1,0:T(8,128)S(1)}, f32[32,512]{1,0:T(8,128)S(1)}, u32[]{:S(2)}, u32[]{:S(2)}) collective-permute-start(f32[32,512]{1,0:T(8,128)S(1)} %add.20), channel_id=1, source_target_pairs={{0,16},{2,18},{4,20},{6,22},{8,24},{10,26},{12,28},{14,30},{16,0},... | collective-permute-start | bytes 196616 | tf_op jit(solution)/shard_map/ppermute | solution.py:17

commit v11 on v10

--- a/solution.py
+++ b/solution.py
@@ -75,55 +75,55 @@
 
 
 def update_kernel(cols_ref, live_ref, chosen_ref, rat_ref, res_ref, user_ref, item_ref, start_ref, upd_ref, part_ref):
-    t = pl.program_id(0)
-    width = rat_ref.shape[2]
-    slots = rat_ref.shape[1]
+    group, slots, width, _ = rat_ref.shape
     tiles = item_ref.shape[1] // width
-    user = user_ref[...]
-    pick = chosen_ref[t] > 0
-    factors, starts, lives = [], [], []
-    for k in range(slots):
-        c = cols_ref[t, k]
-        lives.append(live_ref[t, k] > 0)
-        factor = item_ref[:, 0:width]
-        start = start_ref[:, 0:width]
-        for j in range(1, tiles):
-            factor = jnp.where(c == j, item_ref[:, j * width : (j + 1) * width], factor)
-            start = jnp.where(c == j, start_ref[:, j * width : (j + 1) * width], start)
-        factors.append(factor)
-        starts.append(start)
-    estimate = lax.dot_general(
-        user, jnp.concatenate(factors, axis=1), (((0,), (0,)), ((), ())), preferred_element_type=jnp.float32
-    )
-    fresh = []
-    for k in range(slots):
-        live = lives[k]
-        value = jnp.where(
-            live & pick,
-            rat_ref[0, k].astype(jnp.float32) - estimate[:, k * width : (k + 1) * width],
-            res_ref[0, k].astype(jnp.float32),
+    for r in range(group):
+        t = pl.program_id(0) * group + r
+        user = user_ref[:, r * width : (r + 1) * width]
+        pick = chosen_ref[t] > 0
+        factors, starts, lives = [], [], []
+        for k in range(slots):
+            c = cols_ref[t, k]
+            lives.append(live_ref[t, k] > 0)
+            factor = item_ref[:, 0:width]
+            start = start_ref[:, 0:width]
+            for j in range(1, tiles):
+                factor = jnp.where(c == j, item_ref[:, j * width : (j + 1) * width], factor)
+                start = jnp.where(c == j, start_ref[:, j * width : (j + 1) * width], start)
+            factors.append(factor)
+            starts.append(start)
+        estimate = lax.dot_general(
+            user, jnp.concatenate(factors, axis=1), (((0,), (0,)), ((), ())), preferred_element_type=jnp.float32
         )
-        value = jnp.where(live, value, 0.0).astype(jnp.bfloat16)
-        upd_ref[0, k] = value
-        fresh.append(value)
-    acc = lax.dot_general(
-        jnp.concatenate(starts, axis=1),
-        jnp.concatenate(fresh, axis=1),
-        (((1,), (1,)), ((), ())),
-        preferred_element_type=jnp.float32,
-    )
-    part_ref[...] = acc
+        fresh = []
+        for k in range(slots):
+            live = lives[k]
+            value = jnp.where(
+                live & pick,
+                rat_ref[r, k].astype(jnp.float32) - estimate[:, k * width : (k + 1) * width],
+                res_ref[r, k].astype(jnp.float32),
+            )
+            value = jnp.where(live, value, 0.0).astype(jnp.bfloat16)
+            upd_ref[r, k] = value
+            fresh.append(value)
+        part_ref[:, r * width : (r + 1) * width] = lax.dot_general(
+            jnp.concatenate(starts, axis=1),
+            jnp.concatenate(fresh, axis=1),
+            (((1,), (1,)), ((), ())),
+            preferred_element_type=jnp.float32,
+        )
 
 
 def update(ratings, residual, tile_columns, occupied, chosen, user_factors, items, start):
     rows, slots, width, _ = ratings.shape
     rank = user_factors.shape[0]
     block = start.shape[0]
+    group = 2 if rows % 2 == 0 else 1
     smem = pl.BlockSpec(memory_space=pltpu.SMEM)
-    tile = pl.BlockSpec((1, slots, width, width), lambda t: (t, 0, 0, 0))
+    tile = pl.BlockSpec((group, slots, width, width), lambda t: (t, 0, 0, 0))
     return pl.pallas_call(
         update_kernel,
-        grid=(rows,),
+        grid=(rows // group,),
         out_shape=(
             jax.ShapeDtypeStruct(ratings.shape, jnp.bfloat16),
             jax.ShapeDtypeStruct((block, rows * width), jnp.float32),
@@ -134,11 +134,11 @@
             smem,
             tile,
             tile,
-            pl.BlockSpec((rank, width), lambda t: (0, t)),
+            pl.BlockSpec((rank, group * width), lambda t: (0, t)),
             pl.BlockSpec(items.shape, lambda t: (0, 0)),
             pl.BlockSpec(start.shape, lambda t: (0, 0)),
         ],
-        out_specs=(tile, pl.BlockSpec((block, width), lambda t: (0, t))),
+        out_specs=(tile, pl.BlockSpec((block, group * width), lambda t: (0, t))),
         cost_estimate=pl.CostEstimate(
             flops=2 * rows * slots * width * width * (rank + block),
             transcendentals=0,

time: 33.3 us -> 32.1 us (0.964)
  Pallas kernels: 8.33 us -> 7.26 us
    pallas_call x1, Pallas kernels: 3.85 us -> 2.78 us  [update(): pl.pallas_call(update_kernel, grid=(rows // group,), out_shape=(jax.Shape...]
where the time goes in v11:
time: 32.1 us; the launch traced here: 31.9 us
  waiting for transfers between devices  10.6 us (33%)
  starting transfers between devices  10.1 us (31%)
  Pallas kernels  7.26 us (23%)
  other arithmetic  1.52 us (5%)
  matrix products  0.93 us (3%)
  between operations  0.73 us (2%)
  local copies, waits for them, and re-layouts  0.71 us (2%)
    ppermute x5, waiting for transfers between devices, all_sum(): x = x + lax.ppermute(x, axis, [(i, i ^ step) for i in range(n)])  10.6 us
    ppermute x5, starting transfers between devices, all_sum(): x = x + lax.ppermute(x, axis, [(i, i ^ step) for i in range(n)])  10.1 us
    pallas_call x1, Pallas kernels, tail(): pl.pallas_call(functools.partial(tail_kernel, scale=1.0 / user_total, roo...  4.47 us
    pallas_call x1, Pallas kernels, update(): pl.pallas_call(update_kernel, grid=(rows // group,), out_shape=(jax.Shape...  2.78 us
    add x5, other arithmetic, all_sum(): x = x + lax.ppermute(x, axis, [(i, i ^ step) for i in range(n)])  1.51 us
    unnamed x8, local copies, waits for them, and re-layouts  0.69 us
  transfers between devices with their start and end apart: 5, of which 5 were waited for; matrix products, arithmetic and copies ran while one was open for 0% of the time, Pallas kernels for 0%

profile of v11, /device:TPU:0, one launch (start us, length us, event | category | flops | bytes accessed | tf_op | source)
XLA Modules:
  0.0 31.9 jit_solution(109405011042954828)
XLA Ops:
  0.6 0.0 copy-start.2
  0.6 2.8 %shard_map.103 = (bf16[4,3,128,128]{3,2,1,0:T(8,128)(2,1)}, f32[32,512]{1,0:T(8,128)}) custom-call(s32[4,3]{1,0:T(4,128)} %cols_ref.1, s32[4,3]{1,0:T(4,128)} %live_ref.1, s32[4]{0:T(128)} %chosen_ref.1, bf16[4,3,128,128]{3,2,1,0:T(8,128)(2,1)} %rat_ref.1, bf16[4,3,128,128]{3,2,1,0:T(8,128)(2,1)} %res_ref.1, bf16[64,512]{1,0:T(8,128)(2,1)} %user_ref.1, ...), custom_call_target="tpu_custom_call" | custom-call | flops 37748736 | bytes 1245184 | tf_op jit(solution)/shard_map/pallas_call | solution.py:124
  3.4 0.0 copy-start.1
  3.4 3.0 %collective-permute-start = (f32[32,512]{1,0:T(8,128)}, f32[32,512]{1,0:T(8,128)S(1)}, u32[]{:S(2)}, u32[]{:S(2)}) collective-permute-start(f32[32,512]{1,0:T(8,128)} %get-tuple-element.8), channel_id=1, source_target_pairs={{0,1},{1,0},{2,3},{3,2},{4,5},{5,4},{6,7},{7,6},{8,9},{9,8},{10,11... | collective-permute-start | bytes 196616 | tf_op jit(solution)/shard_map/ppermute | solution.py:17
  6.4 0.0 copy-done.2
  6.4 0.1 copy.12
  6.5 2.4 %collective-permute-done = f32[32,512]{1,0:T(8,128)S(1)} collective-permute-done((f32[32,512]{1,0:T(8,128)}, f32[32,512]{1,0:T(8,128)S(1)}, u32[]{:S(2)}, u32[]{:S(2)}) %collective-permute-start) | collective-permute-done | bytes 65568 | tf_op jit(solution)/shard_map/ppermute | solution.py:17
  8.9 0.8 %add.17.proj_ref = f32[32,512]{1,0:T(8,128)S(1)} add(f32[32,512]{1,0:T(8,128)} %get-tuple-element.8, f32[32,512]{1,0:T(8,128)S(1)} %collective-permute-done) | non-fusion elementwise | flops 16384 | bytes 196608 | tf_op jit(solution)/shard_map/add | solution.py:17
  9.7 0.0 copy-start
  9.8 0.6 %copy-done = f32[32,512]{1,0:T(8,128)} copy-done((f32[32,512]{1,0:T(8,128)}, f32[32,512]{1,0:T(8,128)S(1)}, u32[]{:S(2)}) %copy-start) | copy-done | bytes 65560
  10.4 0.2 fusion.9
  10.6 0.0 copy-done.1
  10.6 0.3 fusion.3
  10.9 0.4 %fusion = f32[3,32,128,1]{2,0,3,1:T(4,128)S(1)} fusion(f32[4,3,128,32]{2,3,1,0:T(8,128)S(1)} %fusion.3, s32[4,3]{0,1:T(4,128)S(1)} %copy.12), kind=kOutput, calls=%fused_computation | convolution fusion | flops 1769508 | bytes 245808 | tf_op jit(solution)/shard_map/jtkb,tkc->jcb/dot_general | solution.py:172
  11.3 0.1 collective-permute-start.1
  11.4 1.2 %collective-permute-done.1 = f32[32,512]{1,0:T(8,128)S(1)} collective-permute-done((f32[32,512]{1,0:T(8,128)S(1)}, f32[32,512]{1,0:T(8,128)S(1)}, u32[]{:S(2)}, u32[]{:S(2)}) %collective-permute-start.1) | collective-permute-done | bytes 65568 | tf_op jit(solution)/shard_map/ppermute | solution.py:17
  12.7 2.1 %collective-permute-start.2 = (f32[32,512]{1,0:T(8,128)S(1)}, f32[32,512]{1,0:T(8,128)S(1)}, u32[]{:S(2)}, u32[]{:S(2)}) collective-permute-start(f32[32,512]{1,0:T(8,128)S(1)} %fusion.8), channel_id=1, source_target_pairs={{0,4},{2,6},{4,0},{6,2},{8,12},{10,14},{12,8},{14,10},{16,20},{18,... | collective-permute-start | bytes 196616 | tf_op jit(solution)/shard_map/ppermute | solution.py:17
  14.8 2.4 %collective-permute-done.2 = f32[32,512]{1,0:T(8,128)S(1)} collective-permute-done((f32[32,512]{1,0:T(8,128)S(1)}, f32[32,512]{1,0:T(8,128)S(1)}, u32[]{:S(2)}, u32[]{:S(2)}) %collective-permute-start.2) | collective-permute-done | bytes 65568 | tf_op jit(solution)/shard_map/ppermute | solution.py:17
  17.2 2.0 %collective-permute-start.3 = (f32[32,512]{1,0:T(8,128)S(1)}, f32[32,512]{1,0:T(8,128)S(1)}, u32[]{:S(2)}, u32[]{:S(2)}) collective-permute-start(f32[32,512]{1,0:T(8,128)S(1)} %add.19), channel_id=1, source_target_pairs={{0,8},{2,10},{4,12},{6,14},{8,0},{10,2},{12,4},{14,6},{16,24},{18,... | collective-permute-start | bytes 196616 | tf_op jit(solution)/shard_map/ppermute | solution.py:17
  19.2 2.4 %collective-permute-done.3 = f32[32,512]{1,0:T(8,128)S(1)} collective-permute-done((f32[32,512]{1,0:T(8,128)S(1)}, f32[32,512]{1,0:T(8,128)S(1)}, u32[]{:S(2)}, u32[]{:S(2)}) %collective-permute-start.3) | collective-permute-done | bytes 65568 | tf_op jit(solution)/shard_map/ppermute | solution.py:17
  21.6 3.0 %collective-permute-start.4 = (f32[32,512]{1,0:T(8,128)S(1)}, f32[32,512]{1,0:T(8,128)S(1)}, u32[]{:S(2)}, u32[]{:S(2)}) collective-permute-start(f32[32,512]{1,0:T(8,128)S(1)} %add.20), channel_id=1, source_target_pairs={{0,16},{2,18},{4,20},{6,22},{8,24},{10,26},{12,28},{14,30},{16,0},... | collective-permute-start | bytes 196616 | tf_op jit(solution)/shard_map/ppermute | solution.py:17
  24.6 2.2 %collective-permute-done.4 = f32[32,512]{1,0:T(8,128)S(1)} collective-permute-done((f32[32,512]{1,0:T(8,128)S(1)}, f32[32,512]{1,0:T(8,128)S(1)}, u32[]{:S(2)}, u32[]{:S(2)}) %collective-permute-start.4) | collective-permute-done | bytes 65568 | tf_op jit(solution)/shard_map/ppermute | solution.py:17
  26.8 0.6 %add.21.reduced_ref = f32[32,512]{1,0:T(8,128)} add(f32[32,512]{1,0:T(8,128)S(1)} %add.20, f32[32,512]{1,0:T(8,128)S(1)} %collective-permute-done.4) | non-fusion elementwise | flops 16384 | bytes 196608 | tf_op jit(solution)/shard_map/add | solution.py:17
  27.4 4.5 %shard_map.104 = (f32[32,512]{1,0:T(8,128)}, f32[32,384]{1,0:T(8,128)}) custom-call(f32[32,512]{1,0:T(8,128)} %add.21.reduced_ref, f32[32,512]{1,0:T(8,128)} %copy-done, bf16[32,384]{1,0:T(8,128)(2,1)} %bitcast.24), custom_call_target="tpu_custom_call" | custom-call | flops 7864320 | bytes 278528 | tf_op jit(solution)/shard_map/pallas_call | solution.py:63
  (6 shorter events, 0.1 us)
Async XLA Ops:
  0.6 5.8 %copy-start.2 = (s32[4,3]{1,0:T(4,128)S(1)}, s32[4,3]{1,0:T(4,128)}, u32[]{:S(2)}) copy-start(s32[4,3]{1,0:T(4,128)} %cols_ref.1) | copy-start | bytes 148
  3.4 7.1 %copy-start.1 = (bf16[4,3,128,128]{3,2,1,0:T(8,128)(2,1)S(1)}, bf16[4,3,128,128]{3,2,1,0:T(8,128)(2,1)}, u32[]{:S(2)}) copy-start(bf16[4,3,128,128]{3,2,1,0:T(8,128)(2,1)} %get-tuple-element.4) | copy-start | bytes 1179652
  3.4 5.5 %collective-permute-start = (f32[32,512]{1,0:T(8,128)}, f32[32,512]{1,0:T(8,128)S(1)}, u32[]{:S(2)}, u32[]{:S(2)}) collective-permute-start(f32[32,512]{1,0:T(8,128)} %get-tuple-element.8), channel_id=1, source_target_pairs={{0,1},{1,0},{2,3},{3,2},{4,5},{5,4},{6,7},{7,6},{8,9},{9,8},{10,11... | collective-permute-start | bytes 196616 | tf_op jit(solution)/shard_map/ppermute | solution.py:17
  9.7 0.6 %copy-start = (f32[32,512]{1,0:T(8,128)}, f32[32,512]{1,0:T(8,128)S(1)}, u32[]{:S(2)}) copy-start(f32[32,512]{1,0:T(8,128)S(1)} %add.17.proj_ref) | copy-start | bytes 196612
  11.3 1.3 %collective-permute-start.1 = (f32[32,512]{1,0:T(8,128)S(1)}, f32[32,512]{1,0:T(8,128)S(1)}, u32[]{:S(2)}, u32[]{:S(2)}) collective-permute-start(f32[32,512]{1,0:T(8,128)S(1)} %select_maximum_fusion), channel_id=1, source_target_pairs={{0,2},{2,0},{4,6},{6,4},{8,10},{10,8},{12,14},{14,12},{16,18},{18,... | collective-permute-start | bytes 196616 | tf_op jit(solution)/shard_map/ppermute | solution.py:17
  12.7 4.5 %collective-permute-start.2 = (f32[32,512]{1,0:T(8,128)S(1)}, f32[32,512]{1,0:T(8,128)S(1)}, u32[]{:S(2)}, u32[]{:S(2)}) collective-permute-start(f32[32,512]{1,0:T(8,128)S(1)} %fusion.8), channel_id=1, source_target_pairs={{0,4},{2,6},{4,0},{6,2},{8,12},{10,14},{12,8},{14,10},{16,20},{18,... | collective-permute-start | bytes 196616 | tf_op jit(solution)/shard_map/ppermute | solution.py:17
  17.2 4.3 %collective-permute-start.3 = (f32[32,512]{1,0:T(8,128)S(1)}, f32[32,512]{1,0:T(8,128)S(1)}, u32[]{:S(2)}, u32[]{:S(2)}) collective-permute-start(f32[32,512]{1,0:T(8,128)S(1)} %add.19), channel_id=1, source_target_pairs={{0,8},{2,10},{4,12},{6,14},{8,0},{10,2},{12,4},{14,6},{16,24},{18,... | collective-permute-start | bytes 196616 | tf_op jit(solution)/shard_map/ppermute | solution.py:17
  21.6 5.2 %collective-permute-start.4 = (f32[32,512]{1,0:T(8,128)S(1)}, f32[32,512]{1,0:T(8,128)S(1)}, u32[]{:S(2)}, u32[]{:S(2)}) collective-permute-start(f32[32,512]{1,0:T(8,128)S(1)} %add.20), channel_id=1, source_target_pairs={{0,16},{2,18},{4,20},{6,22},{8,24},{10,26},{12,28},{14,30},{16,0},... | collective-permute-start | bytes 196616 | tf_op jit(solution)/shard_map/ppermute | solution.py:17

commit v12 on v11

--- a/solution.py
+++ b/solution.py
@@ -118,7 +118,7 @@
     rows, slots, width, _ = ratings.shape
     rank = user_factors.shape[0]
     block = start.shape[0]
-    group = 2 if rows % 2 == 0 else 1
+    group = rows
     smem = pl.BlockSpec(memory_space=pltpu.SMEM)
     tile = pl.BlockSpec((group, slots, width, width), lambda t: (t, 0, 0, 0))
     return pl.pallas_call(

time: 32.1 us -> 31.9 us (level)
  no operation moved by 1% of the time
where the time goes in v12:
time: 31.9 us; the launch traced here: 31.7 us
  waiting for transfers between devices  10.6 us (33%)
  starting transfers between devices  10.1 us (32%)
  Pallas kernels  7.12 us (22%)
  other arithmetic  1.52 us (5%)
  matrix products  0.93 us (3%)
  between operations  0.73 us (2%)
  local copies, waits for them, and re-layouts  0.71 us (2%)
    ppermute x5, waiting for transfers between devices, all_sum(): x = x + lax.ppermute(x, axis, [(i, i ^ step) for i in range(n)])  10.6 us
    ppermute x5, starting transfers between devices, all_sum(): x = x + lax.ppermute(x, axis, [(i, i ^ step) for i in range(n)])  10.1 us
    pallas_call x1, Pallas kernels, tail(): pl.pallas_call(functools.partial(tail_kernel, scale=1.0 / user_total, roo...  4.47 us
    pallas_call x1, Pallas kernels, update(): pl.pallas_call(update_kernel, grid=(rows // group,), out_shape=(jax.Shape...  2.65 us
    add x5, other arithmetic, all_sum(): x = x + lax.ppermute(x, axis, [(i, i ^ step) for i in range(n)])  1.51 us
    unnamed x8, local copies, waits for them, and re-layouts  0.69 us
  transfers between devices with their start and end apart: 5, of which 5 were waited for; matrix products, arithmetic and copies ran while one was open for 0% of the time, Pallas kernels for 0%

profile of v12, /device:TPU:0, one launch (start us, length us, event | category | flops | bytes accessed | tf_op | source)
XLA Modules:
  0.0 31.7 jit_solution(3778864826269520725)
XLA Ops:
  0.6 0.0 copy-start.2
  0.6 2.6 %shard_map.103 = (bf16[4,3,128,128]{3,2,1,0:T(8,128)(2,1)}, f32[32,512]{1,0:T(8,128)}) custom-call(s32[4,3]{1,0:T(4,128)} %cols_ref.1, s32[4,3]{1,0:T(4,128)} %live_ref.1, s32[4]{0:T(128)} %chosen_ref.1, bf16[4,3,128,128]{3,2,1,0:T(8,128)(2,1)} %rat_ref.1, bf16[4,3,128,128]{3,2,1,0:T(8,128)(2,1)} %res_ref.1, bf16[64,512]{1,0:T(8,128)(2,1)} %user_ref.1, ...), custom_call_target="tpu_custom_call" | custom-call | flops 37748736 | bytes 1245184 | tf_op jit(solution)/shard_map/pallas_call | solution.py:124
  3.3 0.0 copy-start.1
  3.3 2.9 %collective-permute-start = (f32[32,512]{1,0:T(8,128)}, f32[32,512]{1,0:T(8,128)S(1)}, u32[]{:S(2)}, u32[]{:S(2)}) collective-permute-start(f32[32,512]{1,0:T(8,128)} %get-tuple-element.8), channel_id=1, source_target_pairs={{0,1},{1,0},{2,3},{3,2},{4,5},{5,4},{6,7},{7,6},{8,9},{9,8},{10,11... | collective-permute-start | bytes 196616 | tf_op jit(solution)/shard_map/ppermute | solution.py:17
  6.2 0.0 copy-done.2
  6.2 0.1 copy.12
  6.3 2.4 %collective-permute-done = f32[32,512]{1,0:T(8,128)S(1)} collective-permute-done((f32[32,512]{1,0:T(8,128)}, f32[32,512]{1,0:T(8,128)S(1)}, u32[]{:S(2)}, u32[]{:S(2)}) %collective-permute-start) | collective-permute-done | bytes 65568 | tf_op jit(solution)/shard_map/ppermute | solution.py:17
  8.7 0.8 %add.17.proj_ref = f32[32,512]{1,0:T(8,128)S(1)} add(f32[32,512]{1,0:T(8,128)} %get-tuple-element.8, f32[32,512]{1,0:T(8,128)S(1)} %collective-permute-done) | non-fusion elementwise | flops 16384 | bytes 196608 | tf_op jit(solution)/shard_map/add | solution.py:17
  9.5 0.0 copy-start
  9.6 0.6 %copy-done = f32[32,512]{1,0:T(8,128)} copy-done((f32[32,512]{1,0:T(8,128)}, f32[32,512]{1,0:T(8,128)S(1)}, u32[]{:S(2)}) %copy-start) | copy-done | bytes 65560
  10.2 0.2 fusion.9
  10.4 0.0 copy-done.1
  10.4 0.3 fusion.3
  10.7 0.4 %fusion = f32[3,32,128,1]{2,0,3,1:T(4,128)S(1)} fusion(f32[4,3,128,32]{2,3,1,0:T(8,128)S(1)} %fusion.3, s32[4,3]{0,1:T(4,128)S(1)} %copy.12), kind=kOutput, calls=%fused_computation | convolution fusion | flops 1769508 | bytes 245808 | tf_op jit(solution)/shard_map/jtkb,tkc->jcb/dot_general | solution.py:172
  11.1 0.1 collective-permute-start.1
  11.2 1.2 %collective-permute-done.1 = f32[32,512]{1,0:T(8,128)S(1)} collective-permute-done((f32[32,512]{1,0:T(8,128)S(1)}, f32[32,512]{1,0:T(8,128)S(1)}, u32[]{:S(2)}, u32[]{:S(2)}) %collective-permute-start.1) | collective-permute-done | bytes 65568 | tf_op jit(solution)/shard_map/ppermute | solution.py:17
  12.5 2.1 %collective-permute-start.2 = (f32[32,512]{1,0:T(8,128)S(1)}, f32[32,512]{1,0:T(8,128)S(1)}, u32[]{:S(2)}, u32[]{:S(2)}) collective-permute-start(f32[32,512]{1,0:T(8,128)S(1)} %fusion.8), channel_id=1, source_target_pairs={{0,4},{2,6},{4,0},{6,2},{8,12},{10,14},{12,8},{14,10},{16,20},{18,... | collective-permute-start | bytes 196616 | tf_op jit(solution)/shard_map/ppermute | solution.py:17
  14.6 2.4 %collective-permute-done.2 = f32[32,512]{1,0:T(8,128)S(1)} collective-permute-done((f32[32,512]{1,0:T(8,128)S(1)}, f32[32,512]{1,0:T(8,128)S(1)}, u32[]{:S(2)}, u32[]{:S(2)}) %collective-permute-start.2) | collective-permute-done | bytes 65568 | tf_op jit(solution)/shard_map/ppermute | solution.py:17
  17.0 2.0 %collective-permute-start.3 = (f32[32,512]{1,0:T(8,128)S(1)}, f32[32,512]{1,0:T(8,128)S(1)}, u32[]{:S(2)}, u32[]{:S(2)}) collective-permute-start(f32[32,512]{1,0:T(8,128)S(1)} %add.19), channel_id=1, source_target_pairs={{0,8},{2,10},{4,12},{6,14},{8,0},{10,2},{12,4},{14,6},{16,24},{18,... | collective-permute-start | bytes 196616 | tf_op jit(solution)/shard_map/ppermute | solution.py:17
  19.0 2.4 %collective-permute-done.3 = f32[32,512]{1,0:T(8,128)S(1)} collective-permute-done((f32[32,512]{1,0:T(8,128)S(1)}, f32[32,512]{1,0:T(8,128)S(1)}, u32[]{:S(2)}, u32[]{:S(2)}) %collective-permute-start.3) | collective-permute-done | bytes 65568 | tf_op jit(solution)/shard_map/ppermute | solution.py:17
  21.4 3.0 %collective-permute-start.4 = (f32[32,512]{1,0:T(8,128)S(1)}, f32[32,512]{1,0:T(8,128)S(1)}, u32[]{:S(2)}, u32[]{:S(2)}) collective-permute-start(f32[32,512]{1,0:T(8,128)S(1)} %add.20), channel_id=1, source_target_pairs={{0,16},{2,18},{4,20},{6,22},{8,24},{10,26},{12,28},{14,30},{16,0},... | collective-permute-start | bytes 196616 | tf_op jit(solution)/shard_map/ppermute | solution.py:17
  24.4 2.2 %collective-permute-done.4 = f32[32,512]{1,0:T(8,128)S(1)} collective-permute-done((f32[32,512]{1,0:T(8,128)S(1)}, f32[32,512]{1,0:T(8,128)S(1)}, u32[]{:S(2)}, u32[]{:S(2)}) %collective-permute-start.4) | collective-permute-done | bytes 65568 | tf_op jit(solution)/shard_map/ppermute | solution.py:17
  26.6 0.6 %add.21.reduced_ref = f32[32,512]{1,0:T(8,128)} add(f32[32,512]{1,0:T(8,128)S(1)} %add.20, f32[32,512]{1,0:T(8,128)S(1)} %collective-permute-done.4) | non-fusion elementwise | flops 16384 | bytes 196608 | tf_op jit(solution)/shard_map/add | solution.py:17
  27.2 4.5 %shard_map.104 = (f32[32,512]{1,0:T(8,128)}, f32[32,384]{1,0:T(8,128)}) custom-call(f32[32,512]{1,0:T(8,128)} %add.21.reduced_ref, f32[32,512]{1,0:T(8,128)} %copy-done, bf16[32,384]{1,0:T(8,128)(2,1)} %bitcast.24), custom_call_target="tpu_custom_call" | custom-call | flops 7864320 | bytes 278528 | tf_op jit(solution)/shard_map/pallas_call | solution.py:63
  (6 shorter events, 0.1 us)
Async XLA Ops:
  0.6 5.6 %copy-start.2 = (s32[4,3]{1,0:T(4,128)S(1)}, s32[4,3]{1,0:T(4,128)}, u32[]{:S(2)}) copy-start(s32[4,3]{1,0:T(4,128)} %cols_ref.1) | copy-start | bytes 148
  3.3 7.1 %copy-start.1 = (bf16[4,3,128,128]{3,2,1,0:T(8,128)(2,1)S(1)}, bf16[4,3,128,128]{3,2,1,0:T(8,128)(2,1)}, u32[]{:S(2)}) copy-start(bf16[4,3,128,128]{3,2,1,0:T(8,128)(2,1)} %get-tuple-element.4) | copy-start | bytes 1179652
  3.3 5.4 %collective-permute-start = (f32[32,512]{1,0:T(8,128)}, f32[32,512]{1,0:T(8,128)S(1)}, u32[]{:S(2)}, u32[]{:S(2)}) collective-permute-start(f32[32,512]{1,0:T(8,128)} %get-tuple-element.8), channel_id=1, source_target_pairs={{0,1},{1,0},{2,3},{3,2},{4,5},{5,4},{6,7},{7,6},{8,9},{9,8},{10,11... | collective-permute-start | bytes 196616 | tf_op jit(solution)/shard_map/ppermute | solution.py:17
  9.5 0.6 %copy-start = (f32[32,512]{1,0:T(8,128)}, f32[32,512]{1,0:T(8,128)S(1)}, u32[]{:S(2)}) copy-start(f32[32,512]{1,0:T(8,128)S(1)} %add.17.proj_ref) | copy-start | bytes 196612
  11.1 1.3 %collective-permute-start.1 = (f32[32,512]{1,0:T(8,128)S(1)}, f32[32,512]{1,0:T(8,128)S(1)}, u32[]{:S(2)}, u32[]{:S(2)}) collective-permute-start(f32[32,512]{1,0:T(8,128)S(1)} %select_maximum_fusion), channel_id=1, source_target_pairs={{0,2},{2,0},{4,6},{6,4},{8,10},{10,8},{12,14},{14,12},{16,18},{18,... | collective-permute-start | bytes 196616 | tf_op jit(solution)/shard_map/ppermute | solution.py:17
  12.5 4.5 %collective-permute-start.2 = (f32[32,512]{1,0:T(8,128)S(1)}, f32[32,512]{1,0:T(8,128)S(1)}, u32[]{:S(2)}, u32[]{:S(2)}) collective-permute-start(f32[32,512]{1,0:T(8,128)S(1)} %fusion.8), channel_id=1, source_target_pairs={{0,4},{2,6},{4,0},{6,2},{8,12},{10,14},{12,8},{14,10},{16,20},{18,... | collective-permute-start | bytes 196616 | tf_op jit(solution)/shard_map/ppermute | solution.py:17
  17.0 4.3 %collective-permute-start.3 = (f32[32,512]{1,0:T(8,128)S(1)}, f32[32,512]{1,0:T(8,128)S(1)}, u32[]{:S(2)}, u32[]{:S(2)}) collective-permute-start(f32[32,512]{1,0:T(8,128)S(1)} %add.19), channel_id=1, source_target_pairs={{0,8},{2,10},{4,12},{6,14},{8,0},{10,2},{12,4},{14,6},{16,24},{18,... | collective-permute-start | bytes 196616 | tf_op jit(solution)/shard_map/ppermute | solution.py:17
  21.4 5.2 %collective-permute-start.4 = (f32[32,512]{1,0:T(8,128)S(1)}, f32[32,512]{1,0:T(8,128)S(1)}, u32[]{:S(2)}, u32[]{:S(2)}) collective-permute-start(f32[32,512]{1,0:T(8,128)S(1)} %add.20), channel_id=1, source_target_pairs={{0,16},{2,18},{4,20},{6,22},{8,24},{10,26},{12,28},{14,30},{16,0},... | collective-permute-start | bytes 196616 | tf_op jit(solution)/shard_map/ppermute | solution.py:17

commit v13 on v12

--- a/solution.py
+++ b/solution.py
@@ -32,7 +32,20 @@
     rows = lax.broadcasted_iota(jnp.int32, (n, 2 * n), 0)
     cols = lax.broadcasted_iota(jnp.int32, (n, 2 * n), 1)
     aug = jnp.concatenate([g, (rows[:, :n] == cols[:, :n]).astype(jnp.float32)], axis=1)
-    for k in range(n):
+    k = 0
+    while k + 1 < n:
+        p, q = k, k + 1
+        inv_p = lax.rsqrt(aug[p : p + 1, p : p + 1])
+        head_p = aug[p : p + 1, :] * inv_p
+        factor_p = jnp.where(rows[:, :1] > p, aug[:, p : p + 1] * inv_p, 0.0)
+        row_q = aug[q : q + 1, :] - factor_p[q : q + 1, :] * head_p
+        inv_q = lax.rsqrt(row_q[:, q : q + 1])
+        head_q = row_q * inv_q
+        factor_q = jnp.where(rows[:, :1] > q, (aug[:, q : q + 1] - factor_p * head_p[:, q : q + 1]) * inv_q, 0.0)
+        rest = (aug - factor_p * head_p) - factor_q * head_q
+        aug = jnp.where(rows == p, head_p, jnp.where(rows == q, head_q, rest))
+        k += 2
+    if k < n:
         inv_pivot = lax.rsqrt(aug[k : k + 1, k : k + 1])
         head = aug[k : k + 1, :] * inv_pivot
         factor = jnp.where(rows[:, :1] > k, aug[:, k : k + 1] * inv_pivot, 0.0)

time: 31.9 us -> 33.7 us (1.056)
  Pallas kernels: 7.12 us -> 8.91 us
    pallas_call x1, Pallas kernels: 4.47 us -> 6.26 us  [tail(): pl.pallas_call(functools.partial(tail_kernel, scale=1.0 / user_total, roo...]
where the time goes in v13:
time: 33.7 us; the launch traced here: 33.5 us
  waiting for transfers between devices  10.6 us (31%)
  starting transfers between devices  10.1 us (30%)
  Pallas kernels  8.91 us (26%)
  other arithmetic  1.52 us (5%)
  matrix products  0.93 us (3%)
  between operations  0.73 us (2%)
  local copies, waits for them, and re-layouts  0.71 us (2%)
    ppermute x5, waiting for transfers between devices, all_sum(): x = x + lax.ppermute(x, axis, [(i, i ^ step) for i in range(n)])  10.6 us
    ppermute x5, starting transfers between devices, all_sum(): x = x + lax.ppermute(x, axis, [(i, i ^ step) for i in range(n)])  10.1 us
    pallas_call x1, Pallas kernels, tail(): pl.pallas_call(functools.partial(tail_kernel, scale=1.0 / user_total, roo...  6.26 us
    pallas_call x1, Pallas kernels, update(): pl.pallas_call(update_kernel, grid=(rows // group,), out_shape=(jax.Shape...  2.65 us
    add x5, other arithmetic, all_sum(): x = x + lax.ppermute(x, axis, [(i, i ^ step) for i in range(n)])  1.51 us
    unnamed x8, local copies, waits for them, and re-layouts  0.69 us
  transfers between devices with their start and end apart: 5, of which 5 were waited for; matrix products, arithmetic and copies ran while one was open for 0% of the time, Pallas kernels for 0%

profile of v13, /device:TPU:0, one launch (start us, length us, event | category | flops | bytes accessed | tf_op | source)
XLA Modules:
  0.0 33.5 jit_solution(16806667151291618974)
XLA Ops:
  0.6 0.0 copy-start.2
  0.6 2.6 %shard_map.103 = (bf16[4,3,128,128]{3,2,1,0:T(8,128)(2,1)}, f32[32,512]{1,0:T(8,128)}) custom-call(s32[4,3]{1,0:T(4,128)} %cols_ref.1, s32[4,3]{1,0:T(4,128)} %live_ref.1, s32[4]{0:T(128)} %chosen_ref.1, bf16[4,3,128,128]{3,2,1,0:T(8,128)(2,1)} %rat_ref.1, bf16[4,3,128,128]{3,2,1,0:T(8,128)(2,1)} %res_ref.1, bf16[64,512]{1,0:T(8,128)(2,1)} %user_ref.1, ...), custom_call_target="tpu_custom_call" | custom-call | flops 37748736 | bytes 1245184 | tf_op jit(solution)/shard_map/pallas_call | solution.py:137
  3.3 0.0 copy-start.1
  3.3 2.9 %collective-permute-start = (f32[32,512]{1,0:T(8,128)}, f32[32,512]{1,0:T(8,128)S(1)}, u32[]{:S(2)}, u32[]{:S(2)}) collective-permute-start(f32[32,512]{1,0:T(8,128)} %get-tuple-element.8), channel_id=1, source_target_pairs={{0,1},{1,0},{2,3},{3,2},{4,5},{5,4},{6,7},{7,6},{8,9},{9,8},{10,11... | collective-permute-start | bytes 196616 | tf_op jit(solution)/shard_map/ppermute | solution.py:17
  6.2 0.0 copy-done.2
  6.2 0.1 copy.12
  6.3 2.4 %collective-permute-done = f32[32,512]{1,0:T(8,128)S(1)} collective-permute-done((f32[32,512]{1,0:T(8,128)}, f32[32,512]{1,0:T(8,128)S(1)}, u32[]{:S(2)}, u32[]{:S(2)}) %collective-permute-start) | collective-permute-done | bytes 65568 | tf_op jit(solution)/shard_map/ppermute | solution.py:17
  8.7 0.8 %add.17.proj_ref = f32[32,512]{1,0:T(8,128)S(1)} add(f32[32,512]{1,0:T(8,128)} %get-tuple-element.8, f32[32,512]{1,0:T(8,128)S(1)} %collective-permute-done) | non-fusion elementwise | flops 16384 | bytes 196608 | tf_op jit(solution)/shard_map/add | solution.py:17
  9.5 0.0 copy-start
  9.6 0.6 %copy-done = f32[32,512]{1,0:T(8,128)} copy-done((f32[32,512]{1,0:T(8,128)}, f32[32,512]{1,0:T(8,128)S(1)}, u32[]{:S(2)}) %copy-start) | copy-done | bytes 65560
  10.2 0.2 fusion.9
  10.4 0.0 copy-done.1
  10.4 0.3 fusion.3
  10.7 0.4 %fusion = f32[3,32,128,1]{2,0,3,1:T(4,128)S(1)} fusion(f32[4,3,128,32]{2,3,1,0:T(8,128)S(1)} %fusion.3, s32[4,3]{0,1:T(4,128)S(1)} %copy.12), kind=kOutput, calls=%fused_computation | convolution fusion | flops 1769508 | bytes 245808 | tf_op jit(solution)/shard_map/jtkb,tkc->jcb/dot_general | solution.py:185
  11.1 0.1 collective-permute-start.1
  11.2 1.2 %collective-permute-done.1 = f32[32,512]{1,0:T(8,128)S(1)} collective-permute-done((f32[32,512]{1,0:T(8,128)S(1)}, f32[32,512]{1,0:T(8,128)S(1)}, u32[]{:S(2)}, u32[]{:S(2)}) %collective-permute-start.1) | collective-permute-done | bytes 65568 | tf_op jit(solution)/shard_map/ppermute | solution.py:17
  12.5 2.1 %collective-permute-start.2 = (f32[32,512]{1,0:T(8,128)S(1)}, f32[32,512]{1,0:T(8,128)S(1)}, u32[]{:S(2)}, u32[]{:S(2)}) collective-permute-start(f32[32,512]{1,0:T(8,128)S(1)} %fusion.8), channel_id=1, source_target_pairs={{0,4},{2,6},{4,0},{6,2},{8,12},{10,14},{12,8},{14,10},{16,20},{18,... | collective-permute-start | bytes 196616 | tf_op jit(solution)/shard_map/ppermute | solution.py:17
  14.6 2.4 %collective-permute-done.2 = f32[32,512]{1,0:T(8,128)S(1)} collective-permute-done((f32[32,512]{1,0:T(8,128)S(1)}, f32[32,512]{1,0:T(8,128)S(1)}, u32[]{:S(2)}, u32[]{:S(2)}) %collective-permute-start.2) | collective-permute-done | bytes 65568 | tf_op jit(solution)/shard_map/ppermute | solution.py:17
  17.0 2.0 %collective-permute-start.3 = (f32[32,512]{1,0:T(8,128)S(1)}, f32[32,512]{1,0:T(8,128)S(1)}, u32[]{:S(2)}, u32[]{:S(2)}) collective-permute-start(f32[32,512]{1,0:T(8,128)S(1)} %add.19), channel_id=1, source_target_pairs={{0,8},{2,10},{4,12},{6,14},{8,0},{10,2},{12,4},{14,6},{16,24},{18,... | collective-permute-start | bytes 196616 | tf_op jit(solution)/shard_map/ppermute | solution.py:17
  19.0 2.4 %collective-permute-done.3 = f32[32,512]{1,0:T(8,128)S(1)} collective-permute-done((f32[32,512]{1,0:T(8,128)S(1)}, f32[32,512]{1,0:T(8,128)S(1)}, u32[]{:S(2)}, u32[]{:S(2)}) %collective-permute-start.3) | collective-permute-done | bytes 65568 | tf_op jit(solution)/shard_map/ppermute | solution.py:17
  21.4 3.0 %collective-permute-start.4 = (f32[32,512]{1,0:T(8,128)S(1)}, f32[32,512]{1,0:T(8,128)S(1)}, u32[]{:S(2)}, u32[]{:S(2)}) collective-permute-start(f32[32,512]{1,0:T(8,128)S(1)} %add.20), channel_id=1, source_target_pairs={{0,16},{2,18},{4,20},{6,22},{8,24},{10,26},{12,28},{14,30},{16,0},... | collective-permute-start | bytes 196616 | tf_op jit(solution)/shard_map/ppermute | solution.py:17
  24.4 2.2 %collective-permute-done.4 = f32[32,512]{1,0:T(8,128)S(1)} collective-permute-done((f32[32,512]{1,0:T(8,128)S(1)}, f32[32,512]{1,0:T(8,128)S(1)}, u32[]{:S(2)}, u32[]{:S(2)}) %collective-permute-start.4) | collective-permute-done | bytes 65568 | tf_op jit(solution)/shard_map/ppermute | solution.py:17
  26.6 0.6 %add.21.reduced_ref = f32[32,512]{1,0:T(8,128)} add(f32[32,512]{1,0:T(8,128)S(1)} %add.20, f32[32,512]{1,0:T(8,128)S(1)} %collective-permute-done.4) | non-fusion elementwise | flops 16384 | bytes 196608 | tf_op jit(solution)/shard_map/add | solution.py:17
  27.2 6.3 %shard_map.104 = (f32[32,512]{1,0:T(8,128)}, f32[32,384]{1,0:T(8,128)}) custom-call(f32[32,512]{1,0:T(8,128)} %add.21.reduced_ref, f32[32,512]{1,0:T(8,128)} %copy-done, bf16[32,384]{1,0:T(8,128)(2,1)} %bitcast.24), custom_call_target="tpu_custom_call" | custom-call | flops 7864320 | bytes 278528 | tf_op jit(solution)/shard_map/pallas_call | solution.py:76
  (6 shorter events, 0.1 us)
Async XLA Ops:
  0.6 5.6 %copy-start.2 = (s32[4,3]{1,0:T(4,128)S(1)}, s32[4,3]{1,0:T(4,128)}, u32[]{:S(2)}) copy-start(s32[4,3]{1,0:T(4,128)} %cols_ref.1) | copy-start | bytes 148
  3.3 7.1 %copy-start.1 = (bf16[4,3,128,128]{3,2,1,0:T(8,128)(2,1)S(1)}, bf16[4,3,128,128]{3,2,1,0:T(8,128)(2,1)}, u32[]{:S(2)}) copy-start(bf16[4,3,128,128]{3,2,1,0:T(8,128)(2,1)} %get-tuple-element.4) | copy-start | bytes 1179652
  3.3 5.4 %collective-permute-start = (f32[32,512]{1,0:T(8,128)}, f32[32,512]{1,0:T(8,128)S(1)}, u32[]{:S(2)}, u32[]{:S(2)}) collective-permute-start(f32[32,512]{1,0:T(8,128)} %get-tuple-element.8), channel_id=1, source_target_pairs={{0,1},{1,0},{2,3},{3,2},{4,5},{5,4},{6,7},{7,6},{8,9},{9,8},{10,11... | collective-permute-start | bytes 196616 | tf_op jit(solution)/shard_map/ppermute | solution.py:17
  9.5 0.6 %copy-start = (f32[32,512]{1,0:T(8,128)}, f32[32,512]{1,0:T(8,128)S(1)}, u32[]{:S(2)}) copy-start(f32[32,512]{1,0:T(8,128)S(1)} %add.17.proj_ref) | copy-start | bytes 196612
  11.1 1.3 %collective-permute-start.1 = (f32[32,512]{1,0:T(8,128)S(1)}, f32[32,512]{1,0:T(8,128)S(1)}, u32[]{:S(2)}, u32[]{:S(2)}) collective-permute-start(f32[32,512]{1,0:T(8,128)S(1)} %select_maximum_fusion), channel_id=1, source_target_pairs={{0,2},{2,0},{4,6},{6,4},{8,10},{10,8},{12,14},{14,12},{16,18},{18,... | collective-permute-start | bytes 196616 | tf_op jit(solution)/shard_map/ppermute | solution.py:17
  12.5 4.5 %collective-permute-start.2 = (f32[32,512]{1,0:T(8,128)S(1)}, f32[32,512]{1,0:T(8,128)S(1)}, u32[]{:S(2)}, u32[]{:S(2)}) collective-permute-start(f32[32,512]{1,0:T(8,128)S(1)} %fusion.8), channel_id=1, source_target_pairs={{0,4},{2,6},{4,0},{6,2},{8,12},{10,14},{12,8},{14,10},{16,20},{18,... | collective-permute-start | bytes 196616 | tf_op jit(solution)/shard_map/ppermute | solution.py:17
  17.0 4.3 %collective-permute-start.3 = (f32[32,512]{1,0:T(8,128)S(1)}, f32[32,512]{1,0:T(8,128)S(1)}, u32[]{:S(2)}, u32[]{:S(2)}) collective-permute-start(f32[32,512]{1,0:T(8,128)S(1)} %add.19), channel_id=1, source_target_pairs={{0,8},{2,10},{4,12},{6,14},{8,0},{10,2},{12,4},{14,6},{16,24},{18,... | collective-permute-start | bytes 196616 | tf_op jit(solution)/shard_map/ppermute | solution.py:17
  21.4 5.2 %collective-permute-start.4 = (f32[32,512]{1,0:T(8,128)S(1)}, f32[32,512]{1,0:T(8,128)S(1)}, u32[]{:S(2)}, u32[]{:S(2)}) collective-permute-start(f32[32,512]{1,0:T(8,128)S(1)} %add.20), channel_id=1, source_target_pairs={{0,16},{2,18},{4,20},{6,22},{8,24},{10,26},{12,28},{14,30},{16,0},... | collective-permute-start | bytes 196616 | tf_op jit(solution)/shard_map/ppermute | solution.py:17

commit v14 on v12

--- a/solution.py
+++ b/solution.py
@@ -19,12 +19,26 @@
     return x
 
 
+def all_sum_parts(x, axis):
+    n = lax.axis_size(axis)
+    if n & (n - 1):
+        return lax.psum(x, axis), jnp.zeros_like(x)
+    step = 1
+    other = jnp.zeros_like(x)
+    while step < n:
+        if step > 1:
+            x = x + other
+        other = lax.ppermute(x, axis, [(i, i ^ step) for i in range(n)])
+        step *= 2
+    return x, other
+
+
 def split(x):
     head = x.astype(jnp.bfloat16)
     return head, (x - head.astype(jnp.float32)).astype(jnp.bfloat16)
 
 
-def tail_kernel(reduced_ref, proj_ref, start_ref, left_ref, right_ref, *, scale, root):
+def tail_kernel(reduced_ref, mine_ref, other_ref, start_ref, left_ref, right_ref, *, scale, root):
     n = start_ref.shape[0]
     lanes = reduced_ref.shape[1] - start_ref.shape[1]
     g = reduced_ref[:, :n] * scale
@@ -49,15 +63,15 @@
             jnp.dot(inv_head, x_tail, preferred_element_type=f32) + jnp.dot(inv_tail, x_head, preferred_element_type=f32)
         )
 
-    left_ref[...] = product(proj_ref[...])
+    left_ref[...] = product(mine_ref[...] + other_ref[...])
     summed = product(reduced_ref[:, lanes:])
     start = start_ref[...]
     start_term = jnp.dot(up_head, start, preferred_element_type=f32) + jnp.dot(up_tail, start, preferred_element_type=f32)
     right_ref[...] = summed / root - root * start_term
 
 
-def tail(reduced, projected, start, user_total):
-    n, users = projected.shape
+def tail(reduced, mine, other, start, user_total):
+    n, users = mine.shape
     items = start.shape[1]
     vmem = pl.BlockSpec(memory_space=pltpu.VMEM)
     return pl.pallas_call(
@@ -66,12 +80,12 @@
             jax.ShapeDtypeStruct((n, users), jnp.float32),
             jax.ShapeDtypeStruct((n, items), jnp.float32),
         ),
-        in_specs=[vmem] * 3,
+        in_specs=[vmem] * 4,
         out_specs=(vmem, vmem),
         cost_estimate=pl.CostEstimate(
             flops=2 * n * n * (users + 2 * items) * 3, transcendentals=n, bytes_accessed=4 * n * (2 * users + 3 * items)
         ),
-    )(reduced, projected, start)
+    )(reduced, mine, other, start)
 
 
 def update_kernel(cols_ref, live_ref, chosen_ref, rat_ref, res_ref, user_ref, item_ref, start_ref, upd_ref, part_ref):
@@ -158,7 +172,8 @@
     updated, partial_products = update(
         ratings, residual, tile_columns, occupied, chosen, user_factors, item_factors[0], start_block[0]
     )
-    projected = all_sum(partial_products, "items")
+    mine, other = all_sum_parts(partial_products, "items")
+    projected = mine + other
     gram_part = jnp.dot(projected, projected.T, precision=lax.Precision.HIGHEST)
     slot_terms = jnp.einsum(
         "jta,tkab->jtkb",
@@ -174,7 +189,7 @@
     lanes = -(-block_size // width) * width
     gram_lanes = jnp.pad(gram_part, ((0, 0), (0, lanes - block_size)))
     reduced = all_sum(jnp.concatenate([gram_lanes, item_terms], axis=1), "users")
-    left_block, right_block = tail(reduced, projected, start_block[0], user_total)
+    left_block, right_block = tail(reduced, mine, other, start_block[0], user_total)
     right_block = right_block.reshape(1, block_size, item_count * width)
     return (updated, left_block, right_block)
 

time: 31.9 us -> 31.4 us (0.984)
  local copies, waits for them, and re-layouts: 0.71 us -> 0.13 us
    ppermute x0 -> x1, starting transfers between devices: none -> 2.94 us  [all_sum_parts(): other = lax.ppermute(x, axis, [(i, i ^ step) for i in range(n)])]
    ppermute x5 -> x4, starting transfers between devices: 10.1 us -> 7.15 us  [all_sum(): x = x + lax.ppermute(x, axis, [(i, i ^ step) for i in range(n)])]
    ppermute x0 -> x1, waiting for transfers between devices: none -> 2.36 us  [all_sum_parts(): other = lax.ppermute(x, axis, [(i, i ^ step) for i in range(n)])]
    ppermute x5 -> x4, waiting for transfers between devices: 10.6 us -> 8.26 us  [all_sum(): x = x + lax.ppermute(x, axis, [(i, i ^ step) for i in range(n)])]
    add x0 -> x1, other arithmetic: none -> 0.87 us  [local(): projected = mine + other]
    add x5 -> x4, other arithmetic: 1.51 us -> 0.66 us  [all_sum(): x = x + lax.ppermute(x, axis, [(i, i ^ step) for i in range(n)])]
    unnamed x8, local copies, waits for them, and re-layouts: 0.69 us -> 0.11 us
where the time goes in v14:
time: 31.4 us; the launch traced here: 31.2 us
  waiting for transfers between devices  10.6 us (34%)
  starting transfers between devices  10.1 us (32%)
  Pallas kernels  7.14 us (23%)
  other arithmetic  1.55 us (5%)
  matrix products  0.93 us (3%)
  between operations  0.73 us (2%)
    ppermute x4, waiting for transfers between devices, all_sum(): x = x + lax.ppermute(x, axis, [(i, i ^ step) for i in range(n)])  8.26 us
    ppermute x4, starting transfers between devices, all_sum(): x = x + lax.ppermute(x, axis, [(i, i ^ step) for i in range(n)])  7.15 us
    pallas_call x1, Pallas kernels, tail(): pl.pallas_call(functools.partial(tail_kernel, scale=1.0 / user_total, roo...  4.51 us
    ppermute x1, starting transfers between devices, all_sum_parts(): other = lax.ppermute(x, axis, [(i, i ^ step) for i in range(n)])  2.94 us
    pallas_call x1, Pallas kernels, update(): pl.pallas_call(update_kernel, grid=(rows // group,), out_shape=(jax.Shape...  2.63 us
    ppermute x1, waiting for transfers between devices, all_sum_parts(): other = lax.ppermute(x, axis, [(i, i ^ step) for i in range(n)])  2.36 us
    add x1, other arithmetic, local(): projected = mine + other  0.87 us
    add x4, other arithmetic, all_sum(): x = x + lax.ppermute(x, axis, [(i, i ^ step) for i in range(n)])  0.66 us
  transfers between devices with their start and end apart: 5, of which 5 were waited for; matrix products, arithmetic and copies ran while one was open for 0% of the time, Pallas kernels for 0%

profile of v14, /device:TPU:0, one launch (start us, length us, event | category | flops | bytes accessed | tf_op | source)
XLA Modules:
  0.0 31.2 jit_solution(3565908663833778627)
XLA Ops:
  0.6 0.0 copy-start.2
  0.6 2.6 %shard_map.103 = (bf16[4,3,128,128]{3,2,1,0:T(8,128)(2,1)}, f32[32,512]{1,0:T(8,128)}) custom-call(s32[4,3]{1,0:T(4,128)} %cols_ref.1, s32[4,3]{1,0:T(4,128)} %live_ref.1, s32[4]{0:T(128)} %chosen_ref.1, bf16[4,3,128,128]{3,2,1,0:T(8,128)(2,1)} %rat_ref.1, bf16[4,3,128,128]{3,2,1,0:T(8,128)(2,1)} %res_ref.1, bf16[64,512]{1,0:T(8,128)(2,1)} %user_ref.1, ...), custom_call_target="tpu_custom_call" | custom-call | flops 37748736 | bytes 1245184 | tf_op jit(solution)/shard_map/pallas_call | solution.py:138
  3.3 0.0 copy-start
  3.3 2.9 %collective-permute-start = (f32[32,512]{1,0:T(8,128)}, f32[32,512]{1,0:T(8,128)S(1)}, u32[]{:S(2)}, u32[]{:S(2)}) collective-permute-start(f32[32,512]{1,0:T(8,128)} %get-tuple-element.8.mine_ref), channel_id=1, source_target_pairs={{0,1},{1,0},{2,3},{3,2},{4,5},{5,4},{6,7},{7,6},{8,9},{9,8},{10,11... | collective-permute-start | bytes 196616 | tf_op jit(solution)/shard_map/ppermute | solution.py:31
  6.2 0.0 copy-done.2
  6.2 0.1 copy.12
  6.3 2.4 %collective-permute-done.other_ref = f32[32,512]{1,0:T(8,128)S(1)} collective-permute-done((f32[32,512]{1,0:T(8,128)}, f32[32,512]{1,0:T(8,128)S(1)}, u32[]{:S(2)}, u32[]{:S(2)}) %collective-permute-start) | collective-permute-done | bytes 65568 | tf_op jit(solution)/shard_map/ppermute | solution.py:31
  8.7 0.0 copy-start.1
  8.7 0.9 %add.17 = f32[32,512]{1,0:T(8,128)S(1)} add(f32[32,512]{1,0:T(8,128)} %get-tuple-element.8.mine_ref, f32[32,512]{1,0:T(8,128)S(1)} %collective-permute-done.other_ref) | non-fusion elementwise | flops 16384 | bytes 196608 | tf_op jit(solution)/shard_map/add | solution.py:176
  9.5 0.0 copy-done.1
  9.6 0.2 fusion.9
  9.8 0.0 copy-done
  9.8 0.3 %fusion.3 = f32[4,3,128,32]{2,3,1,0:T(8,128)S(1)} fusion(bf16[4,3,128,128]{3,2,1,0:T(8,128)(2,1)S(1)} %copy-done, f32[32,4,128,1]{2,1,0,3:T(4,128)S(1)} %reshape.19), kind=kOutput, calls=%fused_computation.5 | convolution fusion | flops 75497472 | bytes 655360 | tf_op jit(solution)/shard_map/jta,tkab->jtkb/dot_general | solution.py:178
  10.1 0.4 %fusion = f32[3,32,128,1]{2,0,3,1:T(4,128)S(1)} fusion(f32[4,3,128,32]{2,3,1,0:T(8,128)S(1)} %fusion.3, s32[4,3]{0,1:T(4,128)S(1)} %copy.12), kind=kOutput, calls=%fused_computation | convolution fusion | flops 1769508 | bytes 245808 | tf_op jit(solution)/shard_map/jtkb,tkc->jcb/dot_general | solution.py:187
  10.6 0.1 collective-permute-start.1
  10.7 1.2 %collective-permute-done.1 = f32[32,512]{1,0:T(8,128)S(1)} collective-permute-done((f32[32,512]{1,0:T(8,128)S(1)}, f32[32,512]{1,0:T(8,128)S(1)}, u32[]{:S(2)}, u32[]{:S(2)}) %collective-permute-start.1) | collective-permute-done | bytes 65568 | tf_op jit(solution)/shard_map/ppermute | solution.py:17
  11.9 2.1 %collective-permute-start.2 = (f32[32,512]{1,0:T(8,128)S(1)}, f32[32,512]{1,0:T(8,128)S(1)}, u32[]{:S(2)}, u32[]{:S(2)}) collective-permute-start(f32[32,512]{1,0:T(8,128)S(1)} %fusion.8), channel_id=1, source_target_pairs={{0,4},{2,6},{4,0},{6,2},{8,12},{10,14},{12,8},{14,10},{16,20},{18,... | collective-permute-start | bytes 196616 | tf_op jit(solution)/shard_map/ppermute | solution.py:17
  14.0 2.4 %collective-permute-done.2 = f32[32,512]{1,0:T(8,128)S(1)} collective-permute-done((f32[32,512]{1,0:T(8,128)S(1)}, f32[32,512]{1,0:T(8,128)S(1)}, u32[]{:S(2)}, u32[]{:S(2)}) %collective-permute-start.2) | collective-permute-done | bytes 65568 | tf_op jit(solution)/shard_map/ppermute | solution.py:17
  16.5 2.0 %collective-permute-start.3 = (f32[32,512]{1,0:T(8,128)S(1)}, f32[32,512]{1,0:T(8,128)S(1)}, u32[]{:S(2)}, u32[]{:S(2)}) collective-permute-start(f32[32,512]{1,0:T(8,128)S(1)} %add.19), channel_id=1, source_target_pairs={{0,8},{2,10},{4,12},{6,14},{8,0},{10,2},{12,4},{14,6},{16,24},{18,... | collective-permute-start | bytes 196616 | tf_op jit(solution)/shard_map/ppermute | solution.py:17
  18.4 2.4 %collective-permute-done.3 = f32[32,512]{1,0:T(8,128)S(1)} collective-permute-done((f32[32,512]{1,0:T(8,128)S(1)}, f32[32,512]{1,0:T(8,128)S(1)}, u32[]{:S(2)}, u32[]{:S(2)}) %collective-permute-start.3) | collective-permute-done | bytes 65568 | tf_op jit(solution)/shard_map/ppermute | solution.py:17
  20.8 3.0 %collective-permute-start.4 = (f32[32,512]{1,0:T(8,128)S(1)}, f32[32,512]{1,0:T(8,128)S(1)}, u32[]{:S(2)}, u32[]{:S(2)}) collective-permute-start(f32[32,512]{1,0:T(8,128)S(1)} %add.20), channel_id=1, source_target_pairs={{0,16},{2,18},{4,20},{6,22},{8,24},{10,26},{12,28},{14,30},{16,0},... | collective-permute-start | bytes 196616 | tf_op jit(solution)/shard_map/ppermute | solution.py:17
  23.8 2.2 %collective-permute-done.4 = f32[32,512]{1,0:T(8,128)S(1)} collective-permute-done((f32[32,512]{1,0:T(8,128)S(1)}, f32[32,512]{1,0:T(8,128)S(1)}, u32[]{:S(2)}, u32[]{:S(2)}) %collective-permute-start.4) | collective-permute-done | bytes 65568 | tf_op jit(solution)/shard_map/ppermute | solution.py:17
  26.0 0.6 %add.21.reduced_ref = f32[32,512]{1,0:T(8,128)} add(f32[32,512]{1,0:T(8,128)S(1)} %add.20, f32[32,512]{1,0:T(8,128)S(1)} %collective-permute-done.4) | non-fusion elementwise | flops 16384 | bytes 196608 | tf_op jit(solution)/shard_map/add | solution.py:17
  26.7 4.5 %shard_map.104 = (f32[32,512]{1,0:T(8,128)}, f32[32,384]{1,0:T(8,128)}) custom-call(f32[32,512]{1,0:T(8,128)} %add.21.reduced_ref, f32[32,512]{1,0:T(8,128)} %get-tuple-element.8.mine_ref, f32[32,512]{1,0:T(8,128)} %copy-done.1, bf16[32,384]{1,0:T(8,128)(2,1)} %bitcast.24), custom_call_target="tpu_custom_call" | custom-call | flops 7864320 | bytes 278528 | tf_op jit(solution)/shard_map/pallas_call | solution.py:77
  (6 shorter events, 0.1 us)
Async XLA Ops:
  0.6 5.6 %copy-start.2 = (s32[4,3]{1,0:T(4,128)S(1)}, s32[4,3]{1,0:T(4,128)}, u32[]{:S(2)}) copy-start(s32[4,3]{1,0:T(4,128)} %cols_ref.1) | copy-start | bytes 148
  3.3 6.5 %copy-start = (bf16[4,3,128,128]{3,2,1,0:T(8,128)(2,1)S(1)}, bf16[4,3,128,128]{3,2,1,0:T(8,128)(2,1)}, u32[]{:S(2)}) copy-start(bf16[4,3,128,128]{3,2,1,0:T(8,128)(2,1)} %get-tuple-element.4) | copy-start | bytes 1179652
  3.3 5.4 %collective-permute-start = (f32[32,512]{1,0:T(8,128)}, f32[32,512]{1,0:T(8,128)S(1)}, u32[]{:S(2)}, u32[]{:S(2)}) collective-permute-start(f32[32,512]{1,0:T(8,128)} %get-tuple-element.8.mine_ref), channel_id=1, source_target_pairs={{0,1},{1,0},{2,3},{3,2},{4,5},{5,4},{6,7},{7,6},{8,9},{9,8},{10,11... | collective-permute-start | bytes 196616 | tf_op jit(solution)/shard_map/ppermute | solution.py:31
  8.7 0.9 %copy-start.1 = (f32[32,512]{1,0:T(8,128)}, f32[32,512]{1,0:T(8,128)S(1)}, u32[]{:S(2)}) copy-start(f32[32,512]{1,0:T(8,128)S(1)} %collective-permute-done.other_ref) | copy-start | bytes 196612
  10.6 1.3 %collective-permute-start.1 = (f32[32,512]{1,0:T(8,128)S(1)}, f32[32,512]{1,0:T(8,128)S(1)}, u32[]{:S(2)}, u32[]{:S(2)}) collective-permute-start(f32[32,512]{1,0:T(8,128)S(1)} %select_maximum_fusion), channel_id=1, source_target_pairs={{0,2},{2,0},{4,6},{6,4},{8,10},{10,8},{12,14},{14,12},{16,18},{18,... | collective-permute-start | bytes 196616 | tf_op jit(solution)/shard_map/ppermute | solution.py:17
  11.9 4.5 %collective-permute-start.2 = (f32[32,512]{1,0:T(8,128)S(1)}, f32[32,512]{1,0:T(8,128)S(1)}, u32[]{:S(2)}, u32[]{:S(2)}) collective-permute-start(f32[32,512]{1,0:T(8,128)S(1)} %fusion.8), channel_id=1, source_target_pairs={{0,4},{2,6},{4,0},{6,2},{8,12},{10,14},{12,8},{14,10},{16,20},{18,... | collective-permute-start | bytes 196616 | tf_op jit(solution)/shard_map/ppermute | solution.py:17
  16.5 4.3 %collective-permute-start.3 = (f32[32,512]{1,0:T(8,128)S(1)}, f32[32,512]{1,0:T(8,128)S(1)}, u32[]{:S(2)}, u32[]{:S(2)}) collective-permute-start(f32[32,512]{1,0:T(8,128)S(1)} %add.19), channel_id=1, source_target_pairs={{0,8},{2,10},{4,12},{6,14},{8,0},{10,2},{12,4},{14,6},{16,24},{18,... | collective-permute-start | bytes 196616 | tf_op jit(solution)/shard_map/ppermute | solution.py:17
  20.8 5.2 %collective-permute-start.4 = (f32[32,512]{1,0:T(8,128)S(1)}, f32[32,512]{1,0:T(8,128)S(1)}, u32[]{:S(2)}, u32[]{:S(2)}) collective-permute-start(f32[32,512]{1,0:T(8,128)S(1)} %add.20), channel_id=1, source_target_pairs={{0,16},{2,18},{4,20},{6,22},{8,24},{10,26},{12,28},{14,30},{16,0},... | collective-permute-start | bytes 196616 | tf_op jit(solution)/shard_map/ppermute | solution.py:17

commit v15 on v14

--- a/solution.py
+++ b/solution.py
@@ -174,17 +174,17 @@
     )
     mine, other = all_sum_parts(partial_products, "items")
     projected = mine + other
-    gram_part = jnp.dot(projected, projected.T, precision=lax.Precision.HIGHEST)
-    slot_terms = jnp.einsum(
-        "jta,tkab->jtkb",
-        projected.reshape(block_size, rows_dev, width),
-        updated.astype(jnp.float32),
-        precision=lax.Precision.HIGHEST,
-    )
-    one_hot = (
-        tile_columns[:, :, None] == jnp.arange(item_count, dtype=jnp.int32)[None, None, :]
-    ).astype(jnp.float32)
-    item_terms = jnp.einsum("jtkb,tkc->jcb", slot_terms, one_hot, precision=lax.Precision.HIGHEST)
+    head, low = split(projected)
+    f32 = jnp.float32
+    gram_part = jnp.dot(head, head.T, preferred_element_type=f32) + (
+        jnp.dot(head, low.T, preferred_element_type=f32) + jnp.dot(low, head.T, preferred_element_type=f32)
+    )
+    rows_of = lambda x: x.reshape(block_size, rows_dev, width)
+    slot_terms = jnp.einsum("jta,tkab->jtkb", rows_of(head), updated, preferred_element_type=f32) + jnp.einsum(
+        "jta,tkab->jtkb", rows_of(low), updated, preferred_element_type=f32
+    )
+    named = tile_columns[:, :, None] == jnp.arange(item_count, dtype=jnp.int32)[None, None, :]
+    item_terms = jnp.sum(jnp.where(named[None, :, :, :, None], slot_terms[:, :, :, None, :], 0.0), axis=(1, 2))
     item_terms = item_terms.reshape(block_size, item_count * width)
     lanes = -(-block_size // width) * width
     gram_lanes = jnp.pad(gram_part, ((0, 0), (0, lanes - block_size)))

time: 31.4 us -> 31.4 us (level)
    convert_element_type x0 -> x1, other arithmetic: none -> 0.87 us  [split(): return (head, (x - head.astype(jnp.float32)).astype(jnp.bfloat16))]
    add x1 -> x0, other arithmetic: 0.87 us -> none  [local(): projected = mine + other]
    dot_general x3 -> x5, matrix products: 0.93 us -> 0.75 us  [the longest x1 0.19 us: local(): jnp.einsum('jta,tkab->jtkb', rows_of(head), updated, preferred_element_ty...]
where the time goes in v15:
time: 31.4 us; the launch traced here: 31.1 us
  waiting for transfers between devices  10.6 us (34%)
  starting transfers between devices  10.1 us (32%)
  Pallas kernels  7.15 us (23%)
  other arithmetic  1.74 us (6%)
  matrix products  0.75 us (2%)
  between operations  0.73 us (2%)
    ppermute x4, waiting for transfers between devices, all_sum(): x = x + lax.ppermute(x, axis, [(i, i ^ step) for i in range(n)])  8.26 us
    ppermute x4, starting transfers between devices, all_sum(): x = x + lax.ppermute(x, axis, [(i, i ^ step) for i in range(n)])  7.15 us
    pallas_call x1, Pallas kernels, tail(): pl.pallas_call(functools.partial(tail_kernel, scale=1.0 / user_total, roo...  4.51 us
    ppermute x1, starting transfers between devices, all_sum_parts(): other = lax.ppermute(x, axis, [(i, i ^ step) for i in range(n)])  2.94 us
    pallas_call x1, Pallas kernels, update(): pl.pallas_call(update_kernel, grid=(rows // group,), out_shape=(jax.Shape...  2.65 us
    ppermute x1, waiting for transfers between devices, all_sum_parts(): other = lax.ppermute(x, axis, [(i, i ^ step) for i in range(n)])  2.38 us
    convert_element_type x1, other arithmetic, split(): return (head, (x - head.astype(jnp.float32)).astype(jnp.bfloat16))  0.87 us
    add x4, other arithmetic, all_sum(): x = x + lax.ppermute(x, axis, [(i, i ^ step) for i in range(n)])  0.67 us
  transfers between devices with their start and end apart: 5, of which 5 were waited for; matrix products, arithmetic and copies ran while one was open for 0% of the time, Pallas kernels for 0%

profile of v15, /device:TPU:0, one launch (start us, length us, event | category | flops | bytes accessed | tf_op | source)
XLA Modules:
  0.0 31.1 jit_solution(13353643889201673594)
XLA Ops:
  0.6 0.0 copy-start.2
  0.6 2.6 %shard_map.103 = (bf16[4,3,128,128]{3,2,1,0:T(8,128)(2,1)}, f32[32,512]{1,0:T(8,128)}) custom-call(s32[4,3]{1,0:T(4,128)} %cols_ref.1, s32[4,3]{1,0:T(4,128)} %live_ref.1, s32[4]{0:T(128)} %chosen_ref.1, bf16[4,3,128,128]{3,2,1,0:T(8,128)(2,1)} %rat_ref.1, bf16[4,3,128,128]{3,2,1,0:T(8,128)(2,1)} %res_ref.1, bf16[64,512]{1,0:T(8,128)(2,1)} %user_ref.1, ...), custom_call_target="tpu_custom_call" | custom-call | flops 37748736 | bytes 1245184 | tf_op jit(solution)/shard_map/pallas_call | solution.py:138
  3.3 0.0 copy-start
  3.3 2.9 %collective-permute-start = (f32[32,512]{1,0:T(8,128)}, f32[32,512]{1,0:T(8,128)S(1)}, u32[]{:S(2)}, u32[]{:S(2)}) collective-permute-start(f32[32,512]{1,0:T(8,128)} %get-tuple-element.8.mine_ref), channel_id=1, source_target_pairs={{0,1},{1,0},{2,3},{3,2},{4,5},{5,4},{6,7},{7,6},{8,9},{9,8},{10,11... | collective-permute-start | bytes 196616 | tf_op jit(solution)/shard_map/ppermute | solution.py:31
  6.2 0.0 copy-done.2
  6.2 0.1 iota_compare_fusion.1
  6.3 2.4 %collective-permute-done.other_ref = f32[32,512]{1,0:T(8,128)S(1)} collective-permute-done((f32[32,512]{1,0:T(8,128)}, f32[32,512]{1,0:T(8,128)S(1)}, u32[]{:S(2)}, u32[]{:S(2)}) %collective-permute-start) | collective-permute-done | bytes 65568 | tf_op jit(solution)/shard_map/ppermute | solution.py:31
  8.7 0.0 copy-start.1
  8.7 0.9 %subtract_convert_fusion = (bf16[32,512]{1,0:T(8,128)(2,1)S(1)}, bf16[32,512]{1,0:T(8,128)(2,1)S(1)}) fusion(f32[32,512]{1,0:T(8,128)} %get-tuple-element.8.mine_ref, f32[32,512]{1,0:T(8,128)S(1)} %collective-permute-done.other_ref), kind=kLoop, calls=%fused_computation.7 | loop fusion | flops 81920 | bytes 196608 | tf_op jit(solution)/shard_map/convert_element_type | solution.py:38
  9.6 0.0 copy-done.1
  9.6 0.1 fusion.5
  9.7 0.1 convolution_add_fusion.1
  9.9 0.1 convolution_add_fusion.2
  10.0 0.0 copy-done
  10.0 0.2 fusion.2
  10.2 0.2 fusion
  10.4 0.1 select_reduce_fusion
  10.5 0.1 collective-permute-start.1
  10.6 1.2 %collective-permute-done.1 = f32[32,512]{1,0:T(8,128)S(1)} collective-permute-done((f32[32,512]{1,0:T(8,128)S(1)}, f32[32,512]{1,0:T(8,128)S(1)}, u32[]{:S(2)}, u32[]{:S(2)}) %collective-permute-start.1) | collective-permute-done | bytes 65568 | tf_op jit(solution)/shard_map/ppermute | solution.py:17
  11.9 2.1 %collective-permute-start.2 = (f32[32,512]{1,0:T(8,128)S(1)}, f32[32,512]{1,0:T(8,128)S(1)}, u32[]{:S(2)}, u32[]{:S(2)}) collective-permute-start(f32[32,512]{1,0:T(8,128)S(1)} %fusion.4), channel_id=1, source_target_pairs={{0,4},{2,6},{4,0},{6,2},{8,12},{10,14},{12,8},{14,10},{16,20},{18,... | collective-permute-start | bytes 196616 | tf_op jit(solution)/shard_map/ppermute | solution.py:17
  14.0 2.4 %collective-permute-done.2 = f32[32,512]{1,0:T(8,128)S(1)} collective-permute-done((f32[32,512]{1,0:T(8,128)S(1)}, f32[32,512]{1,0:T(8,128)S(1)}, u32[]{:S(2)}, u32[]{:S(2)}) %collective-permute-start.2) | collective-permute-done | bytes 65568 | tf_op jit(solution)/shard_map/ppermute | solution.py:17
  16.4 2.0 %collective-permute-start.3 = (f32[32,512]{1,0:T(8,128)S(1)}, f32[32,512]{1,0:T(8,128)S(1)}, u32[]{:S(2)}, u32[]{:S(2)}) collective-permute-start(f32[32,512]{1,0:T(8,128)S(1)} %add.35), channel_id=1, source_target_pairs={{0,8},{2,10},{4,12},{6,14},{8,0},{10,2},{12,4},{14,6},{16,24},{18,... | collective-permute-start | bytes 196616 | tf_op jit(solution)/shard_map/ppermute | solution.py:17
  18.4 2.4 %collective-permute-done.3 = f32[32,512]{1,0:T(8,128)S(1)} collective-permute-done((f32[32,512]{1,0:T(8,128)S(1)}, f32[32,512]{1,0:T(8,128)S(1)}, u32[]{:S(2)}, u32[]{:S(2)}) %collective-permute-start.3) | collective-permute-done | bytes 65568 | tf_op jit(solution)/shard_map/ppermute | solution.py:17
  20.8 3.0 %collective-permute-start.4 = (f32[32,512]{1,0:T(8,128)S(1)}, f32[32,512]{1,0:T(8,128)S(1)}, u32[]{:S(2)}, u32[]{:S(2)}) collective-permute-start(f32[32,512]{1,0:T(8,128)S(1)} %add.36), channel_id=1, source_target_pairs={{0,16},{2,18},{4,20},{6,22},{8,24},{10,26},{12,28},{14,30},{16,0},... | collective-permute-start | bytes 196616 | tf_op jit(solution)/shard_map/ppermute | solution.py:17
  23.8 2.2 %collective-permute-done.4 = f32[32,512]{1,0:T(8,128)S(1)} collective-permute-done((f32[32,512]{1,0:T(8,128)S(1)}, f32[32,512]{1,0:T(8,128)S(1)}, u32[]{:S(2)}, u32[]{:S(2)}) %collective-permute-start.4) | collective-permute-done | bytes 65568 | tf_op jit(solution)/shard_map/ppermute | solution.py:17
  26.0 0.6 %add.37.reduced_ref = f32[32,512]{1,0:T(8,128)} add(f32[32,512]{1,0:T(8,128)S(1)} %add.36, f32[32,512]{1,0:T(8,128)S(1)} %collective-permute-done.4) | non-fusion elementwise | flops 16384 | bytes 196608 | tf_op jit(solution)/shard_map/add | solution.py:17
  26.6 4.5 %shard_map.104 = (f32[32,512]{1,0:T(8,128)}, f32[32,384]{1,0:T(8,128)}) custom-call(f32[32,512]{1,0:T(8,128)} %add.37.reduced_ref, f32[32,512]{1,0:T(8,128)} %get-tuple-element.8.mine_ref, f32[32,512]{1,0:T(8,128)} %copy-done.1, bf16[32,384]{1,0:T(8,128)(2,1)} %bitcast.23), custom_call_target="tpu_custom_call" | custom-call | flops 7864320 | bytes 278528 | tf_op jit(solution)/shard_map/pallas_call | solution.py:77
  (7 shorter events, 0.1 us)
Async XLA Ops:
  0.6 5.6 %copy-start.2 = (s32[4,3]{1,0:T(4,128)S(1)}, s32[4,3]{1,0:T(4,128)}, u32[]{:S(2)}) copy-start(s32[4,3]{1,0:T(4,128)} %cols_ref.1) | copy-start | bytes 148
  3.3 6.7 %copy-start = (bf16[4,3,128,128]{3,2,1,0:T(8,128)(2,1)S(1)}, bf16[4,3,128,128]{3,2,1,0:T(8,128)(2,1)}, u32[]{:S(2)}) copy-start(bf16[4,3,128,128]{3,2,1,0:T(8,128)(2,1)} %get-tuple-element.4) | copy-start | bytes 1179652
  3.3 5.4 %collective-permute-start = (f32[32,512]{1,0:T(8,128)}, f32[32,512]{1,0:T(8,128)S(1)}, u32[]{:S(2)}, u32[]{:S(2)}) collective-permute-start(f32[32,512]{1,0:T(8,128)} %get-tuple-element.8.mine_ref), channel_id=1, source_target_pairs={{0,1},{1,0},{2,3},{3,2},{4,5},{5,4},{6,7},{7,6},{8,9},{9,8},{10,11... | collective-permute-start | bytes 196616 | tf_op jit(solution)/shard_map/ppermute | solution.py:31
  8.7 0.9 %copy-start.1 = (f32[32,512]{1,0:T(8,128)}, f32[32,512]{1,0:T(8,128)S(1)}, u32[]{:S(2)}) copy-start(f32[32,512]{1,0:T(8,128)S(1)} %collective-permute-done.other_ref) | copy-start | bytes 196612
  10.5 1.3 %collective-permute-start.1 = (f32[32,512]{1,0:T(8,128)S(1)}, f32[32,512]{1,0:T(8,128)S(1)}, u32[]{:S(2)}, u32[]{:S(2)}) collective-permute-start(f32[32,512]{1,0:T(8,128)S(1)} %select_maximum_fusion), channel_id=1, source_target_pairs={{0,2},{2,0},{4,6},{6,4},{8,10},{10,8},{12,14},{14,12},{16,18},{18,... | collective-permute-start | bytes 196616 | tf_op jit(solution)/shard_map/ppermute | solution.py:17
  11.9 4.5 %collective-permute-start.2 = (f32[32,512]{1,0:T(8,128)S(1)}, f32[32,512]{1,0:T(8,128)S(1)}, u32[]{:S(2)}, u32[]{:S(2)}) collective-permute-start(f32[32,512]{1,0:T(8,128)S(1)} %fusion.4), channel_id=1, source_target_pairs={{0,4},{2,6},{4,0},{6,2},{8,12},{10,14},{12,8},{14,10},{16,20},{18,... | collective-permute-start | bytes 196616 | tf_op jit(solution)/shard_map/ppermute | solution.py:17
  16.4 4.3 %collective-permute-start.3 = (f32[32,512]{1,0:T(8,128)S(1)}, f32[32,512]{1,0:T(8,128)S(1)}, u32[]{:S(2)}, u32[]{:S(2)}) collective-permute-start(f32[32,512]{1,0:T(8,128)S(1)} %add.35), channel_id=1, source_target_pairs={{0,8},{2,10},{4,12},{6,14},{8,0},{10,2},{12,4},{14,6},{16,24},{18,... | collective-permute-start | bytes 196616 | tf_op jit(solution)/shard_map/ppermute | solution.py:17
  20.8 5.2 %collective-permute-start.4 = (f32[32,512]{1,0:T(8,128)S(1)}, f32[32,512]{1,0:T(8,128)S(1)}, u32[]{:S(2)}, u32[]{:S(2)}) collective-permute-start(f32[32,512]{1,0:T(8,128)S(1)} %add.36), channel_id=1, source_target_pairs={{0,16},{2,18},{4,20},{6,22},{8,24},{10,26},{12,28},{14,30},{16,0},... | collective-permute-start | bytes 196616 | tf_op jit(solution)/shard_map/ppermute | solution.py:17

commit v16 on v14

--- a/solution.py
+++ b/solution.py
@@ -88,7 +88,7 @@
     )(reduced, mine, other, start)
 
 
-def update_kernel(cols_ref, live_ref, chosen_ref, rat_ref, res_ref, user_ref, item_ref, start_ref, upd_ref, part_ref):
+def update_kernel(cols_ref, live_ref, chosen_ref, rat_ref, res_ref, user_ref, item_ref, start_ref, out_ref, *, emit):
     group, slots, width, _ = rat_ref.shape
     tiles = item_ref.shape[1] // width
     for r in range(group):
@@ -118,9 +118,12 @@
                 res_ref[r, k].astype(jnp.float32),
             )
             value = jnp.where(live, value, 0.0).astype(jnp.bfloat16)
-            upd_ref[r, k] = value
+            if emit == "updated":
+                out_ref[r, k] = value
             fresh.append(value)
-        part_ref[:, r * width : (r + 1) * width] = lax.dot_general(
+        if emit == "updated":
+            continue
+        out_ref[:, r * width : (r + 1) * width] = lax.dot_general(
             jnp.concatenate(starts, axis=1),
             jnp.concatenate(fresh, axis=1),
             (((1,), (1,)), ((), ())),
@@ -128,20 +131,23 @@
         )
 
 
-def update(ratings, residual, tile_columns, occupied, chosen, user_factors, items, start):
+def update(ratings, residual, tile_columns, occupied, chosen, user_factors, items, start, emit):
     rows, slots, width, _ = ratings.shape
     rank = user_factors.shape[0]
     block = start.shape[0]
     group = rows
     smem = pl.BlockSpec(memory_space=pltpu.SMEM)
     tile = pl.BlockSpec((group, slots, width, width), lambda t: (t, 0, 0, 0))
+    if emit == "updated":
+        out_shape = jax.ShapeDtypeStruct(ratings.shape, jnp.bfloat16)
+        out_spec = tile
+    else:
+        out_shape = jax.ShapeDtypeStruct((block, rows * width), jnp.float32)
+        out_spec = pl.BlockSpec((block, group * width), lambda t: (0, t))
     return pl.pallas_call(
-        update_kernel,
+        functools.partial(update_kernel, emit=emit),
         grid=(rows // group,),
-        out_shape=(
-            jax.ShapeDtypeStruct(ratings.shape, jnp.bfloat16),
-            jax.ShapeDtypeStruct((block, rows * width), jnp.float32),
-        ),
+        out_shape=out_shape,
         in_specs=[
             smem,
             smem,
@@ -152,7 +158,7 @@
             pl.BlockSpec(items.shape, lambda t: (0, 0)),
             pl.BlockSpec(start.shape, lambda t: (0, 0)),
         ],
-        out_specs=(tile, pl.BlockSpec((block, group * width), lambda t: (0, t))),
+        out_specs=out_spec,
         cost_estimate=pl.CostEstimate(
             flops=2 * rows * slots * width * width * (rank + block),
             transcendentals=0,
@@ -169,9 +175,9 @@
     block_size = start_block.shape[1]
     item_count = item_factors.shape[2] // width
     user_total = user_factors.shape[1] * lax.axis_size("users")
-    updated, partial_products = update(
-        ratings, residual, tile_columns, occupied, chosen, user_factors, item_factors[0], start_block[0]
-    )
+    inputs = (ratings, residual, tile_columns, occupied, chosen, user_factors, item_factors[0], start_block[0])
+    partial_products = update(*inputs, emit="products")
+    updated = update(*inputs, emit="updated")
     mine, other = all_sum_parts(partial_products, "items")
     projected = mine + other
     gram_part = jnp.dot(projected, projected.T, precision=lax.Precision.HIGHEST)

time: 31.4 us -> 31.2 us (level)
  Pallas kernels: 7.14 us -> 9.39 us
  waiting for transfers between devices: 10.6 us -> 8.35 us
  other arithmetic: 1.55 us -> 0.68 us
  local copies, waits for them, and re-layouts: 0.13 us -> 0.81 us
    ppermute x1, waiting for transfers between devices: 2.36 us -> 0.09 us  [all_sum_parts(): other = lax.ppermute(x, axis, [(i, i ^ step) for i in range(n)])]
    pallas_call x1 -> x2, Pallas kernels: 2.63 us -> 4.88 us  [update(): pl.pallas_call(functools.partial(update_kernel, emit=emit), grid=(rows //...]
    add x1, other arithmetic: 0.87 us -> 0.01 us  [local(): projected = mine + other]
    unnamed x8 -> x10, local copies, waits for them, and re-layouts: 0.11 us -> 0.79 us
  transfers between devices with their start and end apart: 5 -> 5, of which waited for: 5 -> 5; matrix products, arithmetic and copies ran while one was open for 0% -> 0% of each run, Pallas kernels for 0% -> 7%
where the time goes in v16:
time: 31.2 us; the launch traced here: 30.9 us
  starting transfers between devices  10 us (32%)
  Pallas kernels  9.39 us (30%)
  waiting for transfers between devices  8.35 us (27%)
  matrix products  0.93 us (3%)
  local copies, waits for them, and re-layouts  0.81 us (3%)
  between operations  0.72 us (2%)
  other arithmetic  0.68 us (2%)
    ppermute x4, waiting for transfers between devices, all_sum(): x = x + lax.ppermute(x, axis, [(i, i ^ step) for i in range(n)])  8.27 us
    ppermute x4, starting transfers between devices, all_sum(): x = x + lax.ppermute(x, axis, [(i, i ^ step) for i in range(n)])  7.09 us
    pallas_call x2, Pallas kernels, update(): pl.pallas_call(functools.partial(update_kernel, emit=emit), grid=(rows //...  4.88 us
    pallas_call x1, Pallas kernels, tail(): pl.pallas_call(functools.partial(tail_kernel, scale=1.0 / user_total, roo...  4.51 us
    ppermute x1, starting transfers between devices, all_sum_parts(): other = lax.ppermute(x, axis, [(i, i ^ step) for i in range(n)])  2.94 us
    unnamed x10, local copies, waits for them, and re-layouts  0.79 us
    add x4, other arithmetic, all_sum(): x = x + lax.ppermute(x, axis, [(i, i ^ step) for i in range(n)])  0.66 us
  transfers between devices with their start and end apart: 5, of which 5 were waited for; matrix products, arithmetic and copies ran while one was open for 0% of the time, Pallas kernels for 7%

profile of v16, /device:TPU:0, one launch (start us, length us, event | category | flops | bytes accessed | tf_op | source)
XLA Modules:
  0.0 30.9 jit_solution(3457953847769225961)
XLA Ops:
  0.6 0.0 copy-start.3
  0.6 2.6 %shard_map.104.mine_ref = f32[32,512]{1,0:T(8,128)} custom-call(s32[4,3]{1,0:T(4,128)} %cols_ref.3, s32[4,3]{1,0:T(4,128)} %live_ref.3, s32[4]{0:T(128)} %chosen_ref.3, bf16[4,3,128,128]{3,2,1,0:T(8,128)(2,1)} %rat_ref.3, bf16[4,3,128,128]{3,2,1,0:T(8,128)(2,1)} %res_ref.3, bf16[64,512]{1,0:T(8,128)(2,1)} %user_ref.3, bf16[64,384]{1,0:T(8,128)(2,1)} %bitcast.26, ...), custom_call_target="tpu_custom_call" | custom-call | flops 37748736 | bytes 1245184 | tf_op jit(solution)/shard_map/pallas_call | solution.py:147
  3.3 2.9 %collective-permute-start = (f32[32,512]{1,0:T(8,128)}, f32[32,512]{1,0:T(8,128)S(1)}, u32[]{:S(2)}, u32[]{:S(2)}) collective-permute-start(f32[32,512]{1,0:T(8,128)} %shard_map.104.mine_ref), channel_id=1, source_target_pairs={{0,1},{1,0},{2,3},{3,2},{4,5},{5,4},{6,7},{7,6},{8,9},{9,8},{10,11... | collective-permute-start | bytes 196616 | tf_op jit(solution)/shard_map/ppermute | solution.py:31
  6.2 0.0 copy-done.3
  6.2 0.1 copy.12
  6.3 0.0 copy-start.1
  6.3 2.3 %shard_map.103 = bf16[4,3,128,128]{3,2,1,0:T(8,128)(2,1)} custom-call(s32[4,3]{1,0:T(4,128)} %cols_ref.3, s32[4,3]{1,0:T(4,128)} %live_ref.3, s32[4]{0:T(128)} %chosen_ref.3, bf16[4,3,128,128]{3,2,1,0:T(8,128)(2,1)} %rat_ref.3, bf16[4,3,128,128]{3,2,1,0:T(8,128)(2,1)} %res_ref.3, bf16[64,512]{1,0:T(8,128)(2,1)} %user_ref.3, bf16[64,384]{1,0:T(8,128)(2,1)} %bitcast.27, ...), custom_call_target="tpu_custom_call" | custom-call | flops 37748736 | bytes 1245184 | tf_op jit(solution)/shard_map/pallas_call | solution.py:147
  8.6 0.0 copy-start
  8.6 0.1 collective-permute-done.other_ref
  8.7 0.0 copy-done.1
  8.7 0.0 copy-start.2
  8.7 0.6 %copy-done.2 = f32[32,512]{1,0:T(8,128)} copy-done((f32[32,512]{1,0:T(8,128)}, f32[32,512]{1,0:T(8,128)S(1)}, u32[]{:S(2)}) %copy-start.2) | copy-done | bytes 65560
  9.3 0.2 fusion.9
  9.5 0.1 copy-done
  9.6 0.3 %fusion.3 = f32[4,3,128,32]{2,3,1,0:T(8,128)S(1)} fusion(bf16[4,3,128,128]{3,2,1,0:T(8,128)(2,1)S(1)} %copy-done, f32[32,4,128,1]{2,1,0,3:T(4,128)S(1)} %reshape.19), kind=kOutput, calls=%fused_computation.5 | convolution fusion | flops 75497472 | bytes 655360 | tf_op jit(solution)/shard_map/jta,tkab->jtkb/dot_general | solution.py:184
  9.9 0.4 %fusion = f32[3,32,128,1]{2,0,3,1:T(4,128)S(1)} fusion(f32[4,3,128,32]{2,3,1,0:T(8,128)S(1)} %fusion.3, s32[4,3]{0,1:T(4,128)S(1)} %copy.12), kind=kOutput, calls=%fused_computation | convolution fusion | flops 1769508 | bytes 245808 | tf_op jit(solution)/shard_map/jtkb,tkc->jcb/dot_general | solution.py:193
  10.4 0.1 collective-permute-start.1
  10.4 1.2 %collective-permute-done.1 = f32[32,512]{1,0:T(8,128)S(1)} collective-permute-done((f32[32,512]{1,0:T(8,128)S(1)}, f32[32,512]{1,0:T(8,128)S(1)}, u32[]{:S(2)}, u32[]{:S(2)}) %collective-permute-start.1) | collective-permute-done | bytes 65568 | tf_op jit(solution)/shard_map/ppermute | solution.py:17
  11.7 2.1 %collective-permute-start.2 = (f32[32,512]{1,0:T(8,128)S(1)}, f32[32,512]{1,0:T(8,128)S(1)}, u32[]{:S(2)}, u32[]{:S(2)}) collective-permute-start(f32[32,512]{1,0:T(8,128)S(1)} %fusion.8), channel_id=1, source_target_pairs={{0,4},{2,6},{4,0},{6,2},{8,12},{10,14},{12,8},{14,10},{16,20},{18,... | collective-permute-start | bytes 196616 | tf_op jit(solution)/shard_map/ppermute | solution.py:17
  13.8 2.4 %collective-permute-done.2 = f32[32,512]{1,0:T(8,128)S(1)} collective-permute-done((f32[32,512]{1,0:T(8,128)S(1)}, f32[32,512]{1,0:T(8,128)S(1)}, u32[]{:S(2)}, u32[]{:S(2)}) %collective-permute-start.2) | collective-permute-done | bytes 65568 | tf_op jit(solution)/shard_map/ppermute | solution.py:17
  16.2 2.0 %collective-permute-start.3 = (f32[32,512]{1,0:T(8,128)S(1)}, f32[32,512]{1,0:T(8,128)S(1)}, u32[]{:S(2)}, u32[]{:S(2)}) collective-permute-start(f32[32,512]{1,0:T(8,128)S(1)} %add.19), channel_id=1, source_target_pairs={{0,8},{2,10},{4,12},{6,14},{8,0},{10,2},{12,4},{14,6},{16,24},{18,... | collective-permute-start | bytes 196616 | tf_op jit(solution)/shard_map/ppermute | solution.py:17
  18.2 2.4 %collective-permute-done.3 = f32[32,512]{1,0:T(8,128)S(1)} collective-permute-done((f32[32,512]{1,0:T(8,128)S(1)}, f32[32,512]{1,0:T(8,128)S(1)}, u32[]{:S(2)}, u32[]{:S(2)}) %collective-permute-start.3) | collective-permute-done | bytes 65568 | tf_op jit(solution)/shard_map/ppermute | solution.py:17
  20.5 3.0 %collective-permute-start.4 = (f32[32,512]{1,0:T(8,128)S(1)}, f32[32,512]{1,0:T(8,128)S(1)}, u32[]{:S(2)}, u32[]{:S(2)}) collective-permute-start(f32[32,512]{1,0:T(8,128)S(1)} %add.20), channel_id=1, source_target_pairs={{0,16},{2,18},{4,20},{6,22},{8,24},{10,26},{12,28},{14,30},{16,0},... | collective-permute-start | bytes 196616 | tf_op jit(solution)/shard_map/ppermute | solution.py:17
  23.5 2.2 %collective-permute-done.4 = f32[32,512]{1,0:T(8,128)S(1)} collective-permute-done((f32[32,512]{1,0:T(8,128)S(1)}, f32[32,512]{1,0:T(8,128)S(1)}, u32[]{:S(2)}, u32[]{:S(2)}) %collective-permute-start.4) | collective-permute-done | bytes 65568 | tf_op jit(solution)/shard_map/ppermute | solution.py:17
  25.8 0.6 %add.21.reduced_ref = f32[32,512]{1,0:T(8,128)} add(f32[32,512]{1,0:T(8,128)S(1)} %add.20, f32[32,512]{1,0:T(8,128)S(1)} %collective-permute-done.4) | non-fusion elementwise | flops 16384 | bytes 196608 | tf_op jit(solution)/shard_map/add | solution.py:17
  26.4 4.5 %shard_map.105 = (f32[32,512]{1,0:T(8,128)}, f32[32,384]{1,0:T(8,128)}) custom-call(f32[32,512]{1,0:T(8,128)} %add.21.reduced_ref, f32[32,512]{1,0:T(8,128)} %shard_map.104.mine_ref, f32[32,512]{1,0:T(8,128)} %copy-done.2, bf16[32,384]{1,0:T(8,128)(2,1)} %bitcast.25), custom_call_target="tpu_custom_call" | custom-call | flops 7864320 | bytes 278528 | tf_op jit(solution)/shard_map/pallas_call | solution.py:77
  (7 shorter events, 0.1 us)
Async XLA Ops:
  0.6 5.6 %copy-start.3 = (s32[4,3]{1,0:T(4,128)S(1)}, s32[4,3]{1,0:T(4,128)}, u32[]{:S(2)}) copy-start(s32[4,3]{1,0:T(4,128)} %cols_ref.3) | copy-start | bytes 148
  3.3 5.4 %collective-permute-start = (f32[32,512]{1,0:T(8,128)}, f32[32,512]{1,0:T(8,128)S(1)}, u32[]{:S(2)}, u32[]{:S(2)}) collective-permute-start(f32[32,512]{1,0:T(8,128)} %shard_map.104.mine_ref), channel_id=1, source_target_pairs={{0,1},{1,0},{2,3},{3,2},{4,5},{5,4},{6,7},{7,6},{8,9},{9,8},{10,11... | collective-permute-start | bytes 196616 | tf_op jit(solution)/shard_map/ppermute | solution.py:31
  6.3 2.4 %copy-start.1 = (f32[32,512]{1,0:T(8,128)S(1)}, f32[32,512]{1,0:T(8,128)}, u32[]{:S(2)}) copy-start(f32[32,512]{1,0:T(8,128)} %shard_map.104.mine_ref) | copy-start | bytes 196612
  8.6 1.0 %copy-start = (bf16[4,3,128,128]{3,2,1,0:T(8,128)(2,1)S(1)}, bf16[4,3,128,128]{3,2,1,0:T(8,128)(2,1)}, u32[]{:S(2)}) copy-start(bf16[4,3,128,128]{3,2,1,0:T(8,128)(2,1)} %shard_map.103) | copy-start | bytes 1179652
  8.7 0.6 %copy-start.2 = (f32[32,512]{1,0:T(8,128)}, f32[32,512]{1,0:T(8,128)S(1)}, u32[]{:S(2)}) copy-start(f32[32,512]{1,0:T(8,128)S(1)} %collective-permute-done.other_ref) | copy-start | bytes 196612
  10.4 1.3 %collective-permute-start.1 = (f32[32,512]{1,0:T(8,128)S(1)}, f32[32,512]{1,0:T(8,128)S(1)}, u32[]{:S(2)}, u32[]{:S(2)}) collective-permute-start(f32[32,512]{1,0:T(8,128)S(1)} %select_maximum_fusion), channel_id=1, source_target_pairs={{0,2},{2,0},{4,6},{6,4},{8,10},{10,8},{12,14},{14,12},{16,18},{18,... | collective-permute-start | bytes 196616 | tf_op jit(solution)/shard_map/ppermute | solution.py:17
  11.7 4.5 %collective-permute-start.2 = (f32[32,512]{1,0:T(8,128)S(1)}, f32[32,512]{1,0:T(8,128)S(1)}, u32[]{:S(2)}, u32[]{:S(2)}) collective-permute-start(f32[32,512]{1,0:T(8,128)S(1)} %fusion.8), channel_id=1, source_target_pairs={{0,4},{2,6},{4,0},{6,2},{8,12},{10,14},{12,8},{14,10},{16,20},{18,... | collective-permute-start | bytes 196616 | tf_op jit(solution)/shard_map/ppermute | solution.py:17
  16.2 4.3 %collective-permute-start.3 = (f32[32,512]{1,0:T(8,128)S(1)}, f32[32,512]{1,0:T(8,128)S(1)}, u32[]{:S(2)}, u32[]{:S(2)}) collective-permute-start(f32[32,512]{1,0:T(8,128)S(1)} %add.19), channel_id=1, source_target_pairs={{0,8},{2,10},{4,12},{6,14},{8,0},{10,2},{12,4},{14,6},{16,24},{18,... | collective-permute-start | bytes 196616 | tf_op jit(solution)/shard_map/ppermute | solution.py:17
  20.5 5.2 %collective-permute-start.4 = (f32[32,512]{1,0:T(8,128)S(1)}, f32[32,512]{1,0:T(8,128)S(1)}, u32[]{:S(2)}, u32[]{:S(2)}) collective-permute-start(f32[32,512]{1,0:T(8,128)S(1)} %add.20), channel_id=1, source_target_pairs={{0,16},{2,18},{4,20},{6,22},{8,24},{10,26},{12,28},{14,30},{16,0},... | collective-permute-start | bytes 196616 | tf_op jit(solution)/shard_map/ppermute | solution.py:17

commit v17 on v16

--- a/solution.py
+++ b/solution.py
@@ -33,15 +33,30 @@
     return x, other
 
 
+def all_sum_split(first, second, axis):
+    n = lax.axis_size(axis)
+    x = jnp.concatenate([first, second], axis=1)
+    cut = first.shape[1]
+    if n & (n - 1) or n < 2:
+        x = lax.psum(x, axis)
+        return x[:, :cut], jnp.zeros_like(first), x[:, cut:], jnp.zeros_like(second)
+    step = 1
+    while step < n // 2:
+        x = x + lax.ppermute(x, axis, [(i, i ^ step) for i in range(n)])
+        step *= 2
+    pairs = [(i, i ^ step) for i in range(n)]
+    head, rest = x[:, :cut], x[:, cut:]
+    return head, lax.ppermute(head, axis, pairs), rest, lax.ppermute(rest, axis, pairs)
+
+
 def split(x):
     head = x.astype(jnp.bfloat16)
     return head, (x - head.astype(jnp.float32)).astype(jnp.bfloat16)
 
 
-def tail_kernel(reduced_ref, mine_ref, other_ref, start_ref, left_ref, right_ref, *, scale, root):
-    n = start_ref.shape[0]
-    lanes = reduced_ref.shape[1] - start_ref.shape[1]
-    g = reduced_ref[:, :n] * scale
+def factor_kernel(mine_ref, other_ref, upper_ref, inverse_ref, *, scale):
+    n = upper_ref.shape[0]
+    g = (mine_ref[...] + other_ref[...])[:, :n] * scale
     g = 0.5 * (g + g.T)
     rows = lax.broadcasted_iota(jnp.int32, (n, 2 * n), 0)
     cols = lax.broadcasted_iota(jnp.int32, (n, 2 * n), 1)
@@ -51,11 +66,14 @@
         head = aug[k : k + 1, :] * inv_pivot
         factor = jnp.where(rows[:, :1] > k, aug[:, k : k + 1] * inv_pivot, 0.0)
         aug = jnp.where(rows == k, head, aug - factor * head)
-    upper = aug[:, :n]
-    inverse = aug[:, n:]
+    upper_ref[...] = aug[:, :n]
+    inverse_ref[...] = aug[:, n:]
+
+
+def finish_kernel(upper_ref, inverse_ref, sums_ref, last_ref, mine_ref, other_ref, start_ref, left_ref, right_ref, *, root):
     f32 = jnp.float32
-    inv_head, inv_tail = split(inverse)
-    up_head, up_tail = split(upper)
+    inv_head, inv_tail = split(inverse_ref[...])
+    up_head, up_tail = split(upper_ref[...])
 
     def product(x):
         x_head, x_tail = split(x)
@@ -64,28 +82,36 @@
         )
 
     left_ref[...] = product(mine_ref[...] + other_ref[...])
-    summed = product(reduced_ref[:, lanes:])
+    summed = product(sums_ref[...] + last_ref[...])
     start = start_ref[...]
     start_term = jnp.dot(up_head, start, preferred_element_type=f32) + jnp.dot(up_tail, start, preferred_element_type=f32)
     right_ref[...] = summed / root - root * start_term
 
 
-def tail(reduced, mine, other, start, user_total):
+def tail(gram_mine, gram_other, sums, last, mine, other, start, user_total):
     n, users = mine.shape
     items = start.shape[1]
     vmem = pl.BlockSpec(memory_space=pltpu.VMEM)
+    square = jax.ShapeDtypeStruct((n, n), jnp.float32)
+    upper, inverse = pl.pallas_call(
+        functools.partial(factor_kernel, scale=1.0 / user_total),
+        out_shape=(square, square),
+        in_specs=[vmem] * 2,
+        out_specs=(vmem, vmem),
+        cost_estimate=pl.CostEstimate(flops=4 * n * n * n, transcendentals=n, bytes_accessed=4 * n * (2 * gram_mine.shape[1] + 2 * n)),
+    )(gram_mine, gram_other)
     return pl.pallas_call(
-        functools.partial(tail_kernel, scale=1.0 / user_total, root=float(user_total) ** 0.5),
+        functools.partial(finish_kernel, root=float(user_total) ** 0.5),
         out_shape=(
             jax.ShapeDtypeStruct((n, users), jnp.float32),
             jax.ShapeDtypeStruct((n, items), jnp.float32),
         ),
-        in_specs=[vmem] * 4,
+        in_specs=[vmem] * 7,
         out_specs=(vmem, vmem),
         cost_estimate=pl.CostEstimate(
-            flops=2 * n * n * (users + 2 * items) * 3, transcendentals=n, bytes_accessed=4 * n * (2 * users + 3 * items)
+            flops=2 * n * n * (users + 2 * items) * 3, transcendentals=0, bytes_accessed=4 * n * (2 * users + 4 * items)
         ),
-    )(reduced, mine, other, start)
+    )(upper, inverse, sums, last, mine, other, start)
 
 
 def update_kernel(cols_ref, live_ref, chosen_ref, rat_ref, res_ref, user_ref, item_ref, start_ref, out_ref, *, emit):
@@ -194,8 +220,8 @@
     item_terms = item_terms.reshape(block_size, item_count * width)
     lanes = -(-block_size // width) * width
     gram_lanes = jnp.pad(gram_part, ((0, 0), (0, lanes - block_size)))
-    reduced = all_sum(jnp.concatenate([gram_lanes, item_terms], axis=1), "users")
-    left_block, right_block = tail(reduced, mine, other, start_block[0], user_total)
+    gram_mine, gram_other, sums, last = all_sum_split(gram_lanes, item_terms, "users")
+    left_block, right_block = tail(gram_mine, gram_other, sums, last, mine, other, start_block[0], user_total)
     right_block = right_block.reshape(1, block_size, item_count * width)
     return (updated, left_block, right_block)
 

time: 31.2 us -> 35.7 us (1.14)
  waiting for transfers between devices: 8.35 us -> 10.6 us
  Pallas kernels: 9.39 us -> 10.8 us
  local copies, waits for them, and re-layouts: 0.81 us -> 2.04 us
  other arithmetic: 0.68 us -> 0.05 us
    ppermute x4 -> x5, waiting for transfers between devices: 8.27 us -> 10.6 us  [the longest x3 6.02 us: all_sum_split(): x = x + lax.ppermute(x, axis, [(i, i ^ step) for i in range(n)])]
    pallas_call x1 -> x2, Pallas kernels: 4.51 us -> 5.91 us  [the longest x1 4.13 us: tail(): pl.pallas_call(functools.partial(factor_kernel, scale=1.0 / user_total),...]
    unnamed x10 -> x18, local copies, waits for them, and re-layouts: 0.79 us -> 2.01 us
    add x4 -> x3, other arithmetic: 0.66 us -> 0.03 us  [all_sum_split(): x = x + lax.ppermute(x, axis, [(i, i ^ step) for i in range(n)])]
    ppermute x4 -> x5, starting transfers between devices: 7.09 us -> 7.18 us  [the longest x3 4.1 us: all_sum_split(): x = x + lax.ppermute(x, axis, [(i, i ^ step) for i in range(n)])]
  transfers between devices with their start and end apart: 5 -> 6, of which waited for: 5 -> 5; matrix products, arithmetic and copies ran while one was open for 0% -> 0% of each run, Pallas kernels for 7% -> 18%
where the time goes in v17:
time: 35.7 us; the launch traced here: 35.3 us
  Pallas kernels  10.8 us (30%)
  waiting for transfers between devices  10.6 us (30%)
  starting transfers between devices  10.1 us (28%)
  local copies, waits for them, and re-layouts  2.04 us (6%)
  matrix products  0.92 us (3%)
  between operations  0.74 us (2%)
    ppermute x3, waiting for transfers between devices, all_sum_split(): x = x + lax.ppermute(x, axis, [(i, i ^ step) for i in range(n)])  6.02 us
    pallas_call x2, Pallas kernels, update(): pl.pallas_call(functools.partial(update_kernel, emit=emit), grid=(rows //...  4.88 us
    ppermute x1, waiting for transfers between devices, all_sum_split(): lax.ppermute(head, axis, pairs)  4.54 us
    pallas_call x1, Pallas kernels, tail(): pl.pallas_call(functools.partial(factor_kernel, scale=1.0 / user_total),...  4.13 us
    ppermute x3, starting transfers between devices, all_sum_split(): x = x + lax.ppermute(x, axis, [(i, i ^ step) for i in range(n)])  4.1 us
    ppermute x1, starting transfers between devices, all_sum_split(): lax.ppermute(rest, axis, pairs)  2.98 us
    ppermute x1, starting transfers between devices, all_sum_parts(): other = lax.ppermute(x, axis, [(i, i ^ step) for i in range(n)])  2.94 us
    unnamed x18, local copies, waits for them, and re-layouts  2.01 us
  transfers between devices with their start and end apart: 6, of which 5 were waited for; matrix products, arithmetic and copies ran while one was open for 0% of the time, Pallas kernels for 18%

profile of v17, /device:TPU:0, one launch (start us, length us, event | category | flops | bytes accessed | tf_op | source)
XLA Modules:
  0.0 35.3 jit_solution(1852452476475218936)
XLA Ops:
  0.6 0.0 copy-start.6
  0.6 2.6 %shard_map.104.mine_ref = f32[32,512]{1,0:T(8,128)} custom-call(s32[4,3]{1,0:T(4,128)} %cols_ref.3, s32[4,3]{1,0:T(4,128)} %live_ref.3, s32[4]{0:T(128)} %chosen_ref.3, bf16[4,3,128,128]{3,2,1,0:T(8,128)(2,1)} %rat_ref.3, bf16[4,3,128,128]{3,2,1,0:T(8,128)(2,1)} %res_ref.3, bf16[64,512]{1,0:T(8,128)(2,1)} %user_ref.3, bf16[64,384]{1,0:T(8,128)(2,1)} %bitcast.26, ...), custom_call_target="tpu_custom_call" | custom-call | flops 37748736 | bytes 1245184 | tf_op jit(solution)/shard_map/pallas_call | solution.py:173
  3.3 2.9 %collective-permute-start = (f32[32,512]{1,0:T(8,128)}, f32[32,512]{1,0:T(8,128)S(1)}, u32[]{:S(2)}, u32[]{:S(2)}) collective-permute-start(f32[32,512]{1,0:T(8,128)} %shard_map.104.mine_ref), channel_id=1, source_target_pairs={{0,1},{1,0},{2,3},{3,2},{4,5},{5,4},{6,7},{7,6},{8,9},{9,8},{10,11... | collective-permute-start | bytes 196616 | tf_op jit(solution)/shard_map/ppermute | solution.py:31
  6.2 0.0 copy-done.6
  6.2 0.1 copy.12
  6.3 0.0 copy-start.1
  6.3 2.3 %shard_map.103 = bf16[4,3,128,128]{3,2,1,0:T(8,128)(2,1)} custom-call(s32[4,3]{1,0:T(4,128)} %cols_ref.3, s32[4,3]{1,0:T(4,128)} %live_ref.3, s32[4]{0:T(128)} %chosen_ref.3, bf16[4,3,128,128]{3,2,1,0:T(8,128)(2,1)} %rat_ref.3, bf16[4,3,128,128]{3,2,1,0:T(8,128)(2,1)} %res_ref.3, bf16[64,512]{1,0:T(8,128)(2,1)} %user_ref.3, bf16[64,384]{1,0:T(8,128)(2,1)} %bitcast.27, ...), custom_call_target="tpu_custom_call" | custom-call | flops 37748736 | bytes 1245184 | tf_op jit(solution)/shard_map/pallas_call | solution.py:173
  8.6 0.0 copy-start
  8.6 0.1 collective-permute-done.other_ref
  8.6 0.0 copy-done.1
  8.7 0.0 copy-start.2
  8.7 0.6 %copy-done.2 = f32[32,512]{1,0:T(8,128)} copy-done((f32[32,512]{1,0:T(8,128)}, f32[32,512]{1,0:T(8,128)S(1)}, u32[]{:S(2)}) %copy-start.2) | copy-done | bytes 65560
  9.3 0.2 fusion.9
  9.5 0.1 copy-done
  9.6 0.3 fusion.3
  9.9 0.4 %fusion = f32[3,32,128,1]{2,0,3,1:T(4,128)S(1)} fusion(f32[4,3,128,32]{2,3,1,0:T(8,128)S(1)} %fusion.3, s32[4,3]{0,1:T(4,128)S(1)} %copy.12), kind=kOutput, calls=%fused_computation | convolution fusion | flops 1769508 | bytes 245808 | tf_op jit(solution)/shard_map/jtkb,tkc->jcb/dot_general | solution.py:219
  10.4 0.1 collective-permute-start.1
  10.4 1.2 %collective-permute-done.1 = f32[32,512]{1,0:T(8,128)S(1)} collective-permute-done((f32[32,512]{1,0:T(8,128)S(1)}, f32[32,512]{1,0:T(8,128)S(1)}, u32[]{:S(2)}, u32[]{:S(2)}) %collective-permute-start.1) | collective-permute-done | bytes 65568 | tf_op jit(solution)/shard_map/ppermute | solution.py:45
  11.7 2.1 %collective-permute-start.2 = (f32[32,512]{1,0:T(8,128)S(1)}, f32[32,512]{1,0:T(8,128)S(1)}, u32[]{:S(2)}, u32[]{:S(2)}) collective-permute-start(f32[32,512]{1,0:T(8,128)S(1)} %fusion.8), channel_id=1, source_target_pairs={{0,4},{2,6},{4,0},{6,2},{8,12},{10,14},{12,8},{14,10},{16,20},{18,... | collective-permute-start | bytes 196616 | tf_op jit(solution)/shard_map/ppermute | solution.py:45
  13.8 2.4 %collective-permute-done.2 = f32[32,512]{1,0:T(8,128)S(1)} collective-permute-done((f32[32,512]{1,0:T(8,128)S(1)}, f32[32,512]{1,0:T(8,128)S(1)}, u32[]{:S(2)}, u32[]{:S(2)}) %collective-permute-start.2) | collective-permute-done | bytes 65568 | tf_op jit(solution)/shard_map/ppermute | solution.py:45
  16.2 2.0 %collective-permute-start.3 = (f32[32,512]{1,0:T(8,128)S(1)}, f32[32,512]{1,0:T(8,128)S(1)}, u32[]{:S(2)}, u32[]{:S(2)}) collective-permute-start(f32[32,512]{1,0:T(8,128)S(1)} %add.16), channel_id=1, source_target_pairs={{0,8},{2,10},{4,12},{6,14},{8,0},{10,2},{12,4},{14,6},{16,24},{18,... | collective-permute-start | bytes 196616 | tf_op jit(solution)/shard_map/ppermute | solution.py:45
  18.2 2.4 %collective-permute-done.3 = f32[32,512]{1,0:T(8,128)S(1)} collective-permute-done((f32[32,512]{1,0:T(8,128)S(1)}, f32[32,512]{1,0:T(8,128)S(1)}, u32[]{:S(2)}, u32[]{:S(2)}) %collective-permute-start.3) | collective-permute-done | bytes 65568 | tf_op jit(solution)/shard_map/ppermute | solution.py:45
  20.5 0.0 copy-start.3
  20.6 3.0 %collective-permute-start.5 = (f32[32,384]{1,0:T(8,128)S(1)}, f32[32,384]{1,0:T(8,128)S(1)}, u32[]{:S(2)}, u32[]{:S(2)}) collective-permute-start(f32[32,384]{1,0:T(8,128)S(1)} %slice.9.sums_ref), channel_id=1, source_target_pairs={{0,16},{2,18},{4,20},{6,22},{8,24},{10,26},{12,28},{14,30},{16,0},... | collective-permute-start | bytes 147464 | tf_op jit(solution)/shard_map/ppermute | solution.py:49
  23.5 0.0 copy-start.4
  23.5 0.1 collective-permute-start.4
  23.6 4.5 %collective-permute-done.4.other_ref = f32[32,128]{1,0:T(8,128)S(1)} collective-permute-done((f32[32,128]{1,0:T(8,128)S(1)}, f32[32,128]{1,0:T(8,128)S(1)}, u32[]{:S(2)}, u32[]{:S(2)}) %collective-permute-start.4) | collective-permute-done | bytes 16416 | tf_op jit(solution)/shard_map/ppermute | solution.py:49
  28.2 0.0 copy-done.4
  28.2 0.0 copy-start.7
  28.2 0.6 %copy-done.7 = f32[32,128]{1,0:T(8,128)} copy-done((f32[32,128]{1,0:T(8,128)}, f32[32,128]{1,0:T(8,128)S(1)}, u32[]{:S(2)}) %copy-start.7) | copy-done | bytes 16408
  28.8 4.1 %shard_map.105 = (f32[32,32]{1,0:T(8,128)}, f32[32,32]{1,0:T(8,128)}) custom-call(f32[32,128]{1,0:T(8,128)} %copy-done.4, f32[32,128]{1,0:T(8,128)} %copy-done.7), custom_call_target="tpu_custom_call" | custom-call | flops 131072 | bytes 40960 | tf_op jit(solution)/shard_map/pallas_call | solution.py:96
  32.9 0.0 collective-permute-done.5.last_ref
  32.9 0.0 copy-start.5
  32.9 0.0 copy-done.3
  32.9 0.6 %copy-done.5 = f32[32,384]{1,0:T(8,128)} copy-done((f32[32,384]{1,0:T(8,128)}, f32[32,384]{1,0:T(8,128)S(1)}, u32[]{:S(2)}) %copy-start.5) | copy-done | bytes 49176
  33.5 1.8 %shard_map.106 = (f32[32,512]{1,0:T(8,128)}, f32[32,384]{1,0:T(8,128)}) custom-call(f32[32,32]{1,0:T(8,128)} %get-tuple-element.7.upper_ref, f32[32,32]{1,0:T(8,128)} %get-tuple-element.8.inverse_ref, f32[32,384]{1,0:T(8,128)} %copy-done.3, f32[32,384]{1,0:T(8,128)} %copy-done.5, f32[32,512]{1,0:T(8,128)} %shard_map.104.mine_ref, f32[32,512]{1,0:T(8,128)} %copy-done.2, ...), custom_call_target="tpu_custom_call" | custom-call | flops 7864320 | bytes 327680 | tf_op jit(solution)/shard_map/pallas_call | solution.py:103
  (9 shorter events, 0.1 us)
Async XLA Ops:
  0.6 5.6 %copy-start.6 = (s32[4,3]{1,0:T(4,128)S(1)}, s32[4,3]{1,0:T(4,128)}, u32[]{:S(2)}) copy-start(s32[4,3]{1,0:T(4,128)} %cols_ref.3) | copy-start | bytes 148
  3.3 5.4 %collective-permute-start = (f32[32,512]{1,0:T(8,128)}, f32[32,512]{1,0:T(8,128)S(1)}, u32[]{:S(2)}, u32[]{:S(2)}) collective-permute-start(f32[32,512]{1,0:T(8,128)} %shard_map.104.mine_ref), channel_id=1, source_target_pairs={{0,1},{1,0},{2,3},{3,2},{4,5},{5,4},{6,7},{7,6},{8,9},{9,8},{10,11... | collective-permute-start | bytes 196616 | tf_op jit(solution)/shard_map/ppermute | solution.py:31
  6.3 2.4 %copy-start.1 = (f32[32,512]{1,0:T(8,128)S(1)}, f32[32,512]{1,0:T(8,128)}, u32[]{:S(2)}) copy-start(f32[32,512]{1,0:T(8,128)} %shard_map.104.mine_ref) | copy-start | bytes 196612
  8.6 1.0 %copy-start = (bf16[4,3,128,128]{3,2,1,0:T(8,128)(2,1)S(1)}, bf16[4,3,128,128]{3,2,1,0:T(8,128)(2,1)}, u32[]{:S(2)}) copy-start(bf16[4,3,128,128]{3,2,1,0:T(8,128)(2,1)} %shard_map.103) | copy-start | bytes 1179652
  8.7 0.6 %copy-start.2 = (f32[32,512]{1,0:T(8,128)}, f32[32,512]{1,0:T(8,128)S(1)}, u32[]{:S(2)}) copy-start(f32[32,512]{1,0:T(8,128)S(1)} %collective-permute-done.other_ref) | copy-start | bytes 196612
  10.4 1.3 %collective-permute-start.1 = (f32[32,512]{1,0:T(8,128)S(1)}, f32[32,512]{1,0:T(8,128)S(1)}, u32[]{:S(2)}, u32[]{:S(2)}) collective-permute-start(f32[32,512]{1,0:T(8,128)S(1)} %select_maximum_fusion), channel_id=1, source_target_pairs={{0,2},{2,0},{4,6},{6,4},{8,10},{10,8},{12,14},{14,12},{16,18},{18,... | collective-permute-start | bytes 196616 | tf_op jit(solution)/shard_map/ppermute | solution.py:45
  11.7 4.5 %collective-permute-start.2 = (f32[32,512]{1,0:T(8,128)S(1)}, f32[32,512]{1,0:T(8,128)S(1)}, u32[]{:S(2)}, u32[]{:S(2)}) collective-permute-start(f32[32,512]{1,0:T(8,128)S(1)} %fusion.8), channel_id=1, source_target_pairs={{0,4},{2,6},{4,0},{6,2},{8,12},{10,14},{12,8},{14,10},{16,20},{18,... | collective-permute-start | bytes 196616 | tf_op jit(solution)/shard_map/ppermute | solution.py:45
  16.2 4.3 %collective-permute-start.3 = (f32[32,512]{1,0:T(8,128)S(1)}, f32[32,512]{1,0:T(8,128)S(1)}, u32[]{:S(2)}, u32[]{:S(2)}) collective-permute-start(f32[32,512]{1,0:T(8,128)S(1)} %add.16), channel_id=1, source_target_pairs={{0,8},{2,10},{4,12},{6,14},{8,0},{10,2},{12,4},{14,6},{16,24},{18,... | collective-permute-start | bytes 196616 | tf_op jit(solution)/shard_map/ppermute | solution.py:45
  20.5 12.4 %copy-start.3 = (f32[32,384]{1,0:T(8,128)}, f32[32,384]{1,0:T(8,128)S(1)}, u32[]{:S(2)}) copy-start(f32[32,384]{1,0:T(8,128)S(1)} %slice.9.sums_ref) | copy-start | bytes 147460
  20.6 12.4 %collective-permute-start.5 = (f32[32,384]{1,0:T(8,128)S(1)}, f32[32,384]{1,0:T(8,128)S(1)}, u32[]{:S(2)}, u32[]{:S(2)}) collective-permute-start(f32[32,384]{1,0:T(8,128)S(1)} %slice.9.sums_ref), channel_id=1, source_target_pairs={{0,16},{2,18},{4,20},{6,22},{8,24},{10,26},{12,28},{14,30},{16,0},... | collective-permute-start | bytes 147464 | tf_op jit(solution)/shard_map/ppermute | solution.py:49
  23.5 4.6 %copy-start.4 = (f32[32,128]{1,0:T(8,128)}, f32[32,128]{1,0:T(8,128)S(1)}, u32[]{:S(2)}) copy-start(f32[32,128]{1,0:T(8,128)S(1)} %slice.8.mine_ref) | copy-start | bytes 49156
  23.5 4.6 %collective-permute-start.4 = (f32[32,128]{1,0:T(8,128)S(1)}, f32[32,128]{1,0:T(8,128)S(1)}, u32[]{:S(2)}, u32[]{:S(2)}) collective-permute-start(f32[32,128]{1,0:T(8,128)S(1)} %slice.8.mine_ref), channel_id=1, source_target_pairs={{0,16},{2,18},{4,20},{6,22},{8,24},{10,26},{12,28},{14,30},{16,0},... | collective-permute-start | bytes 49160 | tf_op jit(solution)/shard_map/ppermute | solution.py:49
  28.2 0.6 %copy-start.7 = (f32[32,128]{1,0:T(8,128)}, f32[32,128]{1,0:T(8,128)S(1)}, u32[]{:S(2)}) copy-start(f32[32,128]{1,0:T(8,128)S(1)} %collective-permute-done.4.other_ref) | copy-start | bytes 49156
  32.9 0.6 %copy-start.5 = (f32[32,384]{1,0:T(8,128)}, f32[32,384]{1,0:T(8,128)S(1)}, u32[]{:S(2)}) copy-start(f32[32,384]{1,0:T(8,128)S(1)} %collective-permute-done.5.last_ref) | copy-start | bytes 147460

commit v18 on v16

--- a/solution.py
+++ b/solution.py
@@ -180,17 +180,19 @@
     updated = update(*inputs, emit="updated")
     mine, other = all_sum_parts(partial_products, "items")
     projected = mine + other
-    gram_part = jnp.dot(projected, projected.T, precision=lax.Precision.HIGHEST)
-    slot_terms = jnp.einsum(
-        "jta,tkab->jtkb",
-        projected.reshape(block_size, rows_dev, width),
-        updated.astype(jnp.float32),
-        precision=lax.Precision.HIGHEST,
-    )
-    one_hot = (
-        tile_columns[:, :, None] == jnp.arange(item_count, dtype=jnp.int32)[None, None, :]
-    ).astype(jnp.float32)
-    item_terms = jnp.einsum("jtkb,tkc->jcb", slot_terms, one_hot, precision=lax.Precision.HIGHEST)
+    head_f32 = lax.reduce_precision(projected, exponent_bits=8, mantissa_bits=7)
+    head = head_f32.astype(jnp.bfloat16)
+    low = (projected - head_f32).astype(jnp.bfloat16)
+    f32 = jnp.float32
+    gram_part = jnp.dot(head, head.T, preferred_element_type=f32) + (
+        jnp.dot(head, low.T, preferred_element_type=f32) + jnp.dot(low, head.T, preferred_element_type=f32)
+    )
+    rows_of = lambda x: x.reshape(block_size, rows_dev, width)
+    slot_terms = jnp.einsum("jta,tkab->jtkb", rows_of(head), updated, preferred_element_type=f32) + jnp.einsum(
+        "jta,tkab->jtkb", rows_of(low), updated, preferred_element_type=f32
+    )
+    named = tile_columns[:, :, None] == jnp.arange(item_count, dtype=jnp.int32)[None, None, :]
+    item_terms = jnp.sum(jnp.where(named[None, :, :, :, None], slot_terms[:, :, :, None, :], 0.0), axis=(1, 2))
     item_terms = item_terms.reshape(block_size, item_count * width)
     lanes = -(-block_size // width) * width
     gram_lanes = jnp.pad(gram_part, ((0, 0), (0, lanes - block_size)))

time: 31.2 us -> 31.1 us (level)
    dot_general x3 -> x5, matrix products: 0.93 us -> 0.75 us  [the longest x1 0.19 us: local(): jnp.einsum('jta,tkab->jtkb', rows_of(head), updated, preferred_element_ty...]
    unnamed x10 -> x8, local copies, waits for them, and re-layouts: 0.79 us -> 0.62 us
where the time goes in v18:
time: 31.1 us; the launch traced here: 30.9 us
  starting transfers between devices  10.1 us (32%)
  Pallas kernels  9.41 us (30%)
  waiting for transfers between devices  8.37 us (27%)
  other arithmetic  0.88 us (3%)
  matrix products  0.75 us (2%)
  between operations  0.71 us (2%)
  local copies, waits for them, and re-layouts  0.65 us (2%)
    ppermute x4, waiting for transfers between devices, all_sum(): x = x + lax.ppermute(x, axis, [(i, i ^ step) for i in range(n)])  8.27 us
    ppermute x4, starting transfers between devices, all_sum(): x = x + lax.ppermute(x, axis, [(i, i ^ step) for i in range(n)])  7.14 us
    pallas_call x2, Pallas kernels, update(): pl.pallas_call(functools.partial(update_kernel, emit=emit), grid=(rows //...  4.9 us
    pallas_call x1, Pallas kernels, tail(): pl.pallas_call(functools.partial(tail_kernel, scale=1.0 / user_total, roo...  4.51 us
    ppermute x1, starting transfers between devices, all_sum_parts(): other = lax.ppermute(x, axis, [(i, i ^ step) for i in range(n)])  2.94 us
    add x4, other arithmetic, all_sum(): x = x + lax.ppermute(x, axis, [(i, i ^ step) for i in range(n)])  0.67 us
  transfers between devices with their start and end apart: 5, of which 5 were waited for; matrix products, arithmetic and copies ran while one was open for 0% of the time, Pallas kernels for 7%

profile of v18, /device:TPU:0, one launch (start us, length us, event | category | flops | bytes accessed | tf_op | source)
XLA Modules:
  0.0 30.9 jit_solution(2225828890365456891)
XLA Ops:
  0.6 0.0 copy-start.3
  0.6 2.6 %shard_map.104.mine_ref = f32[32,512]{1,0:T(8,128)} custom-call(s32[4,3]{1,0:T(4,128)} %cols_ref.3, s32[4,3]{1,0:T(4,128)} %live_ref.3, s32[4]{0:T(128)} %chosen_ref.3, bf16[4,3,128,128]{3,2,1,0:T(8,128)(2,1)} %rat_ref.3, bf16[4,3,128,128]{3,2,1,0:T(8,128)(2,1)} %res_ref.3, bf16[64,512]{1,0:T(8,128)(2,1)} %user_ref.3, bf16[64,384]{1,0:T(8,128)(2,1)} %bitcast.23, ...), custom_call_target="tpu_custom_call" | custom-call | flops 37748736 | bytes 1245184 | tf_op jit(solution)/shard_map/pallas_call | solution.py:147
  3.3 2.9 %collective-permute-start = (f32[32,512]{1,0:T(8,128)}, f32[32,512]{1,0:T(8,128)S(1)}, u32[]{:S(2)}, u32[]{:S(2)}) collective-permute-start(f32[32,512]{1,0:T(8,128)} %shard_map.104.mine_ref), channel_id=1, source_target_pairs={{0,1},{1,0},{2,3},{3,2},{4,5},{5,4},{6,7},{7,6},{8,9},{9,8},{10,11... | collective-permute-start | bytes 196616 | tf_op jit(solution)/shard_map/ppermute | solution.py:31
  6.2 0.0 copy-done.3
  6.2 0.1 iota_compare_fusion.1
  6.3 0.0 copy-start.1
  6.3 2.3 %shard_map.103 = bf16[4,3,128,128]{3,2,1,0:T(8,128)(2,1)} custom-call(s32[4,3]{1,0:T(4,128)} %cols_ref.3, s32[4,3]{1,0:T(4,128)} %live_ref.3, s32[4]{0:T(128)} %chosen_ref.3, bf16[4,3,128,128]{3,2,1,0:T(8,128)(2,1)} %rat_ref.3, bf16[4,3,128,128]{3,2,1,0:T(8,128)(2,1)} %res_ref.3, bf16[64,512]{1,0:T(8,128)(2,1)} %user_ref.3, bf16[64,384]{1,0:T(8,128)(2,1)} %bitcast.24, ...), custom_call_target="tpu_custom_call" | custom-call | flops 37748736 | bytes 1245184 | tf_op jit(solution)/shard_map/pallas_call | solution.py:147
  8.6 0.0 copy-start
  8.6 0.1 collective-permute-done.other_ref
  8.7 0.0 copy-done.1
  8.7 0.0 copy-start.2
  8.7 0.6 %copy-done.2 = f32[32,512]{1,0:T(8,128)} copy-done((f32[32,512]{1,0:T(8,128)}, f32[32,512]{1,0:T(8,128)S(1)}, u32[]{:S(2)}) %copy-start.2) | copy-done | bytes 65560
  9.3 0.1 fusion.6
  9.5 0.1 convolution_add_fusion.1
  9.6 0.1 convolution_add_fusion.2
  9.7 0.0 copy-done
  9.7 0.2 fusion.3
  9.9 0.2 fusion
  10.1 0.1 select_reduce_fusion
  10.2 0.1 collective-permute-start.1
  10.3 1.2 %collective-permute-done.1 = f32[32,512]{1,0:T(8,128)S(1)} collective-permute-done((f32[32,512]{1,0:T(8,128)S(1)}, f32[32,512]{1,0:T(8,128)S(1)}, u32[]{:S(2)}, u32[]{:S(2)}) %collective-permute-start.1) | collective-permute-done | bytes 65568 | tf_op jit(solution)/shard_map/ppermute | solution.py:17
  11.6 2.1 %collective-permute-start.2 = (f32[32,512]{1,0:T(8,128)S(1)}, f32[32,512]{1,0:T(8,128)S(1)}, u32[]{:S(2)}, u32[]{:S(2)}) collective-permute-start(f32[32,512]{1,0:T(8,128)S(1)} %fusion.5), channel_id=1, source_target_pairs={{0,4},{2,6},{4,0},{6,2},{8,12},{10,14},{12,8},{14,10},{16,20},{18,... | collective-permute-start | bytes 196616 | tf_op jit(solution)/shard_map/ppermute | solution.py:17
  13.7 2.4 %collective-permute-done.2 = f32[32,512]{1,0:T(8,128)S(1)} collective-permute-done((f32[32,512]{1,0:T(8,128)S(1)}, f32[32,512]{1,0:T(8,128)S(1)}, u32[]{:S(2)}, u32[]{:S(2)}) %collective-permute-start.2) | collective-permute-done | bytes 65568 | tf_op jit(solution)/shard_map/ppermute | solution.py:17
  16.1 2.0 %collective-permute-start.3 = (f32[32,512]{1,0:T(8,128)S(1)}, f32[32,512]{1,0:T(8,128)S(1)}, u32[]{:S(2)}, u32[]{:S(2)}) collective-permute-start(f32[32,512]{1,0:T(8,128)S(1)} %add.35), channel_id=1, source_target_pairs={{0,8},{2,10},{4,12},{6,14},{8,0},{10,2},{12,4},{14,6},{16,24},{18,... | collective-permute-start | bytes 196616 | tf_op jit(solution)/shard_map/ppermute | solution.py:17
  18.1 2.4 %collective-permute-done.3 = f32[32,512]{1,0:T(8,128)S(1)} collective-permute-done((f32[32,512]{1,0:T(8,128)S(1)}, f32[32,512]{1,0:T(8,128)S(1)}, u32[]{:S(2)}, u32[]{:S(2)}) %collective-permute-start.3) | collective-permute-done | bytes 65568 | tf_op jit(solution)/shard_map/ppermute | solution.py:17
  20.5 3.0 %collective-permute-start.4 = (f32[32,512]{1,0:T(8,128)S(1)}, f32[32,512]{1,0:T(8,128)S(1)}, u32[]{:S(2)}, u32[]{:S(2)}) collective-permute-start(f32[32,512]{1,0:T(8,128)S(1)} %add.36), channel_id=1, source_target_pairs={{0,16},{2,18},{4,20},{6,22},{8,24},{10,26},{12,28},{14,30},{16,0},... | collective-permute-start | bytes 196616 | tf_op jit(solution)/shard_map/ppermute | solution.py:17
  23.5 2.2 %collective-permute-done.4 = f32[32,512]{1,0:T(8,128)S(1)} collective-permute-done((f32[32,512]{1,0:T(8,128)S(1)}, f32[32,512]{1,0:T(8,128)S(1)}, u32[]{:S(2)}, u32[]{:S(2)}) %collective-permute-start.4) | collective-permute-done | bytes 65568 | tf_op jit(solution)/shard_map/ppermute | solution.py:17
  25.7 0.6 %add.37.reduced_ref = f32[32,512]{1,0:T(8,128)} add(f32[32,512]{1,0:T(8,128)S(1)} %add.36, f32[32,512]{1,0:T(8,128)S(1)} %collective-permute-done.4) | non-fusion elementwise | flops 16384 | bytes 196608 | tf_op jit(solution)/shard_map/add | solution.py:17
  26.3 4.5 %shard_map.105 = (f32[32,512]{1,0:T(8,128)}, f32[32,384]{1,0:T(8,128)}) custom-call(f32[32,512]{1,0:T(8,128)} %add.37.reduced_ref, f32[32,512]{1,0:T(8,128)} %shard_map.104.mine_ref, f32[32,512]{1,0:T(8,128)} %copy-done.2, bf16[32,384]{1,0:T(8,128)(2,1)} %bitcast.22), custom_call_target="tpu_custom_call" | custom-call | flops 7864320 | bytes 278528 | tf_op jit(solution)/shard_map/pallas_call | solution.py:77
  (8 shorter events, 0.1 us)
Async XLA Ops:
  0.6 5.6 %copy-start.3 = (s32[4,3]{1,0:T(4,128)S(1)}, s32[4,3]{1,0:T(4,128)}, u32[]{:S(2)}) copy-start(s32[4,3]{1,0:T(4,128)} %cols_ref.3) | copy-start | bytes 148
  3.3 5.4 %collective-permute-start = (f32[32,512]{1,0:T(8,128)}, f32[32,512]{1,0:T(8,128)S(1)}, u32[]{:S(2)}, u32[]{:S(2)}) collective-permute-start(f32[32,512]{1,0:T(8,128)} %shard_map.104.mine_ref), channel_id=1, source_target_pairs={{0,1},{1,0},{2,3},{3,2},{4,5},{5,4},{6,7},{7,6},{8,9},{9,8},{10,11... | collective-permute-start | bytes 196616 | tf_op jit(solution)/shard_map/ppermute | solution.py:31
  6.3 2.4 %copy-start.1 = (f32[32,512]{1,0:T(8,128)S(1)}, f32[32,512]{1,0:T(8,128)}, u32[]{:S(2)}) copy-start(f32[32,512]{1,0:T(8,128)} %shard_map.104.mine_ref) | copy-start | bytes 196612
  8.6 1.1 %copy-start = (bf16[4,3,128,128]{3,2,1,0:T(8,128)(2,1)S(1)}, bf16[4,3,128,128]{3,2,1,0:T(8,128)(2,1)}, u32[]{:S(2)}) copy-start(bf16[4,3,128,128]{3,2,1,0:T(8,128)(2,1)} %shard_map.103) | copy-start | bytes 1179652
  8.7 0.6 %copy-start.2 = (f32[32,512]{1,0:T(8,128)}, f32[32,512]{1,0:T(8,128)S(1)}, u32[]{:S(2)}) copy-start(f32[32,512]{1,0:T(8,128)S(1)} %collective-permute-done.other_ref) | copy-start | bytes 196612
  10.2 1.3 %collective-permute-start.1 = (f32[32,512]{1,0:T(8,128)S(1)}, f32[32,512]{1,0:T(8,128)S(1)}, u32[]{:S(2)}, u32[]{:S(2)}) collective-permute-start(f32[32,512]{1,0:T(8,128)S(1)} %select_maximum_fusion), channel_id=1, source_target_pairs={{0,2},{2,0},{4,6},{6,4},{8,10},{10,8},{12,14},{14,12},{16,18},{18,... | collective-permute-start | bytes 196616 | tf_op jit(solution)/shard_map/ppermute | solution.py:17
  11.6 4.5 %collective-permute-start.2 = (f32[32,512]{1,0:T(8,128)S(1)}, f32[32,512]{1,0:T(8,128)S(1)}, u32[]{:S(2)}, u32[]{:S(2)}) collective-permute-start(f32[32,512]{1,0:T(8,128)S(1)} %fusion.5), channel_id=1, source_target_pairs={{0,4},{2,6},{4,0},{6,2},{8,12},{10,14},{12,8},{14,10},{16,20},{18,... | collective-permute-start | bytes 196616 | tf_op jit(solution)/shard_map/ppermute | solution.py:17
  16.1 4.3 %collective-permute-start.3 = (f32[32,512]{1,0:T(8,128)S(1)}, f32[32,512]{1,0:T(8,128)S(1)}, u32[]{:S(2)}, u32[]{:S(2)}) collective-permute-start(f32[32,512]{1,0:T(8,128)S(1)} %add.35), channel_id=1, source_target_pairs={{0,8},{2,10},{4,12},{6,14},{8,0},{10,2},{12,4},{14,6},{16,24},{18,... | collective-permute-start | bytes 196616 | tf_op jit(solution)/shard_map/ppermute | solution.py:17
  20.5 5.2 %collective-permute-start.4 = (f32[32,512]{1,0:T(8,128)S(1)}, f32[32,512]{1,0:T(8,128)S(1)}, u32[]{:S(2)}, u32[]{:S(2)}) collective-permute-start(f32[32,512]{1,0:T(8,128)S(1)} %add.36), channel_id=1, source_target_pairs={{0,16},{2,18},{4,20},{6,22},{8,24},{10,26},{12,28},{14,30},{16,0},... | collective-permute-start | bytes 196616 | tf_op jit(solution)/shard_map/ppermute | solution.py:17

commit v19 on v18

--- a/solution.py
+++ b/solution.py
@@ -42,7 +42,6 @@
     n = start_ref.shape[0]
     lanes = reduced_ref.shape[1] - start_ref.shape[1]
     g = reduced_ref[:, :n] * scale
-    g = 0.5 * (g + g.T)
     rows = lax.broadcasted_iota(jnp.int32, (n, 2 * n), 0)
     cols = lax.broadcasted_iota(jnp.int32, (n, 2 * n), 1)
     aug = jnp.concatenate([g, (rows[:, :n] == cols[:, :n]).astype(jnp.float32)], axis=1)

time: 31.1 us -> 31 us (level)
  no operation moved by 1% of the time
where the time goes in v19:
time: 31 us; the launch traced here: 30.8 us
  starting transfers between devices  10.1 us (33%)
  Pallas kernels  9.39 us (30%)
  waiting for transfers between devices  8.37 us (27%)
  other arithmetic  0.88 us (3%)
  matrix products  0.75 us (2%)
  between operations  0.71 us (2%)
  local copies, waits for them, and re-layouts  0.65 us (2%)
    ppermute x4, waiting for transfers between devices, all_sum(): x = x + lax.ppermute(x, axis, [(i, i ^ step) for i in range(n)])  8.27 us
    ppermute x4, starting transfers between devices, all_sum(): x = x + lax.ppermute(x, axis, [(i, i ^ step) for i in range(n)])  7.14 us
    pallas_call x2, Pallas kernels, update(): pl.pallas_call(functools.partial(update_kernel, emit=emit), grid=(rows //...  4.9 us
    pallas_call x1, Pallas kernels, tail(): pl.pallas_call(functools.partial(tail_kernel, scale=1.0 / user_total, roo...  4.49 us
    ppermute x1, starting transfers between devices, all_sum_parts(): other = lax.ppermute(x, axis, [(i, i ^ step) for i in range(n)])  2.94 us
    add x4, other arithmetic, all_sum(): x = x + lax.ppermute(x, axis, [(i, i ^ step) for i in range(n)])  0.67 us
  transfers between devices with their start and end apart: 5, of which 5 were waited for; matrix products, arithmetic and copies ran while one was open for 0% of the time, Pallas kernels for 7%

profile of v19, /device:TPU:0, one launch (start us, length us, event | category | flops | bytes accessed | tf_op | source)
XLA Modules:
  0.0 30.8 jit_solution(2365940390247983871)
XLA Ops:
  0.6 0.0 copy-start.3
  0.6 2.6 %shard_map.104.mine_ref = f32[32,512]{1,0:T(8,128)} custom-call(s32[4,3]{1,0:T(4,128)} %cols_ref.3, s32[4,3]{1,0:T(4,128)} %live_ref.3, s32[4]{0:T(128)} %chosen_ref.3, bf16[4,3,128,128]{3,2,1,0:T(8,128)(2,1)} %rat_ref.3, bf16[4,3,128,128]{3,2,1,0:T(8,128)(2,1)} %res_ref.3, bf16[64,512]{1,0:T(8,128)(2,1)} %user_ref.3, bf16[64,384]{1,0:T(8,128)(2,1)} %bitcast.23, ...), custom_call_target="tpu_custom_call" | custom-call | flops 37748736 | bytes 1245184 | tf_op jit(solution)/shard_map/pallas_call | solution.py:146
  3.3 2.9 %collective-permute-start = (f32[32,512]{1,0:T(8,128)}, f32[32,512]{1,0:T(8,128)S(1)}, u32[]{:S(2)}, u32[]{:S(2)}) collective-permute-start(f32[32,512]{1,0:T(8,128)} %shard_map.104.mine_ref), channel_id=1, source_target_pairs={{0,1},{1,0},{2,3},{3,2},{4,5},{5,4},{6,7},{7,6},{8,9},{9,8},{10,11... | collective-permute-start | bytes 196616 | tf_op jit(solution)/shard_map/ppermute | solution.py:31
  6.2 0.0 copy-done.3
  6.2 0.1 iota_compare_fusion.1
  6.3 0.0 copy-start.1
  6.3 2.3 %shard_map.103 = bf16[4,3,128,128]{3,2,1,0:T(8,128)(2,1)} custom-call(s32[4,3]{1,0:T(4,128)} %cols_ref.3, s32[4,3]{1,0:T(4,128)} %live_ref.3, s32[4]{0:T(128)} %chosen_ref.3, bf16[4,3,128,128]{3,2,1,0:T(8,128)(2,1)} %rat_ref.3, bf16[4,3,128,128]{3,2,1,0:T(8,128)(2,1)} %res_ref.3, bf16[64,512]{1,0:T(8,128)(2,1)} %user_ref.3, bf16[64,384]{1,0:T(8,128)(2,1)} %bitcast.24, ...), custom_call_target="tpu_custom_call" | custom-call | flops 37748736 | bytes 1245184 | tf_op jit(solution)/shard_map/pallas_call | solution.py:146
  8.6 0.0 copy-start
  8.6 0.1 collective-permute-done.other_ref
  8.7 0.0 copy-done.1
  8.7 0.0 copy-start.2
  8.7 0.6 %copy-done.2 = f32[32,512]{1,0:T(8,128)} copy-done((f32[32,512]{1,0:T(8,128)}, f32[32,512]{1,0:T(8,128)S(1)}, u32[]{:S(2)}) %copy-start.2) | copy-done | bytes 65560
  9.3 0.1 fusion.6
  9.5 0.1 convolution_add_fusion.1
  9.6 0.1 convolution_add_fusion.2
  9.7 0.0 copy-done
  9.7 0.2 fusion.3
  9.9 0.2 fusion
  10.1 0.1 select_reduce_fusion
  10.2 0.1 collective-permute-start.1
  10.3 1.2 %collective-permute-done.1 = f32[32,512]{1,0:T(8,128)S(1)} collective-permute-done((f32[32,512]{1,0:T(8,128)S(1)}, f32[32,512]{1,0:T(8,128)S(1)}, u32[]{:S(2)}, u32[]{:S(2)}) %collective-permute-start.1) | collective-permute-done | bytes 65568 | tf_op jit(solution)/shard_map/ppermute | solution.py:17
  11.6 2.1 %collective-permute-start.2 = (f32[32,512]{1,0:T(8,128)S(1)}, f32[32,512]{1,0:T(8,128)S(1)}, u32[]{:S(2)}, u32[]{:S(2)}) collective-permute-start(f32[32,512]{1,0:T(8,128)S(1)} %fusion.5), channel_id=1, source_target_pairs={{0,4},{2,6},{4,0},{6,2},{8,12},{10,14},{12,8},{14,10},{16,20},{18,... | collective-permute-start | bytes 196616 | tf_op jit(solution)/shard_map/ppermute | solution.py:17
  13.7 2.4 %collective-permute-done.2 = f32[32,512]{1,0:T(8,128)S(1)} collective-permute-done((f32[32,512]{1,0:T(8,128)S(1)}, f32[32,512]{1,0:T(8,128)S(1)}, u32[]{:S(2)}, u32[]{:S(2)}) %collective-permute-start.2) | collective-permute-done | bytes 65568 | tf_op jit(solution)/shard_map/ppermute | solution.py:17
  16.1 2.0 %collective-permute-start.3 = (f32[32,512]{1,0:T(8,128)S(1)}, f32[32,512]{1,0:T(8,128)S(1)}, u32[]{:S(2)}, u32[]{:S(2)}) collective-permute-start(f32[32,512]{1,0:T(8,128)S(1)} %add.35), channel_id=1, source_target_pairs={{0,8},{2,10},{4,12},{6,14},{8,0},{10,2},{12,4},{14,6},{16,24},{18,... | collective-permute-start | bytes 196616 | tf_op jit(solution)/shard_map/ppermute | solution.py:17
  18.1 2.4 %collective-permute-done.3 = f32[32,512]{1,0:T(8,128)S(1)} collective-permute-done((f32[32,512]{1,0:T(8,128)S(1)}, f32[32,512]{1,0:T(8,128)S(1)}, u32[]{:S(2)}, u32[]{:S(2)}) %collective-permute-start.3) | collective-permute-done | bytes 65568 | tf_op jit(solution)/shard_map/ppermute | solution.py:17
  20.5 3.0 %collective-permute-start.4 = (f32[32,512]{1,0:T(8,128)S(1)}, f32[32,512]{1,0:T(8,128)S(1)}, u32[]{:S(2)}, u32[]{:S(2)}) collective-permute-start(f32[32,512]{1,0:T(8,128)S(1)} %add.36), channel_id=1, source_target_pairs={{0,16},{2,18},{4,20},{6,22},{8,24},{10,26},{12,28},{14,30},{16,0},... | collective-permute-start | bytes 196616 | tf_op jit(solution)/shard_map/ppermute | solution.py:17
  23.5 2.2 %collective-permute-done.4 = f32[32,512]{1,0:T(8,128)S(1)} collective-permute-done((f32[32,512]{1,0:T(8,128)S(1)}, f32[32,512]{1,0:T(8,128)S(1)}, u32[]{:S(2)}, u32[]{:S(2)}) %collective-permute-start.4) | collective-permute-done | bytes 65568 | tf_op jit(solution)/shard_map/ppermute | solution.py:17
  25.7 0.6 %add.37.reduced_ref = f32[32,512]{1,0:T(8,128)} add(f32[32,512]{1,0:T(8,128)S(1)} %add.36, f32[32,512]{1,0:T(8,128)S(1)} %collective-permute-done.4) | non-fusion elementwise | flops 16384 | bytes 196608 | tf_op jit(solution)/shard_map/add | solution.py:17
  26.3 4.5 %shard_map.105 = (f32[32,512]{1,0:T(8,128)}, f32[32,384]{1,0:T(8,128)}) custom-call(f32[32,512]{1,0:T(8,128)} %add.37.reduced_ref, f32[32,512]{1,0:T(8,128)} %shard_map.104.mine_ref, f32[32,512]{1,0:T(8,128)} %copy-done.2, bf16[32,384]{1,0:T(8,128)(2,1)} %bitcast.22), custom_call_target="tpu_custom_call" | custom-call | flops 7864320 | bytes 278528 | tf_op jit(solution)/shard_map/pallas_call | solution.py:76
  (8 shorter events, 0.1 us)
Async XLA Ops:
  0.6 5.6 %copy-start.3 = (s32[4,3]{1,0:T(4,128)S(1)}, s32[4,3]{1,0:T(4,128)}, u32[]{:S(2)}) copy-start(s32[4,3]{1,0:T(4,128)} %cols_ref.3) | copy-start | bytes 148
  3.3 5.4 %collective-permute-start = (f32[32,512]{1,0:T(8,128)}, f32[32,512]{1,0:T(8,128)S(1)}, u32[]{:S(2)}, u32[]{:S(2)}) collective-permute-start(f32[32,512]{1,0:T(8,128)} %shard_map.104.mine_ref), channel_id=1, source_target_pairs={{0,1},{1,0},{2,3},{3,2},{4,5},{5,4},{6,7},{7,6},{8,9},{9,8},{10,11... | collective-permute-start | bytes 196616 | tf_op jit(solution)/shard_map/ppermute | solution.py:31
  6.3 2.4 %copy-start.1 = (f32[32,512]{1,0:T(8,128)S(1)}, f32[32,512]{1,0:T(8,128)}, u32[]{:S(2)}) copy-start(f32[32,512]{1,0:T(8,128)} %shard_map.104.mine_ref) | copy-start | bytes 196612
  8.6 1.1 %copy-start = (bf16[4,3,128,128]{3,2,1,0:T(8,128)(2,1)S(1)}, bf16[4,3,128,128]{3,2,1,0:T(8,128)(2,1)}, u32[]{:S(2)}) copy-start(bf16[4,3,128,128]{3,2,1,0:T(8,128)(2,1)} %shard_map.103) | copy-start | bytes 1179652
  8.7 0.6 %copy-start.2 = (f32[32,512]{1,0:T(8,128)}, f32[32,512]{1,0:T(8,128)S(1)}, u32[]{:S(2)}) copy-start(f32[32,512]{1,0:T(8,128)S(1)} %collective-permute-done.other_ref) | copy-start | bytes 196612
  10.2 1.3 %collective-permute-start.1 = (f32[32,512]{1,0:T(8,128)S(1)}, f32[32,512]{1,0:T(8,128)S(1)}, u32[]{:S(2)}, u32[]{:S(2)}) collective-permute-start(f32[32,512]{1,0:T(8,128)S(1)} %select_maximum_fusion), channel_id=1, source_target_pairs={{0,2},{2,0},{4,6},{6,4},{8,10},{10,8},{12,14},{14,12},{16,18},{18,... | collective-permute-start | bytes 196616 | tf_op jit(solution)/shard_map/ppermute | solution.py:17
  11.6 4.5 %collective-permute-start.2 = (f32[32,512]{1,0:T(8,128)S(1)}, f32[32,512]{1,0:T(8,128)S(1)}, u32[]{:S(2)}, u32[]{:S(2)}) collective-permute-start(f32[32,512]{1,0:T(8,128)S(1)} %fusion.5), channel_id=1, source_target_pairs={{0,4},{2,6},{4,0},{6,2},{8,12},{10,14},{12,8},{14,10},{16,20},{18,... | collective-permute-start | bytes 196616 | tf_op jit(solution)/shard_map/ppermute | solution.py:17
  16.1 4.3 %collective-permute-start.3 = (f32[32,512]{1,0:T(8,128)S(1)}, f32[32,512]{1,0:T(8,128)S(1)}, u32[]{:S(2)}, u32[]{:S(2)}) collective-permute-start(f32[32,512]{1,0:T(8,128)S(1)} %add.35), channel_id=1, source_target_pairs={{0,8},{2,10},{4,12},{6,14},{8,0},{10,2},{12,4},{14,6},{16,24},{18,... | collective-permute-start | bytes 196616 | tf_op jit(solution)/shard_map/ppermute | solution.py:17
  20.5 5.2 %collective-permute-start.4 = (f32[32,512]{1,0:T(8,128)S(1)}, f32[32,512]{1,0:T(8,128)S(1)}, u32[]{:S(2)}, u32[]{:S(2)}) collective-permute-start(f32[32,512]{1,0:T(8,128)S(1)} %add.36), channel_id=1, source_target_pairs={{0,16},{2,18},{4,20},{6,22},{8,24},{10,26},{12,28},{14,30},{16,0},... | collective-permute-start | bytes 196616 | tf_op jit(solution)/shard_map/ppermute | solution.py:17

commit v20 on v18

--- a/solution.py
+++ b/solution.py
@@ -12,10 +12,10 @@
     n = lax.axis_size(axis)
     if n & (n - 1):
         return lax.psum(x, axis)
-    step = 1
-    while step < n:
+    step = n // 2
+    while step >= 1:
         x = x + lax.ppermute(x, axis, [(i, i ^ step) for i in range(n)])
-        step *= 2
+        step //= 2
     return x
 
 

time: 31.1 us -> 31.1 us (level)
  no operation moved by 1% of the time
where the time goes in v20:
time: 31.1 us; the launch traced here: 30.9 us
  starting transfers between devices  10.1 us (32%)
  Pallas kernels  9.41 us (30%)
  waiting for transfers between devices  8.36 us (27%)
  other arithmetic  0.88 us (3%)
  matrix products  0.75 us (2%)
  between operations  0.71 us (2%)
  local copies, waits for them, and re-layouts  0.65 us (2%)
    ppermute x4, waiting for transfers between devices, all_sum(): x = x + lax.ppermute(x, axis, [(i, i ^ step) for i in range(n)])  8.26 us
    ppermute x4, starting transfers between devices, all_sum(): x = x + lax.ppermute(x, axis, [(i, i ^ step) for i in range(n)])  7.15 us
    pallas_call x2, Pallas kernels, update(): pl.pallas_call(functools.partial(update_kernel, emit=emit), grid=(rows //...  4.9 us
    pallas_call x1, Pallas kernels, tail(): pl.pallas_call(functools.partial(tail_kernel, scale=1.0 / user_total, roo...  4.51 us
    ppermute x1, starting transfers between devices, all_sum_parts(): other = lax.ppermute(x, axis, [(i, i ^ step) for i in range(n)])  2.94 us
    add x4, other arithmetic, all_sum(): x = x + lax.ppermute(x, axis, [(i, i ^ step) for i in range(n)])  0.67 us
  transfers between devices with their start and end apart: 5, of which 5 were waited for; matrix products, arithmetic and copies ran while one was open for 0% of the time, Pallas kernels for 7%

profile of v20, /device:TPU:0, one launch (start us, length us, event | category | flops | bytes accessed | tf_op | source)
XLA Modules:
  0.0 30.9 jit_solution(8812135808820218978)
XLA Ops:
  0.6 0.0 copy-start.3
  0.6 2.6 %shard_map.104.mine_ref = f32[32,512]{1,0:T(8,128)} custom-call(s32[4,3]{1,0:T(4,128)} %cols_ref.3, s32[4,3]{1,0:T(4,128)} %live_ref.3, s32[4]{0:T(128)} %chosen_ref.3, bf16[4,3,128,128]{3,2,1,0:T(8,128)(2,1)} %rat_ref.3, bf16[4,3,128,128]{3,2,1,0:T(8,128)(2,1)} %res_ref.3, bf16[64,512]{1,0:T(8,128)(2,1)} %user_ref.3, bf16[64,384]{1,0:T(8,128)(2,1)} %bitcast.23, ...), custom_call_target="tpu_custom_call" | custom-call | flops 37748736 | bytes 1245184 | tf_op jit(solution)/shard_map/pallas_call | solution.py:147
  3.3 2.9 %collective-permute-start = (f32[32,512]{1,0:T(8,128)}, f32[32,512]{1,0:T(8,128)S(1)}, u32[]{:S(2)}, u32[]{:S(2)}) collective-permute-start(f32[32,512]{1,0:T(8,128)} %shard_map.104.mine_ref), channel_id=1, source_target_pairs={{0,1},{1,0},{2,3},{3,2},{4,5},{5,4},{6,7},{7,6},{8,9},{9,8},{10,11... | collective-permute-start | bytes 196616 | tf_op jit(solution)/shard_map/ppermute | solution.py:31
  6.2 0.0 copy-done.3
  6.2 0.1 iota_compare_fusion.1
  6.3 0.0 copy-start.1
  6.3 2.3 %shard_map.103 = bf16[4,3,128,128]{3,2,1,0:T(8,128)(2,1)} custom-call(s32[4,3]{1,0:T(4,128)} %cols_ref.3, s32[4,3]{1,0:T(4,128)} %live_ref.3, s32[4]{0:T(128)} %chosen_ref.3, bf16[4,3,128,128]{3,2,1,0:T(8,128)(2,1)} %rat_ref.3, bf16[4,3,128,128]{3,2,1,0:T(8,128)(2,1)} %res_ref.3, bf16[64,512]{1,0:T(8,128)(2,1)} %user_ref.3, bf16[64,384]{1,0:T(8,128)(2,1)} %bitcast.24, ...), custom_call_target="tpu_custom_call" | custom-call | flops 37748736 | bytes 1245184 | tf_op jit(solution)/shard_map/pallas_call | solution.py:147
  8.6 0.0 copy-start
  8.6 0.1 collective-permute-done.other_ref
  8.7 0.0 copy-done.1
  8.7 0.0 copy-start.2
  8.7 0.6 %copy-done.2 = f32[32,512]{1,0:T(8,128)} copy-done((f32[32,512]{1,0:T(8,128)}, f32[32,512]{1,0:T(8,128)S(1)}, u32[]{:S(2)}) %copy-start.2) | copy-done | bytes 65560
  9.3 0.1 fusion.6
  9.5 0.1 convolution_add_fusion.1
  9.6 0.1 convolution_add_fusion.2
  9.7 0.0 copy-done
  9.7 0.2 fusion.3
  9.9 0.2 fusion
  10.1 0.1 select_reduce_fusion
  10.2 3.2 %collective-permute-start.1 = (f32[32,512]{1,0:T(8,128)S(1)}, f32[32,512]{1,0:T(8,128)S(1)}, u32[]{:S(2)}, u32[]{:S(2)}) collective-permute-start(f32[32,512]{1,0:T(8,128)S(1)} %select_maximum_fusion), channel_id=1, source_target_pairs={{0,16},{2,18},{4,20},{6,22},{8,24},{10,26},{12,28},{14,30},{16,0},... | collective-permute-start | bytes 196616 | tf_op jit(solution)/shard_map/ppermute | solution.py:17
  13.4 2.2 %collective-permute-done.1 = f32[32,512]{1,0:T(8,128)S(1)} collective-permute-done((f32[32,512]{1,0:T(8,128)S(1)}, f32[32,512]{1,0:T(8,128)S(1)}, u32[]{:S(2)}, u32[]{:S(2)}) %collective-permute-start.1) | collective-permute-done | bytes 65568 | tf_op jit(solution)/shard_map/ppermute | solution.py:17
  15.7 2.0 %collective-permute-start.2 = (f32[32,512]{1,0:T(8,128)S(1)}, f32[32,512]{1,0:T(8,128)S(1)}, u32[]{:S(2)}, u32[]{:S(2)}) collective-permute-start(f32[32,512]{1,0:T(8,128)S(1)} %fusion.5), channel_id=1, source_target_pairs={{0,8},{2,10},{4,12},{6,14},{8,0},{10,2},{12,4},{14,6},{16,24},{18,... | collective-permute-start | bytes 196616 | tf_op jit(solution)/shard_map/ppermute | solution.py:17
  17.7 2.4 %collective-permute-done.2 = f32[32,512]{1,0:T(8,128)S(1)} collective-permute-done((f32[32,512]{1,0:T(8,128)S(1)}, f32[32,512]{1,0:T(8,128)S(1)}, u32[]{:S(2)}, u32[]{:S(2)}) %collective-permute-start.2) | collective-permute-done | bytes 65568 | tf_op jit(solution)/shard_map/ppermute | solution.py:17
  20.0 1.9 %collective-permute-start.3 = (f32[32,512]{1,0:T(8,128)S(1)}, f32[32,512]{1,0:T(8,128)S(1)}, u32[]{:S(2)}, u32[]{:S(2)}) collective-permute-start(f32[32,512]{1,0:T(8,128)S(1)} %add.35), channel_id=1, source_target_pairs={{0,4},{2,6},{4,0},{6,2},{8,12},{10,14},{12,8},{14,10},{16,20},{18,... | collective-permute-start | bytes 196616 | tf_op jit(solution)/shard_map/ppermute | solution.py:17
  22.0 2.4 %collective-permute-done.3 = f32[32,512]{1,0:T(8,128)S(1)} collective-permute-done((f32[32,512]{1,0:T(8,128)S(1)}, f32[32,512]{1,0:T(8,128)S(1)}, u32[]{:S(2)}, u32[]{:S(2)}) %collective-permute-start.3) | collective-permute-done | bytes 65568 | tf_op jit(solution)/shard_map/ppermute | solution.py:17
  24.4 0.1 collective-permute-start.4
  24.5 1.2 %collective-permute-done.4 = f32[32,512]{1,0:T(8,128)S(1)} collective-permute-done((f32[32,512]{1,0:T(8,128)S(1)}, f32[32,512]{1,0:T(8,128)S(1)}, u32[]{:S(2)}, u32[]{:S(2)}) %collective-permute-start.4) | collective-permute-done | bytes 65568 | tf_op jit(solution)/shard_map/ppermute | solution.py:17
  25.7 0.6 %add.37.reduced_ref = f32[32,512]{1,0:T(8,128)} add(f32[32,512]{1,0:T(8,128)S(1)} %add.36, f32[32,512]{1,0:T(8,128)S(1)} %collective-permute-done.4) | non-fusion elementwise | flops 16384 | bytes 196608 | tf_op jit(solution)/shard_map/add | solution.py:17
  26.3 4.5 %shard_map.105 = (f32[32,512]{1,0:T(8,128)}, f32[32,384]{1,0:T(8,128)}) custom-call(f32[32,512]{1,0:T(8,128)} %add.37.reduced_ref, f32[32,512]{1,0:T(8,128)} %shard_map.104.mine_ref, f32[32,512]{1,0:T(8,128)} %copy-done.2, bf16[32,384]{1,0:T(8,128)(2,1)} %bitcast.22), custom_call_target="tpu_custom_call" | custom-call | flops 7864320 | bytes 278528 | tf_op jit(solution)/shard_map/pallas_call | solution.py:77
  (8 shorter events, 0.1 us)
Async XLA Ops:
  0.6 5.6 %copy-start.3 = (s32[4,3]{1,0:T(4,128)S(1)}, s32[4,3]{1,0:T(4,128)}, u32[]{:S(2)}) copy-start(s32[4,3]{1,0:T(4,128)} %cols_ref.3) | copy-start | bytes 148
  3.3 5.4 %collective-permute-start = (f32[32,512]{1,0:T(8,128)}, f32[32,512]{1,0:T(8,128)S(1)}, u32[]{:S(2)}, u32[]{:S(2)}) collective-permute-start(f32[32,512]{1,0:T(8,128)} %shard_map.104.mine_ref), channel_id=1, source_target_pairs={{0,1},{1,0},{2,3},{3,2},{4,5},{5,4},{6,7},{7,6},{8,9},{9,8},{10,11... | collective-permute-start | bytes 196616 | tf_op jit(solution)/shard_map/ppermute | solution.py:31
  6.3 2.4 %copy-start.1 = (f32[32,512]{1,0:T(8,128)S(1)}, f32[32,512]{1,0:T(8,128)}, u32[]{:S(2)}) copy-start(f32[32,512]{1,0:T(8,128)} %shard_map.104.mine_ref) | copy-start | bytes 196612
  8.6 1.1 %copy-start = (bf16[4,3,128,128]{3,2,1,0:T(8,128)(2,1)S(1)}, bf16[4,3,128,128]{3,2,1,0:T(8,128)(2,1)}, u32[]{:S(2)}) copy-start(bf16[4,3,128,128]{3,2,1,0:T(8,128)(2,1)} %shard_map.103) | copy-start | bytes 1179652
  8.7 0.6 %copy-start.2 = (f32[32,512]{1,0:T(8,128)}, f32[32,512]{1,0:T(8,128)S(1)}, u32[]{:S(2)}) copy-start(f32[32,512]{1,0:T(8,128)S(1)} %collective-permute-done.other_ref) | copy-start | bytes 196612
  10.2 5.4 %collective-permute-start.1 = (f32[32,512]{1,0:T(8,128)S(1)}, f32[32,512]{1,0:T(8,128)S(1)}, u32[]{:S(2)}, u32[]{:S(2)}) collective-permute-start(f32[32,512]{1,0:T(8,128)S(1)} %select_maximum_fusion), channel_id=1, source_target_pairs={{0,16},{2,18},{4,20},{6,22},{8,24},{10,26},{12,28},{14,30},{16,0},... | collective-permute-start | bytes 196616 | tf_op jit(solution)/shard_map/ppermute | solution.py:17
  15.7 4.3 %collective-permute-start.2 = (f32[32,512]{1,0:T(8,128)S(1)}, f32[32,512]{1,0:T(8,128)S(1)}, u32[]{:S(2)}, u32[]{:S(2)}) collective-permute-start(f32[32,512]{1,0:T(8,128)S(1)} %fusion.5), channel_id=1, source_target_pairs={{0,8},{2,10},{4,12},{6,14},{8,0},{10,2},{12,4},{14,6},{16,24},{18,... | collective-permute-start | bytes 196616 | tf_op jit(solution)/shard_map/ppermute | solution.py:17
  20.0 4.3 %collective-permute-start.3 = (f32[32,512]{1,0:T(8,128)S(1)}, f32[32,512]{1,0:T(8,128)S(1)}, u32[]{:S(2)}, u32[]{:S(2)}) collective-permute-start(f32[32,512]{1,0:T(8,128)S(1)} %add.35), channel_id=1, source_target_pairs={{0,4},{2,6},{4,0},{6,2},{8,12},{10,14},{12,8},{14,10},{16,20},{18,... | collective-permute-start | bytes 196616 | tf_op jit(solution)/shard_map/ppermute | solution.py:17
  24.4 1.3 %collective-permute-start.4 = (f32[32,512]{1,0:T(8,128)S(1)}, f32[32,512]{1,0:T(8,128)S(1)}, u32[]{:S(2)}, u32[]{:S(2)}) collective-permute-start(f32[32,512]{1,0:T(8,128)S(1)} %add.36), channel_id=1, source_target_pairs={{0,2},{2,0},{4,6},{6,4},{8,10},{10,8},{12,14},{14,12},{16,18},{18,... | collective-permute-start | bytes 196616 | tf_op jit(solution)/shard_map/ppermute | solution.py:17

commit v21 on v18

--- a/solution.py
+++ b/solution.py
@@ -135,7 +135,7 @@
     rows, slots, width, _ = ratings.shape
     rank = user_factors.shape[0]
     block = start.shape[0]
-    group = rows
+    group = rows // 2 if emit == "products" and rows % 2 == 0 else rows
     smem = pl.BlockSpec(memory_space=pltpu.SMEM)
     tile = pl.BlockSpec((group, slots, width, width), lambda t: (t, 0, 0, 0))
     if emit == "updated":

time: 31.1 us -> 31.2 us (level)
  no operation moved by 1% of the time
where the time goes in v21:
time: 31.2 us; the launch traced here: 31 us
  starting transfers between devices  10.1 us (32%)
  Pallas kernels  9.54 us (31%)
  waiting for transfers between devices  8.36 us (27%)
  other arithmetic  0.88 us (3%)
  matrix products  0.75 us (2%)
  between operations  0.71 us (2%)
  local copies, waits for them, and re-layouts  0.65 us (2%)
    ppermute x4, waiting for transfers between devices, all_sum(): x = x + lax.ppermute(x, axis, [(i, i ^ step) for i in range(n)])  8.26 us
    ppermute x4, starting transfers between devices, all_sum(): x = x + lax.ppermute(x, axis, [(i, i ^ step) for i in range(n)])  7.15 us
    pallas_call x2, Pallas kernels, update(): pl.pallas_call(functools.partial(update_kernel, emit=emit), grid=(rows //...  5.04 us
    pallas_call x1, Pallas kernels, tail(): pl.pallas_call(functools.partial(tail_kernel, scale=1.0 / user_total, roo...  4.51 us
    ppermute x1, starting transfers between devices, all_sum_parts(): other = lax.ppermute(x, axis, [(i, i ^ step) for i in range(n)])  2.94 us
    add x4, other arithmetic, all_sum(): x = x + lax.ppermute(x, axis, [(i, i ^ step) for i in range(n)])  0.67 us
  transfers between devices with their start and end apart: 5, of which 5 were waited for; matrix products, arithmetic and copies ran while one was open for 0% of the time, Pallas kernels for 7%

profile of v21, /device:TPU:0, one launch (start us, length us, event | category | flops | bytes accessed | tf_op | source)
XLA Modules:
  0.0 31.0 jit_solution(4935433627903102351)
XLA Ops:
  0.6 0.0 copy-start.3
  0.6 2.8 %shard_map.104.mine_ref = f32[32,512]{1,0:T(8,128)} custom-call(s32[4,3]{1,0:T(4,128)} %cols_ref.3, s32[4,3]{1,0:T(4,128)} %live_ref.3, s32[4]{0:T(128)} %chosen_ref.3, bf16[4,3,128,128]{3,2,1,0:T(8,128)(2,1)} %rat_ref.3, bf16[4,3,128,128]{3,2,1,0:T(8,128)(2,1)} %res_ref.3, bf16[64,512]{1,0:T(8,128)(2,1)} %user_ref.3, bf16[64,384]{1,0:T(8,128)(2,1)} %bitcast.23, ...), custom_call_target="tpu_custom_call" | custom-call | flops 37748736 | bytes 1245184 | tf_op jit(solution)/shard_map/pallas_call | solution.py:147
  3.4 2.9 %collective-permute-start = (f32[32,512]{1,0:T(8,128)}, f32[32,512]{1,0:T(8,128)S(1)}, u32[]{:S(2)}, u32[]{:S(2)}) collective-permute-start(f32[32,512]{1,0:T(8,128)} %shard_map.104.mine_ref), channel_id=1, source_target_pairs={{0,1},{1,0},{2,3},{3,2},{4,5},{5,4},{6,7},{7,6},{8,9},{9,8},{10,11... | collective-permute-start | bytes 196616 | tf_op jit(solution)/shard_map/ppermute | solution.py:31
  6.3 0.0 copy-done.3
  6.4 0.1 iota_compare_fusion.1
  6.4 0.0 copy-start.1
  6.4 2.3 %shard_map.103 = bf16[4,3,128,128]{3,2,1,0:T(8,128)(2,1)} custom-call(s32[4,3]{1,0:T(4,128)} %cols_ref.3, s32[4,3]{1,0:T(4,128)} %live_ref.3, s32[4]{0:T(128)} %chosen_ref.3, bf16[4,3,128,128]{3,2,1,0:T(8,128)(2,1)} %rat_ref.3, bf16[4,3,128,128]{3,2,1,0:T(8,128)(2,1)} %res_ref.3, bf16[64,512]{1,0:T(8,128)(2,1)} %user_ref.3, bf16[64,384]{1,0:T(8,128)(2,1)} %bitcast.24, ...), custom_call_target="tpu_custom_call" | custom-call | flops 37748736 | bytes 1245184 | tf_op jit(solution)/shard_map/pallas_call | solution.py:147
  8.7 0.0 copy-start
  8.7 0.1 collective-permute-done.other_ref
  8.8 0.0 copy-done.1
  8.8 0.0 copy-start.2
  8.8 0.6 %copy-done.2 = f32[32,512]{1,0:T(8,128)} copy-done((f32[32,512]{1,0:T(8,128)}, f32[32,512]{1,0:T(8,128)S(1)}, u32[]{:S(2)}) %copy-start.2) | copy-done | bytes 65560
  9.4 0.1 fusion.6
  9.6 0.1 convolution_add_fusion.1
  9.7 0.1 convolution_add_fusion.2
  9.8 0.0 copy-done
  9.8 0.2 fusion.3
  10.0 0.2 fusion
  10.2 0.1 select_reduce_fusion
  10.4 0.1 collective-permute-start.1
  10.5 1.2 %collective-permute-done.1 = f32[32,512]{1,0:T(8,128)S(1)} collective-permute-done((f32[32,512]{1,0:T(8,128)S(1)}, f32[32,512]{1,0:T(8,128)S(1)}, u32[]{:S(2)}, u32[]{:S(2)}) %collective-permute-start.1) | collective-permute-done | bytes 65568 | tf_op jit(solution)/shard_map/ppermute | solution.py:17
  11.7 2.1 %collective-permute-start.2 = (f32[32,512]{1,0:T(8,128)S(1)}, f32[32,512]{1,0:T(8,128)S(1)}, u32[]{:S(2)}, u32[]{:S(2)}) collective-permute-start(f32[32,512]{1,0:T(8,128)S(1)} %fusion.5), channel_id=1, source_target_pairs={{0,4},{2,6},{4,0},{6,2},{8,12},{10,14},{12,8},{14,10},{16,20},{18,... | collective-permute-start | bytes 196616 | tf_op jit(solution)/shard_map/ppermute | solution.py:17
  13.8 2.4 %collective-permute-done.2 = f32[32,512]{1,0:T(8,128)S(1)} collective-permute-done((f32[32,512]{1,0:T(8,128)S(1)}, f32[32,512]{1,0:T(8,128)S(1)}, u32[]{:S(2)}, u32[]{:S(2)}) %collective-permute-start.2) | collective-permute-done | bytes 65568 | tf_op jit(solution)/shard_map/ppermute | solution.py:17
  16.3 2.0 %collective-permute-start.3 = (f32[32,512]{1,0:T(8,128)S(1)}, f32[32,512]{1,0:T(8,128)S(1)}, u32[]{:S(2)}, u32[]{:S(2)}) collective-permute-start(f32[32,512]{1,0:T(8,128)S(1)} %add.35), channel_id=1, source_target_pairs={{0,8},{2,10},{4,12},{6,14},{8,0},{10,2},{12,4},{14,6},{16,24},{18,... | collective-permute-start | bytes 196616 | tf_op jit(solution)/shard_map/ppermute | solution.py:17
  18.2 2.4 %collective-permute-done.3 = f32[32,512]{1,0:T(8,128)S(1)} collective-permute-done((f32[32,512]{1,0:T(8,128)S(1)}, f32[32,512]{1,0:T(8,128)S(1)}, u32[]{:S(2)}, u32[]{:S(2)}) %collective-permute-start.3) | collective-permute-done | bytes 65568 | tf_op jit(solution)/shard_map/ppermute | solution.py:17
  20.6 3.0 %collective-permute-start.4 = (f32[32,512]{1,0:T(8,128)S(1)}, f32[32,512]{1,0:T(8,128)S(1)}, u32[]{:S(2)}, u32[]{:S(2)}) collective-permute-start(f32[32,512]{1,0:T(8,128)S(1)} %add.36), channel_id=1, source_target_pairs={{0,16},{2,18},{4,20},{6,22},{8,24},{10,26},{12,28},{14,30},{16,0},... | collective-permute-start | bytes 196616 | tf_op jit(solution)/shard_map/ppermute | solution.py:17
  23.6 2.2 %collective-permute-done.4 = f32[32,512]{1,0:T(8,128)S(1)} collective-permute-done((f32[32,512]{1,0:T(8,128)S(1)}, f32[32,512]{1,0:T(8,128)S(1)}, u32[]{:S(2)}, u32[]{:S(2)}) %collective-permute-start.4) | collective-permute-done | bytes 65568 | tf_op jit(solution)/shard_map/ppermute | solution.py:17
  25.8 0.6 %add.37.reduced_ref = f32[32,512]{1,0:T(8,128)} add(f32[32,512]{1,0:T(8,128)S(1)} %add.36, f32[32,512]{1,0:T(8,128)S(1)} %collective-permute-done.4) | non-fusion elementwise | flops 16384 | bytes 196608 | tf_op jit(solution)/shard_map/add | solution.py:17
  26.5 4.5 %shard_map.105 = (f32[32,512]{1,0:T(8,128)}, f32[32,384]{1,0:T(8,128)}) custom-call(f32[32,512]{1,0:T(8,128)} %add.37.reduced_ref, f32[32,512]{1,0:T(8,128)} %shard_map.104.mine_ref, f32[32,512]{1,0:T(8,128)} %copy-done.2, bf16[32,384]{1,0:T(8,128)(2,1)} %bitcast.22), custom_call_target="tpu_custom_call" | custom-call | flops 7864320 | bytes 278528 | tf_op jit(solution)/shard_map/pallas_call | solution.py:77
  (8 shorter events, 0.1 us)
Async XLA Ops:
  0.6 5.7 %copy-start.3 = (s32[4,3]{1,0:T(4,128)S(1)}, s32[4,3]{1,0:T(4,128)}, u32[]{:S(2)}) copy-start(s32[4,3]{1,0:T(4,128)} %cols_ref.3) | copy-start | bytes 148
  3.4 5.4 %collective-permute-start = (f32[32,512]{1,0:T(8,128)}, f32[32,512]{1,0:T(8,128)S(1)}, u32[]{:S(2)}, u32[]{:S(2)}) collective-permute-start(f32[32,512]{1,0:T(8,128)} %shard_map.104.mine_ref), channel_id=1, source_target_pairs={{0,1},{1,0},{2,3},{3,2},{4,5},{5,4},{6,7},{7,6},{8,9},{9,8},{10,11... | collective-permute-start | bytes 196616 | tf_op jit(solution)/shard_map/ppermute | solution.py:31
  6.4 2.4 %copy-start.1 = (f32[32,512]{1,0:T(8,128)S(1)}, f32[32,512]{1,0:T(8,128)}, u32[]{:S(2)}) copy-start(f32[32,512]{1,0:T(8,128)} %shard_map.104.mine_ref) | copy-start | bytes 196612
  8.7 1.1 %copy-start = (bf16[4,3,128,128]{3,2,1,0:T(8,128)(2,1)S(1)}, bf16[4,3,128,128]{3,2,1,0:T(8,128)(2,1)}, u32[]{:S(2)}) copy-start(bf16[4,3,128,128]{3,2,1,0:T(8,128)(2,1)} %shard_map.103) | copy-start | bytes 1179652
  8.8 0.6 %copy-start.2 = (f32[32,512]{1,0:T(8,128)}, f32[32,512]{1,0:T(8,128)S(1)}, u32[]{:S(2)}) copy-start(f32[32,512]{1,0:T(8,128)S(1)} %collective-permute-done.other_ref) | copy-start | bytes 196612
  10.4 1.3 %collective-permute-start.1 = (f32[32,512]{1,0:T(8,128)S(1)}, f32[32,512]{1,0:T(8,128)S(1)}, u32[]{:S(2)}, u32[]{:S(2)}) collective-permute-start(f32[32,512]{1,0:T(8,128)S(1)} %select_maximum_fusion), channel_id=1, source_target_pairs={{0,2},{2,0},{4,6},{6,4},{8,10},{10,8},{12,14},{14,12},{16,18},{18,... | collective-permute-start | bytes 196616 | tf_op jit(solution)/shard_map/ppermute | solution.py:17
  11.7 4.5 %collective-permute-start.2 = (f32[32,512]{1,0:T(8,128)S(1)}, f32[32,512]{1,0:T(8,128)S(1)}, u32[]{:S(2)}, u32[]{:S(2)}) collective-permute-start(f32[32,512]{1,0:T(8,128)S(1)} %fusion.5), channel_id=1, source_target_pairs={{0,4},{2,6},{4,0},{6,2},{8,12},{10,14},{12,8},{14,10},{16,20},{18,... | collective-permute-start | bytes 196616 | tf_op jit(solution)/shard_map/ppermute | solution.py:17
  16.3 4.3 %collective-permute-start.3 = (f32[32,512]{1,0:T(8,128)S(1)}, f32[32,512]{1,0:T(8,128)S(1)}, u32[]{:S(2)}, u32[]{:S(2)}) collective-permute-start(f32[32,512]{1,0:T(8,128)S(1)} %add.35), channel_id=1, source_target_pairs={{0,8},{2,10},{4,12},{6,14},{8,0},{10,2},{12,4},{14,6},{16,24},{18,... | collective-permute-start | bytes 196616 | tf_op jit(solution)/shard_map/ppermute | solution.py:17
  20.6 5.2 %collective-permute-start.4 = (f32[32,512]{1,0:T(8,128)S(1)}, f32[32,512]{1,0:T(8,128)S(1)}, u32[]{:S(2)}, u32[]{:S(2)}) collective-permute-start(f32[32,512]{1,0:T(8,128)S(1)} %add.36), channel_id=1, source_target_pairs={{0,16},{2,18},{4,20},{6,22},{8,24},{10,26},{12,28},{14,30},{16,0},... | collective-permute-start | bytes 196616 | tf_op jit(solution)/shard_map/ppermute | solution.py:17

commit v22 on v18

--- a/solution.py
+++ b/solution.py
@@ -124,11 +124,11 @@
         if emit == "updated":
             continue
         out_ref[:, r * width : (r + 1) * width] = lax.dot_general(
+            jnp.concatenate(fresh, axis=1),
             jnp.concatenate(starts, axis=1),
-            jnp.concatenate(fresh, axis=1),
             (((1,), (1,)), ((), ())),
             preferred_element_type=jnp.float32,
-        )
+        ).T
 
 
 def update(ratings, residual, tile_columns, occupied, chosen, user_factors, items, start, emit):

time: 31.1 us -> 31.1 us (level)
  no operation moved by 1% of the time
where the time goes in v22:
time: 31.1 us; the launch traced here: 30.9 us
  starting transfers between devices  10.1 us (32%)
  Pallas kernels  9.42 us (30%)
  waiting for transfers between devices  8.37 us (27%)
  other arithmetic  0.88 us (3%)
  matrix products  0.75 us (2%)
  between operations  0.71 us (2%)
  local copies, waits for them, and re-layouts  0.65 us (2%)
    ppermute x4, waiting for transfers between devices, all_sum(): x = x + lax.ppermute(x, axis, [(i, i ^ step) for i in range(n)])  8.26 us
    ppermute x4, starting transfers between devices, all_sum(): x = x + lax.ppermute(x, axis, [(i, i ^ step) for i in range(n)])  7.14 us
    pallas_call x2, Pallas kernels, update(): pl.pallas_call(functools.partial(update_kernel, emit=emit), grid=(rows //...  4.91 us
    pallas_call x1, Pallas kernels, tail(): pl.pallas_call(functools.partial(tail_kernel, scale=1.0 / user_total, roo...  4.5 us
    ppermute x1, starting transfers between devices, all_sum_parts(): other = lax.ppermute(x, axis, [(i, i ^ step) for i in range(n)])  2.94 us
    add x4, other arithmetic, all_sum(): x = x + lax.ppermute(x, axis, [(i, i ^ step) for i in range(n)])  0.67 us
  transfers between devices with their start and end apart: 5, of which 5 were waited for; matrix products, arithmetic and copies ran while one was open for 0% of the time, Pallas kernels for 7%

profile of v22, /device:TPU:0, one launch (start us, length us, event | category | flops | bytes accessed | tf_op | source)
XLA Modules:
  0.0 30.9 jit_solution(1679313828410532307)
XLA Ops:
  0.6 0.0 copy-start.3
  0.6 2.6 %shard_map.104.mine_ref = f32[32,512]{1,0:T(8,128)} custom-call(s32[4,3]{1,0:T(4,128)} %cols_ref.3, s32[4,3]{1,0:T(4,128)} %live_ref.3, s32[4]{0:T(128)} %chosen_ref.3, bf16[4,3,128,128]{3,2,1,0:T(8,128)(2,1)} %rat_ref.3, bf16[4,3,128,128]{3,2,1,0:T(8,128)(2,1)} %res_ref.3, bf16[64,512]{1,0:T(8,128)(2,1)} %user_ref.3, bf16[64,384]{1,0:T(8,128)(2,1)} %bitcast.23, ...), custom_call_target="tpu_custom_call" | custom-call | flops 37748736 | bytes 1245184 | tf_op jit(solution)/shard_map/pallas_call | solution.py:147
  3.3 2.9 %collective-permute-start = (f32[32,512]{1,0:T(8,128)}, f32[32,512]{1,0:T(8,128)S(1)}, u32[]{:S(2)}, u32[]{:S(2)}) collective-permute-start(f32[32,512]{1,0:T(8,128)} %shard_map.104.mine_ref), channel_id=1, source_target_pairs={{0,1},{1,0},{2,3},{3,2},{4,5},{5,4},{6,7},{7,6},{8,9},{9,8},{10,11... | collective-permute-start | bytes 196616 | tf_op jit(solution)/shard_map/ppermute | solution.py:31
  6.2 0.0 copy-done.3
  6.2 0.1 iota_compare_fusion.1
  6.3 0.0 copy-start.1
  6.3 2.3 %shard_map.103 = bf16[4,3,128,128]{3,2,1,0:T(8,128)(2,1)} custom-call(s32[4,3]{1,0:T(4,128)} %cols_ref.3, s32[4,3]{1,0:T(4,128)} %live_ref.3, s32[4]{0:T(128)} %chosen_ref.3, bf16[4,3,128,128]{3,2,1,0:T(8,128)(2,1)} %rat_ref.3, bf16[4,3,128,128]{3,2,1,0:T(8,128)(2,1)} %res_ref.3, bf16[64,512]{1,0:T(8,128)(2,1)} %user_ref.3, bf16[64,384]{1,0:T(8,128)(2,1)} %bitcast.24, ...), custom_call_target="tpu_custom_call" | custom-call | flops 37748736 | bytes 1245184 | tf_op jit(solution)/shard_map/pallas_call | solution.py:147
  8.6 0.0 copy-start
  8.6 0.1 collective-permute-done.other_ref
  8.7 0.0 copy-done.1
  8.7 0.0 copy-start.2
  8.7 0.6 %copy-done.2 = f32[32,512]{1,0:T(8,128)} copy-done((f32[32,512]{1,0:T(8,128)}, f32[32,512]{1,0:T(8,128)S(1)}, u32[]{:S(2)}) %copy-start.2) | copy-done | bytes 65560
  9.3 0.1 fusion.6
  9.5 0.1 convolution_add_fusion.1
  9.6 0.1 convolution_add_fusion.2
  9.7 0.0 copy-done
  9.7 0.2 fusion.3
  9.9 0.2 fusion
  10.1 0.1 select_reduce_fusion
  10.3 0.1 collective-permute-start.1
  10.3 1.2 %collective-permute-done.1 = f32[32,512]{1,0:T(8,128)S(1)} collective-permute-done((f32[32,512]{1,0:T(8,128)S(1)}, f32[32,512]{1,0:T(8,128)S(1)}, u32[]{:S(2)}, u32[]{:S(2)}) %collective-permute-start.1) | collective-permute-done | bytes 65568 | tf_op jit(solution)/shard_map/ppermute | solution.py:17
  11.6 2.1 %collective-permute-start.2 = (f32[32,512]{1,0:T(8,128)S(1)}, f32[32,512]{1,0:T(8,128)S(1)}, u32[]{:S(2)}, u32[]{:S(2)}) collective-permute-start(f32[32,512]{1,0:T(8,128)S(1)} %fusion.5), channel_id=1, source_target_pairs={{0,4},{2,6},{4,0},{6,2},{8,12},{10,14},{12,8},{14,10},{16,20},{18,... | collective-permute-start | bytes 196616 | tf_op jit(solution)/shard_map/ppermute | solution.py:17
  13.7 2.4 %collective-permute-done.2 = f32[32,512]{1,0:T(8,128)S(1)} collective-permute-done((f32[32,512]{1,0:T(8,128)S(1)}, f32[32,512]{1,0:T(8,128)S(1)}, u32[]{:S(2)}, u32[]{:S(2)}) %collective-permute-start.2) | collective-permute-done | bytes 65568 | tf_op jit(solution)/shard_map/ppermute | solution.py:17
  16.1 2.0 %collective-permute-start.3 = (f32[32,512]{1,0:T(8,128)S(1)}, f32[32,512]{1,0:T(8,128)S(1)}, u32[]{:S(2)}, u32[]{:S(2)}) collective-permute-start(f32[32,512]{1,0:T(8,128)S(1)} %add.35), channel_id=1, source_target_pairs={{0,8},{2,10},{4,12},{6,14},{8,0},{10,2},{12,4},{14,6},{16,24},{18,... | collective-permute-start | bytes 196616 | tf_op jit(solution)/shard_map/ppermute | solution.py:17
  18.1 2.4 %collective-permute-done.3 = f32[32,512]{1,0:T(8,128)S(1)} collective-permute-done((f32[32,512]{1,0:T(8,128)S(1)}, f32[32,512]{1,0:T(8,128)S(1)}, u32[]{:S(2)}, u32[]{:S(2)}) %collective-permute-start.3) | collective-permute-done | bytes 65568 | tf_op jit(solution)/shard_map/ppermute | solution.py:17
  20.5 3.0 %collective-permute-start.4 = (f32[32,512]{1,0:T(8,128)S(1)}, f32[32,512]{1,0:T(8,128)S(1)}, u32[]{:S(2)}, u32[]{:S(2)}) collective-permute-start(f32[32,512]{1,0:T(8,128)S(1)} %add.36), channel_id=1, source_target_pairs={{0,16},{2,18},{4,20},{6,22},{8,24},{10,26},{12,28},{14,30},{16,0},... | collective-permute-start | bytes 196616 | tf_op jit(solution)/shard_map/ppermute | solution.py:17
  23.5 2.2 %collective-permute-done.4 = f32[32,512]{1,0:T(8,128)S(1)} collective-permute-done((f32[32,512]{1,0:T(8,128)S(1)}, f32[32,512]{1,0:T(8,128)S(1)}, u32[]{:S(2)}, u32[]{:S(2)}) %collective-permute-start.4) | collective-permute-done | bytes 65568 | tf_op jit(solution)/shard_map/ppermute | solution.py:17
  25.7 0.6 %add.37.reduced_ref = f32[32,512]{1,0:T(8,128)} add(f32[32,512]{1,0:T(8,128)S(1)} %add.36, f32[32,512]{1,0:T(8,128)S(1)} %collective-permute-done.4) | non-fusion elementwise | flops 16384 | bytes 196608 | tf_op jit(solution)/shard_map/add | solution.py:17
  26.4 4.5 %shard_map.105 = (f32[32,512]{1,0:T(8,128)}, f32[32,384]{1,0:T(8,128)}) custom-call(f32[32,512]{1,0:T(8,128)} %add.37.reduced_ref, f32[32,512]{1,0:T(8,128)} %shard_map.104.mine_ref, f32[32,512]{1,0:T(8,128)} %copy-done.2, bf16[32,384]{1,0:T(8,128)(2,1)} %bitcast.22), custom_call_target="tpu_custom_call" | custom-call | flops 7864320 | bytes 278528 | tf_op jit(solution)/shard_map/pallas_call | solution.py:77
  (8 shorter events, 0.1 us)
Async XLA Ops:
  0.6 5.6 %copy-start.3 = (s32[4,3]{1,0:T(4,128)S(1)}, s32[4,3]{1,0:T(4,128)}, u32[]{:S(2)}) copy-start(s32[4,3]{1,0:T(4,128)} %cols_ref.3) | copy-start | bytes 148
  3.3 5.4 %collective-permute-start = (f32[32,512]{1,0:T(8,128)}, f32[32,512]{1,0:T(8,128)S(1)}, u32[]{:S(2)}, u32[]{:S(2)}) collective-permute-start(f32[32,512]{1,0:T(8,128)} %shard_map.104.mine_ref), channel_id=1, source_target_pairs={{0,1},{1,0},{2,3},{3,2},{4,5},{5,4},{6,7},{7,6},{8,9},{9,8},{10,11... | collective-permute-start | bytes 196616 | tf_op jit(solution)/shard_map/ppermute | solution.py:31
  6.3 2.4 %copy-start.1 = (f32[32,512]{1,0:T(8,128)S(1)}, f32[32,512]{1,0:T(8,128)}, u32[]{:S(2)}) copy-start(f32[32,512]{1,0:T(8,128)} %shard_map.104.mine_ref) | copy-start | bytes 196612
  8.6 1.1 %copy-start = (bf16[4,3,128,128]{3,2,1,0:T(8,128)(2,1)S(1)}, bf16[4,3,128,128]{3,2,1,0:T(8,128)(2,1)}, u32[]{:S(2)}) copy-start(bf16[4,3,128,128]{3,2,1,0:T(8,128)(2,1)} %shard_map.103) | copy-start | bytes 1179652
  8.7 0.6 %copy-start.2 = (f32[32,512]{1,0:T(8,128)}, f32[32,512]{1,0:T(8,128)S(1)}, u32[]{:S(2)}) copy-start(f32[32,512]{1,0:T(8,128)S(1)} %collective-permute-done.other_ref) | copy-start | bytes 196612
  10.3 1.3 %collective-permute-start.1 = (f32[32,512]{1,0:T(8,128)S(1)}, f32[32,512]{1,0:T(8,128)S(1)}, u32[]{:S(2)}, u32[]{:S(2)}) collective-permute-start(f32[32,512]{1,0:T(8,128)S(1)} %select_maximum_fusion), channel_id=1, source_target_pairs={{0,2},{2,0},{4,6},{6,4},{8,10},{10,8},{12,14},{14,12},{16,18},{18,... | collective-permute-start | bytes 196616 | tf_op jit(solution)/shard_map/ppermute | solution.py:17
  11.6 4.5 %collective-permute-start.2 = (f32[32,512]{1,0:T(8,128)S(1)}, f32[32,512]{1,0:T(8,128)S(1)}, u32[]{:S(2)}, u32[]{:S(2)}) collective-permute-start(f32[32,512]{1,0:T(8,128)S(1)} %fusion.5), channel_id=1, source_target_pairs={{0,4},{2,6},{4,0},{6,2},{8,12},{10,14},{12,8},{14,10},{16,20},{18,... | collective-permute-start | bytes 196616 | tf_op jit(solution)/shard_map/ppermute | solution.py:17
  16.1 4.3 %collective-permute-start.3 = (f32[32,512]{1,0:T(8,128)S(1)}, f32[32,512]{1,0:T(8,128)S(1)}, u32[]{:S(2)}, u32[]{:S(2)}) collective-permute-start(f32[32,512]{1,0:T(8,128)S(1)} %add.35), channel_id=1, source_target_pairs={{0,8},{2,10},{4,12},{6,14},{8,0},{10,2},{12,4},{14,6},{16,24},{18,... | collective-permute-start | bytes 196616 | tf_op jit(solution)/shard_map/ppermute | solution.py:17
  20.5 5.2 %collective-permute-start.4 = (f32[32,512]{1,0:T(8,128)S(1)}, f32[32,512]{1,0:T(8,128)S(1)}, u32[]{:S(2)}, u32[]{:S(2)}) collective-permute-start(f32[32,512]{1,0:T(8,128)S(1)} %add.36), channel_id=1, source_target_pairs={{0,16},{2,18},{4,20},{6,22},{8,24},{10,26},{12,28},{14,30},{16,0},... | collective-permute-start | bytes 196616 | tf_op jit(solution)/shard_map/ppermute | solution.py:17
